TPU v7x, 256 devices: a whole 4x4x8 slice. The times are simulated.
256 devices in a mesh: outer: 4 (over y_hi, core), dp: 4 (over x), mp: 16 (over z, y_lo).
Axes of the slice: x: 4, y: 4 (y_hi: 2, y_lo: 2; y = y_hi * 2 + y_lo), z: 8, core: 2. Of those that a mesh axis runs over, the one named last changes fastest.
Arguments:
- tokens: bfloat16 [4, 4096, 2048], P('outer', 'dp'), may hold values from -6 to 6
- cotangent: bfloat16 [4, 4096, 2048], P('outer', 'dp'), may hold values from -0.59765625 to 0.59765625
- gate_weight: bfloat16 [4, 2048, 6144], P('outer', 'dp', 'mp'), may hold values from -0.125 to 0.125
- up_weight: bfloat16 [4, 2048, 6144], P('outer', 'dp', 'mp'), may hold values from -0.125 to 0.125
- down_master: float32 [4, 6144, 2048], P('outer', 'mp', 'dp'), may hold values from -0.0375 to 0.0375
- first_moment: float32 [4, 6144, 2048], P('outer', 'mp', 'dp'), may hold values from -0.6 to 0.6
- second_moment: float32 [4, 6144, 2048], P('outer', 'mp', 'dp'), may hold values from 1 to 10
- anchor: float32 [6144, 2048], P('mp', 'dp'), may hold values from -0.0375 to 0.0375
- outer_momentum: float32 [6144, 2048], P('mp', 'dp'), may hold values from -0.00018 to 0.00018
Outputs:
- new_params: float32 [6144, 2048], P('mp', 'dp')
- first_out: float32 [4, 6144, 2048], P('outer', 'mp', 'dp')
- second_out: float32 [4, 6144, 2048], P('outer', 'mp', 'dp')
- momentum_out: float32 [6144, 2048], P('mp', 'dp')
- input_grad: bfloat16 [4, 4096, 2048], P('outer', ('dp', 'mp'))
All inputs are finite; a program needn't handle non-finite values.
Results may differ from a plain program's by a relative error of at most 0.023.
Values may be sent and summed in bfloat16 or wider, within the bound.
No kernel may reach another device: no remote copies, remote signals or barrier semaphores. Data moves between devices by JAX's collectives and lax.ppermute only.
A program may use at most 128 MiB of HBM per device.

v0:
```python
import jax
import jax.numpy as jnp
from jax import lax
from jax.sharding import PartitionSpec as P

bias_one = 1.0 - (0.9**50) ** 2
bias_two = 1.0 - (0.999**50) ** 2


def shards(
    tokens,
    cotangent,
    gate_weight,
    up_weight,
    down_master,
    first_moment,
    second_moment,
    anchor,
    outer_momentum,
):
    inputs = tokens[0]
    upstream = cotangent[0]
    gate_full, up_full = (
        lax.all_gather(gate_weight[0], "dp", axis=0, tiled=True),
        lax.all_gather(up_weight[0], "dp", axis=0, tiled=True),
    )
    gate_pre = jnp.dot(inputs, gate_full, preferred_element_type=jnp.float32)
    up_pre = jnp.dot(inputs, up_full, preferred_element_type=jnp.float32)
    gate_sigmoid = jax.nn.sigmoid(gate_pre)
    active = gate_pre * gate_sigmoid
    hidden = (active * up_pre).astype(jnp.bfloat16)
    master = down_master[0]
    down_half = master.astype(jnp.bfloat16)
    grad_hidden = lax.dot_general(
        upstream,
        lax.all_gather(down_half, "dp", axis=1, tiled=True),
        (((1,), (1,)), ((), ())),
        preferred_element_type=jnp.float32,
    )
    grad_up = (grad_hidden * active).astype(jnp.bfloat16)
    grad_gate = (
        grad_hidden * up_pre * gate_sigmoid * (1.0 + gate_pre * (1.0 - gate_sigmoid))
    ).astype(jnp.bfloat16)
    first_part = lax.dot_general(
        grad_gate, gate_full, (((1,), (1,)), ((), ())), preferred_element_type=jnp.float32
    )
    second_part = lax.dot_general(
        grad_up, up_full, (((1,), (1,)), ((), ())), preferred_element_type=jnp.float32
    )
    input_grad = lax.psum_scatter(
        (first_part + second_part).astype(jnp.bfloat16), "mp", scatter_dimension=0, tiled=True
    )
    full_grad = lax.dot_general(
        hidden, upstream, (((0,), (0,)), ((), ())), preferred_element_type=jnp.float32
    )
    grad_down = lax.psum_scatter(
        full_grad.astype(jnp.bfloat16), "dp", scatter_dimension=1, tiled=True
    ).astype(jnp.float32)
    first_new = 0.9 * first_moment[0] + 0.1 * grad_down
    second_new = 0.999 * second_moment[0] + 0.001 * grad_down * grad_down
    adam_step = first_new / bias_one / (jnp.sqrt(second_new / bias_two) + 1e-08) + 0.1 * master
    inner_params = master - 0.001 * adam_step
    drift_local = anchor - inner_params
    mean_drift = lax.psum(drift_local.astype(jnp.bfloat16), "outer").astype(
        jnp.float32
    ) / lax.axis_size("outer")
    momentum_out = 0.9 * outer_momentum + mean_drift
    new_params = anchor - 0.7 * (mean_drift + 0.9 * momentum_out)
    return (new_params, first_new[None], second_new[None], momentum_out, input_grad[None])


def solution(mesh):
    return jax.shard_map(
        shards,
        mesh=mesh,
        in_specs=(
            P("outer", "dp", None),
            P("outer", "dp", None),
            P("outer", "dp", "mp"),
            P("outer", "dp", "mp"),
            P("outer", "mp", "dp"),
            P("outer", "mp", "dp"),
            P("outer", "mp", "dp"),
            P("mp", "dp"),
            P("mp", "dp"),
        ),
        out_specs=(
            P("mp", "dp"),
            P("outer", "mp", "dp"),
            P("outer", "mp", "dp"),
            P("mp", "dp"),
            P("outer", ("dp", "mp"), None),
        ),
        check_vma=False,
    )
```

profile of v0, /device:TPU:8, one launch (start us, length us, event | category | flops | bytes accessed | tf_op | source)
XLA Modules:
  0.0 293.5 jit_solution(9334009142262254615)
XLA Ops:
  7.2 0.0 all-gather.8.cloned.1.call-start
  7.2 0.7 all-gather.8.cloned.1.call-update
  7.9 0.0 all-gather.10.cloned.1.call-start
  7.9 0.7 all-gather.10.cloned.1.call-update
  8.6 0.0 all-gather.6.cloned.1.call-start
  8.7 1.9 bitcast_convert_fusion
  10.6 0.0 all-gather.6.cloned.1.call-update
  10.6 0.0 reduce-scatter.3.cloned.1.call-start
  10.7 31.1 %all-gather.8.cloned.1.call-done = bf16[1,2048,384]{2,1,0:T(8,128)(2,1)} async-done(((bf16[1,512,384]{2,1,0:T(8,128)(2,1)}), bf16[1,2048,384]{2,1,0:T(8,128)(2,1)}) %all-gather.8.cloned.1.call-update) | async-done | bytes 1572880 | tf_op jit(solution)/shard_map/all_gather | solution.py:24
  41.8 5.0 %fusion.6 = f32[1024,384]{1,0:T(8,128)S(1)} fusion(bf16[1,1024,2048]{2,1,0:T(8,128)(2,1)} %param.9, bf16[1,2048,384]{2,1,0:T(8,128)(2,1)} %all-gather.8.cloned.1.call-done), kind=kOutput, calls=%fused_computation.7 | convolution fusion | flops 1610612736 | bytes 7340032 | tf_op jit(solution)/shard_map/dot_general | solution.py:27
  46.8 26.0 %all-gather.10.cloned.1.call-done = bf16[1,2048,384]{2,1,0:T(8,128)(2,1)} async-done(((bf16[1,512,384]{2,1,0:T(8,128)(2,1)}), bf16[1,2048,384]{2,1,0:T(8,128)(2,1)}) %all-gather.10.cloned.1.call-update) | async-done | bytes 1572880 | tf_op jit(solution)/shard_map/all_gather | solution.py:25
  72.8 0.0 copy-start.3
  72.8 5.1 %fusion.4 = f32[1024,384]{1,0:T(8,128)S(1)} fusion(bf16[1,1024,2048]{2,1,0:T(8,128)(2,1)} %param.9, bf16[1,2048,384]{2,1,0:T(8,128)(2,1)} %all-gather.10.cloned.1.call-done), kind=kOutput, calls=%fused_computation.5 | convolution fusion | flops 1610612736 | bytes 7340032 | tf_op jit(solution)/shard_map/dot_general | solution.py:28
  77.9 0.0 copy-start
  77.9 1.1 copy-done
  79.1 0.0 copy-done.3
  79.1 3.2 %fusion.8 = bf16[384,2048]{1,0:T(8,128)(2,1)} fusion(bf16[1,1024,2048]{2,1,0:T(8,128)(2,1)S(1)} %copy-done.3, f32[1024,384]{1,0:T(8,128)S(1)} %fusion.4, f32[1024,384]{1,0:T(8,128)S(1)} %fusion.6), kind=kOutput, calls=%fused_computation.9 | convolution fusion | flops 1613758464 | bytes 8912896 | tf_op jit(solution)/shard_map/dot_general | solution.py:53
  82.3 0.0 reduce-scatter.3.cloned.1.call-update
  82.3 0.0 all-reduce.2.cloned.1.call-start
  82.4 22.0 %all-gather.6.cloned.1.call-done = bf16[384,2048]{1,0:T(8,128)(2,1)} async-done(((bf16[384,512]{1,0:T(8,128)(2,1)}), bf16[384,2048]{1,0:T(8,128)(2,1)}) %all-gather.6.cloned.1.call-update) | async-done | bytes 1572880 | tf_op jit(solution)/shard_map/all_gather | solution.py:36
  104.4 5.0 %fusion = f32[1024,384]{1,0:T(8,128)S(1)} fusion(bf16[384,2048]{1,0:T(8,128)(2,1)} %all-gather.6.cloned.1.call-done, bf16[1,1024,2048]{2,1,0:T(8,128)(2,1)} %param.10), kind=kOutput, calls=%fused_computation.1 | convolution fusion | flops 1610612736 | bytes 7340032 | tf_op jit(solution)/shard_map/dot_general | solution.py:34
  109.4 7.9 %fusion.13 = f32[1024,2048]{1,0:T(8,128)} fusion(bf16[1,2048,384]{2,1,0:T(8,128)(2,1)} %all-gather.8.cloned.1.call-done, f32[1024,384]{1,0:T(8,128)S(1)} %fusion.6, f32[1024,384]{1,0:T(8,128)S(1)} %fusion, f32[1024,384]{1,0:T(8,128)} %copy-done), kind=kOutput, calls=%fused_computation.12 | convolution fusion | flops 1614544896 | bytes 14680064 | tf_op jit(solution)/shard_map/dot_general | solution.py:44
  117.2 17.9 %reduce-scatter.3.cloned.1.call-done = bf16[384,512]{1,0:T(8,128)(2,1)} async-done(((bf16[384,2048]{1,0:T(8,128)(2,1)}), bf16[384,512]{1,0:T(8,128)(2,1)}) %reduce-scatter.3.cloned.1.call-update) | async-done | bytes 393232 | tf_op jit(solution)/shard_map/reduce_scatter | solution.py:56
  135.1 3.9 %fusion.25 = (f32[1,384,512]{2,1,0:T(8,128)}, bf16[384,512]{1,0:T(8,128)(2,1)}, f32[1,384,512]{2,1,0:T(8,128)}) fusion(bf16[384,512]{1,0:T(8,128)(2,1)} %reduce-scatter.3.cloned.1.call-done, f32[1,384,512]{2,1,0:T(8,128)} %param.15, f32[384,512]{1,0:T(8,128)} %param.16, f32[1,384,512]{2,1,0:T(8,128)} %param.14, f32[1,384,512]{2,1,0:T(8,128)} %param.13), kind=kLoop, calls=%fused_computation.36 | loop fusion | flops 3538944 | bytes 5505024 | tf_op jit(solution)/shard_map/broadcast_in_dim | solution.py:69
  139.0 0.0 all-reduce.2.cloned.1.call-update
  139.1 0.0 reduce-scatter.5.cloned.1.call-start
  139.1 8.3 %add_convert_fusion = bf16[1024,2048]{1,0:T(8,128)(2,1)} fusion(f32[1024,2048]{1,0:T(8,128)} %fusion.13, bf16[1,2048,384]{2,1,0:T(8,128)(2,1)} %all-gather.10.cloned.1.call-done, f32[1024,384]{1,0:T(8,128)S(1)} %fusion, f32[1024,384]{1,0:T(8,128)S(1)} %fusion.6), kind=kOutput, calls=%fused_computation | convolution fusion | flops 1617166336 | bytes 17301504 | tf_op jit(solution)/shard_map/dot_general | solution.py:47
  147.4 0.0 copy-start.1
  147.4 0.0 copy-start.2
  147.4 0.0 reduce-scatter.5.cloned.1.call-update
  147.5 37.1 %all-reduce.2.cloned.1.call-done = bf16[384,512]{1,0:T(8,128)(2,1)} async-done(((bf16[384,512]{1,0:T(8,128)(2,1)}), bf16[384,512]{1,0:T(8,128)(2,1)}) %all-reduce.2.cloned.1.call-update) | async-done | bytes 393232 | tf_op jit(solution)/shard_map/psum | solution.py:64
  184.6 0.0 copy-done.1
  184.6 0.0 copy-done.2
  184.6 2.4 multiply_subtract_fusion
  187.0 99.7 %reduce-scatter.5.cloned.1.call-done = bf16[64,2048]{1,0:T(8,128)(2,1)} async-done(((bf16[1024,2048]{1,0:T(8,128)(2,1)}), bf16[64,2048]{1,0:T(8,128)(2,1)}) %reduce-scatter.5.cloned.1.call-update) | async-done | bytes 262160 | tf_op jit(solution)/shard_map/reduce_scatter | solution.py:50
Async XLA Ops:
  7.2 34.6 %all-gather.8.cloned.1.call-start = ((), (), s32[]{:S(2)}) async-start(), calls=%async_computation.6 | async-start | bytes 1966080 | tf_op jit(solution)/shard_map/all_gather | solution.py:24
  7.9 64.9 %all-gather.10.cloned.1.call-start = ((), (), s32[]{:S(2)}) async-start(), calls=%async_computation.7 | async-start | bytes 1966080 | tf_op jit(solution)/shard_map/all_gather | solution.py:25
  8.6 95.7 %all-gather.6.cloned.1.call-start = ((), (), s32[]{:S(2)}) async-start(), calls=%async_computation.4 | async-start | bytes 1966080 | tf_op jit(solution)/shard_map/all_gather | solution.py:36
  10.6 124.5 %reduce-scatter.3.cloned.1.call-start = ((), (), s32[]{:S(2)}) async-start(), calls=%async_computation.2 | async-start | bytes 1966080 | tf_op jit(solution)/shard_map/reduce_scatter | solution.py:56
  72.8 6.3 %copy-start.3 = (bf16[1,1024,2048]{2,1,0:T(8,128)(2,1)S(1)}, bf16[1,1024,2048]{2,1,0:T(8,128)(2,1)}, u32[]{:S(2)}) copy-start(bf16[1,1024,2048]{2,1,0:T(8,128)(2,1)} %param.10) | copy-start | bytes 12582916
  77.9 1.2 copy-start
  82.3 102.3 %all-reduce.2.cloned.1.call-start = ((), (), s32[]{:S(2)}) async-start(), calls=%async_computation.3 | async-start | bytes 786432 | tf_op jit(solution)/shard_map/psum | solution.py:64
  139.1 147.6 %reduce-scatter.5.cloned.1.call-start = ((), (), s32[]{:S(2)}) async-start(), calls=%async_computation.5 | async-start | bytes 4456448 | tf_op jit(solution)/shard_map/reduce_scatter | solution.py:50
  147.4 37.2 %copy-start.1 = (f32[384,512]{1,0:T(8,128)S(1)}, f32[384,512]{1,0:T(8,128)}, u32[]{:S(2)}) copy-start(f32[384,512]{1,0:T(8,128)} %param.16) | copy-start | bytes 2359300
  147.4 37.2 %copy-start.2 = (f32[384,512]{1,0:T(8,128)S(1)}, f32[384,512]{1,0:T(8,128)}, u32[]{:S(2)}) copy-start(f32[384,512]{1,0:T(8,128)} %param.17) | copy-start | bytes 2359300
Sparse Core Ops, SparseCore 0:
  9.8 31.9 all-gather.7
  43.6 29.1 all-gather.9
  75.2 29.1 all-gather.5
  106.8 28.3 reduce-scatter.2
  139.2 45.3 all-reduce.1
  187.7 98.9 reduce-scatter.4
where the time goes:
time: 295 us; the launch traced here: 294 us
  waiting for transfers between devices  235 us (80%)
  matrix products  34.6 us (12%)
  between operations  14.1 us (5%)
  other arithmetic  8.25 us (3%)
    reduce_scatter x1, waiting for transfers between devices, shards(): lax.psum_scatter((first_part + second_part).astype(jnp.bfloat16), 'mp', s...  99.7 us
    psum x1, waiting for transfers between devices, shards(): lax.psum(drift_local.astype(jnp.bfloat16), 'outer').astype(jnp.float32)  37.1 us
    all_gather x1, waiting for transfers between devices, shards(): lax.all_gather(gate_weight[0], 'dp', axis=0, tiled=True)  31.1 us
    all_gather x1, waiting for transfers between devices, shards(): lax.all_gather(up_weight[0], 'dp', axis=0, tiled=True)  26 us
    all_gather x1, waiting for transfers between devices, shards(): lax.all_gather(down_half, 'dp', axis=1, tiled=True)  22 us
    reduce_scatter x1, waiting for transfers between devices, shards(): lax.psum_scatter(full_grad.astype(jnp.bfloat16), 'dp', scatter_dimension=...  17.9 us
    dot_general x1, matrix products, shards(): lax.dot_general(grad_up, up_full, (((1,), (1,)), ((), ())), preferred_ele...  8.32 us
    dot_general x1, matrix products, shards(): lax.dot_general(grad_gate, gate_full, (((1,), (1,)), ((), ())), preferred...  7.85 us
  transfers between devices with their start and end apart: 6, of which 6 were waited for; matrix products, arithmetic and copies ran while one was open for 13% of the time, Pallas kernels for 0%

commit v1 on v0

v1 whole, which is shorter than its diff:
```python
import jax
import jax.numpy as jnp
from jax import lax
from jax.sharding import PartitionSpec as P

bias_one = 1.0 - (0.9**50) ** 2
bias_two = 1.0 - (0.999**50) ** 2


def _shift(n, s):
    return [(i, (i + s) % n) for i in range(n)]


def shards(
    tokens,
    cotangent,
    gate_weight,
    up_weight,
    down_master,
    first_moment,
    second_moment,
    anchor,
    outer_momentum,
):
    ndp = lax.axis_size("dp")
    j = lax.axis_index("dp")
    inputs = tokens[0]
    upstream = cotangent[0]
    master = down_master[0]
    down_half = master.astype(jnp.bfloat16)
    ff = master.shape[0]

    shard = jnp.concatenate([gate_weight[0], up_weight[0], down_half.T], axis=1)
    rows = shard.shape[0]
    half = rows // 2
    a, b = shard[:half], shard[half:]
    pieces = [(j, 0, a), (j, 1, b)]
    for s in range(1, ndp):
        a = lax.ppermute(a, "dp", _shift(ndp, 1))
        b = lax.ppermute(b, "dp", _shift(ndp, -1))
        pieces.append(((j - s) % ndp, 0, a))
        pieces.append(((j + s) % ndp, 1, b))

    gu_pre = None
    grad_hidden = None
    weights_full = jnp.zeros((rows * ndp, 2 * ff), jnp.bfloat16)
    for src, h, piece in pieces:
        start = src * rows + h * half
        xs = lax.dynamic_slice_in_dim(inputs, start, half, axis=1)
        gs = lax.dynamic_slice_in_dim(upstream, start, half, axis=1)
        p1 = jnp.dot(xs, piece[:, : 2 * ff], preferred_element_type=jnp.float32)
        p2 = jnp.dot(gs, piece[:, 2 * ff :], preferred_element_type=jnp.float32)
        gu_pre = p1 if gu_pre is None else gu_pre + p1
        grad_hidden = p2 if grad_hidden is None else grad_hidden + p2
        weights_full = lax.dynamic_update_slice(weights_full, piece[:, : 2 * ff], (start, 0))

    gate_pre = gu_pre[:, :ff]
    up_pre = gu_pre[:, ff:]
    gate_sigmoid = jax.nn.sigmoid(gate_pre)
    active = gate_pre * gate_sigmoid
    hidden = (active * up_pre).astype(jnp.bfloat16)
    grad_up = (grad_hidden * active).astype(jnp.bfloat16)
    grad_gate = (
        grad_hidden * up_pre * gate_sigmoid * (1.0 + gate_pre * (1.0 - gate_sigmoid))
    ).astype(jnp.bfloat16)

    full_grad = lax.dot_general(
        hidden, upstream, (((0,), (0,)), ((), ())), preferred_element_type=jnp.float32
    )
    cols = full_grad.shape[1] // ndp
    grad_down = lax.dynamic_slice_in_dim(full_grad, j * cols, cols, axis=1)
    for s in range(1, ndp):
        blk = lax.dynamic_slice_in_dim(full_grad, ((j + s) % ndp) * cols, cols, axis=1)
        got = lax.ppermute(blk.astype(jnp.bfloat16), "dp", _shift(ndp, s))
        grad_down = grad_down + got.astype(jnp.float32)

    both = jnp.concatenate([grad_gate, grad_up], axis=1)
    partial_sum = lax.dot_general(
        both, weights_full, (((1,), (1,)), ((), ())), preferred_element_type=jnp.float32
    )
    input_grad = lax.psum_scatter(
        partial_sum.astype(jnp.bfloat16), "mp", scatter_dimension=0, tiled=True
    )

    first_new = 0.9 * first_moment[0] + 0.1 * grad_down
    second_new = 0.999 * second_moment[0] + 0.001 * grad_down * grad_down
    adam_step = first_new / bias_one / (jnp.sqrt(second_new / bias_two) + 1e-08) + 0.1 * master
    inner_params = master - 0.001 * adam_step
    drift_local = anchor - inner_params

    nout = lax.axis_size("outer")
    total = drift_local.astype(jnp.bfloat16)
    step = 1
    while step < nout:
        perm = [(i, i ^ step) for i in range(nout)]
        mine = total.astype(jnp.bfloat16)
        total = mine.astype(jnp.float32) + lax.ppermute(mine, "outer", perm).astype(jnp.float32)
        step *= 2
    mean_drift = total / nout
    momentum_out = 0.9 * outer_momentum + mean_drift
    new_params = anchor - 0.7 * (mean_drift + 0.9 * momentum_out)
    return (new_params, first_new[None], second_new[None], momentum_out, input_grad[None])


def solution(mesh):
    return jax.shard_map(
        shards,
        mesh=mesh,
        in_specs=(
            P("outer", "dp", None),
            P("outer", "dp", None),
            P("outer", "dp", "mp"),
            P("outer", "dp", "mp"),
            P("outer", "mp", "dp"),
            P("outer", "mp", "dp"),
            P("outer", "mp", "dp"),
            P("mp", "dp"),
            P("mp", "dp"),
        ),
        out_specs=(
            P("mp", "dp"),
            P("outer", "mp", "dp"),
            P("outer", "mp", "dp"),
            P("mp", "dp"),
            P("outer", ("dp", "mp"), None),
        ),
        check_vma=False,
    )
```

time: 295 us -> 201 us (0.68)
  waiting for transfers between devices: 235 us -> 110 us
  starting transfers between devices: 0.24 us -> 13.9 us
  local copies, waits for them, and re-layouts: 1.16 us -> 10.4 us
  matrix products: 34.6 us -> 43.5 us
    all_gather x3 -> x0, waiting for transfers between devices: 79 us -> none  [the longest x1 31.1 us: shards(): lax.all_gather(gate_weight[0], 'dp', axis=0, tiled=True)]
    reduce_scatter x2 -> x1, waiting for transfers between devices: 118 us -> 47.6 us  [shards(): lax.psum_scatter(partial_sum.astype(jnp.bfloat16), 'mp', scatter_dimensio...]
    ppermute x0 -> x11, waiting for transfers between devices: none -> 62.8 us  [the longest x2 30.7 us: shards(): lax.ppermute(mine, 'outer', perm).astype(jnp.float32)]
    psum x1 -> x0, waiting for transfers between devices: 37.1 us -> none  [shards(): lax.psum(drift_local.astype(jnp.bfloat16), 'outer').astype(jnp.float32)]
    ppermute x0 -> x11, starting transfers between devices: none -> 13.8 us  [the longest x3 5.99 us: shards(): b = lax.ppermute(b, 'dp', _shift(ndp, -1))]
    dot_general x5 -> x17, matrix products: 31.3 us -> 39.4 us  [the longest x8 19 us: shards(): p2 = jnp.dot(gs, piece[:, 2 * ff:], preferred_element_type=jnp.float32)]
    dynamic_update_slice x0 -> x6, local copies, waits for them, and re-layouts: none -> 4.9 us  [shards(): lax.dynamic_update_slice(weights_full, piece[:, :2 * ff], (start, 0))]
  transfers between devices with their start and end apart: 6 -> 12, of which waited for: 6 -> 8; matrix products, arithmetic and copies ran while one was open for 13% -> 21% of each run, Pallas kernels for 0% -> 0%
where the time goes in v1:
time: 201 us; the launch traced here: 200 us
  waiting for transfers between devices  110 us (55%)
  matrix products  43.5 us (22%)
  between operations  14.3 us (7%)
  starting transfers between devices  13.9 us (7%)
  local copies, waits for them, and re-layouts  10.4 us (5%)
  other arithmetic  7.23 us (4%)
    reduce_scatter x1, waiting for transfers between devices, shards(): lax.psum_scatter(partial_sum.astype(jnp.bfloat16), 'mp', scatter_dimensio...  47.6 us
    ppermute x2, waiting for transfers between devices, shards(): lax.ppermute(mine, 'outer', perm).astype(jnp.float32)  30.7 us
    dot_general x8, matrix products, shards(): p2 = jnp.dot(gs, piece[:, 2 * ff:], preferred_element_type=jnp.float32)  19 us
    ppermute x3, waiting for transfers between devices, shards(): got = lax.ppermute(blk.astype(jnp.bfloat16), 'dp', _shift(ndp, s))  15.2 us
    dot_general x8, matrix products, shards(): p1 = jnp.dot(xs, piece[:, :2 * ff], preferred_element_type=jnp.float32)  13.5 us
    ppermute x3, waiting for transfers between devices, shards(): a = lax.ppermute(a, 'dp', _shift(ndp, 1))  12.8 us
    dot_general x1, matrix products, shards(): lax.dot_general(both, weights_full, (((1,), (1,)), ((), ())), preferred_e...  6.95 us
    ppermute x3, starting transfers between devices, shards(): b = lax.ppermute(b, 'dp', _shift(ndp, -1))  5.99 us
  transfers between devices with their start and end apart: 12, of which 8 were waited for; matrix products, arithmetic and copies ran while one was open for 21% of the time, Pallas kernels for 0%

profile of v1, /device:TPU:8, one launch (start us, length us, event | category | flops | bytes accessed | tf_op | source)
XLA Modules:
  0.0 199.7 jit_solution(14258007871237274156)
XLA Ops:
  7.2 0.0 reduce-scatter.2.cloned.1.call-start
  7.2 1.2 copy.14
  8.4 1.2 copy.15
  9.6 1.2 fusion.63
  10.7 0.1 pad_maximum_fusion
  10.8 0.1 fusion.103
  10.9 1.6 collective-permute-start
  12.5 1.7 collective-permute-start.1
  14.2 3.3 %fusion.43 = f32[1024,768]{0,1:T(8,128)} fusion(bf16[1,1024,2048]{2,1,0:T(8,128)(2,1)} %param.9, s32[]{:T(128)S(6)} %select_n.84, bf16[512,384]{0,1:T(8,128)(2,1)S(1)} %bitcast.101, bf16[512,384]{0,1:T(8,128)(2,1)S(1)} %bitcast.96), kind=kOutput, calls=%fused_computation.62 | convolution fusion | flops 403439616 | bytes 4456452 | tf_op jit(solution)/shard_map/dot_general | solution.py:51
  17.5 2.6 %fusion.25 = f32[1024,384]{0,1:T(8,128)} fusion(bf16[1,1024,2048]{2,1,0:T(8,128)(2,1)} %param.10, s32[]{:T(128)S(6)} %select_n.84, bf16[512,384]{0,1:T(8,128)(2,1)S(1)} %fusion.63), kind=kOutput, calls=%fused_computation.46 | convolution fusion | flops 201326592 | bytes 2293764 | tf_op jit(solution)/shard_map/dot_general | solution.py:52
  20.1 2.1 %broadcast_in_dim.14 = bf16[2048,768]{0,1:T(8,128)(2,1)} broadcast(bf16[]{:T(256)} %constant.108.clone.1), dimensions={} | broadcast | bytes 3145730 | tf_op jit(solution)/shard_map/broadcast_in_dim | solution.py:46
  22.2 0.8 constant_dynamic-update-slice_fusion
  23.0 3.3 %fusion.45 = f32[1024,768]{0,1:T(8,128)} fusion(bf16[1,1024,2048]{2,1,0:T(8,128)(2,1)} %param.9, s32[]{:T(128)S(6)} %select_n.83, bf16[512,384]{0,1:T(8,128)(2,1)S(1)} %bitcast.98, bf16[512,384]{0,1:T(8,128)(2,1)S(1)} %bitcast.103), kind=kOutput, calls=%fused_computation.64 | convolution fusion | flops 403439616 | bytes 4456452 | tf_op jit(solution)/shard_map/dot_general | solution.py:51
  26.3 2.6 %fusion.27 = f32[1024,384]{0,1:T(8,128)} fusion(bf16[1,1024,2048]{2,1,0:T(8,128)(2,1)} %param.10, s32[]{:T(128)S(6)} %select_n.83, bf16[512,384]{0,1:T(8,128)(2,1)S(1)} %fusion.63), kind=kOutput, calls=%fused_computation.48 | convolution fusion | flops 201326592 | bytes 2293764 | tf_op jit(solution)/shard_map/dot_general | solution.py:52
  28.9 0.8 fusion.82
  29.8 0.0 collective-permute-done.1
  29.8 1.5 collective-permute-start.3
  31.3 2.6 %fusion.21 = f32[1024,384]{0,1:T(8,128)} fusion(bf16[1,1024,2048]{2,1,0:T(8,128)(2,1)} %param.10, s32[]{:T(128)S(6)} %select_n.88, bf16[256,1152]{0,1:T(8,128)(2,1)S(1)} %collective-permute-done.1), kind=kOutput, calls=%fused_computation.42 | convolution fusion | flops 201326592 | bytes 2293764 | tf_op jit(solution)/shard_map/dot_general | solution.py:52
  33.9 1.8 fusion.39
  35.7 0.6 collective-permute-start.2
  36.3 1.6 fusion.23
  37.9 0.8 slice_dynamic-update-slice_fusion.5
  38.7 0.6 fusion.41
  39.3 0.8 slice_dynamic-update-slice_fusion.4
  40.1 4.1 %collective-permute-done.3 = bf16[256,1152]{0,1:T(8,128)(2,1)S(1)} collective-permute-done((bf16[256,1152]{0,1:T(8,128)(2,1)S(1)}, bf16[256,1152]{0,1:T(8,128)(2,1)S(1)}, u32[]{:S(2)}, u32[]{:S(2)}) %collective-permute-start.3) | collective-permute-done | bytes 589856 | tf_op jit(solution)/shard_map/ppermute | solution.py:40
  44.3 2.7 %collective-permute-start.5 = (bf16[256,1152]{0,1:T(8,128)(2,1)S(1)}, bf16[256,1152]{0,1:T(8,128)(2,1)S(1)}, u32[]{:S(2)}, u32[]{:S(2)}) collective-permute-start(bf16[256,1152]{0,1:T(8,128)(2,1)S(1)} %collective-permute-done.3), channel_id=1, source_target_pairs={{0,48},{16,0},{32,16},{48,32},{1,49},{17,1},{33,17},{49,33},{2,50}... | collective-permute-start | bytes 1769480 | tf_op jit(solution)/shard_map/ppermute | solution.py:40
  47.0 1.6 fusion.17
  48.6 0.6 fusion.35
  49.2 2.1 %collective-permute-done.2 = bf16[256,1152]{0,1:T(8,128)(2,1)S(1)} collective-permute-done((bf16[256,1152]{0,1:T(8,128)(2,1)S(1)}, bf16[256,1152]{0,1:T(8,128)(2,1)S(1)}, u32[]{:S(2)}, u32[]{:S(2)}) %collective-permute-start.2) | collective-permute-done | bytes 589856 | tf_op jit(solution)/shard_map/ppermute | solution.py:39
  51.2 0.0 collective-permute-start.4
  51.2 0.8 slice_dynamic-update-slice_fusion.3
  52.1 0.8 slice_dynamic-update-slice_fusion.2
  52.9 1.6 fusion.19
  54.5 0.6 fusion.37
  55.1 10.7 %collective-permute-done.4 = bf16[256,1152]{0,1:T(8,128)(2,1)S(1)} collective-permute-done((bf16[256,1152]{0,1:T(8,128)(2,1)S(1)}, bf16[256,1152]{0,1:T(8,128)(2,1)S(1)}, u32[]{:S(2)}, u32[]{:S(2)}) %collective-permute-start.4) | collective-permute-done | bytes 589856 | tf_op jit(solution)/shard_map/ppermute | solution.py:39
  65.8 0.8 slice_dynamic-update-slice_fusion.1
  66.6 1.6 fusion.15
  68.2 0.6 fusion.33
  68.8 0.0 copy-start.9
  68.8 0.8 copy-done.9
  69.6 0.8 slice_dynamic-update-slice_fusion
  70.4 2.6 %add_add_fusion = f32[1024,768]{0,1:T(8,128)S(1)} fusion(f32[1024,768]{0,1:T(8,128)S(1)} %fusion.33, f32[1024,768]{0,1:T(8,128)S(1)} %fusion.35, f32[1024,768]{0,1:T(8,128)S(1)} %fusion.37, f32[1024,768]{0,1:T(8,128)S(1)} %fusion.39, f32[1024,768]{0,1:T(8,128)S(1)} %fusion.41, f32[1024,768]{0,1:T(8,128)S(1)} %copy-done.1, f32[1024,768]{0,1:T(8,128)S(1)} %copy-done, ...), kind=kOutput, calls=%fused_computation.3 | convolution fusion | flops 408158208 | bytes 26083332 | tf_op jit(solution)/shard_map/dot_general | solution.py:51
  73.1 4.9 %multiply_convert_fusion.1 = (bf16[1024,384]{0,1:T(8,128)(2,1)S(1)}, bf16[1024,384]{0,1:T(8,128)(2,1)S(1)}) fusion(f32[1024,768]{0,1:T(8,128)S(1)} %add_add_fusion, bf16[256,1152]{0,1:T(8,128)(2,1)} %copy-done.9, bf16[1,1024,2048]{2,1,0:T(8,128)(2,1)} %param.10, s32[]{:T(128)S(6)} %select_n.96, f32[1024,384]{0,1:T(8,128)} %fusion.15, ...), kind=kOutput, calls=%fused_computation.8 | convolution fusion | flops 209190912 | bytes 16449540 | tf_op jit(solution)/shard_map/dot_general | solution.py:52
  78.0 6.9 %convolution_convert_fusion = bf16[1024,2048]{1,0:T(8,128)(2,1)} fusion(bf16[2048,768]{0,1:T(8,128)(2,1)} %slice_dynamic-update-slice_fusion, bf16[1024,384]{0,1:T(8,128)(2,1)S(1)} %get-tuple-element.10, bf16[1024,384]{0,1:T(8,128)(2,1)S(1)} %get-tuple-element.9), kind=kOutput, calls=%fused_computation.2 | convolution fusion | flops 3226468352 | bytes 8912896 | tf_op jit(solution)/shard_map/dot_general | solution.py:78
  84.9 0.0 reduce-scatter.2.cloned.1.call-update
  85.0 0.0 copy-start.6
  85.0 4.1 %fusion = f32[384,2048]{1,0:T(8,128)S(1)} fusion(bf16[1,1024,2048]{2,1,0:T(8,128)(2,1)} %param.10, f32[1024,768]{0,1:T(8,128)S(1)} %add_add_fusion), kind=kOutput, calls=%fused_computation | convolution fusion | flops 1612972032 | bytes 10485760 | tf_op jit(solution)/shard_map/dot_general | solution.py:67
  89.1 0.0 copy-start.7
  89.1 0.0 copy-start.8
  89.1 0.0 copy-start.10
  89.1 0.2 dynamic-slice_convert_fusion.2
  89.3 0.1 collective-permute-start.6
  89.4 1.0 collective-permute-start.7
  90.4 2.3 %collective-permute-start.8 = (bf16[384,512]{1,0:T(8,128)(2,1)S(1)}, bf16[384,512]{1,0:T(8,128)(2,1)S(1)}, u32[]{:S(2)}, u32[]{:S(2)}) collective-permute-start(bf16[384,512]{1,0:T(8,128)(2,1)S(1)} %get-tuple-element.12), channel_id=1, source_target_pairs={{0,48},{16,0},{32,16},{48,32},{1,49},{17,1},{33,17},{49,33},{2,50}... | collective-permute-start | bytes 1179656 | tf_op jit(solution)/shard_map/ppermute | solution.py:74
  92.6 14.6 %collective-permute-done.6 = bf16[384,512]{1,0:T(8,128)(2,1)S(1)} collective-permute-done((bf16[384,512]{1,0:T(8,128)(2,1)S(1)}, bf16[384,512]{1,0:T(8,128)(2,1)S(1)}, u32[]{:S(2)}, u32[]{:S(2)}) %collective-permute-start.6) | collective-permute-done | bytes 393248 | tf_op jit(solution)/shard_map/ppermute | solution.py:74
  107.2 0.6 collective-permute-done.8
  107.8 1.2 fusion.72
  109.1 1.6 fusion.71
  110.6 1.7 collective-permute-done.9
  112.4 0.1 add_convert_fusion
  112.5 2.4 %collective-permute-start.10 = (bf16[384,512]{1,0:T(8,128)(2,1)S(1)}, bf16[384,512]{1,0:T(8,128)(2,1)S(1)}, u32[]{:S(2)}, u32[]{:S(2)}) collective-permute-start(bf16[384,512]{1,0:T(8,128)(2,1)S(1)} %add_convert_fusion), channel_id=1, source_target_pairs={{0,128},{64,192},{128,0},{192,64},{1,129},{65,193},{129,1},{193,65... | collective-permute-start | bytes 1179656 | tf_op jit(solution)/shard_map/ppermute | solution.py:97
  114.9 29.0 %collective-permute-done.10 = bf16[384,512]{1,0:T(8,128)(2,1)S(1)} collective-permute-done((bf16[384,512]{1,0:T(8,128)(2,1)S(1)}, bf16[384,512]{1,0:T(8,128)(2,1)S(1)}, u32[]{:S(2)}, u32[]{:S(2)}) %collective-permute-start.10) | collective-permute-done | bytes 393248 | tf_op jit(solution)/shard_map/ppermute | solution.py:97
  143.8 1.4 multiply_subtract_fusion
  145.3 47.6 %reduce-scatter.2.cloned.1.call-done = bf16[64,2048]{1,0:T(8,128)(2,1)} async-done(((bf16[1024,2048]{1,0:T(8,128)(2,1)}), bf16[64,2048]{1,0:T(8,128)(2,1)}) %reduce-scatter.2.cloned.1.call-update) | async-done | bytes 262160 | tf_op jit(solution)/shard_map/reduce_scatter | solution.py:81
  (22 shorter events, 0.0 us)
Async XLA Ops:
  7.2 185.7 %reduce-scatter.2.cloned.1.call-start = ((), (), s32[]{:S(2)}) async-start(), calls=%async_computation.1 | async-start | bytes 4456448 | tf_op jit(solution)/shard_map/reduce_scatter | solution.py:81
  10.9 24.8 %collective-permute-start = (bf16[256,1152]{0,1:T(8,128)(2,1)S(1)}, bf16[256,1152]{0,1:T(8,128)(2,1)S(1)}, u32[]{:S(2)}, u32[]{:S(2)}) collective-permute-start(bf16[256,1152]{0,1:T(8,128)(2,1)S(1)} %get-tuple-element.17), channel_id=1, source_target_pairs={{0,16},{16,32},{32,48},{48,0},{1,17},{17,33},{33,49},{49,1},{2,18}... | collective-permute-start | bytes 1769480 | tf_op jit(solution)/shard_map/ppermute | solution.py:39
  12.5 17.3 %collective-permute-start.1 = (bf16[256,1152]{0,1:T(8,128)(2,1)S(1)}, bf16[256,1152]{0,1:T(8,128)(2,1)S(1)}, u32[]{:S(2)}, u32[]{:S(2)}) collective-permute-start(bf16[256,1152]{0,1:T(8,128)(2,1)S(1)} %get-tuple-element.16), channel_id=1, source_target_pairs={{0,48},{16,0},{32,16},{48,32},{1,49},{17,1},{33,17},{49,33},{2,50}... | collective-permute-start | bytes 1769480 | tf_op jit(solution)/shard_map/ppermute | solution.py:40
  29.8 6.5 %copy-start.5 = (bf16[1,1024,2048]{2,1,0:T(8,128)(2,1)S(1)}, bf16[1,1024,2048]{2,1,0:T(8,128)(2,1)}, u32[]{:S(2)}) copy-start(bf16[1,1024,2048]{2,1,0:T(8,128)(2,1)} %param.10) | copy-start | bytes 12582916
  29.8 14.5 %collective-permute-start.3 = (bf16[256,1152]{0,1:T(8,128)(2,1)S(1)}, bf16[256,1152]{0,1:T(8,128)(2,1)S(1)}, u32[]{:S(2)}, u32[]{:S(2)}) collective-permute-start(bf16[256,1152]{0,1:T(8,128)(2,1)S(1)} %collective-permute-done.1), channel_id=1, source_target_pairs={{0,48},{16,0},{32,16},{48,32},{1,49},{17,1},{33,17},{49,33},{2,50}... | collective-permute-start | bytes 1769480 | tf_op jit(solution)/shard_map/ppermute | solution.py:40
  33.9 4.8 %copy-start.4 = (bf16[1,1024,2048]{2,1,0:T(8,128)(2,1)S(1)}, bf16[1,1024,2048]{2,1,0:T(8,128)(2,1)}, u32[]{:S(2)}) copy-start(bf16[1,1024,2048]{2,1,0:T(8,128)(2,1)} %param.9) | copy-start | bytes 12582916
  35.7 15.5 %collective-permute-start.2 = (bf16[256,1152]{0,1:T(8,128)(2,1)S(1)}, bf16[256,1152]{0,1:T(8,128)(2,1)S(1)}, u32[]{:S(2)}, u32[]{:S(2)}) collective-permute-start(bf16[256,1152]{0,1:T(8,128)(2,1)S(1)} %collective-permute-done), channel_id=1, source_target_pairs={{0,16},{16,32},{32,48},{48,0},{1,17},{17,33},{33,49},{49,1},{2,18}... | collective-permute-start | bytes 1769480 | tf_op jit(solution)/shard_map/ppermute | solution.py:39
  44.3 24.5 %collective-permute-start.5 = (bf16[256,1152]{0,1:T(8,128)(2,1)S(1)}, bf16[256,1152]{0,1:T(8,128)(2,1)S(1)}, u32[]{:S(2)}, u32[]{:S(2)}) collective-permute-start(bf16[256,1152]{0,1:T(8,128)(2,1)S(1)} %collective-permute-done.3), channel_id=1, source_target_pairs={{0,48},{16,0},{32,16},{48,32},{1,49},{17,1},{33,17},{49,33},{2,50}... | collective-permute-start | bytes 1769480 | tf_op jit(solution)/shard_map/ppermute | solution.py:40
  51.2 14.5 %collective-permute-start.4 = (bf16[256,1152]{0,1:T(8,128)(2,1)S(1)}, bf16[256,1152]{0,1:T(8,128)(2,1)S(1)}, u32[]{:S(2)}, u32[]{:S(2)}) collective-permute-start(bf16[256,1152]{0,1:T(8,128)(2,1)S(1)} %collective-permute-done.2), channel_id=1, source_target_pairs={{0,16},{16,32},{32,48},{48,0},{1,17},{17,33},{33,49},{49,1},{2,18}... | collective-permute-start | bytes 1769480 | tf_op jit(solution)/shard_map/ppermute | solution.py:39
  66.6 3.8 %copy-start = (f32[1024,768]{0,1:T(8,128)S(1)}, f32[1024,768]{0,1:T(8,128)}, u32[]{:S(2)}) copy-start(f32[1024,768]{0,1:T(8,128)} %fusion.43) | copy-start | bytes 9437188
  66.6 3.8 %copy-start.1 = (f32[1024,768]{0,1:T(8,128)S(1)}, f32[1024,768]{0,1:T(8,128)}, u32[]{:S(2)}) copy-start(f32[1024,768]{0,1:T(8,128)} %fusion.45) | copy-start | bytes 9437188
  68.8 0.8 copy-start.9
  70.4 2.6 %copy-start.2 = (f32[1024,384]{0,1:T(8,128)S(1)}, f32[1024,384]{0,1:T(8,128)}, u32[]{:S(2)}) copy-start(f32[1024,384]{0,1:T(8,128)} %fusion.25) | copy-start | bytes 4718596
  70.4 2.7 %copy-start.3 = (f32[1024,384]{0,1:T(8,128)S(1)}, f32[1024,384]{0,1:T(8,128)}, u32[]{:S(2)}) copy-start(f32[1024,384]{0,1:T(8,128)} %fusion.27) | copy-start | bytes 4718596
  85.0 22.8 %copy-start.6 = (f32[1,384,512]{2,1,0:T(8,128)S(1)}, f32[1,384,512]{2,1,0:T(8,128)}, u32[]{:S(2)}) copy-start(f32[1,384,512]{2,1,0:T(8,128)} %param.15) | copy-start | bytes 2359300
  89.1 20.0 %copy-start.7 = (f32[1,384,512]{2,1,0:T(8,128)S(1)}, f32[1,384,512]{2,1,0:T(8,128)}, u32[]{:S(2)}) copy-start(f32[1,384,512]{2,1,0:T(8,128)} %param.13) | copy-start | bytes 2359300
  89.1 20.0 %copy-start.8 = (f32[384,512]{1,0:T(8,128)S(1)}, f32[384,512]{1,0:T(8,128)}, u32[]{:S(2)}) copy-start(f32[384,512]{1,0:T(8,128)} %param.16) | copy-start | bytes 2359300
  89.1 20.0 %copy-start.10 = (f32[1,384,512]{2,1,0:T(8,128)S(1)}, f32[1,384,512]{2,1,0:T(8,128)}, u32[]{:S(2)}) copy-start(f32[1,384,512]{2,1,0:T(8,128)} %param.14) | copy-start | bytes 2359300
  89.3 17.9 %collective-permute-start.6 = (bf16[384,512]{1,0:T(8,128)(2,1)S(1)}, bf16[384,512]{1,0:T(8,128)(2,1)S(1)}, u32[]{:S(2)}, u32[]{:S(2)}) collective-permute-start(bf16[384,512]{1,0:T(8,128)(2,1)S(1)} %get-tuple-element.11), channel_id=1, source_target_pairs={{0,16},{16,32},{32,48},{48,0},{1,17},{17,33},{33,49},{49,1},{2,18}... | collective-permute-start | bytes 1179656 | tf_op jit(solution)/shard_map/ppermute | solution.py:74
  89.4 17.8 %collective-permute-start.7 = (bf16[384,512]{1,0:T(8,128)(2,1)S(1)}, bf16[384,512]{1,0:T(8,128)(2,1)S(1)}, u32[]{:S(2)}, u32[]{:S(2)}) collective-permute-start(bf16[384,512]{1,0:T(8,128)(2,1)S(1)} %get-tuple-element.13), channel_id=1, source_target_pairs={{0,32},{16,48},{32,0},{48,16},{1,33},{17,49},{33,1},{49,17},{2,34}... | collective-permute-start | bytes 1179656 | tf_op jit(solution)/shard_map/ppermute | solution.py:74
  90.4 17.5 %collective-permute-start.8 = (bf16[384,512]{1,0:T(8,128)(2,1)S(1)}, bf16[384,512]{1,0:T(8,128)(2,1)S(1)}, u32[]{:S(2)}, u32[]{:S(2)}) collective-permute-start(bf16[384,512]{1,0:T(8,128)(2,1)S(1)} %get-tuple-element.12), channel_id=1, source_target_pairs={{0,48},{16,0},{32,16},{48,32},{1,49},{17,1},{33,17},{49,33},{2,50}... | collective-permute-start | bytes 1179656 | tf_op jit(solution)/shard_map/ppermute | solution.py:74
  109.1 34.8 %copy-start.11 = (f32[384,512]{1,0:T(8,128)S(1)}, f32[384,512]{1,0:T(8,128)}, u32[]{:S(2)}) copy-start(f32[384,512]{1,0:T(8,128)} %param.17) | copy-start | bytes 2359300
  110.6 1.7 collective-permute-start.9
  112.5 31.4 %collective-permute-start.10 = (bf16[384,512]{1,0:T(8,128)(2,1)S(1)}, bf16[384,512]{1,0:T(8,128)(2,1)S(1)}, u32[]{:S(2)}, u32[]{:S(2)}) collective-permute-start(bf16[384,512]{1,0:T(8,128)(2,1)S(1)} %add_convert_fusion), channel_id=1, source_target_pairs={{0,128},{64,192},{128,0},{192,64},{1,129},{65,193},{129,1},{193,65... | collective-permute-start | bytes 1179656 | tf_op jit(solution)/shard_map/ppermute | solution.py:97
Sparse Core Ops, SparseCore 0:
  85.1 107.7 reduce-scatter.1

commit v2 on v1

--- a/solution.py
+++ b/solution.py
@@ -9,6 +9,37 @@
 
 def _shift(n, s):
     return [(i, (i + s) % n) for i in range(n)]
+
+
+def _ring_reduce_scatter(part):
+    nmp = lax.axis_size("mp")
+    m = lax.axis_index("mp")
+    nlo = 2
+    nz = nmp // nlo
+    z = m // nlo
+    lo = m % nlo
+    rows = part.shape[0] // nz
+    halfc = part.shape[1] // 2
+    up = [(i, ((i // nlo + 1) % nz) * nlo + i % nlo) for i in range(nmp)]
+    down = [(i, ((i // nlo - 1) % nz) * nlo + i % nlo) for i in range(nmp)]
+
+    def chunk(c, h):
+        blk = lax.dynamic_slice_in_dim(part, c * rows, rows, axis=0)
+        return blk[:, h * halfc : (h + 1) * halfc].astype(jnp.float32)
+
+    acc_a = chunk((z - 1) % nz, 0)
+    acc_b = chunk((z + 1) % nz, 1)
+    for t in range(1, nz):
+        got_a = lax.ppermute(acc_a.astype(jnp.bfloat16), "mp", up)
+        got_b = lax.ppermute(acc_b.astype(jnp.bfloat16), "mp", down)
+        acc_a = got_a.astype(jnp.float32) + chunk((z - t - 1) % nz, 0)
+        acc_b = got_b.astype(jnp.float32) + chunk((z + t + 1) % nz, 1)
+    acc = jnp.concatenate([acc_a, acc_b], axis=1)
+    sub = rows // nlo
+    mine = lax.dynamic_slice_in_dim(acc, lo * sub, sub, axis=0)
+    other = lax.dynamic_slice_in_dim(acc, (1 - lo) * sub, sub, axis=0)
+    got = lax.ppermute(other.astype(jnp.bfloat16), "mp", [(i, i ^ 1) for i in range(nmp)])
+    return (mine + got.astype(jnp.float32)).astype(jnp.bfloat16)
 
 
 def shards(
@@ -78,9 +109,7 @@
     partial_sum = lax.dot_general(
         both, weights_full, (((1,), (1,)), ((), ())), preferred_element_type=jnp.float32
     )
-    input_grad = lax.psum_scatter(
-        partial_sum.astype(jnp.bfloat16), "mp", scatter_dimension=0, tiled=True
-    )
+    input_grad = _ring_reduce_scatter(partial_sum.astype(jnp.bfloat16))
 
     first_new = 0.9 * first_moment[0] + 0.1 * grad_down
     second_new = 0.999 * second_moment[0] + 0.001 * grad_down * grad_down

time: 201 us -> 167 us (0.83)
  waiting for transfers between devices: 110 us -> 49.4 us
  starting transfers between devices: 13.9 us -> 40.2 us
  between operations: 14.3 us -> 0.92 us
  other arithmetic: 7.23 us -> 18.8 us
  local copies, waits for them, and re-layouts: 10.4 us -> 14.7 us
    reduce_scatter x1 -> x0, waiting for transfers between devices: 47.6 us -> none  [shards(): lax.psum_scatter(partial_sum.astype(jnp.bfloat16), 'mp', scatter_dimensio...]
    ppermute x0 -> x15, starting transfers between devices: none -> 26.5 us  [the longest x7 15.7 us: _ring_reduce_scatter(): got_b = lax.ppermute(acc_b.astype(jnp.bfloat16), 'mp', down)]
    ppermute x2, waiting for transfers between devices: 30.7 us -> 6.53 us  [shards(): lax.ppermute(mine, 'outer', perm).astype(jnp.float32)]
    ppermute x0 -> x15, waiting for transfers between devices: none -> 23.6 us  [the longest x7 18.5 us: _ring_reduce_scatter(): got_a = lax.ppermute(acc_a.astype(jnp.bfloat16), 'mp', up)]
    ppermute x3, waiting for transfers between devices: 15.2 us -> 2.4 us  [shards(): got = lax.ppermute(blk.astype(jnp.bfloat16), 'dp', _shift(ndp, s))]
    convert_element_type x0 -> x7, other arithmetic: none -> 8.53 us  [the longest x6 8.5 us: _ring_reduce_scatter(): got_b = lax.ppermute(acc_b.astype(jnp.bfloat16), 'mp', down)]
    unnamed x26 -> x32, local copies, waits for them, and re-layouts: 3.19 us -> 5.88 us
  transfers between devices with their start and end apart: 12 -> 26, of which waited for: 8 -> 16; matrix products, arithmetic and copies ran while one was open for 21% -> 28% of each run, Pallas kernels for 0% -> 0%
where the time goes in v2:
time: 167 us; the launch traced here: 166 us
  waiting for transfers between devices  49.4 us (30%)
  matrix products  42.1 us (25%)
  starting transfers between devices  40.2 us (24%)
  other arithmetic  18.8 us (11%)
  local copies, waits for them, and re-layouts  14.7 us (9%)
    dot_general x8, matrix products, shards(): p2 = jnp.dot(gs, piece[:, 2 * ff:], preferred_element_type=jnp.float32)  19 us
    ppermute x7, waiting for transfers between devices, _ring_reduce_scatter(): got_a = lax.ppermute(acc_a.astype(jnp.bfloat16), 'mp', up)  18.5 us
    ppermute x7, starting transfers between devices, _ring_reduce_scatter(): got_b = lax.ppermute(acc_b.astype(jnp.bfloat16), 'mp', down)  15.7 us
    dot_general x8, matrix products, shards(): p1 = jnp.dot(xs, piece[:, :2 * ff], preferred_element_type=jnp.float32)  13.5 us
    ppermute x3, waiting for transfers between devices, shards(): a = lax.ppermute(a, 'dp', _shift(ndp, 1))  12.8 us
    ppermute x7, starting transfers between devices, _ring_reduce_scatter(): got_a = lax.ppermute(acc_a.astype(jnp.bfloat16), 'mp', up)  10.3 us
    convert_element_type x6, other arithmetic, _ring_reduce_scatter(): got_b = lax.ppermute(acc_b.astype(jnp.bfloat16), 'mp', down)  8.5 us
    ppermute x2, waiting for transfers between devices, shards(): lax.ppermute(mine, 'outer', perm).astype(jnp.float32)  6.53 us
  transfers between devices with their start and end apart: 26, of which 16 were waited for; matrix products, arithmetic and copies ran while one was open for 28% of the time, Pallas kernels for 0%

profile of v2, /device:TPU:8, one launch (start us, length us, event | category | flops | bytes accessed | tf_op | source)
XLA Modules:
  0.0 166.1 jit_solution(12582384571537647635)
XLA Ops:
  0.6 1.2 copy.14
  1.8 1.2 copy.15
  3.0 1.2 fusion.68
  4.3 1.6 collective-permute-start
  5.9 1.7 %collective-permute-start.1 = (bf16[256,1152]{0,1:T(8,128)(2,1)S(1)}, bf16[256,1152]{0,1:T(8,128)(2,1)S(1)}, u32[]{:S(2)}, u32[]{:S(2)}) collective-permute-start(bf16[256,1152]{0,1:T(8,128)(2,1)S(1)} %get-tuple-element.32), channel_id=1, source_target_pairs={{0,48},{16,0},{32,16},{48,32},{1,49},{17,1},{33,17},{49,33},{2,50}... | collective-permute-start | bytes 1769480 | tf_op jit(solution)/shard_map/ppermute | solution.py:71
  7.7 3.3 %fusion.48 = f32[1024,768]{0,1:T(8,128)} fusion(bf16[1,1024,2048]{2,1,0:T(8,128)(2,1)} %param.9, s32[]{:T(128)S(6)} %select_n.210, bf16[512,384]{0,1:T(8,128)(2,1)S(1)} %bitcast.102, bf16[512,384]{0,1:T(8,128)(2,1)S(1)} %bitcast.97), kind=kOutput, calls=%fused_computation.71 | convolution fusion | flops 403439616 | bytes 4456452 | tf_op jit(solution)/shard_map/dot_general | solution.py:82
  11.0 3.3 %fusion.50 = f32[1024,768]{0,1:T(8,128)} fusion(bf16[1,1024,2048]{2,1,0:T(8,128)(2,1)} %param.9, s32[]{:T(128)S(6)} %select_n.209, bf16[512,384]{0,1:T(8,128)(2,1)S(1)} %bitcast.98, bf16[512,384]{0,1:T(8,128)(2,1)S(1)} %bitcast.103), kind=kOutput, calls=%fused_computation.73 | convolution fusion | flops 403439616 | bytes 4456452 | tf_op jit(solution)/shard_map/dot_general | solution.py:82
  14.2 2.1 %broadcast_in_dim.14 = bf16[2048,768]{0,1:T(8,128)(2,1)} broadcast(bf16[]{:T(256)} %constant.229.clone.1), dimensions={} | broadcast | bytes 3145730 | tf_op jit(solution)/shard_map/broadcast_in_dim | solution.py:77
  18.0 2.6 %fusion.30 = f32[1024,384]{0,1:T(8,128)} fusion(bf16[1,1024,2048]{2,1,0:T(8,128)(2,1)} %param.10, s32[]{:T(128)S(6)} %select_n.210, bf16[512,384]{0,1:T(8,128)(2,1)S(1)} %fusion.68), kind=kOutput, calls=%fused_computation.55 | convolution fusion | flops 201326592 | bytes 2293764 | tf_op jit(solution)/shard_map/dot_general | solution.py:83
  20.6 2.6 %fusion.32 = f32[1024,384]{0,1:T(8,128)} fusion(bf16[1,1024,2048]{2,1,0:T(8,128)(2,1)} %param.10, s32[]{:T(128)S(6)} %select_n.209, bf16[512,384]{0,1:T(8,128)(2,1)S(1)} %fusion.68), kind=kOutput, calls=%fused_computation.57 | convolution fusion | flops 201326592 | bytes 2293764 | tf_op jit(solution)/shard_map/dot_general | solution.py:83
  23.2 1.5 collective-permute-start.3
  24.7 2.6 %fusion.26 = f32[1024,384]{0,1:T(8,128)} fusion(bf16[1,1024,2048]{2,1,0:T(8,128)(2,1)} %param.10, s32[]{:T(128)S(6)} %select_n.214, bf16[256,1152]{0,1:T(8,128)(2,1)S(1)} %collective-permute-done.1), kind=kOutput, calls=%fused_computation.51 | convolution fusion | flops 201326592 | bytes 2293764 | tf_op jit(solution)/shard_map/dot_general | solution.py:83
  27.3 1.8 %fusion.44 = f32[1024,768]{0,1:T(8,128)S(1)} fusion(bf16[1,1024,2048]{2,1,0:T(8,128)(2,1)} %param.9, s32[]{:T(128)S(6)} %select_n.214, bf16[256,1152]{0,1:T(8,128)(2,1)S(1)} %collective-permute-done.1), kind=kOutput, calls=%fused_computation.67 | convolution fusion | flops 402653184 | bytes 4063236 | tf_op jit(solution)/shard_map/dot_general | solution.py:82
  29.7 1.7 %fusion.28 = f32[1024,384]{0,1:T(8,128)} fusion(bf16[1,1024,2048]{2,1,0:T(8,128)(2,1)S(1)} %copy-done.5, s32[]{:T(128)S(6)} %select_n.212, bf16[256,1152]{0,1:T(8,128)(2,1)S(1)} %collective-permute-done), kind=kOutput, calls=%fused_computation.53 | convolution fusion | flops 201326592 | bytes 2293764 | tf_op jit(solution)/shard_map/dot_general | solution.py:83
  33.6 4.1 %collective-permute-done.3 = bf16[256,1152]{0,1:T(8,128)(2,1)S(1)} collective-permute-done((bf16[256,1152]{0,1:T(8,128)(2,1)S(1)}, bf16[256,1152]{0,1:T(8,128)(2,1)S(1)}, u32[]{:S(2)}, u32[]{:S(2)}) %collective-permute-start.3) | collective-permute-done | bytes 589856 | tf_op jit(solution)/shard_map/ppermute | solution.py:71
  37.7 2.7 %collective-permute-start.5 = (bf16[256,1152]{0,1:T(8,128)(2,1)S(1)}, bf16[256,1152]{0,1:T(8,128)(2,1)S(1)}, u32[]{:S(2)}, u32[]{:S(2)}) collective-permute-start(bf16[256,1152]{0,1:T(8,128)(2,1)S(1)} %collective-permute-done.3), channel_id=1, source_target_pairs={{0,48},{16,0},{32,16},{48,32},{1,49},{17,1},{33,17},{49,33},{2,50}... | collective-permute-start | bytes 1769480 | tf_op jit(solution)/shard_map/ppermute | solution.py:71
  40.4 1.6 fusion.22
  42.6 2.0 %collective-permute-done.2 = bf16[256,1152]{0,1:T(8,128)(2,1)S(1)} collective-permute-done((bf16[256,1152]{0,1:T(8,128)(2,1)S(1)}, bf16[256,1152]{0,1:T(8,128)(2,1)S(1)}, u32[]{:S(2)}, u32[]{:S(2)}) %collective-permute-start.2) | collective-permute-done | bytes 589856 | tf_op jit(solution)/shard_map/ppermute | solution.py:70
  45.4 0.8 slice_dynamic-update-slice_fusion.2
  46.3 1.6 fusion.24
  48.5 10.7 %collective-permute-done.4 = bf16[256,1152]{0,1:T(8,128)(2,1)S(1)} collective-permute-done((bf16[256,1152]{0,1:T(8,128)(2,1)S(1)}, bf16[256,1152]{0,1:T(8,128)(2,1)S(1)}, u32[]{:S(2)}, u32[]{:S(2)}) %collective-permute-start.4) | collective-permute-done | bytes 589856 | tf_op jit(solution)/shard_map/ppermute | solution.py:70
  60.0 1.6 fusion.20
  63.8 2.6 %add_add_fusion = f32[1024,768]{0,1:T(8,128)S(1)} fusion(f32[1024,768]{0,1:T(8,128)S(1)} %fusion.38, f32[1024,768]{0,1:T(8,128)S(1)} %fusion.40, f32[1024,768]{0,1:T(8,128)S(1)} %fusion.42, f32[1024,768]{0,1:T(8,128)S(1)} %fusion.44, f32[1024,768]{0,1:T(8,128)S(1)} %fusion.46, f32[1024,768]{0,1:T(8,128)S(1)} %copy-done.1, f32[1024,768]{0,1:T(8,128)S(1)} %copy-done, ...), kind=kOutput, calls=%fused_computation.3 | convolution fusion | flops 408158208 | bytes 26083332 | tf_op jit(solution)/shard_map/dot_general | solution.py:82
  66.5 4.9 %multiply_convert_fusion.1 = (bf16[1024,384]{0,1:T(8,128)(2,1)S(1)}, bf16[1024,384]{0,1:T(8,128)(2,1)S(1)}) fusion(f32[1024,768]{0,1:T(8,128)S(1)} %add_add_fusion, bf16[256,1152]{0,1:T(8,128)(2,1)} %copy-done.10, bf16[1,1024,2048]{2,1,0:T(8,128)(2,1)} %param.10, s32[]{:T(128)S(6)} %select_n.222, f32[1024,384]{0,1:T(8,128)} %fusion.20, ...), kind=kOutput, calls=%fused_computation.8 | convolution fusion | flops 209190912 | bytes 16449540 | tf_op jit(solution)/shard_map/dot_general | solution.py:83
  71.4 5.6 %convolution_convert_fusion = bf16[1024,2048]{1,0:T(8,128)(2,1)S(1)} fusion(bf16[2048,768]{0,1:T(8,128)(2,1)} %slice_dynamic-update-slice_fusion, bf16[1024,384]{0,1:T(8,128)(2,1)S(1)} %get-tuple-element.10, bf16[1024,384]{0,1:T(8,128)(2,1)S(1)} %get-tuple-element.9), kind=kOutput, calls=%fused_computation.2 | convolution fusion | flops 3226468352 | bytes 8912896 | tf_op jit(solution)/shard_map/dot_general | solution.py:109
  77.0 2.0 %copy-done.6 = bf16[1024,2048]{1,0:T(8,128)(2,1)} copy-done((bf16[1024,2048]{1,0:T(8,128)(2,1)}, bf16[1024,2048]{1,0:T(8,128)(2,1)S(1)}, u32[]{:S(2)}) %copy-start.6) | copy-done | bytes 4194328
  79.8 1.9 %collective-permute-start.11 = (bf16[128,1024]{1,0:T(8,128)(2,1)}, bf16[128,1024]{1,0:T(8,128)(2,1)S(1)}, u32[]{:S(2)}, u32[]{:S(2)}) collective-permute-start(bf16[128,1024]{1,0:T(8,128)(2,1)} %get-tuple-element.26), channel_id=1, source_target_pairs={{0,2},{1,3},{2,4},{3,5},{4,6},{5,7},{6,8},{7,9},{8,10},{9,11},{10,... | collective-permute-start | bytes 786440 | tf_op jit(solution)/shard_map/ppermute | solution.py:33
  81.8 3.9 %collective-permute-start.18 = (bf16[128,1024]{1,0:T(8,128)(2,1)}, bf16[128,1024]{1,0:T(8,128)(2,1)}, u32[]{:S(2)}, u32[]{:S(2)}) collective-permute-start(bf16[128,1024]{1,0:T(8,128)(2,1)} %get-tuple-element.25), channel_id=1, source_target_pairs={{0,14},{1,15},{2,0},{3,1},{4,2},{5,3},{6,4},{7,5},{8,6},{9,7},{10,... | collective-permute-start | bytes 786440 | tf_op jit(solution)/shard_map/ppermute | solution.py:34
  85.7 4.6 %collective-permute-done.11 = bf16[128,1024]{1,0:T(8,128)(2,1)S(1)} collective-permute-done((bf16[128,1024]{1,0:T(8,128)(2,1)}, bf16[128,1024]{1,0:T(8,128)(2,1)S(1)}, u32[]{:S(2)}, u32[]{:S(2)}) %collective-permute-start.11) | collective-permute-done | bytes 262176 | tf_op jit(solution)/shard_map/ppermute | solution.py:33
  91.0 2.1 %add_convert_fusion.6 = (bf16[128,1024]{1,0:T(8,128)(2,1)S(1)}, bf16[128,1024]{1,0:T(8,128)(2,1)}) fusion(bf16[128,1024]{1,0:T(8,128)(2,1)} %collective-permute-done.18, bf16[1024,2048]{1,0:T(8,128)(2,1)} %copy-done.6, s32[]{:T(128)S(6)} %select_n.246, s32[]{:T(128)S(6)} %add.525, s32[]{:T(128)S(6)} %select_n.230, bf16[128,1024]{1,0:T(8,128)(2,1)} %copy-done.14), kind=kLoop, calls=%fused_computation.81 | loop fusion | flops 1048576 | bytes 1572876 | tf_op jit(solution)/shard_map/convert_element_type | solution.py:34
  93.0 3.2 %collective-permute-start.19 = (bf16[128,1024]{1,0:T(8,128)(2,1)S(1)}, bf16[128,1024]{1,0:T(8,128)(2,1)}, u32[]{:S(2)}, u32[]{:S(2)}) collective-permute-start(bf16[128,1024]{1,0:T(8,128)(2,1)S(1)} %get-tuple-element.23), channel_id=1, source_target_pairs={{0,14},{1,15},{2,0},{3,1},{4,2},{5,3},{6,4},{7,5},{8,6},{9,7},{10,... | collective-permute-start | bytes 786440 | tf_op jit(solution)/shard_map/ppermute | solution.py:34
  96.3 4.7 %collective-permute-done.12 = bf16[128,1024]{1,0:T(8,128)(2,1)} collective-permute-done((bf16[128,1024]{1,0:T(8,128)(2,1)}, bf16[128,1024]{1,0:T(8,128)(2,1)}, u32[]{:S(2)}, u32[]{:S(2)}) %collective-permute-start.12) | collective-permute-done | bytes 262176 | tf_op jit(solution)/shard_map/ppermute | solution.py:33
  100.9 1.4 add_convert_fusion.5
  102.3 2.3 %collective-permute-start.13 = (bf16[128,1024]{1,0:T(8,128)(2,1)S(1)}, bf16[128,1024]{1,0:T(8,128)(2,1)S(1)}, u32[]{:S(2)}, u32[]{:S(2)}) collective-permute-start(bf16[128,1024]{1,0:T(8,128)(2,1)S(1)} %get-tuple-element.22), channel_id=1, source_target_pairs={{0,2},{1,3},{2,4},{3,5},{4,6},{5,7},{6,8},{7,9},{8,10},{9,11},{10,... | collective-permute-start | bytes 786440 | tf_op jit(solution)/shard_map/ppermute | solution.py:33
  104.6 1.1 collective-permute-start.20
  105.7 4.0 %fusion = f32[384,2048]{1,0:T(8,128)S(1)} fusion(bf16[1,1024,2048]{2,1,0:T(8,128)(2,1)} %param.10, f32[1024,768]{0,1:T(8,128)S(1)} %add_add_fusion), kind=kOutput, calls=%fused_computation | convolution fusion | flops 1612972032 | bytes 10485760 | tf_op jit(solution)/shard_map/dot_general | solution.py:98
  110.0 1.9 %collective-permute-done.20 = bf16[128,1024]{1,0:T(8,128)(2,1)S(1)} collective-permute-done((bf16[128,1024]{1,0:T(8,128)(2,1)S(1)}, bf16[128,1024]{1,0:T(8,128)(2,1)S(1)}, u32[]{:S(2)}, u32[]{:S(2)}) %collective-permute-start.20) | collective-permute-done | bytes 262176 | tf_op jit(solution)/shard_map/ppermute | solution.py:34
  111.9 1.2 add_convert_fusion.4
  113.2 2.4 %collective-permute-start.14 = (bf16[128,1024]{1,0:T(8,128)(2,1)S(1)}, bf16[128,1024]{1,0:T(8,128)(2,1)S(1)}, u32[]{:S(2)}, u32[]{:S(2)}) collective-permute-start(bf16[128,1024]{1,0:T(8,128)(2,1)S(1)} %get-tuple-element.20), channel_id=1, source_target_pairs={{0,2},{1,3},{2,4},{3,5},{4,6},{5,7},{6,8},{7,9},{8,10},{9,11},{10,... | collective-permute-start | bytes 786440 | tf_op jit(solution)/shard_map/ppermute | solution.py:33
  115.5 0.9 collective-permute-start.21
  116.5 0.9 dynamic-slice_convert_fusion.2
  117.4 1.0 collective-permute-start.7
  118.4 2.2 %collective-permute-start.8 = (bf16[384,512]{1,0:T(8,128)(2,1)S(1)}, bf16[384,512]{1,0:T(8,128)(2,1)S(1)}, u32[]{:S(2)}, u32[]{:S(2)}) collective-permute-start(bf16[384,512]{1,0:T(8,128)(2,1)S(1)} %get-tuple-element.28), channel_id=1, source_target_pairs={{0,48},{16,0},{32,16},{48,32},{1,49},{17,1},{33,17},{49,33},{2,50}... | collective-permute-start | bytes 1179656 | tf_op jit(solution)/shard_map/ppermute | solution.py:105
  120.6 2.1 %collective-permute-done.14 = bf16[128,1024]{1,0:T(8,128)(2,1)S(1)} collective-permute-done((bf16[128,1024]{1,0:T(8,128)(2,1)S(1)}, bf16[128,1024]{1,0:T(8,128)(2,1)S(1)}, u32[]{:S(2)}, u32[]{:S(2)}) %collective-permute-start.14) | collective-permute-done | bytes 262176 | tf_op jit(solution)/shard_map/ppermute | solution.py:33
  122.7 1.7 %collective-permute-done.21 = bf16[128,1024]{1,0:T(8,128)(2,1)} collective-permute-done((bf16[128,1024]{1,0:T(8,128)(2,1)S(1)}, bf16[128,1024]{1,0:T(8,128)(2,1)}, u32[]{:S(2)}, u32[]{:S(2)}) %collective-permute-start.21) | collective-permute-done | bytes 262176 | tf_op jit(solution)/shard_map/ppermute | solution.py:34
  124.4 1.3 add_convert_fusion.3
  125.8 2.0 %collective-permute-start.15 = (bf16[128,1024]{1,0:T(8,128)(2,1)S(1)}, bf16[128,1024]{1,0:T(8,128)(2,1)S(1)}, u32[]{:S(2)}, u32[]{:S(2)}) collective-permute-start(bf16[128,1024]{1,0:T(8,128)(2,1)S(1)} %get-tuple-element.18), channel_id=1, source_target_pairs={{0,2},{1,3},{2,4},{3,5},{4,6},{5,7},{6,8},{7,9},{8,10},{9,11},{10,... | collective-permute-start | bytes 786440 | tf_op jit(solution)/shard_map/ppermute | solution.py:33
  127.8 1.3 collective-permute-start.22
  129.1 1.9 %collective-permute-done.6 = bf16[384,512]{1,0:T(8,128)(2,1)S(1)} collective-permute-done((bf16[384,512]{1,0:T(8,128)(2,1)}, bf16[384,512]{1,0:T(8,128)(2,1)S(1)}, u32[]{:S(2)}, u32[]{:S(2)}) %collective-permute-start.6) | collective-permute-done | bytes 393248 | tf_op jit(solution)/shard_map/ppermute | solution.py:105
  131.5 2.3 %fusion.78 = (f32[1,384,512]{2,1,0:T(8,128)}, f32[384,512]{1,0:T(8,128)S(1)}) fusion(f32[1,384,512]{2,1,0:T(8,128)S(1)} %copy-done.7, bf16[384,512]{1,0:T(8,128)(2,1)S(1)} %collective-permute-done.8, bf16[384,512]{1,0:T(8,128)(2,1)S(1)} %collective-permute-done.7, bf16[384,512]{1,0:T(8,128)(2,1)S(1)} %collective-permute-done.6, f32[384,2048]{1,0:T(8,128)} %copy-done.11, ...), kind=kLoop, calls=%fused_computation.122 | loop fusion | flops 1966080 | bytes 4325380 | tf_op jit(solution)/shard_map/broadcast_in_dim | solution.py:131
  133.8 2.4 %collective-permute-done.15 = bf16[128,1024]{1,0:T(8,128)(2,1)S(1)} collective-permute-done((bf16[128,1024]{1,0:T(8,128)(2,1)S(1)}, bf16[128,1024]{1,0:T(8,128)(2,1)S(1)}, u32[]{:S(2)}, u32[]{:S(2)}) %collective-permute-start.15) | collective-permute-done | bytes 262176 | tf_op jit(solution)/shard_map/ppermute | solution.py:33
  136.2 1.2 add_convert_fusion.2
  138.0 2.7 %collective-permute-start.23 = (bf16[128,1024]{1,0:T(8,128)(2,1)S(1)}, bf16[128,1024]{1,0:T(8,128)(2,1)}, u32[]{:S(2)}, u32[]{:S(2)}) collective-permute-start(bf16[128,1024]{1,0:T(8,128)(2,1)S(1)} %get-tuple-element.15), channel_id=1, source_target_pairs={{0,14},{1,15},{2,0},{3,1},{4,2},{5,3},{6,4},{7,5},{8,6},{9,7},{10,... | collective-permute-start | bytes 786440 | tf_op jit(solution)/shard_map/ppermute | solution.py:34
  140.7 1.5 fusion.77
  142.3 2.8 %collective-permute-done.16 = bf16[128,1024]{1,0:T(8,128)(2,1)S(1)} collective-permute-done((bf16[128,1024]{1,0:T(8,128)(2,1)S(1)}, bf16[128,1024]{1,0:T(8,128)(2,1)S(1)}, u32[]{:S(2)}, u32[]{:S(2)}) %collective-permute-start.16) | collective-permute-done | bytes 262176 | tf_op jit(solution)/shard_map/ppermute | solution.py:33
  145.1 1.3 add_convert_fusion.1
  146.4 1.1 collective-permute-start.17
  147.4 2.4 %collective-permute-start.24 = (bf16[128,1024]{1,0:T(8,128)(2,1)S(1)}, bf16[128,1024]{1,0:T(8,128)(2,1)S(1)}, u32[]{:S(2)}, u32[]{:S(2)}) collective-permute-start(bf16[128,1024]{1,0:T(8,128)(2,1)S(1)} %get-tuple-element.13), channel_id=1, source_target_pairs={{0,14},{1,15},{2,0},{3,1},{4,2},{5,3},{6,4},{7,5},{8,6},{9,7},{10,... | collective-permute-start | bytes 786440 | tf_op jit(solution)/shard_map/ppermute | solution.py:34
  150.0 2.3 %collective-permute-start.10 = (bf16[384,512]{1,0:T(8,128)(2,1)S(1)}, bf16[384,512]{1,0:T(8,128)(2,1)S(1)}, u32[]{:S(2)}, u32[]{:S(2)}) collective-permute-start(bf16[384,512]{1,0:T(8,128)(2,1)S(1)} %add_convert_fusion), channel_id=1, source_target_pairs={{0,128},{64,192},{128,0},{192,64},{1,129},{65,193},{129,1},{193,65... | collective-permute-start | bytes 1179656 | tf_op jit(solution)/shard_map/ppermute | solution.py:126
  152.3 1.9 %collective-permute-done.17 = bf16[128,1024]{1,0:T(8,128)(2,1)S(1)} collective-permute-done((bf16[128,1024]{1,0:T(8,128)(2,1)S(1)}, bf16[128,1024]{1,0:T(8,128)(2,1)S(1)}, u32[]{:S(2)}, u32[]{:S(2)}) %collective-permute-start.17) | collective-permute-done | bytes 262176 | tf_op jit(solution)/shard_map/ppermute | solution.py:33
  154.2 1.2 convert_add_fusion.1
  155.9 6.5 %collective-permute-done.10 = bf16[384,512]{1,0:T(8,128)(2,1)S(1)} collective-permute-done((bf16[384,512]{1,0:T(8,128)(2,1)S(1)}, bf16[384,512]{1,0:T(8,128)(2,1)S(1)}, u32[]{:S(2)}, u32[]{:S(2)}) %collective-permute-start.10) | collective-permute-done | bytes 393248 | tf_op jit(solution)/shard_map/ppermute | solution.py:126
  162.5 1.5 multiply_subtract_fusion
  163.9 1.4 collective-permute-done.25
  (65 shorter events, 14.0 us)
Async XLA Ops:
  4.3 24.7 %collective-permute-start = (bf16[256,1152]{0,1:T(8,128)(2,1)S(1)}, bf16[256,1152]{0,1:T(8,128)(2,1)S(1)}, u32[]{:S(2)}, u32[]{:S(2)}) collective-permute-start(bf16[256,1152]{0,1:T(8,128)(2,1)S(1)} %get-tuple-element.33), channel_id=1, source_target_pairs={{0,16},{16,32},{32,48},{48,0},{1,17},{17,33},{33,49},{49,1},{2,18}... | collective-permute-start | bytes 1769480 | tf_op jit(solution)/shard_map/ppermute | solution.py:70
  5.9 17.3 %collective-permute-start.1 = (bf16[256,1152]{0,1:T(8,128)(2,1)S(1)}, bf16[256,1152]{0,1:T(8,128)(2,1)S(1)}, u32[]{:S(2)}, u32[]{:S(2)}) collective-permute-start(bf16[256,1152]{0,1:T(8,128)(2,1)S(1)} %get-tuple-element.32), channel_id=1, source_target_pairs={{0,48},{16,0},{32,16},{48,32},{1,49},{17,1},{33,17},{49,33},{2,50}... | collective-permute-start | bytes 1769480 | tf_op jit(solution)/shard_map/ppermute | solution.py:71
  23.2 6.5 %copy-start.5 = (bf16[1,1024,2048]{2,1,0:T(8,128)(2,1)S(1)}, bf16[1,1024,2048]{2,1,0:T(8,128)(2,1)}, u32[]{:S(2)}) copy-start(bf16[1,1024,2048]{2,1,0:T(8,128)(2,1)} %param.10) | copy-start | bytes 12582916
  23.2 14.5 %collective-permute-start.3 = (bf16[256,1152]{0,1:T(8,128)(2,1)S(1)}, bf16[256,1152]{0,1:T(8,128)(2,1)S(1)}, u32[]{:S(2)}, u32[]{:S(2)}) collective-permute-start(bf16[256,1152]{0,1:T(8,128)(2,1)S(1)} %collective-permute-done.1), channel_id=1, source_target_pairs={{0,48},{16,0},{32,16},{48,32},{1,49},{17,1},{33,17},{49,33},{2,50}... | collective-permute-start | bytes 1769480 | tf_op jit(solution)/shard_map/ppermute | solution.py:71
  27.3 4.9 %copy-start.4 = (bf16[1,1024,2048]{2,1,0:T(8,128)(2,1)S(1)}, bf16[1,1024,2048]{2,1,0:T(8,128)(2,1)}, u32[]{:S(2)}) copy-start(bf16[1,1024,2048]{2,1,0:T(8,128)(2,1)} %param.9) | copy-start | bytes 12582916
  29.1 15.5 %collective-permute-start.2 = (bf16[256,1152]{0,1:T(8,128)(2,1)S(1)}, bf16[256,1152]{0,1:T(8,128)(2,1)S(1)}, u32[]{:S(2)}, u32[]{:S(2)}) collective-permute-start(bf16[256,1152]{0,1:T(8,128)(2,1)S(1)} %collective-permute-done), channel_id=1, source_target_pairs={{0,16},{16,32},{32,48},{48,0},{1,17},{17,33},{33,49},{49,1},{2,18}... | collective-permute-start | bytes 1769480 | tf_op jit(solution)/shard_map/ppermute | solution.py:70
  37.7 24.5 %collective-permute-start.5 = (bf16[256,1152]{0,1:T(8,128)(2,1)S(1)}, bf16[256,1152]{0,1:T(8,128)(2,1)S(1)}, u32[]{:S(2)}, u32[]{:S(2)}) collective-permute-start(bf16[256,1152]{0,1:T(8,128)(2,1)S(1)} %collective-permute-done.3), channel_id=1, source_target_pairs={{0,48},{16,0},{32,16},{48,32},{1,49},{17,1},{33,17},{49,33},{2,50}... | collective-permute-start | bytes 1769480 | tf_op jit(solution)/shard_map/ppermute | solution.py:71
  44.6 14.5 %collective-permute-start.4 = (bf16[256,1152]{0,1:T(8,128)(2,1)S(1)}, bf16[256,1152]{0,1:T(8,128)(2,1)S(1)}, u32[]{:S(2)}, u32[]{:S(2)}) collective-permute-start(bf16[256,1152]{0,1:T(8,128)(2,1)S(1)} %collective-permute-done.2), channel_id=1, source_target_pairs={{0,16},{16,32},{32,48},{48,0},{1,17},{17,33},{33,49},{49,1},{2,18}... | collective-permute-start | bytes 1769480 | tf_op jit(solution)/shard_map/ppermute | solution.py:70
  60.0 3.8 %copy-start = (f32[1024,768]{0,1:T(8,128)S(1)}, f32[1024,768]{0,1:T(8,128)}, u32[]{:S(2)}) copy-start(f32[1024,768]{0,1:T(8,128)} %fusion.48) | copy-start | bytes 9437188
  60.0 3.8 %copy-start.1 = (f32[1024,768]{0,1:T(8,128)S(1)}, f32[1024,768]{0,1:T(8,128)}, u32[]{:S(2)}) copy-start(f32[1024,768]{0,1:T(8,128)} %fusion.50) | copy-start | bytes 9437188
  62.2 0.8 copy-start.10
  63.8 2.6 %copy-start.2 = (f32[1024,384]{0,1:T(8,128)S(1)}, f32[1024,384]{0,1:T(8,128)}, u32[]{:S(2)}) copy-start(f32[1024,384]{0,1:T(8,128)} %fusion.30) | copy-start | bytes 4718596
  63.8 2.7 %copy-start.3 = (f32[1024,384]{0,1:T(8,128)S(1)}, f32[1024,384]{0,1:T(8,128)}, u32[]{:S(2)}) copy-start(f32[1024,384]{0,1:T(8,128)} %fusion.32) | copy-start | bytes 4718596
  77.0 2.0 %copy-start.6 = (bf16[1024,2048]{1,0:T(8,128)(2,1)}, bf16[1024,2048]{1,0:T(8,128)(2,1)S(1)}, u32[]{:S(2)}) copy-start(bf16[1024,2048]{1,0:T(8,128)(2,1)S(1)} %convolution_convert_fusion) | copy-start | bytes 12582916
  79.8 10.4 %collective-permute-start.11 = (bf16[128,1024]{1,0:T(8,128)(2,1)}, bf16[128,1024]{1,0:T(8,128)(2,1)S(1)}, u32[]{:S(2)}, u32[]{:S(2)}) collective-permute-start(bf16[128,1024]{1,0:T(8,128)(2,1)} %get-tuple-element.26), channel_id=1, source_target_pairs={{0,2},{1,3},{2,4},{3,5},{4,6},{5,7},{6,8},{7,9},{8,10},{9,11},{10,... | collective-permute-start | bytes 786440 | tf_op jit(solution)/shard_map/ppermute | solution.py:33
  81.8 9.2 %collective-permute-start.18 = (bf16[128,1024]{1,0:T(8,128)(2,1)}, bf16[128,1024]{1,0:T(8,128)(2,1)}, u32[]{:S(2)}, u32[]{:S(2)}) collective-permute-start(bf16[128,1024]{1,0:T(8,128)(2,1)} %get-tuple-element.25), channel_id=1, source_target_pairs={{0,14},{1,15},{2,0},{3,1},{4,2},{5,3},{6,4},{7,5},{8,6},{9,7},{10,... | collective-permute-start | bytes 786440 | tf_op jit(solution)/shard_map/ppermute | solution.py:34
  90.2 0.7 copy-start.14
  93.0 7.9 %collective-permute-start.12 = (bf16[128,1024]{1,0:T(8,128)(2,1)}, bf16[128,1024]{1,0:T(8,128)(2,1)}, u32[]{:S(2)}, u32[]{:S(2)}) collective-permute-start(bf16[128,1024]{1,0:T(8,128)(2,1)} %get-tuple-element.24), channel_id=1, source_target_pairs={{0,2},{1,3},{2,4},{3,5},{4,6},{5,7},{6,8},{7,9},{8,10},{9,11},{10,... | collective-permute-start | bytes 786440 | tf_op jit(solution)/shard_map/ppermute | solution.py:33
  93.0 7.9 %collective-permute-start.19 = (bf16[128,1024]{1,0:T(8,128)(2,1)S(1)}, bf16[128,1024]{1,0:T(8,128)(2,1)}, u32[]{:S(2)}, u32[]{:S(2)}) collective-permute-start(bf16[128,1024]{1,0:T(8,128)(2,1)S(1)} %get-tuple-element.23), channel_id=1, source_target_pairs={{0,14},{1,15},{2,0},{3,1},{4,2},{5,3},{6,4},{7,5},{8,6},{9,7},{10,... | collective-permute-start | bytes 786440 | tf_op jit(solution)/shard_map/ppermute | solution.py:34
  102.3 7.7 %collective-permute-start.13 = (bf16[128,1024]{1,0:T(8,128)(2,1)S(1)}, bf16[128,1024]{1,0:T(8,128)(2,1)S(1)}, u32[]{:S(2)}, u32[]{:S(2)}) collective-permute-start(bf16[128,1024]{1,0:T(8,128)(2,1)S(1)} %get-tuple-element.22), channel_id=1, source_target_pairs={{0,2},{1,3},{2,4},{3,5},{4,6},{5,7},{6,8},{7,9},{8,10},{9,11},{10,... | collective-permute-start | bytes 786440 | tf_op jit(solution)/shard_map/ppermute | solution.py:33
  104.6 7.3 %collective-permute-start.20 = (bf16[128,1024]{1,0:T(8,128)(2,1)S(1)}, bf16[128,1024]{1,0:T(8,128)(2,1)S(1)}, u32[]{:S(2)}, u32[]{:S(2)}) collective-permute-start(bf16[128,1024]{1,0:T(8,128)(2,1)S(1)} %get-tuple-element.21), channel_id=1, source_target_pairs={{0,14},{1,15},{2,0},{3,1},{4,2},{5,3},{6,4},{7,5},{8,6},{9,7},{10,... | collective-permute-start | bytes 786440 | tf_op jit(solution)/shard_map/ppermute | solution.py:34
  109.8 6.7 %copy-start.11 = (f32[384,2048]{1,0:T(8,128)}, f32[384,2048]{1,0:T(8,128)S(1)}, u32[]{:S(2)}) copy-start(f32[384,2048]{1,0:T(8,128)S(1)} %fusion) | copy-start | bytes 9437188
  109.8 21.7 %copy-start.7 = (f32[1,384,512]{2,1,0:T(8,128)S(1)}, f32[1,384,512]{2,1,0:T(8,128)}, u32[]{:S(2)}) copy-start(f32[1,384,512]{2,1,0:T(8,128)} %param.15) | copy-start | bytes 2359300
  113.2 9.5 %collective-permute-start.14 = (bf16[128,1024]{1,0:T(8,128)(2,1)S(1)}, bf16[128,1024]{1,0:T(8,128)(2,1)S(1)}, u32[]{:S(2)}, u32[]{:S(2)}) collective-permute-start(bf16[128,1024]{1,0:T(8,128)(2,1)S(1)} %get-tuple-element.20), channel_id=1, source_target_pairs={{0,2},{1,3},{2,4},{3,5},{4,6},{5,7},{6,8},{7,9},{8,10},{9,11},{10,... | collective-permute-start | bytes 786440 | tf_op jit(solution)/shard_map/ppermute | solution.py:33
  115.5 8.9 %collective-permute-start.21 = (bf16[128,1024]{1,0:T(8,128)(2,1)S(1)}, bf16[128,1024]{1,0:T(8,128)(2,1)}, u32[]{:S(2)}, u32[]{:S(2)}) collective-permute-start(bf16[128,1024]{1,0:T(8,128)(2,1)S(1)} %get-tuple-element.19), channel_id=1, source_target_pairs={{0,14},{1,15},{2,0},{3,1},{4,2},{5,3},{6,4},{7,5},{8,6},{9,7},{10,... | collective-permute-start | bytes 786440 | tf_op jit(solution)/shard_map/ppermute | solution.py:34
  117.4 13.6 %collective-permute-start.6 = (bf16[384,512]{1,0:T(8,128)(2,1)}, bf16[384,512]{1,0:T(8,128)(2,1)S(1)}, u32[]{:S(2)}, u32[]{:S(2)}) collective-permute-start(bf16[384,512]{1,0:T(8,128)(2,1)} %get-tuple-element.27), channel_id=1, source_target_pairs={{0,16},{16,32},{32,48},{48,0},{1,17},{17,33},{33,49},{49,1},{2,18}... | collective-permute-start | bytes 1179656 | tf_op jit(solution)/shard_map/ppermute | solution.py:105
  117.4 13.6 %collective-permute-start.7 = (bf16[384,512]{1,0:T(8,128)(2,1)S(1)}, bf16[384,512]{1,0:T(8,128)(2,1)S(1)}, u32[]{:S(2)}, u32[]{:S(2)}) collective-permute-start(bf16[384,512]{1,0:T(8,128)(2,1)S(1)} %get-tuple-element.29), channel_id=1, source_target_pairs={{0,32},{16,48},{32,0},{48,16},{1,33},{17,49},{33,1},{49,17},{2,34}... | collective-permute-start | bytes 1179656 | tf_op jit(solution)/shard_map/ppermute | solution.py:105
  118.4 13.1 %collective-permute-start.8 = (bf16[384,512]{1,0:T(8,128)(2,1)S(1)}, bf16[384,512]{1,0:T(8,128)(2,1)S(1)}, u32[]{:S(2)}, u32[]{:S(2)}) collective-permute-start(bf16[384,512]{1,0:T(8,128)(2,1)S(1)} %get-tuple-element.28), channel_id=1, source_target_pairs={{0,48},{16,0},{32,16},{48,32},{1,49},{17,1},{33,17},{49,33},{2,50}... | collective-permute-start | bytes 1179656 | tf_op jit(solution)/shard_map/ppermute | solution.py:105
  125.7 15.0 %copy-start.8 = (f32[1,384,512]{2,1,0:T(8,128)S(1)}, f32[1,384,512]{2,1,0:T(8,128)}, u32[]{:S(2)}) copy-start(f32[1,384,512]{2,1,0:T(8,128)} %param.13) | copy-start | bytes 2359300
  125.7 15.0 %copy-start.9 = (f32[384,512]{1,0:T(8,128)S(1)}, f32[384,512]{1,0:T(8,128)}, u32[]{:S(2)}) copy-start(f32[384,512]{1,0:T(8,128)} %param.16) | copy-start | bytes 2359300
  125.8 15.0 %copy-start.12 = (f32[1,384,512]{2,1,0:T(8,128)S(1)}, f32[1,384,512]{2,1,0:T(8,128)}, u32[]{:S(2)}) copy-start(f32[1,384,512]{2,1,0:T(8,128)} %param.14) | copy-start | bytes 2359300
  125.8 10.4 %collective-permute-start.15 = (bf16[128,1024]{1,0:T(8,128)(2,1)S(1)}, bf16[128,1024]{1,0:T(8,128)(2,1)S(1)}, u32[]{:S(2)}, u32[]{:S(2)}) collective-permute-start(bf16[128,1024]{1,0:T(8,128)(2,1)S(1)} %get-tuple-element.18), channel_id=1, source_target_pairs={{0,2},{1,3},{2,4},{3,5},{4,6},{5,7},{6,8},{7,9},{8,10},{9,11},{10,... | collective-permute-start | bytes 786440 | tf_op jit(solution)/shard_map/ppermute | solution.py:33
  127.8 8.4 %collective-permute-start.22 = (bf16[128,1024]{1,0:T(8,128)(2,1)S(1)}, bf16[128,1024]{1,0:T(8,128)(2,1)S(1)}, u32[]{:S(2)}, u32[]{:S(2)}) collective-permute-start(bf16[128,1024]{1,0:T(8,128)(2,1)S(1)} %get-tuple-element.17), channel_id=1, source_target_pairs={{0,14},{1,15},{2,0},{3,1},{4,2},{5,3},{6,4},{7,5},{8,6},{9,7},{10,... | collective-permute-start | bytes 786440 | tf_op jit(solution)/shard_map/ppermute | solution.py:34
  137.4 7.7 %collective-permute-start.16 = (bf16[128,1024]{1,0:T(8,128)(2,1)S(1)}, bf16[128,1024]{1,0:T(8,128)(2,1)S(1)}, u32[]{:S(2)}, u32[]{:S(2)}) collective-permute-start(bf16[128,1024]{1,0:T(8,128)(2,1)S(1)} %get-tuple-element.16), channel_id=1, source_target_pairs={{0,2},{1,3},{2,4},{3,5},{4,6},{5,7},{6,8},{7,9},{8,10},{9,11},{10,... | collective-permute-start | bytes 786440 | tf_op jit(solution)/shard_map/ppermute | solution.py:33
  138.0 7.1 %collective-permute-start.23 = (bf16[128,1024]{1,0:T(8,128)(2,1)S(1)}, bf16[128,1024]{1,0:T(8,128)(2,1)}, u32[]{:S(2)}, u32[]{:S(2)}) collective-permute-start(bf16[128,1024]{1,0:T(8,128)(2,1)S(1)} %get-tuple-element.15), channel_id=1, source_target_pairs={{0,14},{1,15},{2,0},{3,1},{4,2},{5,3},{6,4},{7,5},{8,6},{9,7},{10,... | collective-permute-start | bytes 786440 | tf_op jit(solution)/shard_map/ppermute | solution.py:34
  142.3 7.6 %collective-permute-start.9 = (bf16[384,512]{1,0:T(8,128)(2,1)S(1)}, bf16[384,512]{1,0:T(8,128)(2,1)S(1)}, u32[]{:S(2)}, u32[]{:S(2)}) collective-permute-start(bf16[384,512]{1,0:T(8,128)(2,1)S(1)} %get-tuple-element.31), channel_id=1, source_target_pairs={{0,64},{64,0},{128,192},{192,128},{1,65},{65,1},{129,193},{193,129... | collective-permute-start | bytes 1179656 | tf_op jit(solution)/shard_map/ppermute | solution.py:126
  142.3 20.2 %copy-start.13 = (f32[384,512]{1,0:T(8,128)S(1)}, f32[384,512]{1,0:T(8,128)}, u32[]{:S(2)}) copy-start(f32[384,512]{1,0:T(8,128)} %param.17) | copy-start | bytes 2359300
  146.4 7.8 %collective-permute-start.17 = (bf16[128,1024]{1,0:T(8,128)(2,1)S(1)}, bf16[128,1024]{1,0:T(8,128)(2,1)S(1)}, u32[]{:S(2)}, u32[]{:S(2)}) collective-permute-start(bf16[128,1024]{1,0:T(8,128)(2,1)S(1)} %get-tuple-element.14), channel_id=1, source_target_pairs={{0,2},{1,3},{2,4},{3,5},{4,6},{5,7},{6,8},{7,9},{8,10},{9,11},{10,... | collective-permute-start | bytes 786440 | tf_op jit(solution)/shard_map/ppermute | solution.py:33
  147.4 6.7 %collective-permute-start.24 = (bf16[128,1024]{1,0:T(8,128)(2,1)S(1)}, bf16[128,1024]{1,0:T(8,128)(2,1)S(1)}, u32[]{:S(2)}, u32[]{:S(2)}) collective-permute-start(bf16[128,1024]{1,0:T(8,128)(2,1)S(1)} %get-tuple-element.13), channel_id=1, source_target_pairs={{0,14},{1,15},{2,0},{3,1},{4,2},{5,3},{6,4},{7,5},{8,6},{9,7},{10,... | collective-permute-start | bytes 786440 | tf_op jit(solution)/shard_map/ppermute | solution.py:34
  150.0 12.5 %collective-permute-start.10 = (bf16[384,512]{1,0:T(8,128)(2,1)S(1)}, bf16[384,512]{1,0:T(8,128)(2,1)S(1)}, u32[]{:S(2)}, u32[]{:S(2)}) collective-permute-start(bf16[384,512]{1,0:T(8,128)(2,1)S(1)} %add_convert_fusion), channel_id=1, source_target_pairs={{0,128},{64,192},{128,0},{192,64},{1,129},{65,193},{129,1},{193,65... | collective-permute-start | bytes 1179656 | tf_op jit(solution)/shard_map/ppermute | solution.py:126
  155.4 9.9 %collective-permute-start.25 = (bf16[64,2048]{1,0:T(8,128)(2,1)S(1)}, bf16[64,2048]{1,0:T(8,128)(2,1)S(1)}, u32[]{:S(2)}, u32[]{:S(2)}) collective-permute-start(bf16[64,2048]{1,0:T(8,128)(2,1)S(1)} %fusion.12), channel_id=1, source_target_pairs={{0,1},{1,0},{2,3},{3,2},{4,5},{5,4},{6,7},{7,6},{8,9},{9,8},{10,11... | collective-permute-start | bytes 786440 | tf_op jit(solution)/shard_map/ppermute | solution.py:41

commit v3 on v2

--- a/solution.py
+++ b/solution.py
@@ -16,6 +16,7 @@
     m = lax.axis_index("mp")
     nlo = 2
     nz = nmp // nlo
+    far = nz // 2
     z = m // nlo
     lo = m % nlo
     rows = part.shape[0] // nz
@@ -23,18 +24,24 @@
     up = [(i, ((i // nlo + 1) % nz) * nlo + i % nlo) for i in range(nmp)]
     down = [(i, ((i // nlo - 1) % nz) * nlo + i % nlo) for i in range(nmp)]
 
-    def chunk(c, h):
-        blk = lax.dynamic_slice_in_dim(part, c * rows, rows, axis=0)
-        return blk[:, h * halfc : (h + 1) * halfc].astype(jnp.float32)
+    def chunk(c):
+        return lax.dynamic_slice_in_dim(part, (c % nz) * rows, rows, axis=0).astype(jnp.float32)
 
-    acc_a = chunk((z - 1) % nz, 0)
-    acc_b = chunk((z + 1) % nz, 1)
-    for t in range(1, nz):
-        got_a = lax.ppermute(acc_a.astype(jnp.bfloat16), "mp", up)
-        got_b = lax.ppermute(acc_b.astype(jnp.bfloat16), "mp", down)
-        acc_a = got_a.astype(jnp.float32) + chunk((z - t - 1) % nz, 0)
-        acc_b = got_b.astype(jnp.float32) + chunk((z + t + 1) % nz, 1)
-    acc = jnp.concatenate([acc_a, acc_b], axis=1)
+    first = chunk(z + far)
+    send_a = first[:, :halfc]
+    send_b = first[:, halfc:]
+    for r in range(2, far + 2):
+        got_a = lax.ppermute(send_a.astype(jnp.bfloat16), "mp", up).astype(jnp.float32)
+        got_b = lax.ppermute(send_b.astype(jnp.bfloat16), "mp", down).astype(jnp.float32)
+        own_a = chunk(z + far + 1 - r)
+        own_b = chunk(z - far - 1 + r)
+        if r == 2:
+            got_a = jnp.concatenate([got_a, jnp.zeros_like(got_a)], axis=1)
+            got_b = jnp.concatenate([jnp.zeros_like(got_b), got_b], axis=1)
+        if r <= far:
+            send_a = got_a + own_a
+            send_b = got_b + own_b
+    acc = own_a + got_a + got_b
     sub = rows // nlo
     mine = lax.dynamic_slice_in_dim(acc, lo * sub, sub, axis=0)
     other = lax.dynamic_slice_in_dim(acc, (1 - lo) * sub, sub, axis=0)
@@ -61,24 +68,29 @@
     down_half = master.astype(jnp.bfloat16)
     ff = master.shape[0]
 
+    assert ndp == 4
     shard = jnp.concatenate([gate_weight[0], up_weight[0], down_half.T], axis=1)
     rows = shard.shape[0]
     half = rows // 2
-    a, b = shard[:half], shard[half:]
-    pieces = [(j, 0, a), (j, 1, b)]
-    for s in range(1, ndp):
-        a = lax.ppermute(a, "dp", _shift(ndp, 1))
-        b = lax.ppermute(b, "dp", _shift(ndp, -1))
-        pieces.append(((j - s) % ndp, 0, a))
-        pieces.append(((j + s) % ndp, 1, b))
+    from_left = lax.ppermute(shard, "dp", _shift(ndp, 1))
+    from_right = lax.ppermute(shard, "dp", _shift(ndp, -1))
+    far_a = lax.ppermute(from_left[:half], "dp", _shift(ndp, 1))
+    far_b = lax.ppermute(from_right[half:], "dp", _shift(ndp, -1))
+    pieces = [
+        (j * rows, shard),
+        (((j - 1) % ndp) * rows, from_left),
+        (((j + 1) % ndp) * rows, from_right),
+        (((j + 2) % ndp) * rows, far_a),
+        (((j + 2) % ndp) * rows + half, far_b),
+    ]
 
     gu_pre = None
     grad_hidden = None
     weights_full = jnp.zeros((rows * ndp, 2 * ff), jnp.bfloat16)
-    for src, h, piece in pieces:
-        start = src * rows + h * half
-        xs = lax.dynamic_slice_in_dim(inputs, start, half, axis=1)
-        gs = lax.dynamic_slice_in_dim(upstream, start, half, axis=1)
+    for start, piece in pieces:
+        size = piece.shape[0]
+        xs = lax.dynamic_slice_in_dim(inputs, start, size, axis=1)
+        gs = lax.dynamic_slice_in_dim(upstream, start, size, axis=1)
         p1 = jnp.dot(xs, piece[:, : 2 * ff], preferred_element_type=jnp.float32)
         p2 = jnp.dot(gs, piece[:, 2 * ff :], preferred_element_type=jnp.float32)
         gu_pre = p1 if gu_pre is None else gu_pre + p1

time: 167 us -> 130 us (0.78)
  matrix products: 42.1 us -> 18.5 us
  starting transfers between devices: 40.2 us -> 30.6 us
  waiting for transfers between devices: 49.4 us -> 56.7 us
  other arithmetic: 18.8 us -> 12 us
  local copies, waits for them, and re-layouts: 14.7 us -> 11.2 us
    dot_general x8 -> x5, matrix products: 19 us -> 4.26 us  [shards(): p2 = jnp.dot(gs, piece[:, 2 * ff:], preferred_element_type=jnp.float32)]
    ppermute x20 -> x12, starting transfers between devices: 34.1 us -> 22.7 us  [the longest x4 15.6 us: _ring_reduce_scatter(): lax.ppermute(send_b.astype(jnp.bfloat16), 'mp', down).astype(jnp.float32)]
    dot_general x8 -> x5, matrix products: 13.5 us -> 5.6 us  [shards(): p1 = jnp.dot(xs, piece[:, :2 * ff], preferred_element_type=jnp.float32)]
    ppermute x3, waiting for transfers between devices: 2.4 us -> 9.54 us  [shards(): got = lax.ppermute(blk.astype(jnp.bfloat16), 'dp', _shift(ndp, s))]
    ppermute x2, waiting for transfers between devices: 6.53 us -> 0.01 us  [shards(): lax.ppermute(mine, 'outer', perm).astype(jnp.float32)]
    convert_element_type x7 -> x3, other arithmetic: 8.53 us -> 2.12 us  [_ring_reduce_scatter(): send_a.astype(jnp.bfloat16)]
    ppermute x1, waiting for transfers between devices: 1.38 us -> 6.03 us  [_ring_reduce_scatter(): lax.ppermute(other.astype(jnp.bfloat16), 'mp', [(i, i ^ 1) for i in range...]
    dynamic_update_slice x6 -> x4, local copies, waits for them, and re-layouts: 4.88 us -> 1.44 us  [shards(): lax.dynamic_update_slice(weights_full, piece[:, :2 * ff], (start, 0))]
  transfers between devices with their start and end apart: 26 -> 18, of which waited for: 16 -> 8; matrix products, arithmetic and copies ran while one was open for 28% -> 18% of each run, Pallas kernels for 0% -> 0%
where the time goes in v3:
time: 130 us
  waiting for transfers between devices  56.7 us (44%)
  starting transfers between devices  30.6 us (24%)
  matrix products  18.5 us (14%)
  other arithmetic  12 us (9%)
  local copies, waits for them, and re-layouts  11.2 us (9%)
    ppermute x1, waiting for transfers between devices, shards(): from_left = lax.ppermute(shard, 'dp', _shift(ndp, 1))  20.7 us
    ppermute x4, starting transfers between devices, _ring_reduce_scatter(): lax.ppermute(send_b.astype(jnp.bfloat16), 'mp', down).astype(jnp.float32)  15.6 us
    ppermute x4, waiting for transfers between devices, _ring_reduce_scatter(): lax.ppermute(send_a.astype(jnp.bfloat16), 'mp', up).astype(jnp.float32)  12.5 us
    ppermute x3, waiting for transfers between devices, shards(): got = lax.ppermute(blk.astype(jnp.bfloat16), 'dp', _shift(ndp, s))  9.54 us
    unnamed x22, local copies, waits for them, and re-layouts  8.03 us
    ppermute x1, waiting for transfers between devices, _ring_reduce_scatter(): lax.ppermute(other.astype(jnp.bfloat16), 'mp', [(i, i ^ 1) for i in range...  6.03 us
    dot_general x5, matrix products, shards(): p1 = jnp.dot(xs, piece[:, :2 * ff], preferred_element_type=jnp.float32)  5.6 us
    ppermute x3, starting transfers between devices, shards(): got = lax.ppermute(blk.astype(jnp.bfloat16), 'dp', _shift(ndp, s))  4.99 us
  transfers between devices with their start and end apart: 18, of which 8 were waited for; matrix products, arithmetic and copies ran while one was open for 18% of the time, Pallas kernels for 0%

profile of v3, /device:TPU:8, one launch (start us, length us, event | category | flops | bytes accessed | tf_op | source)
XLA Modules:
  0.0 129.9 jit_solution(2358100967622704662)
XLA Ops:
  0.6 1.2 copy.14
  1.8 1.2 copy.15
  3.0 1.2 fusion.48
  4.2 1.1 pad_maximum_fusion
  5.3 1.5 %collective-permute-start = (bf16[512,1152]{0,1:T(8,128)(2,1)}, bf16[512,1152]{0,1:T(8,128)(2,1)S(1)}, u32[]{:S(2)}, u32[]{:S(2)}) collective-permute-start(bf16[512,1152]{0,1:T(8,128)(2,1)} %pad_maximum_fusion), channel_id=1, source_target_pairs={{0,16},{16,32},{32,48},{48,0},{1,17},{17,33},{33,49},{49,1},{2,18}... | collective-permute-start | bytes 3538952 | tf_op jit(solution)/shard_map/ppermute | solution.py:75
  6.8 1.7 %collective-permute-start.1 = (bf16[512,1152]{0,1:T(8,128)(2,1)}, bf16[512,1152]{0,1:T(8,128)(2,1)}, u32[]{:S(2)}, u32[]{:S(2)}) collective-permute-start(bf16[512,1152]{0,1:T(8,128)(2,1)} %pad_maximum_fusion), channel_id=1, source_target_pairs={{0,48},{16,0},{32,16},{48,32},{1,49},{17,1},{33,17},{49,33},{2,50}... | collective-permute-start | bytes 3538952 | tf_op jit(solution)/shard_map/ppermute | solution.py:76
  8.5 0.4 broadcast_in_dim.14
  8.9 0.1 fusion.47
  9.0 1.7 %copy-done.9 = bf16[1,1024,2048]{2,1,0:T(8,128)(2,1)S(1)} copy-done((bf16[1,1024,2048]{2,1,0:T(8,128)(2,1)S(1)}, bf16[1,1024,2048]{2,1,0:T(8,128)(2,1)}, u32[]{:S(2)}) %copy-start.9) | copy-done | bytes 4194328
  10.7 1.0 fusion.16
  11.7 0.1 copy-done
  11.8 1.3 %copy-done.3 = bf16[1,1024,2048]{2,1,0:T(8,128)(2,1)S(1)} copy-done((bf16[1,1024,2048]{2,1,0:T(8,128)(2,1)S(1)}, bf16[1,1024,2048]{2,1,0:T(8,128)(2,1)}, u32[]{:S(2)}) %copy-start.3) | copy-done | bytes 4194328
  13.1 0.6 fusion.10
  13.7 20.7 %collective-permute-done = bf16[512,1152]{0,1:T(8,128)(2,1)S(1)} collective-permute-done((bf16[512,1152]{0,1:T(8,128)(2,1)}, bf16[512,1152]{0,1:T(8,128)(2,1)S(1)}, u32[]{:S(2)}, u32[]{:S(2)}) %collective-permute-start) | collective-permute-done | bytes 1179680 | tf_op jit(solution)/shard_map/ppermute | solution.py:75
  34.4 0.4 collective-permute-start.2
  34.8 1.1 slice.69
  35.9 3.2 %collective-permute-start.3 = (bf16[256,1152]{0,1:T(8,128)(2,1)S(1)}, bf16[256,1152]{0,1:T(8,128)(2,1)S(1)}, u32[]{:S(2)}, u32[]{:S(2)}) collective-permute-start(bf16[256,1152]{0,1:T(8,128)(2,1)S(1)} %slice.69), channel_id=1, source_target_pairs={{0,48},{16,0},{32,16},{48,32},{1,49},{17,1},{33,17},{49,33},{2,50}... | collective-permute-start | bytes 1769480 | tf_op jit(solution)/shard_map/ppermute | solution.py:78
  39.1 2.1 %fusion.12 = f32[1024,768]{0,1:T(8,128)S(1)} fusion(bf16[1,1024,2048]{2,1,0:T(8,128)(2,1)S(1)} %copy-done.9, s32[]{:T(128)S(6)} %select_n.130, bf16[512,1152]{0,1:T(8,128)(2,1)} %collective-permute-done.1), kind=kOutput, calls=%fused_computation.21 | convolution fusion | flops 805306368 | bytes 4980740 | tf_op jit(solution)/shard_map/dot_general | solution.py:94
  41.3 1.6 %fusion.6 = f32[1024,384]{0,1:T(8,128)S(1)} fusion(bf16[1,1024,2048]{2,1,0:T(8,128)(2,1)S(1)} %copy-done.3, s32[]{:T(128)S(6)} %select_n.130, bf16[512,1152]{0,1:T(8,128)(2,1)} %collective-permute-done.1), kind=kOutput, calls=%fused_computation.15 | convolution fusion | flops 402653184 | bytes 3014660 | tf_op jit(solution)/shard_map/dot_general | solution.py:95
  42.9 0.6 fusion.8
  43.5 0.1 slice_dynamic-update-slice_fusion.1
  43.6 1.2 slice_dynamic-update-slice_fusion
  44.9 1.0 fusion.14
  45.9 4.0 %collective-permute-done.2 = bf16[256,1152]{0,1:T(8,128)(2,1)S(1)} collective-permute-done((bf16[256,1152]{0,1:T(8,128)(2,1)S(1)}, bf16[256,1152]{0,1:T(8,128)(2,1)S(1)}, u32[]{:S(2)}, u32[]{:S(2)}) %collective-permute-start.2) | collective-permute-done | bytes 589856 | tf_op jit(solution)/shard_map/ppermute | solution.py:77
  50.0 0.4 fusion.35
  50.4 0.6 fusion.41
  51.0 0.0 collective-permute-done.3
  51.1 0.8 add_add_fusion
  51.9 1.0 multiply_convert_fusion.1
  52.9 0.6 copy-done.4
  53.6 3.7 %convolution_convert_fusion = bf16[1024,2048]{1,0:T(8,128)(2,1)S(1)} fusion(bf16[2048,768]{0,1:T(8,128)(2,1)S(1)} %slice_dynamic-update-slice_fusion.2, bf16[1024,384]{0,1:T(8,128)(2,1)S(1)} %get-tuple-element.10, bf16[1024,384]{0,1:T(8,128)(2,1)S(1)} %get-tuple-element.9), kind=kOutput, calls=%fused_computation.2 | convolution fusion | flops 3226468352 | bytes 8912896 | tf_op jit(solution)/shard_map/dot_general | solution.py:121
  57.3 2.0 %copy-done.1 = bf16[1024,2048]{1,0:T(8,128)(2,1)} copy-done((bf16[1024,2048]{1,0:T(8,128)(2,1)}, bf16[1024,2048]{1,0:T(8,128)(2,1)S(1)}, u32[]{:S(2)}) %copy-start.1) | copy-done | bytes 4194328
  59.3 5.9 %collective-permute-start.13 = (bf16[128,1024]{1,0:T(8,128)(2,1)S(1)}, bf16[128,1024]{1,0:T(8,128)(2,1)S(1)}, u32[]{:S(2)}, u32[]{:S(2)}) collective-permute-start(bf16[128,1024]{1,0:T(8,128)(2,1)S(1)} %get-tuple-element.18), channel_id=1, source_target_pairs={{0,14},{1,15},{2,0},{3,1},{4,2},{5,3},{6,4},{7,5},{8,6},{9,7},{10,... | collective-permute-start | bytes 786440 | tf_op jit(solution)/shard_map/ppermute | solution.py:35
  65.2 3.9 %collective-permute-done.13 = bf16[128,1024]{1,0:T(8,128)(2,1)S(1)} collective-permute-done((bf16[128,1024]{1,0:T(8,128)(2,1)S(1)}, bf16[128,1024]{1,0:T(8,128)(2,1)S(1)}, u32[]{:S(2)}, u32[]{:S(2)}) %collective-permute-start.13) | collective-permute-done | bytes 262176 | tf_op jit(solution)/shard_map/ppermute | solution.py:35
  69.1 3.7 %collective-permute-done.9 = bf16[128,1024]{1,0:T(8,128)(2,1)S(1)} collective-permute-done((bf16[128,1024]{1,0:T(8,128)(2,1)S(1)}, bf16[128,1024]{1,0:T(8,128)(2,1)S(1)}, u32[]{:S(2)}, u32[]{:S(2)}) %collective-permute-start.9) | collective-permute-done | bytes 262176 | tf_op jit(solution)/shard_map/ppermute | solution.py:34
  72.8 1.4 %add_convert_fusion.5 = (bf16[128,2048]{1,0:T(8,128)(2,1)S(1)}, bf16[128,2048]{1,0:T(8,128)(2,1)S(1)}) fusion(bf16[1024,2048]{1,0:T(8,128)(2,1)} %copy-done.1, s32[]{:T(128)S(6)} %select_n.142, bf16[128,1024]{1,0:T(8,128)(2,1)S(1)} %collective-permute-done.9, s32[]{:T(128)S(6)} %select_n.148, bf16[128,1024]{1,0:T(8,128)(2,1)S(1)} %collective-permute-done.13), kind=kLoop, calls=%fused_computation.33 | loop fusion | flops 2097152 | bytes 2621448 | tf_op jit(solution)/shard_map/convert_element_type | solution.py:34
  74.2 0.1 collective-permute-start.10
  74.3 3.2 %collective-permute-start.14 = (bf16[128,2048]{1,0:T(8,128)(2,1)S(1)}, bf16[128,2048]{1,0:T(8,128)(2,1)S(1)}, u32[]{:S(2)}, u32[]{:S(2)}) collective-permute-start(bf16[128,2048]{1,0:T(8,128)(2,1)S(1)} %get-tuple-element.16), channel_id=1, source_target_pairs={{0,14},{1,15},{2,0},{3,1},{4,2},{5,3},{6,4},{7,5},{8,6},{9,7},{10,... | collective-permute-start | bytes 1572872 | tf_op jit(solution)/shard_map/ppermute | solution.py:35
  77.5 5.0 %fusion = f32[384,2048]{1,0:T(8,128)S(1)} fusion(bf16[1,1024,2048]{2,1,0:T(8,128)(2,1)} %param.10, f32[1024,768]{0,1:T(8,128)} %copy-done.4), kind=kOutput, calls=%fused_computation | convolution fusion | flops 1612972032 | bytes 10485760 | tf_op jit(solution)/shard_map/dot_general | solution.py:110
  82.5 0.0 copy-start.5
  82.5 0.2 dynamic-slice_convert_fusion.2
  82.6 1.0 collective-permute-start.4
  83.6 4.0 %collective-permute-start.5 = (bf16[384,512]{1,0:T(8,128)(2,1)S(1)}, bf16[384,512]{1,0:T(8,128)(2,1)S(1)}, u32[]{:S(2)}, u32[]{:S(2)}) collective-permute-start(bf16[384,512]{1,0:T(8,128)(2,1)S(1)} %get-tuple-element.21), channel_id=1, source_target_pairs={{0,32},{16,48},{32,0},{48,16},{1,33},{17,49},{33,1},{49,17},{2,34}... | collective-permute-start | bytes 1179656 | tf_op jit(solution)/shard_map/ppermute | solution.py:117
  87.6 0.0 collective-permute-start.6
  87.6 0.0 collective-permute-done.10
  87.7 0.4 add_convert_fusion.4
  88.0 0.1 collective-permute-start.11
  88.1 3.2 %collective-permute-start.15 = (bf16[128,2048]{1,0:T(8,128)(2,1)S(1)}, bf16[128,2048]{1,0:T(8,128)(2,1)S(1)}, u32[]{:S(2)}, u32[]{:S(2)}) collective-permute-start(bf16[128,2048]{1,0:T(8,128)(2,1)S(1)} %get-tuple-element.14), channel_id=1, source_target_pairs={{0,14},{1,15},{2,0},{3,1},{4,2},{5,3},{6,4},{7,5},{8,6},{9,7},{10,... | collective-permute-start | bytes 1572872 | tf_op jit(solution)/shard_map/ppermute | solution.py:35
  91.4 4.8 %collective-permute-done.4 = bf16[384,512]{1,0:T(8,128)(2,1)S(1)} collective-permute-done((bf16[384,512]{1,0:T(8,128)(2,1)S(1)}, bf16[384,512]{1,0:T(8,128)(2,1)S(1)}, u32[]{:S(2)}, u32[]{:S(2)}) %collective-permute-start.4) | collective-permute-done | bytes 393248 | tf_op jit(solution)/shard_map/ppermute | solution.py:117
  96.1 4.7 %collective-permute-done.5 = bf16[384,512]{1,0:T(8,128)(2,1)S(1)} collective-permute-done((bf16[384,512]{1,0:T(8,128)(2,1)S(1)}, bf16[384,512]{1,0:T(8,128)(2,1)S(1)}, u32[]{:S(2)}, u32[]{:S(2)}) %collective-permute-start.5) | collective-permute-done | bytes 393248 | tf_op jit(solution)/shard_map/ppermute | solution.py:117
  100.9 1.2 fusion.57
  102.1 1.5 %fusion.56 = (f32[1,384,512]{2,1,0:T(8,128)}, bf16[384,512]{1,0:T(8,128)(2,1)S(1)}) fusion(f32[384,512]{1,0:T(8,128)S(1)} %get-tuple-element.6, f32[1,384,512]{2,1,0:T(8,128)S(1)} %copy-done.7, f32[384,512]{1,0:T(8,128)S(1)} %copy-done.6, f32[1,384,512]{2,1,0:T(8,128)S(1)} %copy-done.5, f32[1,384,512]{2,1,0:T(8,128)S(1)} %copy-done), kind=kLoop, calls=%fused_computation.87 | loop fusion | flops 3342336 | bytes 5111808 | tf_op jit(solution)/shard_map/broadcast_in_dim | solution.py:143
  103.7 0.0 collective-permute-start.7
  103.7 0.4 add_convert_fusion.3
  104.1 0.1 collective-permute-start.12
  104.2 3.2 %collective-permute-start.16 = (bf16[128,2048]{1,0:T(8,128)(2,1)S(1)}, bf16[128,2048]{1,0:T(8,128)(2,1)}, u32[]{:S(2)}, u32[]{:S(2)}) collective-permute-start(bf16[128,2048]{1,0:T(8,128)(2,1)S(1)} %get-tuple-element.12), channel_id=1, source_target_pairs={{0,14},{1,15},{2,0},{3,1},{4,2},{5,3},{6,4},{7,5},{8,6},{9,7},{10,... | collective-permute-start | bytes 1572872 | tf_op jit(solution)/shard_map/ppermute | solution.py:35
  107.4 1.1 add_convert_fusion.6
  108.5 2.4 %collective-permute-start.8 = (bf16[384,512]{1,0:T(8,128)(2,1)S(1)}, bf16[384,512]{1,0:T(8,128)(2,1)S(1)}, u32[]{:S(2)}, u32[]{:S(2)}) collective-permute-start(bf16[384,512]{1,0:T(8,128)(2,1)S(1)} %add_convert_fusion.6), channel_id=1, source_target_pairs={{0,128},{64,192},{128,0},{192,64},{1,129},{65,193},{129,1},{193,65... | collective-permute-start | bytes 1179656 | tf_op jit(solution)/shard_map/ppermute | solution.py:138
  110.9 8.8 %collective-permute-done.12 = bf16[128,2048]{1,0:T(8,128)(2,1)S(1)} collective-permute-done((bf16[128,2048]{1,0:T(8,128)(2,1)S(1)}, bf16[128,2048]{1,0:T(8,128)(2,1)S(1)}, u32[]{:S(2)}, u32[]{:S(2)}) %collective-permute-start.12) | collective-permute-done | bytes 524320 | tf_op jit(solution)/shard_map/ppermute | solution.py:34
  119.7 1.4 %convert_add_fusion = f32[128,2048]{1,0:T(8,128)S(1)} fusion(bf16[128,2048]{1,0:T(8,128)(2,1)} %collective-permute-done.16, bf16[128,2048]{1,0:T(8,128)(2,1)S(1)} %collective-permute-done.12, bf16[1024,2048]{1,0:T(8,128)(2,1)} %copy-done.1, s32[]{:T(128)S(6)} %select_n.138), kind=kLoop, calls=%fused_computation.27 | loop fusion | flops 1310720 | bytes 2621444 | tf_op jit(solution)/shard_map/add | solution.py:44
  121.2 0.5 collective-permute-start.17
  121.7 1.4 %multiply_subtract_fusion = (f32[384,512]{1,0:T(8,128)}, f32[384,512]{1,0:T(8,128)}) fusion(f32[384,512]{1,0:T(8,128)S(1)} %copy-done.6, bf16[384,512]{1,0:T(8,128)(2,1)S(1)} %collective-permute-done.8, bf16[384,512]{1,0:T(8,128)(2,1)S(1)} %add_convert_fusion.6, f32[384,512]{1,0:T(8,128)S(1)} %copy-done.8), kind=kLoop, calls=%fused_computation.50 | loop fusion | flops 1966080 | bytes 3932160 | tf_op jit(solution)/shard_map/sub | solution.py:142
  123.2 6.0 %collective-permute-done.17 = bf16[64,2048]{1,0:T(8,128)(2,1)S(1)} collective-permute-done((bf16[64,2048]{1,0:T(8,128)(2,1)S(1)}, bf16[64,2048]{1,0:T(8,128)(2,1)S(1)}, u32[]{:S(2)}, u32[]{:S(2)}) %collective-permute-start.17) | collective-permute-done | bytes 262176 | tf_op jit(solution)/shard_map/ppermute | solution.py:48
  129.2 0.7 fusion.55
  (28 shorter events, 0.3 us)
Async XLA Ops:
  5.3 29.1 %collective-permute-start = (bf16[512,1152]{0,1:T(8,128)(2,1)}, bf16[512,1152]{0,1:T(8,128)(2,1)S(1)}, u32[]{:S(2)}, u32[]{:S(2)}) collective-permute-start(bf16[512,1152]{0,1:T(8,128)(2,1)} %pad_maximum_fusion), channel_id=1, source_target_pairs={{0,16},{16,32},{32,48},{48,0},{1,17},{17,33},{33,49},{49,1},{2,18}... | collective-permute-start | bytes 3538952 | tf_op jit(solution)/shard_map/ppermute | solution.py:75
  6.8 28.0 %collective-permute-start.1 = (bf16[512,1152]{0,1:T(8,128)(2,1)}, bf16[512,1152]{0,1:T(8,128)(2,1)}, u32[]{:S(2)}, u32[]{:S(2)}) collective-permute-start(bf16[512,1152]{0,1:T(8,128)(2,1)} %pad_maximum_fusion), channel_id=1, source_target_pairs={{0,48},{16,0},{32,16},{48,32},{1,49},{17,1},{33,17},{49,33},{2,50}... | collective-permute-start | bytes 3538952 | tf_op jit(solution)/shard_map/ppermute | solution.py:76
  8.5 2.2 %copy-start.9 = (bf16[1,1024,2048]{2,1,0:T(8,128)(2,1)S(1)}, bf16[1,1024,2048]{2,1,0:T(8,128)(2,1)}, u32[]{:S(2)}) copy-start(bf16[1,1024,2048]{2,1,0:T(8,128)(2,1)} %param.9) | copy-start | bytes 12582916
  10.7 1.1 copy-start
  10.7 2.4 %copy-start.3 = (bf16[1,1024,2048]{2,1,0:T(8,128)(2,1)S(1)}, bf16[1,1024,2048]{2,1,0:T(8,128)(2,1)}, u32[]{:S(2)}) copy-start(bf16[1,1024,2048]{2,1,0:T(8,128)(2,1)} %param.10) | copy-start | bytes 12582916
  34.4 15.5 %collective-permute-start.2 = (bf16[256,1152]{0,1:T(8,128)(2,1)S(1)}, bf16[256,1152]{0,1:T(8,128)(2,1)S(1)}, u32[]{:S(2)}, u32[]{:S(2)}) collective-permute-start(bf16[256,1152]{0,1:T(8,128)(2,1)S(1)} %slice.67), channel_id=1, source_target_pairs={{0,16},{16,32},{32,48},{48,0},{1,17},{17,33},{33,49},{49,1},{2,18}... | collective-permute-start | bytes 1769480 | tf_op jit(solution)/shard_map/ppermute | solution.py:77
  35.9 15.1 %collective-permute-start.3 = (bf16[256,1152]{0,1:T(8,128)(2,1)S(1)}, bf16[256,1152]{0,1:T(8,128)(2,1)S(1)}, u32[]{:S(2)}, u32[]{:S(2)}) collective-permute-start(bf16[256,1152]{0,1:T(8,128)(2,1)S(1)} %slice.69), channel_id=1, source_target_pairs={{0,48},{16,0},{32,16},{48,32},{1,49},{17,1},{33,17},{49,33},{2,50}... | collective-permute-start | bytes 1769480 | tf_op jit(solution)/shard_map/ppermute | solution.py:78
  51.9 1.7 %copy-start.4 = (f32[1024,768]{0,1:T(8,128)}, f32[1024,768]{0,1:T(8,128)S(1)}, u32[]{:S(2)}) copy-start(f32[1024,768]{0,1:T(8,128)S(1)} %add_add_fusion) | copy-start | bytes 9437188
  57.3 2.0 %copy-start.1 = (bf16[1024,2048]{1,0:T(8,128)(2,1)}, bf16[1024,2048]{1,0:T(8,128)(2,1)S(1)}, u32[]{:S(2)}) copy-start(bf16[1024,2048]{1,0:T(8,128)(2,1)S(1)} %convolution_convert_fusion) | copy-start | bytes 12582916
  59.3 9.8 %collective-permute-start.13 = (bf16[128,1024]{1,0:T(8,128)(2,1)S(1)}, bf16[128,1024]{1,0:T(8,128)(2,1)S(1)}, u32[]{:S(2)}, u32[]{:S(2)}) collective-permute-start(bf16[128,1024]{1,0:T(8,128)(2,1)S(1)} %get-tuple-element.18), channel_id=1, source_target_pairs={{0,14},{1,15},{2,0},{3,1},{4,2},{5,3},{6,4},{7,5},{8,6},{9,7},{10,... | collective-permute-start | bytes 786440 | tf_op jit(solution)/shard_map/ppermute | solution.py:35
  65.2 7.6 %collective-permute-start.9 = (bf16[128,1024]{1,0:T(8,128)(2,1)S(1)}, bf16[128,1024]{1,0:T(8,128)(2,1)S(1)}, u32[]{:S(2)}, u32[]{:S(2)}) collective-permute-start(bf16[128,1024]{1,0:T(8,128)(2,1)S(1)} %get-tuple-element.17), channel_id=1, source_target_pairs={{0,2},{1,3},{2,4},{3,5},{4,6},{5,7},{6,8},{7,9},{8,10},{9,11},{10,... | collective-permute-start | bytes 786440 | tf_op jit(solution)/shard_map/ppermute | solution.py:34
  74.2 13.5 %collective-permute-start.10 = (bf16[128,2048]{1,0:T(8,128)(2,1)S(1)}, bf16[128,2048]{1,0:T(8,128)(2,1)S(1)}, u32[]{:S(2)}, u32[]{:S(2)}) collective-permute-start(bf16[128,2048]{1,0:T(8,128)(2,1)S(1)} %get-tuple-element.15), channel_id=1, source_target_pairs={{0,2},{1,3},{2,4},{3,5},{4,6},{5,7},{6,8},{7,9},{8,10},{9,11},{10,... | collective-permute-start | bytes 1572872 | tf_op jit(solution)/shard_map/ppermute | solution.py:34
  74.3 13.4 %copy-start.2 = (bf16[1024,2048]{1,0:T(8,128)(2,1)S(1)}, bf16[1024,2048]{1,0:T(8,128)(2,1)}, u32[]{:S(2)}) copy-start(bf16[1024,2048]{1,0:T(8,128)(2,1)} %copy-done.1) | copy-start | bytes 12582916
  74.3 13.4 %collective-permute-start.14 = (bf16[128,2048]{1,0:T(8,128)(2,1)S(1)}, bf16[128,2048]{1,0:T(8,128)(2,1)S(1)}, u32[]{:S(2)}, u32[]{:S(2)}) collective-permute-start(bf16[128,2048]{1,0:T(8,128)(2,1)S(1)} %get-tuple-element.16), channel_id=1, source_target_pairs={{0,14},{1,15},{2,0},{3,1},{4,2},{5,3},{6,4},{7,5},{8,6},{9,7},{10,... | collective-permute-start | bytes 1572872 | tf_op jit(solution)/shard_map/ppermute | solution.py:35
  82.5 18.4 %copy-start.5 = (f32[1,384,512]{2,1,0:T(8,128)S(1)}, f32[1,384,512]{2,1,0:T(8,128)}, u32[]{:S(2)}) copy-start(f32[1,384,512]{2,1,0:T(8,128)} %param.15) | copy-start | bytes 2359300
  82.6 13.5 %collective-permute-start.4 = (bf16[384,512]{1,0:T(8,128)(2,1)S(1)}, bf16[384,512]{1,0:T(8,128)(2,1)S(1)}, u32[]{:S(2)}, u32[]{:S(2)}) collective-permute-start(bf16[384,512]{1,0:T(8,128)(2,1)S(1)} %get-tuple-element.19), channel_id=1, source_target_pairs={{0,16},{16,32},{32,48},{48,0},{1,17},{17,33},{33,49},{49,1},{2,18}... | collective-permute-start | bytes 1179656 | tf_op jit(solution)/shard_map/ppermute | solution.py:117
  83.6 17.3 %collective-permute-start.5 = (bf16[384,512]{1,0:T(8,128)(2,1)S(1)}, bf16[384,512]{1,0:T(8,128)(2,1)S(1)}, u32[]{:S(2)}, u32[]{:S(2)}) collective-permute-start(bf16[384,512]{1,0:T(8,128)(2,1)S(1)} %get-tuple-element.21), channel_id=1, source_target_pairs={{0,32},{16,48},{32,0},{48,16},{1,33},{17,49},{33,1},{49,17},{2,34}... | collective-permute-start | bytes 1179656 | tf_op jit(solution)/shard_map/ppermute | solution.py:117
  87.6 14.5 %copy-start.6 = (f32[384,512]{1,0:T(8,128)S(1)}, f32[384,512]{1,0:T(8,128)}, u32[]{:S(2)}) copy-start(f32[384,512]{1,0:T(8,128)} %param.16) | copy-start | bytes 2359300
  87.6 14.5 %copy-start.7 = (f32[1,384,512]{2,1,0:T(8,128)S(1)}, f32[1,384,512]{2,1,0:T(8,128)}, u32[]{:S(2)}) copy-start(f32[1,384,512]{2,1,0:T(8,128)} %param.14) | copy-start | bytes 2359300
  87.6 13.3 %collective-permute-start.6 = (bf16[384,512]{1,0:T(8,128)(2,1)S(1)}, bf16[384,512]{1,0:T(8,128)(2,1)S(1)}, u32[]{:S(2)}, u32[]{:S(2)}) collective-permute-start(bf16[384,512]{1,0:T(8,128)(2,1)S(1)} %get-tuple-element.20), channel_id=1, source_target_pairs={{0,48},{16,0},{32,16},{48,32},{1,49},{17,1},{33,17},{49,33},{2,50}... | collective-permute-start | bytes 1179656 | tf_op jit(solution)/shard_map/ppermute | solution.py:117
  88.0 15.6 %collective-permute-start.11 = (bf16[128,2048]{1,0:T(8,128)(2,1)S(1)}, bf16[128,2048]{1,0:T(8,128)(2,1)S(1)}, u32[]{:S(2)}, u32[]{:S(2)}) collective-permute-start(bf16[128,2048]{1,0:T(8,128)(2,1)S(1)} %get-tuple-element.13), channel_id=1, source_target_pairs={{0,2},{1,3},{2,4},{3,5},{4,6},{5,7},{6,8},{7,9},{8,10},{9,11},{10,... | collective-permute-start | bytes 1572872 | tf_op jit(solution)/shard_map/ppermute | solution.py:34
  88.1 15.6 %collective-permute-start.15 = (bf16[128,2048]{1,0:T(8,128)(2,1)S(1)}, bf16[128,2048]{1,0:T(8,128)(2,1)S(1)}, u32[]{:S(2)}, u32[]{:S(2)}) collective-permute-start(bf16[128,2048]{1,0:T(8,128)(2,1)S(1)} %get-tuple-element.14), channel_id=1, source_target_pairs={{0,14},{1,15},{2,0},{3,1},{4,2},{5,3},{6,4},{7,5},{8,6},{9,7},{10,... | collective-permute-start | bytes 1572872 | tf_op jit(solution)/shard_map/ppermute | solution.py:35
  103.7 18.0 %copy-start.8 = (f32[384,512]{1,0:T(8,128)S(1)}, f32[384,512]{1,0:T(8,128)}, u32[]{:S(2)}) copy-start(f32[384,512]{1,0:T(8,128)} %param.17) | copy-start | bytes 2359300
  103.7 3.7 %collective-permute-start.7 = (bf16[384,512]{1,0:T(8,128)(2,1)S(1)}, bf16[384,512]{1,0:T(8,128)(2,1)}, u32[]{:S(2)}, u32[]{:S(2)}) collective-permute-start(bf16[384,512]{1,0:T(8,128)(2,1)S(1)} %get-tuple-element.23), channel_id=1, source_target_pairs={{0,64},{64,0},{128,192},{192,128},{1,65},{65,1},{129,193},{193,129... | collective-permute-start | bytes 1179656 | tf_op jit(solution)/shard_map/ppermute | solution.py:138
  104.1 15.6 %collective-permute-start.12 = (bf16[128,2048]{1,0:T(8,128)(2,1)S(1)}, bf16[128,2048]{1,0:T(8,128)(2,1)S(1)}, u32[]{:S(2)}, u32[]{:S(2)}) collective-permute-start(bf16[128,2048]{1,0:T(8,128)(2,1)S(1)} %get-tuple-element.11), channel_id=1, source_target_pairs={{0,2},{1,3},{2,4},{3,5},{4,6},{5,7},{6,8},{7,9},{8,10},{9,11},{10,... | collective-permute-start | bytes 1572872 | tf_op jit(solution)/shard_map/ppermute | solution.py:34
  104.2 15.5 %collective-permute-start.16 = (bf16[128,2048]{1,0:T(8,128)(2,1)S(1)}, bf16[128,2048]{1,0:T(8,128)(2,1)}, u32[]{:S(2)}, u32[]{:S(2)}) collective-permute-start(bf16[128,2048]{1,0:T(8,128)(2,1)S(1)} %get-tuple-element.12), channel_id=1, source_target_pairs={{0,14},{1,15},{2,0},{3,1},{4,2},{5,3},{6,4},{7,5},{8,6},{9,7},{10,... | collective-permute-start | bytes 1572872 | tf_op jit(solution)/shard_map/ppermute | solution.py:35
  108.5 13.2 %collective-permute-start.8 = (bf16[384,512]{1,0:T(8,128)(2,1)S(1)}, bf16[384,512]{1,0:T(8,128)(2,1)S(1)}, u32[]{:S(2)}, u32[]{:S(2)}) collective-permute-start(bf16[384,512]{1,0:T(8,128)(2,1)S(1)} %add_convert_fusion.6), channel_id=1, source_target_pairs={{0,128},{64,192},{128,0},{192,64},{1,129},{65,193},{129,1},{193,65... | collective-permute-start | bytes 1179656 | tf_op jit(solution)/shard_map/ppermute | solution.py:138
  121.2 8.0 %collective-permute-start.17 = (bf16[64,2048]{1,0:T(8,128)(2,1)S(1)}, bf16[64,2048]{1,0:T(8,128)(2,1)S(1)}, u32[]{:S(2)}, u32[]{:S(2)}) collective-permute-start(bf16[64,2048]{1,0:T(8,128)(2,1)S(1)} %dynamic-slice_convert_fusion.3), channel_id=1, source_target_pairs={{0,1},{1,0},{2,3},{3,2},{4,5},{5,4},{6,7},{7,6},{8,9},{9,8},{10,11... | collective-permute-start | bytes 786440 | tf_op jit(solution)/shard_map/ppermute | solution.py:48

commit v4 on v3

--- a/solution.py
+++ b/solution.py
@@ -11,21 +11,12 @@
     return [(i, (i + s) % n) for i in range(n)]
 
 
-def _ring_reduce_scatter(part):
-    nmp = lax.axis_size("mp")
-    m = lax.axis_index("mp")
-    nlo = 2
-    nz = nmp // nlo
+def _z_reduce_scatter(chunks, z, nz, up, down):
     far = nz // 2
-    z = m // nlo
-    lo = m % nlo
-    rows = part.shape[0] // nz
-    halfc = part.shape[1] // 2
-    up = [(i, ((i // nlo + 1) % nz) * nlo + i % nlo) for i in range(nmp)]
-    down = [(i, ((i // nlo - 1) % nz) * nlo + i % nlo) for i in range(nmp)]
+    halfc = chunks.shape[2] // 2
 
     def chunk(c):
-        return lax.dynamic_slice_in_dim(part, (c % nz) * rows, rows, axis=0).astype(jnp.float32)
+        return lax.dynamic_index_in_dim(chunks, c % nz, axis=0, keepdims=False).astype(jnp.float32)
 
     first = chunk(z + far)
     send_a = first[:, :halfc]
@@ -41,12 +32,38 @@
         if r <= far:
             send_a = got_a + own_a
             send_b = got_b + own_b
-    acc = own_a + got_a + got_b
+    return own_a + got_a + got_b
+
+
+def _ring_reduce_scatter(part):
+    nmp = lax.axis_size("mp")
+    m = lax.axis_index("mp")
+    nlo = 2
+    nz = nmp // nlo
+    z = m // nlo
+    lo = m % nlo
+    rows = part.shape[0] // nz
     sub = rows // nlo
-    mine = lax.dynamic_slice_in_dim(acc, lo * sub, sub, axis=0)
-    other = lax.dynamic_slice_in_dim(acc, (1 - lo) * sub, sub, axis=0)
-    got = lax.ppermute(other.astype(jnp.bfloat16), "mp", [(i, i ^ 1) for i in range(nmp)])
-    return (mine + got.astype(jnp.float32)).astype(jnp.bfloat16)
+    halfc = part.shape[1] // 2
+    up = [(i, ((i // nlo + 1) % nz) * nlo + i % nlo) for i in range(nmp)]
+    down = [(i, ((i // nlo - 1) % nz) * nlo + i % nlo) for i in range(nmp)]
+    pair = [(i, i ^ 1) for i in range(nmp)]
+
+    py = part[:, halfc:].reshape(nz, nlo, sub, halfc)
+    keep = lax.dynamic_index_in_dim(py, lo, axis=1, keepdims=False)
+    give = lax.dynamic_index_in_dim(py, 1 - lo, axis=1, keepdims=False)
+    got_y = lax.ppermute(give, "mp", pair)
+    acc_y = keep.astype(jnp.float32) + got_y.astype(jnp.float32)
+
+    pz = part[:, :halfc].reshape(nz, rows, halfc)
+    acc_z = _z_reduce_scatter(pz, z, nz, up, down)
+    mine = lax.dynamic_slice_in_dim(acc_z, lo * sub, sub, axis=0)
+    other = lax.dynamic_slice_in_dim(acc_z, (1 - lo) * sub, sub, axis=0)
+    got = lax.ppermute(other.astype(jnp.bfloat16), "mp", pair)
+    out_z = mine + got.astype(jnp.float32)
+
+    out_y = _z_reduce_scatter(acc_y.astype(jnp.bfloat16), z, nz, up, down)
+    return jnp.concatenate([out_z, out_y], axis=1).astype(jnp.bfloat16)
 
 
 def shards(

time: 130 us -> 130 us (level)
  starting transfers between devices: 30.6 us -> 40.9 us
  waiting for transfers between devices: 56.7 us -> 48 us
  matrix products: 18.5 us -> 16 us
  local copies, waits for them, and re-layouts: 11.2 us -> 12.6 us
  other arithmetic: 12 us -> 10.7 us
    ppermute x9 -> x18, starting transfers between devices: 16.4 us -> 27 us  [the longest x8 25 us: _z_reduce_scatter(): lax.ppermute(send_b.astype(jnp.bfloat16), 'mp', down).astype(jnp.float32)]
    ppermute x9 -> x18, waiting for transfers between devices: 22.4 us -> 12.7 us  [the longest x8 10.7 us: _z_reduce_scatter(): lax.ppermute(send_a.astype(jnp.bfloat16), 'mp', up).astype(jnp.float32)]
    dot_general x1, matrix products: 4.96 us -> 1.89 us  [shards(): lax.dot_general(hidden, upstream, (((0,), (0,)), ((), ())), preferred_ele...]
    unnamed x22 -> x20, local copies, waits for them, and re-layouts: 8.03 us -> 5.29 us
    slice x1 -> x3, local copies, waits for them, and re-layouts: 0.03 us -> 1.85 us  [the longest x1 1.82 us: _ring_reduce_scatter(): pz = part[:, :halfc].reshape(nz, rows, halfc)]
    squeeze x0 -> x1, local copies, waits for them, and re-layouts: none -> 1.37 us  [_ring_reduce_scatter(): give = lax.dynamic_index_in_dim(py, 1 - lo, axis=1, keepdims=False)]
    broadcast_in_dim x1, other arithmetic: 1.23 us -> 2.55 us  [shards(): second_new[None]]
    convert_element_type x3 -> x7, other arithmetic: 2.12 us -> 2.84 us  [the longest x6 2.4 us: _z_reduce_scatter(): send_a.astype(jnp.bfloat16)]
  transfers between devices with their start and end apart: 18 -> 27, of which waited for: 8 -> 12; matrix products, arithmetic and copies ran while one was open for 18% -> 18% of each run, Pallas kernels for 0% -> 0%
where the time goes in v4:
time: 130 us; the launch traced here: 129 us
  waiting for transfers between devices  48 us (37%)
  starting transfers between devices  40.9 us (31%)
  matrix products  16 us (12%)
  local copies, waits for them, and re-layouts  12.6 us (10%)
  other arithmetic  10.7 us (8%)
    ppermute x8, starting transfers between devices, _z_reduce_scatter(): lax.ppermute(send_b.astype(jnp.bfloat16), 'mp', down).astype(jnp.float32)  25 us
    ppermute x1, waiting for transfers between devices, shards(): from_left = lax.ppermute(shard, 'dp', _shift(ndp, 1))  20.9 us
    ppermute x8, waiting for transfers between devices, _z_reduce_scatter(): lax.ppermute(send_a.astype(jnp.bfloat16), 'mp', up).astype(jnp.float32)  10.7 us
    ppermute x3, waiting for transfers between devices, shards(): got = lax.ppermute(blk.astype(jnp.bfloat16), 'dp', _shift(ndp, s))  10.4 us
    dot_general x5, matrix products, shards(): p1 = jnp.dot(xs, piece[:, :2 * ff], preferred_element_type=jnp.float32)  5.91 us
    unnamed x20, local copies, waits for them, and re-layouts  5.29 us
    ppermute x3, starting transfers between devices, shards(): got = lax.ppermute(blk.astype(jnp.bfloat16), 'dp', _shift(ndp, s))  4.7 us
    dot_general x5, matrix products, shards(): p2 = jnp.dot(gs, piece[:, 2 * ff:], preferred_element_type=jnp.float32)  4.36 us
  transfers between devices with their start and end apart: 27, of which 12 were waited for; matrix products, arithmetic and copies ran while one was open for 18% of the time, Pallas kernels for 0%

profile of v4, /device:TPU:8, one launch (start us, length us, event | category | flops | bytes accessed | tf_op | source)
XLA Modules:
  0.0 129.1 jit_solution(14926859624756511089)
XLA Ops:
  0.6 1.2 copy.14
  1.9 1.2 copy.15
  3.1 1.1 pad_maximum_fusion
  4.3 1.5 %collective-permute-start = (bf16[512,1152]{0,1:T(8,128)(2,1)}, bf16[512,1152]{0,1:T(8,128)(2,1)S(1)}, u32[]{:S(2)}, u32[]{:S(2)}) collective-permute-start(bf16[512,1152]{0,1:T(8,128)(2,1)} %pad_maximum_fusion), channel_id=1, source_target_pairs={{0,16},{16,32},{32,48},{48,0},{1,17},{17,33},{33,49},{49,1},{2,18}... | collective-permute-start | bytes 3538952 | tf_op jit(solution)/shard_map/ppermute | solution.py:92
  5.8 1.7 %collective-permute-start.1 = (bf16[512,1152]{0,1:T(8,128)(2,1)}, bf16[512,1152]{0,1:T(8,128)(2,1)}, u32[]{:S(2)}, u32[]{:S(2)}) collective-permute-start(bf16[512,1152]{0,1:T(8,128)(2,1)} %pad_maximum_fusion), channel_id=1, source_target_pairs={{0,48},{16,0},{32,16},{48,32},{1,49},{17,1},{33,17},{49,33},{2,50}... | collective-permute-start | bytes 3538952 | tf_op jit(solution)/shard_map/ppermute | solution.py:93
  7.5 0.4 broadcast_in_dim.12
  7.9 0.1 fusion.55
  8.0 1.7 %copy-done.8 = bf16[1,1024,2048]{2,1,0:T(8,128)(2,1)S(1)} copy-done((bf16[1,1024,2048]{2,1,0:T(8,128)(2,1)S(1)}, bf16[1,1024,2048]{2,1,0:T(8,128)(2,1)}, u32[]{:S(2)}) %copy-start.8) | copy-done | bytes 4194328
  9.7 1.0 fusion.17
  10.7 1.2 copy-done.2
  11.9 0.6 fusion.11
  12.5 20.9 %collective-permute-done = bf16[512,1152]{0,1:T(8,128)(2,1)S(1)} collective-permute-done((bf16[512,1152]{0,1:T(8,128)(2,1)}, bf16[512,1152]{0,1:T(8,128)(2,1)S(1)}, u32[]{:S(2)}, u32[]{:S(2)}) %collective-permute-start) | collective-permute-done | bytes 1179680 | tf_op jit(solution)/shard_map/ppermute | solution.py:92
  33.4 0.4 collective-permute-start.2
  33.8 1.1 slice.87
  34.9 3.2 %collective-permute-start.3 = (bf16[256,1152]{0,1:T(8,128)(2,1)S(1)}, bf16[256,1152]{0,1:T(8,128)(2,1)S(1)}, u32[]{:S(2)}, u32[]{:S(2)}) collective-permute-start(bf16[256,1152]{0,1:T(8,128)(2,1)S(1)} %slice.87), channel_id=1, source_target_pairs={{0,48},{16,0},{32,16},{48,32},{1,49},{17,1},{33,17},{49,33},{2,50}... | collective-permute-start | bytes 1769480 | tf_op jit(solution)/shard_map/ppermute | solution.py:95
  38.1 2.2 %fusion.13 = f32[1024,768]{0,1:T(8,128)S(1)} fusion(bf16[1,1024,2048]{2,1,0:T(8,128)(2,1)S(1)} %copy-done.8, s32[]{:T(128)S(6)} %select_n.163, bf16[512,1152]{0,1:T(8,128)(2,1)} %collective-permute-done.1), kind=kOutput, calls=%fused_computation.23 | convolution fusion | flops 805306368 | bytes 4980740 | tf_op jit(solution)/shard_map/dot_general | solution.py:111
  40.3 1.6 %fusion.7 = f32[1024,384]{0,1:T(8,128)S(1)} fusion(bf16[1,1024,2048]{2,1,0:T(8,128)(2,1)S(1)} %copy-done.2, s32[]{:T(128)S(6)} %select_n.163, bf16[512,1152]{0,1:T(8,128)(2,1)} %collective-permute-done.1), kind=kOutput, calls=%fused_computation.17 | convolution fusion | flops 402653184 | bytes 3014660 | tf_op jit(solution)/shard_map/dot_general | solution.py:112
  41.9 0.6 fusion.9
  42.5 0.1 slice_dynamic-update-slice_fusion.1
  42.6 1.2 slice_dynamic-update-slice_fusion
  43.9 1.0 fusion.15
  44.9 4.0 %collective-permute-done.2 = bf16[256,1152]{0,1:T(8,128)(2,1)S(1)} collective-permute-done((bf16[256,1152]{0,1:T(8,128)(2,1)S(1)}, bf16[256,1152]{0,1:T(8,128)(2,1)S(1)}, u32[]{:S(2)}, u32[]{:S(2)}) %collective-permute-start.2) | collective-permute-done | bytes 589856 | tf_op jit(solution)/shard_map/ppermute | solution.py:94
  49.0 0.4 fusion.43
  49.4 0.6 fusion.49
  50.1 1.1 add_add_fusion
  51.2 1.1 multiply_convert_fusion.1
  52.2 3.8 %convolution_convert_fusion = bf16[1024,2048]{1,0:T(8,128)(2,1)S(1)} fusion(bf16[2048,768]{0,1:T(8,128)(2,1)S(1)} %slice_dynamic-update-slice_fusion.2, bf16[1024,384]{0,1:T(8,128)(2,1)S(1)} %get-tuple-element.10, bf16[1024,384]{0,1:T(8,128)(2,1)S(1)} %get-tuple-element.9), kind=kOutput, calls=%fused_computation.2 | convolution fusion | flops 3226468352 | bytes 8912896 | tf_op jit(solution)/shard_map/dot_general | solution.py:138
  56.1 1.8 %fusion.91 = (bf16[1024,1024]{1,0:T(8,128)(2,1)S(1)}, bf16[1024,1024]{1,0:T(8,128)(2,1)}) fusion(bf16[1024,2048]{1,0:T(8,128)(2,1)S(1)} %convolution_convert_fusion), kind=kLoop, calls=%fused_computation.133 | loop fusion | bytes 8388608 | tf_op jit(solution)/shard_map/slice | solution.py:58
  57.9 5.9 %collective-permute-start.13 = (bf16[128,512]{1,0:T(8,128)(2,1)S(1)}, bf16[128,512]{1,0:T(8,128)(2,1)S(1)}, u32[]{:S(2)}, u32[]{:S(2)}) collective-permute-start(bf16[128,512]{1,0:T(8,128)(2,1)S(1)} %get-tuple-element.31), channel_id=1, source_target_pairs={{0,14},{1,15},{2,0},{3,1},{4,2},{5,3},{6,4},{7,5},{8,6},{9,7},{10,... | collective-permute-start | bytes 393224 | tf_op jit(solution)/shard_map/ppermute | solution.py:26
  63.9 1.9 %fusion = f32[384,2048]{1,0:T(8,128)S(1)} fusion(bf16[1,1024,2048]{2,1,0:T(8,128)(2,1)S(1)} %copy-done.2, f32[1024,768]{0,1:T(8,128)S(1)} %add_add_fusion), kind=kOutput, calls=%fused_computation | convolution fusion | flops 1612972032 | bytes 10485760 | tf_op jit(solution)/shard_map/dot_general | solution.py:127
  65.8 0.6 collective-permute-done.13
  66.4 3.7 %collective-permute-done.9 = bf16[128,512]{1,0:T(8,128)(2,1)S(1)} collective-permute-done((bf16[128,512]{1,0:T(8,128)(2,1)S(1)}, bf16[128,512]{1,0:T(8,128)(2,1)S(1)}, u32[]{:S(2)}, u32[]{:S(2)}) %collective-permute-start.9) | collective-permute-done | bytes 131104 | tf_op jit(solution)/shard_map/ppermute | solution.py:25
  70.1 0.9 fusion.37
  70.9 3.2 %collective-permute-start.14 = (bf16[128,1024]{1,0:T(8,128)(2,1)}, bf16[128,1024]{1,0:T(8,128)(2,1)}, u32[]{:S(2)}, u32[]{:S(2)}) collective-permute-start(bf16[128,1024]{1,0:T(8,128)(2,1)} %get-tuple-element.21), channel_id=1, source_target_pairs={{0,14},{1,15},{2,0},{3,1},{4,2},{5,3},{6,4},{7,5},{8,6},{9,7},{10,... | collective-permute-start | bytes 786440 | tf_op jit(solution)/shard_map/ppermute | solution.py:26
  74.2 1.1 dynamic-slice_convert_fusion.2
  75.2 0.7 collective-permute-start.4
  75.9 4.0 %collective-permute-start.5 = (bf16[384,512]{1,0:T(8,128)(2,1)}, bf16[384,512]{1,0:T(8,128)(2,1)}, u32[]{:S(2)}, u32[]{:S(2)}) collective-permute-start(bf16[384,512]{1,0:T(8,128)(2,1)} %get-tuple-element.15), channel_id=1, source_target_pairs={{0,32},{16,48},{32,0},{48,16},{1,33},{17,49},{33,1},{49,17},{2,34}... | collective-permute-start | bytes 1179656 | tf_op jit(solution)/shard_map/ppermute | solution.py:134
  79.9 1.4 %dynamic-slice_bitcast_fusion = bf16[8,64,1024]{2,1,0:T(8,128)(2,1)S(1)} fusion(bf16[8,2,64,1024]{3,2,1,0:T(8,128)(2,1)} %bitcast.143, s32[]{:T(128)S(6)} %select_n.190), kind=kLoop, calls=%fused_computation.29 | loop fusion | bytes 2097156 | tf_op jit(solution)/shard_map/jit(dynamic_index_in_dim)/squeeze | solution.py:54
  81.3 0.5 collective-permute-start.18
  81.9 1.1 fusion.36
  83.1 5.6 %collective-permute-done.4 = bf16[384,512]{1,0:T(8,128)(2,1)S(1)} collective-permute-done((bf16[384,512]{1,0:T(8,128)(2,1)}, bf16[384,512]{1,0:T(8,128)(2,1)S(1)}, u32[]{:S(2)}, u32[]{:S(2)}) %collective-permute-start.4) | collective-permute-done | bytes 393248 | tf_op jit(solution)/shard_map/ppermute | solution.py:134
  88.7 4.8 %collective-permute-done.5 = bf16[384,512]{1,0:T(8,128)(2,1)} collective-permute-done((bf16[384,512]{1,0:T(8,128)(2,1)}, bf16[384,512]{1,0:T(8,128)(2,1)}, u32[]{:S(2)}, u32[]{:S(2)}) %collective-permute-start.5) | collective-permute-done | bytes 393248 | tf_op jit(solution)/shard_map/ppermute | solution.py:134
  93.5 2.6 %fusion.72 = (f32[1,384,512]{2,1,0:T(8,128)}, f32[384,512]{1,0:T(8,128)S(1)}) fusion(f32[1,384,512]{2,1,0:T(8,128)S(1)} %copy-done.3, bf16[384,512]{1,0:T(8,128)(2,1)} %collective-permute-done.6, bf16[384,512]{1,0:T(8,128)(2,1)} %collective-permute-done.5, bf16[384,512]{1,0:T(8,128)(2,1)S(1)} %collective-permute-done.4, f32[384,2048]{1,0:T(8,128)} %copy-done.5, ...), kind=kLoop, calls=%fused_computation.114 | loop fusion | flops 1966080 | bytes 4325380 | tf_op jit(solution)/shard_map/broadcast_in_dim | solution.py:160
  96.1 1.5 %fusion.71 = (f32[1,384,512]{2,1,0:T(8,128)}, bf16[384,512]{1,0:T(8,128)(2,1)S(1)}) fusion(f32[384,512]{1,0:T(8,128)S(1)} %get-tuple-element.6, f32[1,384,512]{2,1,0:T(8,128)S(1)} %copy-done.6, f32[384,512]{1,0:T(8,128)S(1)} %copy-done.4, f32[1,384,512]{2,1,0:T(8,128)S(1)} %copy-done.3, f32[1,384,512]{2,1,0:T(8,128)S(1)} %copy-done.1), kind=kLoop, calls=%fused_computation.113 | loop fusion | flops 3342336 | bytes 5111808 | tf_op jit(solution)/shard_map/broadcast_in_dim | solution.py:160
  97.6 0.2 fusion.35
  97.9 3.2 %collective-permute-start.16 = (bf16[128,1024]{1,0:T(8,128)(2,1)S(1)}, bf16[128,1024]{1,0:T(8,128)(2,1)S(1)}, u32[]{:S(2)}, u32[]{:S(2)}) collective-permute-start(bf16[128,1024]{1,0:T(8,128)(2,1)S(1)} %get-tuple-element.17), channel_id=1, source_target_pairs={{0,14},{1,15},{2,0},{3,1},{4,2},{5,3},{6,4},{7,5},{8,6},{9,7},{10,... | collective-permute-start | bytes 786440 | tf_op jit(solution)/shard_map/ppermute | solution.py:26
  101.1 0.5 collective-permute-done.18
  101.7 0.4 fusion.2
  102.3 3.2 %collective-permute-start.23 = (bf16[64,512]{1,0:T(8,128)(2,1)S(1)}, bf16[64,512]{1,0:T(8,128)(2,1)S(1)}, u32[]{:S(2)}, u32[]{:S(2)}) collective-permute-start(bf16[64,512]{1,0:T(8,128)(2,1)S(1)} %get-tuple-element.33), channel_id=1, source_target_pairs={{0,14},{1,15},{2,0},{3,1},{4,2},{5,3},{6,4},{7,5},{8,6},{9,7},{10,... | collective-permute-start | bytes 196616 | tf_op jit(solution)/shard_map/ppermute | solution.py:26
  105.5 0.1 add_convert_fusion
  105.6 2.4 %collective-permute-start.8 = (bf16[384,512]{1,0:T(8,128)(2,1)S(1)}, bf16[384,512]{1,0:T(8,128)(2,1)S(1)}, u32[]{:S(2)}, u32[]{:S(2)}) collective-permute-start(bf16[384,512]{1,0:T(8,128)(2,1)S(1)} %add_convert_fusion), channel_id=1, source_target_pairs={{0,128},{64,192},{128,0},{192,64},{1,129},{65,193},{129,1},{193,65... | collective-permute-start | bytes 1179656 | tf_op jit(solution)/shard_map/ppermute | solution.py:155
  108.0 1.2 collective-permute-done.19
  109.4 3.3 %collective-permute-start.24 = (bf16[64,1024]{1,0:T(8,128)(2,1)S(1)}, bf16[64,1024]{1,0:T(8,128)(2,1)S(1)}, u32[]{:S(2)}, u32[]{:S(2)}) collective-permute-start(bf16[64,1024]{1,0:T(8,128)(2,1)S(1)} %get-tuple-element.29), channel_id=1, source_target_pairs={{0,14},{1,15},{2,0},{3,1},{4,2},{5,3},{6,4},{7,5},{8,6},{9,7},{10,... | collective-permute-start | bytes 393224 | tf_op jit(solution)/shard_map/ppermute | solution.py:26
  112.7 0.1 fusion.38
  112.8 0.5 collective-permute-start.17
  113.4 2.3 %collective-permute-done.20 = bf16[64,1024]{1,0:T(8,128)(2,1)S(1)} collective-permute-done((bf16[64,1024]{1,0:T(8,128)(2,1)S(1)}, bf16[64,1024]{1,0:T(8,128)(2,1)S(1)}, u32[]{:S(2)}, u32[]{:S(2)}) %collective-permute-start.20) | collective-permute-done | bytes 131104 | tf_op jit(solution)/shard_map/ppermute | solution.py:25
  115.9 3.2 %collective-permute-start.25 = (bf16[64,1024]{1,0:T(8,128)(2,1)S(1)}, bf16[64,1024]{1,0:T(8,128)(2,1)S(1)}, u32[]{:S(2)}, u32[]{:S(2)}) collective-permute-start(bf16[64,1024]{1,0:T(8,128)(2,1)S(1)} %get-tuple-element.27), channel_id=1, source_target_pairs={{0,14},{1,15},{2,0},{3,1},{4,2},{5,3},{6,4},{7,5},{8,6},{9,7},{10,... | collective-permute-start | bytes 393224 | tf_op jit(solution)/shard_map/ppermute | solution.py:26
  119.1 0.9 collective-permute-done.17
  120.0 2.0 %collective-permute-done.21 = bf16[64,1024]{1,0:T(8,128)(2,1)S(1)} collective-permute-done((bf16[64,1024]{1,0:T(8,128)(2,1)S(1)}, bf16[64,1024]{1,0:T(8,128)(2,1)S(1)}, u32[]{:S(2)}, u32[]{:S(2)}) %collective-permute-start.21) | collective-permute-done | bytes 131104 | tf_op jit(solution)/shard_map/ppermute | solution.py:25
  122.1 0.6 collective-permute-start.22
  122.7 2.8 %collective-permute-start.26 = (bf16[64,1024]{1,0:T(8,128)(2,1)S(1)}, bf16[64,1024]{1,0:T(8,128)(2,1)S(1)}, u32[]{:S(2)}, u32[]{:S(2)}) collective-permute-start(bf16[64,1024]{1,0:T(8,128)(2,1)S(1)} %get-tuple-element.25), channel_id=1, source_target_pairs={{0,14},{1,15},{2,0},{3,1},{4,2},{5,3},{6,4},{7,5},{8,6},{9,7},{10,... | collective-permute-start | bytes 393224 | tf_op jit(solution)/shard_map/ppermute | solution.py:26
  125.5 1.4 %multiply_subtract_fusion = (f32[384,512]{1,0:T(8,128)}, f32[384,512]{1,0:T(8,128)}) fusion(f32[384,512]{1,0:T(8,128)S(1)} %copy-done.4, bf16[384,512]{1,0:T(8,128)(2,1)S(1)} %collective-permute-done.8, bf16[384,512]{1,0:T(8,128)(2,1)S(1)} %add_convert_fusion, f32[384,512]{1,0:T(8,128)S(1)} %copy-done.7), kind=kLoop, calls=%fused_computation.46 | loop fusion | flops 1966080 | bytes 3932160 | tf_op jit(solution)/shard_map/sub | solution.py:159
  127.0 1.4 %collective-permute-done.22 = bf16[64,1024]{1,0:T(8,128)(2,1)S(1)} collective-permute-done((bf16[64,1024]{1,0:T(8,128)(2,1)S(1)}, bf16[64,1024]{1,0:T(8,128)(2,1)S(1)}, u32[]{:S(2)}, u32[]{:S(2)}) %collective-permute-start.22) | collective-permute-done | bytes 131104 | tf_op jit(solution)/shard_map/ppermute | solution.py:25
  128.4 0.7 pad_maximum_fusion.3
  (55 shorter events, 1.0 us)
Async XLA Ops:
  0.6 2.4 %copy-start.1 = (f32[1,384,512]{2,1,0:T(8,128)S(1)}, f32[1,384,512]{2,1,0:T(8,128)}, u32[]{:S(2)}) copy-start(f32[1,384,512]{2,1,0:T(8,128)} %param.13) | copy-start | bytes 2359300
  4.3 29.1 %collective-permute-start = (bf16[512,1152]{0,1:T(8,128)(2,1)}, bf16[512,1152]{0,1:T(8,128)(2,1)S(1)}, u32[]{:S(2)}, u32[]{:S(2)}) collective-permute-start(bf16[512,1152]{0,1:T(8,128)(2,1)} %pad_maximum_fusion), channel_id=1, source_target_pairs={{0,16},{16,32},{32,48},{48,0},{1,17},{17,33},{33,49},{49,1},{2,18}... | collective-permute-start | bytes 3538952 | tf_op jit(solution)/shard_map/ppermute | solution.py:92
  5.8 28.0 %collective-permute-start.1 = (bf16[512,1152]{0,1:T(8,128)(2,1)}, bf16[512,1152]{0,1:T(8,128)(2,1)}, u32[]{:S(2)}, u32[]{:S(2)}) collective-permute-start(bf16[512,1152]{0,1:T(8,128)(2,1)} %pad_maximum_fusion), channel_id=1, source_target_pairs={{0,48},{16,0},{32,16},{48,32},{1,49},{17,1},{33,17},{49,33},{2,50}... | collective-permute-start | bytes 3538952 | tf_op jit(solution)/shard_map/ppermute | solution.py:93
  7.5 2.2 %copy-start.8 = (bf16[1,1024,2048]{2,1,0:T(8,128)(2,1)S(1)}, bf16[1,1024,2048]{2,1,0:T(8,128)(2,1)}, u32[]{:S(2)}) copy-start(bf16[1,1024,2048]{2,1,0:T(8,128)(2,1)} %param.9) | copy-start | bytes 12582916
  9.7 2.2 %copy-start.2 = (bf16[1,1024,2048]{2,1,0:T(8,128)(2,1)S(1)}, bf16[1,1024,2048]{2,1,0:T(8,128)(2,1)}, u32[]{:S(2)}) copy-start(bf16[1,1024,2048]{2,1,0:T(8,128)(2,1)} %param.10) | copy-start | bytes 12582916
  33.4 15.5 %collective-permute-start.2 = (bf16[256,1152]{0,1:T(8,128)(2,1)S(1)}, bf16[256,1152]{0,1:T(8,128)(2,1)S(1)}, u32[]{:S(2)}, u32[]{:S(2)}) collective-permute-start(bf16[256,1152]{0,1:T(8,128)(2,1)S(1)} %slice.85), channel_id=1, source_target_pairs={{0,16},{16,32},{32,48},{48,0},{1,17},{17,33},{33,49},{49,1},{2,18}... | collective-permute-start | bytes 1769480 | tf_op jit(solution)/shard_map/ppermute | solution.py:94
  34.9 15.1 %collective-permute-start.3 = (bf16[256,1152]{0,1:T(8,128)(2,1)S(1)}, bf16[256,1152]{0,1:T(8,128)(2,1)S(1)}, u32[]{:S(2)}, u32[]{:S(2)}) collective-permute-start(bf16[256,1152]{0,1:T(8,128)(2,1)S(1)} %slice.87), channel_id=1, source_target_pairs={{0,48},{16,0},{32,16},{48,32},{1,49},{17,1},{33,17},{49,33},{2,50}... | collective-permute-start | bytes 1769480 | tf_op jit(solution)/shard_map/ppermute | solution.py:95
  57.9 8.5 %collective-permute-start.13 = (bf16[128,512]{1,0:T(8,128)(2,1)S(1)}, bf16[128,512]{1,0:T(8,128)(2,1)S(1)}, u32[]{:S(2)}, u32[]{:S(2)}) collective-permute-start(bf16[128,512]{1,0:T(8,128)(2,1)S(1)} %get-tuple-element.31), channel_id=1, source_target_pairs={{0,14},{1,15},{2,0},{3,1},{4,2},{5,3},{6,4},{7,5},{8,6},{9,7},{10,... | collective-permute-start | bytes 393224 | tf_op jit(solution)/shard_map/ppermute | solution.py:26
  63.9 6.2 %collective-permute-start.9 = (bf16[128,512]{1,0:T(8,128)(2,1)S(1)}, bf16[128,512]{1,0:T(8,128)(2,1)S(1)}, u32[]{:S(2)}, u32[]{:S(2)}) collective-permute-start(bf16[128,512]{1,0:T(8,128)(2,1)S(1)} %get-tuple-element.30), channel_id=1, source_target_pairs={{0,2},{1,3},{2,4},{3,5},{4,6},{5,7},{6,8},{7,9},{8,10},{9,11},{10,... | collective-permute-start | bytes 393224 | tf_op jit(solution)/shard_map/ppermute | solution.py:25
  65.8 8.4 %copy-start.5 = (f32[384,2048]{1,0:T(8,128)}, f32[384,2048]{1,0:T(8,128)S(1)}, u32[]{:S(2)}) copy-start(f32[384,2048]{1,0:T(8,128)S(1)} %fusion) | copy-start | bytes 9437188
  70.9 10.4 %collective-permute-start.10 = (bf16[128,1024]{1,0:T(8,128)(2,1)}, bf16[128,1024]{1,0:T(8,128)(2,1)S(1)}, u32[]{:S(2)}, u32[]{:S(2)}) collective-permute-start(bf16[128,1024]{1,0:T(8,128)(2,1)} %get-tuple-element.20), channel_id=1, source_target_pairs={{0,2},{1,3},{2,4},{3,5},{4,6},{5,7},{6,8},{7,9},{8,10},{9,11},{10,... | collective-permute-start | bytes 786440 | tf_op jit(solution)/shard_map/ppermute | solution.py:25
  70.9 10.9 %collective-permute-start.14 = (bf16[128,1024]{1,0:T(8,128)(2,1)}, bf16[128,1024]{1,0:T(8,128)(2,1)}, u32[]{:S(2)}, u32[]{:S(2)}) collective-permute-start(bf16[128,1024]{1,0:T(8,128)(2,1)} %get-tuple-element.21), channel_id=1, source_target_pairs={{0,14},{1,15},{2,0},{3,1},{4,2},{5,3},{6,4},{7,5},{8,6},{9,7},{10,... | collective-permute-start | bytes 786440 | tf_op jit(solution)/shard_map/ppermute | solution.py:26
  75.2 13.4 %collective-permute-start.4 = (bf16[384,512]{1,0:T(8,128)(2,1)}, bf16[384,512]{1,0:T(8,128)(2,1)S(1)}, u32[]{:S(2)}, u32[]{:S(2)}) collective-permute-start(bf16[384,512]{1,0:T(8,128)(2,1)} %get-tuple-element.13), channel_id=1, source_target_pairs={{0,16},{16,32},{32,48},{48,0},{1,17},{17,33},{33,49},{49,1},{2,18}... | collective-permute-start | bytes 1179656 | tf_op jit(solution)/shard_map/ppermute | solution.py:134
  75.9 17.6 %collective-permute-start.5 = (bf16[384,512]{1,0:T(8,128)(2,1)}, bf16[384,512]{1,0:T(8,128)(2,1)}, u32[]{:S(2)}, u32[]{:S(2)}) collective-permute-start(bf16[384,512]{1,0:T(8,128)(2,1)} %get-tuple-element.15), channel_id=1, source_target_pairs={{0,32},{16,48},{32,0},{48,16},{1,33},{17,49},{33,1},{49,17},{2,34}... | collective-permute-start | bytes 1179656 | tf_op jit(solution)/shard_map/ppermute | solution.py:134
  79.9 13.6 %collective-permute-start.6 = (bf16[384,512]{1,0:T(8,128)(2,1)}, bf16[384,512]{1,0:T(8,128)(2,1)}, u32[]{:S(2)}, u32[]{:S(2)}) collective-permute-start(bf16[384,512]{1,0:T(8,128)(2,1)} %get-tuple-element.14), channel_id=1, source_target_pairs={{0,48},{16,0},{32,16},{48,32},{1,49},{17,1},{33,17},{49,33},{2,50}... | collective-permute-start | bytes 1179656 | tf_op jit(solution)/shard_map/ppermute | solution.py:134
  79.9 13.6 %copy-start.3 = (f32[1,384,512]{2,1,0:T(8,128)S(1)}, f32[1,384,512]{2,1,0:T(8,128)}, u32[]{:S(2)}) copy-start(f32[1,384,512]{2,1,0:T(8,128)} %param.15) | copy-start | bytes 2359300
  81.3 20.4 %collective-permute-start.18 = (bf16[8,64,1024]{2,1,0:T(8,128)(2,1)S(1)}, bf16[8,64,1024]{2,1,0:T(8,128)(2,1)S(1)}, u32[]{:S(2)}, u32[]{:S(2)}) collective-permute-start(bf16[8,64,1024]{2,1,0:T(8,128)(2,1)S(1)} %dynamic-slice_bitcast_fusion), channel_id=1, source_target_pairs={{0,1},{1,0},{2,3},{3,2},{4,5},{5,4},{6,7},{7,6},{8,9},{9,8},{10,11... | collective-permute-start | bytes 3145736 | tf_op jit(solution)/shard_map/ppermute | solution.py:55
  83.0 14.6 %collective-permute-start.11 = (bf16[128,1024]{1,0:T(8,128)(2,1)S(1)}, bf16[128,1024]{1,0:T(8,128)(2,1)S(1)}, u32[]{:S(2)}, u32[]{:S(2)}) collective-permute-start(bf16[128,1024]{1,0:T(8,128)(2,1)S(1)} %get-tuple-element.18), channel_id=1, source_target_pairs={{0,2},{1,3},{2,4},{3,5},{4,6},{5,7},{6,8},{7,9},{8,10},{9,11},{10,... | collective-permute-start | bytes 786440 | tf_op jit(solution)/shard_map/ppermute | solution.py:25
  88.6 7.4 %copy-start.4 = (f32[384,512]{1,0:T(8,128)S(1)}, f32[384,512]{1,0:T(8,128)}, u32[]{:S(2)}) copy-start(f32[384,512]{1,0:T(8,128)} %param.16) | copy-start | bytes 2359300
  88.6 7.4 %copy-start.6 = (f32[1,384,512]{2,1,0:T(8,128)S(1)}, f32[1,384,512]{2,1,0:T(8,128)}, u32[]{:S(2)}) copy-start(f32[1,384,512]{2,1,0:T(8,128)} %param.14) | copy-start | bytes 2359300
  88.6 9.0 %collective-permute-start.15 = (bf16[128,1024]{1,0:T(8,128)(2,1)S(1)}, bf16[128,1024]{1,0:T(8,128)(2,1)S(1)}, u32[]{:S(2)}, u32[]{:S(2)}) collective-permute-start(bf16[128,1024]{1,0:T(8,128)(2,1)S(1)} %get-tuple-element.19), channel_id=1, source_target_pairs={{0,14},{1,15},{2,0},{3,1},{4,2},{5,3},{6,4},{7,5},{8,6},{9,7},{10,... | collective-permute-start | bytes 786440 | tf_op jit(solution)/shard_map/ppermute | solution.py:26
  96.0 5.6 %copy-start = (bf16[1024,1024]{1,0:T(8,128)(2,1)S(1)}, bf16[1024,1024]{1,0:T(8,128)(2,1)}, u32[]{:S(2)}) copy-start(bf16[1024,1024]{1,0:T(8,128)(2,1)} %get-tuple-element.12) | copy-start | bytes 6291460
  97.6 7.9 %collective-permute-start.7 = (bf16[384,512]{1,0:T(8,128)(2,1)S(1)}, bf16[384,512]{1,0:T(8,128)(2,1)S(1)}, u32[]{:S(2)}, u32[]{:S(2)}) collective-permute-start(bf16[384,512]{1,0:T(8,128)(2,1)S(1)} %get-tuple-element.23), channel_id=1, source_target_pairs={{0,64},{64,0},{128,192},{192,128},{1,65},{65,1},{129,193},{193,129... | collective-permute-start | bytes 1179656 | tf_op jit(solution)/shard_map/ppermute | solution.py:155
  97.8 14.8 %collective-permute-start.12 = (bf16[128,1024]{1,0:T(8,128)(2,1)S(1)}, bf16[128,1024]{1,0:T(8,128)(2,1)S(1)}, u32[]{:S(2)}, u32[]{:S(2)}) collective-permute-start(bf16[128,1024]{1,0:T(8,128)(2,1)S(1)} %get-tuple-element.16), channel_id=1, source_target_pairs={{0,2},{1,3},{2,4},{3,5},{4,6},{5,7},{6,8},{7,9},{8,10},{9,11},{10,... | collective-permute-start | bytes 786440 | tf_op jit(solution)/shard_map/ppermute | solution.py:25
  97.9 14.7 %collective-permute-start.16 = (bf16[128,1024]{1,0:T(8,128)(2,1)S(1)}, bf16[128,1024]{1,0:T(8,128)(2,1)S(1)}, u32[]{:S(2)}, u32[]{:S(2)}) collective-permute-start(bf16[128,1024]{1,0:T(8,128)(2,1)S(1)} %get-tuple-element.17), channel_id=1, source_target_pairs={{0,14},{1,15},{2,0},{3,1},{4,2},{5,3},{6,4},{7,5},{8,6},{9,7},{10,... | collective-permute-start | bytes 786440 | tf_op jit(solution)/shard_map/ppermute | solution.py:26
  102.2 7.1 %collective-permute-start.19 = (bf16[64,512]{1,0:T(8,128)(2,1)S(1)}, bf16[64,512]{1,0:T(8,128)(2,1)S(1)}, u32[]{:S(2)}, u32[]{:S(2)}) collective-permute-start(bf16[64,512]{1,0:T(8,128)(2,1)S(1)} %get-tuple-element.32), channel_id=1, source_target_pairs={{0,2},{1,3},{2,4},{3,5},{4,6},{5,7},{6,8},{7,9},{8,10},{9,11},{10,... | collective-permute-start | bytes 196616 | tf_op jit(solution)/shard_map/ppermute | solution.py:25
  102.3 7.0 %collective-permute-start.23 = (bf16[64,512]{1,0:T(8,128)(2,1)S(1)}, bf16[64,512]{1,0:T(8,128)(2,1)S(1)}, u32[]{:S(2)}, u32[]{:S(2)}) collective-permute-start(bf16[64,512]{1,0:T(8,128)(2,1)S(1)} %get-tuple-element.33), channel_id=1, source_target_pairs={{0,14},{1,15},{2,0},{3,1},{4,2},{5,3},{6,4},{7,5},{8,6},{9,7},{10,... | collective-permute-start | bytes 196616 | tf_op jit(solution)/shard_map/ppermute | solution.py:26
  105.6 19.9 %copy-start.7 = (f32[384,512]{1,0:T(8,128)S(1)}, f32[384,512]{1,0:T(8,128)}, u32[]{:S(2)}) copy-start(f32[384,512]{1,0:T(8,128)} %param.17) | copy-start | bytes 2359300
  105.6 19.9 %collective-permute-start.8 = (bf16[384,512]{1,0:T(8,128)(2,1)S(1)}, bf16[384,512]{1,0:T(8,128)(2,1)S(1)}, u32[]{:S(2)}, u32[]{:S(2)}) collective-permute-start(bf16[384,512]{1,0:T(8,128)(2,1)S(1)} %add_convert_fusion), channel_id=1, source_target_pairs={{0,128},{64,192},{128,0},{192,64},{1,129},{65,193},{129,1},{193,65... | collective-permute-start | bytes 1179656 | tf_op jit(solution)/shard_map/ppermute | solution.py:155
  109.3 6.4 %collective-permute-start.20 = (bf16[64,1024]{1,0:T(8,128)(2,1)S(1)}, bf16[64,1024]{1,0:T(8,128)(2,1)S(1)}, u32[]{:S(2)}, u32[]{:S(2)}) collective-permute-start(bf16[64,1024]{1,0:T(8,128)(2,1)S(1)} %get-tuple-element.28), channel_id=1, source_target_pairs={{0,2},{1,3},{2,4},{3,5},{4,6},{5,7},{6,8},{7,9},{8,10},{9,11},{10,... | collective-permute-start | bytes 393224 | tf_op jit(solution)/shard_map/ppermute | solution.py:25
  109.4 6.3 %collective-permute-start.24 = (bf16[64,1024]{1,0:T(8,128)(2,1)S(1)}, bf16[64,1024]{1,0:T(8,128)(2,1)S(1)}, u32[]{:S(2)}, u32[]{:S(2)}) collective-permute-start(bf16[64,1024]{1,0:T(8,128)(2,1)S(1)} %get-tuple-element.29), channel_id=1, source_target_pairs={{0,14},{1,15},{2,0},{3,1},{4,2},{5,3},{6,4},{7,5},{8,6},{9,7},{10,... | collective-permute-start | bytes 393224 | tf_op jit(solution)/shard_map/ppermute | solution.py:26
  112.8 7.2 %collective-permute-start.17 = (bf16[64,1024]{1,0:T(8,128)(2,1)S(1)}, bf16[64,1024]{1,0:T(8,128)(2,1)S(1)}, u32[]{:S(2)}, u32[]{:S(2)}) collective-permute-start(bf16[64,1024]{1,0:T(8,128)(2,1)S(1)} %dynamic-slice_convert_fusion.3), channel_id=1, source_target_pairs={{0,1},{1,0},{2,3},{3,2},{4,5},{5,4},{6,7},{7,6},{8,9},{9,8},{10,11... | collective-permute-start | bytes 393224 | tf_op jit(solution)/shard_map/ppermute | solution.py:62
  115.8 6.3 %collective-permute-start.21 = (bf16[64,1024]{1,0:T(8,128)(2,1)S(1)}, bf16[64,1024]{1,0:T(8,128)(2,1)S(1)}, u32[]{:S(2)}, u32[]{:S(2)}) collective-permute-start(bf16[64,1024]{1,0:T(8,128)(2,1)S(1)} %get-tuple-element.26), channel_id=1, source_target_pairs={{0,2},{1,3},{2,4},{3,5},{4,6},{5,7},{6,8},{7,9},{8,10},{9,11},{10,... | collective-permute-start | bytes 393224 | tf_op jit(solution)/shard_map/ppermute | solution.py:25
  115.9 6.2 %collective-permute-start.25 = (bf16[64,1024]{1,0:T(8,128)(2,1)S(1)}, bf16[64,1024]{1,0:T(8,128)(2,1)S(1)}, u32[]{:S(2)}, u32[]{:S(2)}) collective-permute-start(bf16[64,1024]{1,0:T(8,128)(2,1)S(1)} %get-tuple-element.27), channel_id=1, source_target_pairs={{0,14},{1,15},{2,0},{3,1},{4,2},{5,3},{6,4},{7,5},{8,6},{9,7},{10,... | collective-permute-start | bytes 393224 | tf_op jit(solution)/shard_map/ppermute | solution.py:26
  122.1 6.3 %collective-permute-start.22 = (bf16[64,1024]{1,0:T(8,128)(2,1)S(1)}, bf16[64,1024]{1,0:T(8,128)(2,1)S(1)}, u32[]{:S(2)}, u32[]{:S(2)}) collective-permute-start(bf16[64,1024]{1,0:T(8,128)(2,1)S(1)} %get-tuple-element.24), channel_id=1, source_target_pairs={{0,2},{1,3},{2,4},{3,5},{4,6},{5,7},{6,8},{7,9},{8,10},{9,11},{10,... | collective-permute-start | bytes 393224 | tf_op jit(solution)/shard_map/ppermute | solution.py:25
  122.7 5.7 %collective-permute-start.26 = (bf16[64,1024]{1,0:T(8,128)(2,1)S(1)}, bf16[64,1024]{1,0:T(8,128)(2,1)S(1)}, u32[]{:S(2)}, u32[]{:S(2)}) collective-permute-start(bf16[64,1024]{1,0:T(8,128)(2,1)S(1)} %get-tuple-element.25), channel_id=1, source_target_pairs={{0,14},{1,15},{2,0},{3,1},{4,2},{5,3},{6,4},{7,5},{8,6},{9,7},{10,... | collective-permute-start | bytes 393224 | tf_op jit(solution)/shard_map/ppermute | solution.py:26

commit v5 on v4

--- a/solution.py
+++ b/solution.py
@@ -35,35 +35,30 @@
     return own_a + got_a + got_b
 
 
-def _ring_reduce_scatter(part):
+def _ring_reduce_scatter(part_z, part_y):
     nmp = lax.axis_size("mp")
     m = lax.axis_index("mp")
     nlo = 2
     nz = nmp // nlo
     z = m // nlo
     lo = m % nlo
-    rows = part.shape[0] // nz
+    rows = part_z.shape[0] // nz
     sub = rows // nlo
-    halfc = part.shape[1] // 2
+    halfc = part_z.shape[1]
     up = [(i, ((i // nlo + 1) % nz) * nlo + i % nlo) for i in range(nmp)]
     down = [(i, ((i // nlo - 1) % nz) * nlo + i % nlo) for i in range(nmp)]
     pair = [(i, i ^ 1) for i in range(nmp)]
 
-    py = part[:, halfc:].reshape(nz, nlo, sub, halfc)
-    keep = lax.dynamic_index_in_dim(py, lo, axis=1, keepdims=False)
-    give = lax.dynamic_index_in_dim(py, 1 - lo, axis=1, keepdims=False)
-    got_y = lax.ppermute(give, "mp", pair)
-    acc_y = keep.astype(jnp.float32) + got_y.astype(jnp.float32)
+    out_y = lax.psum_scatter(part_y, "mp", scatter_dimension=0, tiled=True)
 
-    pz = part[:, :halfc].reshape(nz, rows, halfc)
+    pz = part_z.reshape(nz, rows, halfc)
     acc_z = _z_reduce_scatter(pz, z, nz, up, down)
     mine = lax.dynamic_slice_in_dim(acc_z, lo * sub, sub, axis=0)
     other = lax.dynamic_slice_in_dim(acc_z, (1 - lo) * sub, sub, axis=0)
     got = lax.ppermute(other.astype(jnp.bfloat16), "mp", pair)
     out_z = mine + got.astype(jnp.float32)
 
-    out_y = _z_reduce_scatter(acc_y.astype(jnp.bfloat16), z, nz, up, down)
-    return jnp.concatenate([out_z, out_y], axis=1).astype(jnp.bfloat16)
+    return jnp.concatenate([out_z.astype(jnp.bfloat16), out_y], axis=1)
 
 
 def shards(
@@ -135,10 +130,15 @@
         grad_down = grad_down + got.astype(jnp.float32)
 
     both = jnp.concatenate([grad_gate, grad_up], axis=1)
-    partial_sum = lax.dot_general(
-        both, weights_full, (((1,), (1,)), ((), ())), preferred_element_type=jnp.float32
-    )
-    input_grad = _ring_reduce_scatter(partial_sum.astype(jnp.bfloat16))
+    dcols = weights_full.shape[0] // 2
+    part_y = lax.dot_general(
+        both, weights_full[dcols:], (((1,), (1,)), ((), ())), preferred_element_type=jnp.float32
+    ).astype(jnp.bfloat16)
+    part_y, both = lax.optimization_barrier((part_y, both))
+    part_z = lax.dot_general(
+        both, weights_full[:dcols], (((1,), (1,)), ((), ())), preferred_element_type=jnp.float32
+    ).astype(jnp.bfloat16)
+    input_grad = _ring_reduce_scatter(part_z, part_y)
 
     first_new = 0.9 * first_moment[0] + 0.1 * grad_down
     second_new = 0.999 * second_moment[0] + 0.001 * grad_down * grad_down

time: 130 us -> 156 us (1.20); the launches traced: 129 us -> 154 us
  waiting for transfers between devices: 48 us -> 64 us
  between operations: 1.02 us -> 14.4 us
  starting transfers between devices: 40.9 us -> 30 us
  other arithmetic: 10.7 us -> 14.1 us
  matrix products: 16 us -> 19.4 us
    ppermute x1, waiting for transfers between devices: 0.9 us -> 18.1 us  [_ring_reduce_scatter(): got = lax.ppermute(other.astype(jnp.bfloat16), 'mp', pair)]
    ppermute x8 -> x4, starting transfers between devices: 25 us -> 15.6 us  [_z_reduce_scatter(): lax.ppermute(send_b.astype(jnp.bfloat16), 'mp', down).astype(jnp.float32)]
    dot_general x1 -> x2, matrix products: 3.82 us -> 6.64 us  [the longest x1 3.4 us: shards(): lax.dot_general(both, weights_full[:dcols], (((1,), (1,)), ((), ())), pre...]
    ppermute x3, waiting for transfers between devices: 10.4 us -> 8.07 us  [shards(): got = lax.ppermute(blk.astype(jnp.bfloat16), 'dp', _shift(ndp, s))]
    unnamed x20 -> x28, local copies, waits for them, and re-layouts: 5.29 us -> 7.58 us
    convert_element_type x6 -> x3, other arithmetic: 2.4 us -> 4.46 us  [_z_reduce_scatter(): send_a.astype(jnp.bfloat16)]
    slice x1 -> x0, local copies, waits for them, and re-layouts: 1.82 us -> none  [_ring_reduce_scatter(): pz = part[:, :halfc].reshape(nz, rows, halfc)]
    broadcast_in_dim x0 -> x1, other arithmetic: none -> 1.62 us  [shards(): input_grad[None]]
  transfers between devices with their start and end apart: 27 -> 19, of which waited for: 12 -> 9; matrix products, arithmetic and copies ran while one was open for 18% -> 19% of each run, Pallas kernels for 0% -> 0%
where the time goes in v5:
time: 156 us; the launch traced here: 154 us
  waiting for transfers between devices  64 us (41%)
  starting transfers between devices  30 us (19%)
  matrix products  19.4 us (12%)
  between operations  14.4 us (9%)
  other arithmetic  14.1 us (9%)
  local copies, waits for them, and re-layouts  11.6 us (7%)
    ppermute x1, waiting for transfers between devices, shards(): from_left = lax.ppermute(shard, 'dp', _shift(ndp, 1))  20.9 us
    ppermute x1, waiting for transfers between devices, _ring_reduce_scatter(): got = lax.ppermute(other.astype(jnp.bfloat16), 'mp', pair)  18.1 us
    ppermute x4, starting transfers between devices, _z_reduce_scatter(): lax.ppermute(send_b.astype(jnp.bfloat16), 'mp', down).astype(jnp.float32)  15.6 us
    ppermute x4, waiting for transfers between devices, _z_reduce_scatter(): lax.ppermute(send_a.astype(jnp.bfloat16), 'mp', up).astype(jnp.float32)  11.2 us
    ppermute x3, waiting for transfers between devices, shards(): got = lax.ppermute(blk.astype(jnp.bfloat16), 'dp', _shift(ndp, s))  8.07 us
    unnamed x28, local copies, waits for them, and re-layouts  7.58 us
    dot_general x5, matrix products, shards(): p1 = jnp.dot(xs, piece[:, :2 * ff], preferred_element_type=jnp.float32)  6.63 us
    ppermute x3, starting transfers between devices, shards(): got = lax.ppermute(blk.astype(jnp.bfloat16), 'dp', _shift(ndp, s))  4.74 us
  transfers between devices with their start and end apart: 19, of which 9 were waited for; matrix products, arithmetic and copies ran while one was open for 19% of the time, Pallas kernels for 0%

profile of v5, /device:TPU:8, one launch (start us, length us, event | category | flops | bytes accessed | tf_op | source)
XLA Modules:
  0.0 153.6 jit_solution(12428925242072606994)
XLA Ops:
  7.2 0.0 reduce-scatter.2.cloned.1.call-start
  7.2 1.2 copy.14
  8.5 1.2 copy.15
  9.6 0.1 fusion.54
  9.7 1.1 pad_maximum_fusion.1
  10.8 1.5 collective-permute-start
  12.3 1.7 %collective-permute-start.1 = (bf16[512,1152]{0,1:T(8,128)(2,1)}, bf16[512,1152]{0,1:T(8,128)(2,1)}, u32[]{:S(2)}, u32[]{:S(2)}) collective-permute-start(bf16[512,1152]{0,1:T(8,128)(2,1)} %pad_maximum_fusion.1), channel_id=1, source_target_pairs={{0,48},{16,0},{32,16},{48,32},{1,49},{17,1},{33,17},{49,33},{2,50}... | collective-permute-start | bytes 3538952 | tf_op jit(solution)/shard_map/ppermute | solution.py:88
  14.1 0.4 broadcast_in_dim.14
  14.4 0.1 fusion.53
  14.6 1.7 %copy-done.12 = bf16[1,1024,2048]{2,1,0:T(8,128)(2,1)S(1)} copy-done((bf16[1,1024,2048]{2,1,0:T(8,128)(2,1)S(1)}, bf16[1,1024,2048]{2,1,0:T(8,128)(2,1)}, u32[]{:S(2)}) %copy-start.12) | copy-done | bytes 4194328
  16.2 1.0 fusion.15
  17.3 1.2 copy-done.1
  18.4 0.6 fusion.9
  19.0 20.9 %collective-permute-done = bf16[512,1152]{0,1:T(8,128)(2,1)S(1)} collective-permute-done((bf16[512,1152]{0,1:T(8,128)(2,1)}, bf16[512,1152]{0,1:T(8,128)(2,1)S(1)}, u32[]{:S(2)}, u32[]{:S(2)}) %collective-permute-start) | collective-permute-done | bytes 1179680 | tf_op jit(solution)/shard_map/ppermute | solution.py:87
  40.0 0.4 collective-permute-start.2
  40.4 0.0 collective-permute-done.1
  40.4 1.1 slice.77
  41.5 3.2 %collective-permute-start.3 = (bf16[256,1152]{0,1:T(8,128)(2,1)S(1)}, bf16[256,1152]{0,1:T(8,128)(2,1)S(1)}, u32[]{:S(2)}, u32[]{:S(2)}) collective-permute-start(bf16[256,1152]{0,1:T(8,128)(2,1)S(1)} %slice.77), channel_id=1, source_target_pairs={{0,48},{16,0},{32,16},{48,32},{1,49},{17,1},{33,17},{49,33},{2,50}... | collective-permute-start | bytes 1769480 | tf_op jit(solution)/shard_map/ppermute | solution.py:90
  44.7 2.1 %fusion.11 = f32[1024,768]{0,1:T(8,128)S(1)} fusion(bf16[1,1024,2048]{2,1,0:T(8,128)(2,1)S(1)} %copy-done.12, s32[]{:T(128)S(6)} %select_n.131, bf16[512,1152]{0,1:T(8,128)(2,1)} %collective-permute-done.1), kind=kOutput, calls=%fused_computation.22 | convolution fusion | flops 805306368 | bytes 4980740 | tf_op jit(solution)/shard_map/dot_general | solution.py:106
  46.8 1.6 %fusion.5 = f32[1024,384]{0,1:T(8,128)S(1)} fusion(bf16[1,1024,2048]{2,1,0:T(8,128)(2,1)S(1)} %copy-done.1, s32[]{:T(128)S(6)} %select_n.131, bf16[512,1152]{0,1:T(8,128)(2,1)} %collective-permute-done.1), kind=kOutput, calls=%fused_computation.16 | convolution fusion | flops 402653184 | bytes 3014660 | tf_op jit(solution)/shard_map/dot_general | solution.py:107
  48.4 0.6 fusion.7
  49.1 0.1 slice_dynamic-update-slice_fusion.1
  49.2 1.0 fusion.13
  50.2 1.2 slice_dynamic-update-slice_fusion
  51.5 4.0 %collective-permute-done.2 = bf16[256,1152]{0,1:T(8,128)(2,1)S(1)} collective-permute-done((bf16[256,1152]{0,1:T(8,128)(2,1)S(1)}, bf16[256,1152]{0,1:T(8,128)(2,1)S(1)}, u32[]{:S(2)}, u32[]{:S(2)}) %collective-permute-start.2) | collective-permute-done | bytes 589856 | tf_op jit(solution)/shard_map/ppermute | solution.py:89
  55.5 0.4 fusion.41
  55.9 0.6 fusion.47
  56.5 1.8 %add_add_fusion = f32[1024,768]{0,1:T(8,128)S(1)} fusion(f32[1024,768]{0,1:T(8,128)S(1)} %fusion.47, f32[1024,768]{0,1:T(8,128)S(1)} %fusion.11, f32[1024,768]{0,1:T(8,128)S(1)} %fusion.15, f32[1024,768]{0,1:T(8,128)S(1)} %fusion.13, bf16[1,1024,2048]{2,1,0:T(8,128)(2,1)} %param.9, s32[]{:T(128)S(6)} %select_n.134, ...), kind=kOutput, calls=%fused_computation.2 | convolution fusion | flops 405798912 | bytes 16646148 | tf_op jit(solution)/shard_map/dot_general | solution.py:106
  58.4 1.0 multiply_convert_fusion.1
  59.4 0.6 copy-done.3
  60.0 0.1 pad_maximum_fusion
  60.2 1.7 %copy-done.6 = bf16[2048,768]{0,1:T(8,128)(2,1)} copy-done((bf16[2048,768]{0,1:T(8,128)(2,1)}, bf16[2048,768]{0,1:T(8,128)(2,1)S(1)}, u32[]{:S(2)}) %copy-start.6) | copy-done | bytes 3145752
  61.9 3.2 %convolution_convert_fusion.1 = bf16[1024,1024]{1,0:T(8,128)(2,1)} fusion(bf16[2048,768]{0,1:T(8,128)(2,1)S(1)} %slice_dynamic-update-slice_fusion.2, bf16[1024,384]{0,1:T(8,128)(2,1)S(1)} %get-tuple-element.14, bf16[1024,384]{0,1:T(8,128)(2,1)S(1)} %get-tuple-element.13), kind=kOutput, calls=%fused_computation.4 | convolution fusion | flops 1614807040 | bytes 5242880 | tf_op jit(solution)/shard_map/dot_general | solution.py:134
  65.2 0.0 reduce-scatter.2.cloned.1.call-update
  65.2 0.0 copy-start.2
  65.2 3.4 %convolution_convert_fusion = bf16[1024,1024]{1,0:T(8,128)(2,1)S(1)} fusion(bf16[1024,768]{0,1:T(8,128)(2,1)S(1)} %pad_maximum_fusion, bf16[2048,768]{0,1:T(8,128)(2,1)} %copy-done.6), kind=kOutput, calls=%fused_computation.3 | convolution fusion | flops 1611661312 | bytes 5242880 | tf_op jit(solution)/shard_map/dot_general | solution.py:138
  68.7 5.9 %collective-permute-start.13 = (bf16[128,512]{1,0:T(8,128)(2,1)S(1)}, bf16[128,512]{1,0:T(8,128)(2,1)S(1)}, u32[]{:S(2)}, u32[]{:S(2)}) collective-permute-start(bf16[128,512]{1,0:T(8,128)(2,1)S(1)} %get-tuple-element.27), channel_id=1, source_target_pairs={{0,14},{1,15},{2,0},{3,1},{4,2},{5,3},{6,4},{7,5},{8,6},{9,7},{10,... | collective-permute-start | bytes 393224 | tf_op jit(solution)/shard_map/ppermute | solution.py:26
  74.6 1.9 %fusion = f32[384,2048]{1,0:T(8,128)S(1)} fusion(bf16[1,1024,2048]{2,1,0:T(8,128)(2,1)S(1)} %copy-done.2, f32[1024,768]{0,1:T(8,128)S(1)} %copy-done.4), kind=kOutput, calls=%fused_computation | convolution fusion | flops 1612972032 | bytes 10485760 | tf_op jit(solution)/shard_map/dot_general | solution.py:122
  76.5 0.6 collective-permute-done.13
  77.2 3.7 %collective-permute-done.9 = bf16[128,512]{1,0:T(8,128)(2,1)S(1)} collective-permute-done((bf16[128,512]{1,0:T(8,128)(2,1)S(1)}, bf16[128,512]{1,0:T(8,128)(2,1)S(1)}, u32[]{:S(2)}, u32[]{:S(2)}) %collective-permute-start.9) | collective-permute-done | bytes 131104 | tf_op jit(solution)/shard_map/ppermute | solution.py:25
  80.8 0.1 fusion.35
  80.9 0.0 copy-start.5
  80.9 0.3 collective-permute-start.10
  81.2 3.2 %collective-permute-start.14 = (bf16[128,1024]{1,0:T(8,128)(2,1)S(1)}, bf16[128,1024]{1,0:T(8,128)(2,1)}, u32[]{:S(2)}, u32[]{:S(2)}) collective-permute-start(bf16[128,1024]{1,0:T(8,128)(2,1)S(1)} %get-tuple-element.23), channel_id=1, source_target_pairs={{0,14},{1,15},{2,0},{3,1},{4,2},{5,3},{6,4},{7,5},{8,6},{9,7},{10,... | collective-permute-start | bytes 786440 | tf_op jit(solution)/shard_map/ppermute | solution.py:26
  84.5 1.0 dynamic-slice_convert_fusion.2
  85.5 0.7 collective-permute-start.4
  86.2 4.0 %collective-permute-start.5 = (bf16[384,512]{1,0:T(8,128)(2,1)}, bf16[384,512]{1,0:T(8,128)(2,1)S(1)}, u32[]{:S(2)}, u32[]{:S(2)}) collective-permute-start(bf16[384,512]{1,0:T(8,128)(2,1)} %get-tuple-element.17), channel_id=1, source_target_pairs={{0,32},{16,48},{32,0},{48,16},{1,33},{17,49},{33,1},{49,17},{2,34}... | collective-permute-start | bytes 1179656 | tf_op jit(solution)/shard_map/ppermute | solution.py:129
  90.2 2.1 %fusion.34 = (bf16[128,1024]{1,0:T(8,128)(2,1)}, bf16[128,1024]{1,0:T(8,128)(2,1)}) fusion(bf16[128,1024]{1,0:T(8,128)(2,1)S(1)} %collective-permute-done.10, bf16[8,128,1024]{2,1,0:T(8,128)(2,1)} %bitcast.113, s32[]{:T(128)S(6)} %select_n.145, s32[]{:T(128)S(6)} %select_n.151, bf16[128,1024]{1,0:T(8,128)(2,1)} %collective-permute-done.14), kind=kLoop, calls=%fused_computation.65 | loop fusion | flops 1048576 | bytes 1572872 | tf_op jit(solution)/shard_map/convert_element_type | solution.py:25
  92.4 3.2 %collective-permute-start.15 = (bf16[128,1024]{1,0:T(8,128)(2,1)}, bf16[128,1024]{1,0:T(8,128)(2,1)}, u32[]{:S(2)}, u32[]{:S(2)}) collective-permute-start(bf16[128,1024]{1,0:T(8,128)(2,1)} %get-tuple-element.21), channel_id=1, source_target_pairs={{0,14},{1,15},{2,0},{3,1},{4,2},{5,3},{6,4},{7,5},{8,6},{9,7},{10,... | collective-permute-start | bytes 786440 | tf_op jit(solution)/shard_map/ppermute | solution.py:26
  95.6 3.3 %collective-permute-done.4 = bf16[384,512]{1,0:T(8,128)(2,1)S(1)} collective-permute-done((bf16[384,512]{1,0:T(8,128)(2,1)}, bf16[384,512]{1,0:T(8,128)(2,1)S(1)}, u32[]{:S(2)}, u32[]{:S(2)}) %collective-permute-start.4) | collective-permute-done | bytes 393248 | tf_op jit(solution)/shard_map/ppermute | solution.py:129
  98.9 4.7 %collective-permute-done.5 = bf16[384,512]{1,0:T(8,128)(2,1)S(1)} collective-permute-done((bf16[384,512]{1,0:T(8,128)(2,1)}, bf16[384,512]{1,0:T(8,128)(2,1)S(1)}, u32[]{:S(2)}, u32[]{:S(2)}) %collective-permute-start.5) | collective-permute-done | bytes 393248 | tf_op jit(solution)/shard_map/ppermute | solution.py:129
  103.7 2.4 %fusion.62 = (f32[1,384,512]{2,1,0:T(8,128)}, f32[384,512]{1,0:T(8,128)S(1)}) fusion(f32[1,384,512]{2,1,0:T(8,128)S(1)} %copy-done.5, bf16[384,512]{1,0:T(8,128)(2,1)} %collective-permute-done.6, bf16[384,512]{1,0:T(8,128)(2,1)S(1)} %collective-permute-done.5, bf16[384,512]{1,0:T(8,128)(2,1)S(1)} %collective-permute-done.4, f32[384,2048]{1,0:T(8,128)} %copy-done.9, ...), kind=kLoop, calls=%fused_computation.97 | loop fusion | flops 1966080 | bytes 4325380 | tf_op jit(solution)/shard_map/broadcast_in_dim | solution.py:160
  106.1 1.5 %fusion.61 = (f32[1,384,512]{2,1,0:T(8,128)}, bf16[384,512]{1,0:T(8,128)(2,1)S(1)}) fusion(f32[384,512]{1,0:T(8,128)S(1)} %get-tuple-element.10, f32[1,384,512]{2,1,0:T(8,128)S(1)} %copy-done.10, f32[384,512]{1,0:T(8,128)S(1)} %copy-done.7, f32[1,384,512]{2,1,0:T(8,128)S(1)} %copy-done.5, f32[1,384,512]{2,1,0:T(8,128)S(1)} %copy-done), kind=kLoop, calls=%fused_computation.96 | loop fusion | flops 3342336 | bytes 5111808 | tf_op jit(solution)/shard_map/broadcast_in_dim | solution.py:160
  107.7 2.3 %fusion.33 = (bf16[128,1024]{1,0:T(8,128)(2,1)}, bf16[128,1024]{1,0:T(8,128)(2,1)}) fusion(bf16[128,1024]{1,0:T(8,128)(2,1)} %collective-permute-done.11, bf16[8,128,1024]{2,1,0:T(8,128)(2,1)} %bitcast.114, s32[]{:T(128)S(6)} %select_n.147, s32[]{:T(128)S(6)} %select_n.153, bf16[128,1024]{1,0:T(8,128)(2,1)} %collective-permute-done.15), kind=kLoop, calls=%fused_computation.63 | loop fusion | flops 1048576 | bytes 1572872 | tf_op jit(solution)/shard_map/convert_element_type | solution.py:25
  109.9 3.2 %collective-permute-start.16 = (bf16[128,1024]{1,0:T(8,128)(2,1)}, bf16[128,1024]{1,0:T(8,128)(2,1)}, u32[]{:S(2)}, u32[]{:S(2)}) collective-permute-start(bf16[128,1024]{1,0:T(8,128)(2,1)} %get-tuple-element.19), channel_id=1, source_target_pairs={{0,14},{1,15},{2,0},{3,1},{4,2},{5,3},{6,4},{7,5},{8,6},{9,7},{10,... | collective-permute-start | bytes 786440 | tf_op jit(solution)/shard_map/ppermute | solution.py:26
  113.2 0.1 add_convert_fusion
  113.3 2.4 %collective-permute-start.8 = (bf16[384,512]{1,0:T(8,128)(2,1)S(1)}, bf16[384,512]{1,0:T(8,128)(2,1)S(1)}, u32[]{:S(2)}, u32[]{:S(2)}) collective-permute-start(bf16[384,512]{1,0:T(8,128)(2,1)S(1)} %add_convert_fusion), channel_id=1, source_target_pairs={{0,128},{64,192},{128,0},{192,64},{1,129},{65,193},{129,1},{193,65... | collective-permute-start | bytes 1179656 | tf_op jit(solution)/shard_map/ppermute | solution.py:155
  115.7 7.6 %collective-permute-done.12 = bf16[128,1024]{1,0:T(8,128)(2,1)S(1)} collective-permute-done((bf16[128,1024]{1,0:T(8,128)(2,1)}, bf16[128,1024]{1,0:T(8,128)(2,1)S(1)}, u32[]{:S(2)}, u32[]{:S(2)}) %collective-permute-start.12) | collective-permute-done | bytes 262176 | tf_op jit(solution)/shard_map/ppermute | solution.py:25
  123.2 1.1 fusion.36
  124.4 0.1 collective-permute-start.17
  124.5 18.1 %collective-permute-done.17 = bf16[64,1024]{1,0:T(8,128)(2,1)S(1)} collective-permute-done((bf16[64,1024]{1,0:T(8,128)(2,1)S(1)}, bf16[64,1024]{1,0:T(8,128)(2,1)S(1)}, u32[]{:S(2)}, u32[]{:S(2)}) %collective-permute-start.17) | collective-permute-done | bytes 131104 | tf_op jit(solution)/shard_map/ppermute | solution.py:58
  142.7 1.4 multiply_subtract_fusion
  144.1 1.0 reduce-scatter.2.cloned.1.call-done
  145.1 1.6 %maximum_bitcast_fusion = bf16[1,64,2048]{2,1,0:T(8,128)(2,1)} fusion(bf16[64,1024]{1,0:T(8,128)(2,1)} %reduce-scatter.2.cloned.1.call-done, bf16[64,1024]{1,0:T(8,128)(2,1)S(1)} %add_convert_fusion.1), kind=kLoop, calls=%fused_computation.92 | loop fusion | flops 524288 | bytes 524288 | tf_op jit(solution)/shard_map/broadcast_in_dim | solution.py:160
  (41 shorter events, 0.3 us)
Async XLA Ops:
  7.2 2.5 %copy-start = (f32[1,384,512]{2,1,0:T(8,128)S(1)}, f32[1,384,512]{2,1,0:T(8,128)}, u32[]{:S(2)}) copy-start(f32[1,384,512]{2,1,0:T(8,128)} %param.13) | copy-start | bytes 2359300
  7.2 137.9 %reduce-scatter.2.cloned.1.call-start = ((), (), s32[]{:S(2)}) async-start(), calls=%async_computation.1 | async-start | bytes 2228224 | tf_op jit(solution)/shard_map/reduce_scatter | solution.py:52
  10.8 29.1 %collective-permute-start = (bf16[512,1152]{0,1:T(8,128)(2,1)}, bf16[512,1152]{0,1:T(8,128)(2,1)S(1)}, u32[]{:S(2)}, u32[]{:S(2)}) collective-permute-start(bf16[512,1152]{0,1:T(8,128)(2,1)} %pad_maximum_fusion.1), channel_id=1, source_target_pairs={{0,16},{16,32},{32,48},{48,0},{1,17},{17,33},{33,49},{49,1},{2,18}... | collective-permute-start | bytes 3538952 | tf_op jit(solution)/shard_map/ppermute | solution.py:87
  12.3 28.0 %collective-permute-start.1 = (bf16[512,1152]{0,1:T(8,128)(2,1)}, bf16[512,1152]{0,1:T(8,128)(2,1)}, u32[]{:S(2)}, u32[]{:S(2)}) collective-permute-start(bf16[512,1152]{0,1:T(8,128)(2,1)} %pad_maximum_fusion.1), channel_id=1, source_target_pairs={{0,48},{16,0},{32,16},{48,32},{1,49},{17,1},{33,17},{49,33},{2,50}... | collective-permute-start | bytes 3538952 | tf_op jit(solution)/shard_map/ppermute | solution.py:88
  14.1 2.2 %copy-start.12 = (bf16[1,1024,2048]{2,1,0:T(8,128)(2,1)S(1)}, bf16[1,1024,2048]{2,1,0:T(8,128)(2,1)}, u32[]{:S(2)}) copy-start(bf16[1,1024,2048]{2,1,0:T(8,128)(2,1)} %param.9) | copy-start | bytes 12582916
  16.2 2.2 %copy-start.1 = (bf16[1,1024,2048]{2,1,0:T(8,128)(2,1)S(1)}, bf16[1,1024,2048]{2,1,0:T(8,128)(2,1)}, u32[]{:S(2)}) copy-start(bf16[1,1024,2048]{2,1,0:T(8,128)(2,1)} %param.10) | copy-start | bytes 12582916
  40.0 15.5 %collective-permute-start.2 = (bf16[256,1152]{0,1:T(8,128)(2,1)S(1)}, bf16[256,1152]{0,1:T(8,128)(2,1)S(1)}, u32[]{:S(2)}, u32[]{:S(2)}) collective-permute-start(bf16[256,1152]{0,1:T(8,128)(2,1)S(1)} %slice.75), channel_id=1, source_target_pairs={{0,16},{16,32},{32,48},{48,0},{1,17},{17,33},{33,49},{49,1},{2,18}... | collective-permute-start | bytes 1769480 | tf_op jit(solution)/shard_map/ppermute | solution.py:89
  41.5 15.1 %collective-permute-start.3 = (bf16[256,1152]{0,1:T(8,128)(2,1)S(1)}, bf16[256,1152]{0,1:T(8,128)(2,1)S(1)}, u32[]{:S(2)}, u32[]{:S(2)}) collective-permute-start(bf16[256,1152]{0,1:T(8,128)(2,1)S(1)} %slice.77), channel_id=1, source_target_pairs={{0,48},{16,0},{32,16},{48,32},{1,49},{17,1},{33,17},{49,33},{2,50}... | collective-permute-start | bytes 1769480 | tf_op jit(solution)/shard_map/ppermute | solution.py:90
  58.4 1.6 %copy-start.3 = (f32[1024,768]{0,1:T(8,128)}, f32[1024,768]{0,1:T(8,128)S(1)}, u32[]{:S(2)}) copy-start(f32[1024,768]{0,1:T(8,128)S(1)} %add_add_fusion) | copy-start | bytes 9437188
  60.2 1.7 %copy-start.6 = (bf16[2048,768]{0,1:T(8,128)(2,1)}, bf16[2048,768]{0,1:T(8,128)(2,1)S(1)}, u32[]{:S(2)}) copy-start(bf16[2048,768]{0,1:T(8,128)(2,1)S(1)} %slice_dynamic-update-slice_fusion.2) | copy-start | bytes 9437188
  65.2 9.4 %copy-start.2 = (bf16[1,1024,2048]{2,1,0:T(8,128)(2,1)S(1)}, bf16[1,1024,2048]{2,1,0:T(8,128)(2,1)}, u32[]{:S(2)}) copy-start(bf16[1,1024,2048]{2,1,0:T(8,128)(2,1)} %param.10) | copy-start | bytes 12582916
  65.2 9.4 %copy-start.4 = (f32[1024,768]{0,1:T(8,128)S(1)}, f32[1024,768]{0,1:T(8,128)}, u32[]{:S(2)}) copy-start(f32[1024,768]{0,1:T(8,128)} %copy-done.3) | copy-start | bytes 9437188
  68.6 12.2 %copy-start.8 = (bf16[1024,1024]{1,0:T(8,128)(2,1)}, bf16[1024,1024]{1,0:T(8,128)(2,1)S(1)}, u32[]{:S(2)}) copy-start(bf16[1024,1024]{1,0:T(8,128)(2,1)S(1)} %convolution_convert_fusion) | copy-start | bytes 6291460
  68.7 8.5 %collective-permute-start.13 = (bf16[128,512]{1,0:T(8,128)(2,1)S(1)}, bf16[128,512]{1,0:T(8,128)(2,1)S(1)}, u32[]{:S(2)}, u32[]{:S(2)}) collective-permute-start(bf16[128,512]{1,0:T(8,128)(2,1)S(1)} %get-tuple-element.27), channel_id=1, source_target_pairs={{0,14},{1,15},{2,0},{3,1},{4,2},{5,3},{6,4},{7,5},{8,6},{9,7},{10,... | collective-permute-start | bytes 393224 | tf_op jit(solution)/shard_map/ppermute | solution.py:26
  74.6 6.2 %collective-permute-start.9 = (bf16[128,512]{1,0:T(8,128)(2,1)S(1)}, bf16[128,512]{1,0:T(8,128)(2,1)S(1)}, u32[]{:S(2)}, u32[]{:S(2)}) collective-permute-start(bf16[128,512]{1,0:T(8,128)(2,1)S(1)} %get-tuple-element.26), channel_id=1, source_target_pairs={{0,2},{1,3},{2,4},{3,5},{4,6},{5,7},{6,8},{7,9},{8,10},{9,11},{10,... | collective-permute-start | bytes 393224 | tf_op jit(solution)/shard_map/ppermute | solution.py:25
  76.5 7.9 %copy-start.9 = (f32[384,2048]{1,0:T(8,128)}, f32[384,2048]{1,0:T(8,128)S(1)}, u32[]{:S(2)}) copy-start(f32[384,2048]{1,0:T(8,128)S(1)} %fusion) | copy-start | bytes 9437188
  80.9 22.8 %copy-start.5 = (f32[1,384,512]{2,1,0:T(8,128)S(1)}, f32[1,384,512]{2,1,0:T(8,128)}, u32[]{:S(2)}) copy-start(f32[1,384,512]{2,1,0:T(8,128)} %param.15) | copy-start | bytes 2359300
  80.9 9.3 %collective-permute-start.10 = (bf16[128,1024]{1,0:T(8,128)(2,1)S(1)}, bf16[128,1024]{1,0:T(8,128)(2,1)S(1)}, u32[]{:S(2)}, u32[]{:S(2)}) collective-permute-start(bf16[128,1024]{1,0:T(8,128)(2,1)S(1)} %get-tuple-element.22), channel_id=1, source_target_pairs={{0,2},{1,3},{2,4},{3,5},{4,6},{5,7},{6,8},{7,9},{8,10},{9,11},{10,... | collective-permute-start | bytes 786440 | tf_op jit(solution)/shard_map/ppermute | solution.py:25
  81.2 9.0 %collective-permute-start.14 = (bf16[128,1024]{1,0:T(8,128)(2,1)S(1)}, bf16[128,1024]{1,0:T(8,128)(2,1)}, u32[]{:S(2)}, u32[]{:S(2)}) collective-permute-start(bf16[128,1024]{1,0:T(8,128)(2,1)S(1)} %get-tuple-element.23), channel_id=1, source_target_pairs={{0,14},{1,15},{2,0},{3,1},{4,2},{5,3},{6,4},{7,5},{8,6},{9,7},{10,... | collective-permute-start | bytes 786440 | tf_op jit(solution)/shard_map/ppermute | solution.py:26
  85.5 13.4 %collective-permute-start.4 = (bf16[384,512]{1,0:T(8,128)(2,1)}, bf16[384,512]{1,0:T(8,128)(2,1)S(1)}, u32[]{:S(2)}, u32[]{:S(2)}) collective-permute-start(bf16[384,512]{1,0:T(8,128)(2,1)} %get-tuple-element.15), channel_id=1, source_target_pairs={{0,16},{16,32},{32,48},{48,0},{1,17},{17,33},{33,49},{49,1},{2,18}... | collective-permute-start | bytes 1179656 | tf_op jit(solution)/shard_map/ppermute | solution.py:129
  86.2 17.5 %collective-permute-start.5 = (bf16[384,512]{1,0:T(8,128)(2,1)}, bf16[384,512]{1,0:T(8,128)(2,1)S(1)}, u32[]{:S(2)}, u32[]{:S(2)}) collective-permute-start(bf16[384,512]{1,0:T(8,128)(2,1)} %get-tuple-element.17), channel_id=1, source_target_pairs={{0,32},{16,48},{32,0},{48,16},{1,33},{17,49},{33,1},{49,17},{2,34}... | collective-permute-start | bytes 1179656 | tf_op jit(solution)/shard_map/ppermute | solution.py:129
  90.2 13.5 %collective-permute-start.6 = (bf16[384,512]{1,0:T(8,128)(2,1)S(1)}, bf16[384,512]{1,0:T(8,128)(2,1)}, u32[]{:S(2)}, u32[]{:S(2)}) collective-permute-start(bf16[384,512]{1,0:T(8,128)(2,1)S(1)} %get-tuple-element.16), channel_id=1, source_target_pairs={{0,48},{16,0},{32,16},{48,32},{1,49},{17,1},{33,17},{49,33},{2,50}... | collective-permute-start | bytes 1179656 | tf_op jit(solution)/shard_map/ppermute | solution.py:129
  92.3 15.3 %collective-permute-start.11 = (bf16[128,1024]{1,0:T(8,128)(2,1)}, bf16[128,1024]{1,0:T(8,128)(2,1)}, u32[]{:S(2)}, u32[]{:S(2)}) collective-permute-start(bf16[128,1024]{1,0:T(8,128)(2,1)} %get-tuple-element.20), channel_id=1, source_target_pairs={{0,2},{1,3},{2,4},{3,5},{4,6},{5,7},{6,8},{7,9},{8,10},{9,11},{10,... | collective-permute-start | bytes 786440 | tf_op jit(solution)/shard_map/ppermute | solution.py:25
  92.3 13.8 %copy-start.7 = (f32[384,512]{1,0:T(8,128)S(1)}, f32[384,512]{1,0:T(8,128)}, u32[]{:S(2)}) copy-start(f32[384,512]{1,0:T(8,128)} %param.16) | copy-start | bytes 2359300
  92.4 13.8 %copy-start.10 = (f32[1,384,512]{2,1,0:T(8,128)S(1)}, f32[1,384,512]{2,1,0:T(8,128)}, u32[]{:S(2)}) copy-start(f32[1,384,512]{2,1,0:T(8,128)} %param.14) | copy-start | bytes 2359300
  92.4 15.3 %collective-permute-start.15 = (bf16[128,1024]{1,0:T(8,128)(2,1)}, bf16[128,1024]{1,0:T(8,128)(2,1)}, u32[]{:S(2)}, u32[]{:S(2)}) collective-permute-start(bf16[128,1024]{1,0:T(8,128)(2,1)} %get-tuple-element.21), channel_id=1, source_target_pairs={{0,14},{1,15},{2,0},{3,1},{4,2},{5,3},{6,4},{7,5},{8,6},{9,7},{10,... | collective-permute-start | bytes 786440 | tf_op jit(solution)/shard_map/ppermute | solution.py:26
  107.7 5.5 %collective-permute-start.7 = (bf16[384,512]{1,0:T(8,128)(2,1)S(1)}, bf16[384,512]{1,0:T(8,128)(2,1)S(1)}, u32[]{:S(2)}, u32[]{:S(2)}) collective-permute-start(bf16[384,512]{1,0:T(8,128)(2,1)S(1)} %get-tuple-element.25), channel_id=1, source_target_pairs={{0,64},{64,0},{128,192},{192,128},{1,65},{65,1},{129,193},{193,129... | collective-permute-start | bytes 1179656 | tf_op jit(solution)/shard_map/ppermute | solution.py:155
  107.7 35.0 %copy-start.11 = (f32[384,512]{1,0:T(8,128)S(1)}, f32[384,512]{1,0:T(8,128)}, u32[]{:S(2)}) copy-start(f32[384,512]{1,0:T(8,128)} %param.17) | copy-start | bytes 2359300
  109.9 13.3 %collective-permute-start.12 = (bf16[128,1024]{1,0:T(8,128)(2,1)}, bf16[128,1024]{1,0:T(8,128)(2,1)S(1)}, u32[]{:S(2)}, u32[]{:S(2)}) collective-permute-start(bf16[128,1024]{1,0:T(8,128)(2,1)} %get-tuple-element.18), channel_id=1, source_target_pairs={{0,2},{1,3},{2,4},{3,5},{4,6},{5,7},{6,8},{7,9},{8,10},{9,11},{10,... | collective-permute-start | bytes 786440 | tf_op jit(solution)/shard_map/ppermute | solution.py:25
  109.9 13.3 %collective-permute-start.16 = (bf16[128,1024]{1,0:T(8,128)(2,1)}, bf16[128,1024]{1,0:T(8,128)(2,1)}, u32[]{:S(2)}, u32[]{:S(2)}) collective-permute-start(bf16[128,1024]{1,0:T(8,128)(2,1)} %get-tuple-element.19), channel_id=1, source_target_pairs={{0,14},{1,15},{2,0},{3,1},{4,2},{5,3},{6,4},{7,5},{8,6},{9,7},{10,... | collective-permute-start | bytes 786440 | tf_op jit(solution)/shard_map/ppermute | solution.py:26
  113.3 29.4 %collective-permute-start.8 = (bf16[384,512]{1,0:T(8,128)(2,1)S(1)}, bf16[384,512]{1,0:T(8,128)(2,1)S(1)}, u32[]{:S(2)}, u32[]{:S(2)}) collective-permute-start(bf16[384,512]{1,0:T(8,128)(2,1)S(1)} %add_convert_fusion), channel_id=1, source_target_pairs={{0,128},{64,192},{128,0},{192,64},{1,129},{65,193},{129,1},{193,65... | collective-permute-start | bytes 1179656 | tf_op jit(solution)/shard_map/ppermute | solution.py:155
  124.4 18.2 %collective-permute-start.17 = (bf16[64,1024]{1,0:T(8,128)(2,1)S(1)}, bf16[64,1024]{1,0:T(8,128)(2,1)S(1)}, u32[]{:S(2)}, u32[]{:S(2)}) collective-permute-start(bf16[64,1024]{1,0:T(8,128)(2,1)S(1)} %dynamic-slice_convert_fusion.3), channel_id=1, source_target_pairs={{0,1},{1,0},{2,3},{3,2},{4,5},{5,4},{6,7},{7,6},{8,9},{9,8},{10,11... | collective-permute-start | bytes 393224 | tf_op jit(solution)/shard_map/ppermute | solution.py:58
Sparse Core Ops, SparseCore 0:
  65.3 79.7 reduce-scatter.1

commit v6 on v5

--- a/solution.py
+++ b/solution.py
@@ -11,7 +11,7 @@
     return [(i, (i + s) % n) for i in range(n)]
 
 
-def _z_reduce_scatter(chunks, z, nz, up, down):
+def _z_reduce_scatter(chunks, z, nz, up, down, sync=None, sync_round=3):
     far = nz // 2
     halfc = chunks.shape[2] // 2
 
@@ -22,6 +22,8 @@
     send_a = first[:, :halfc]
     send_b = first[:, halfc:]
     for r in range(2, far + 2):
+        if sync is not None and r == sync_round + 1:
+            send_a, send_b, sync = lax.optimization_barrier((send_a, send_b, sync))
         got_a = lax.ppermute(send_a.astype(jnp.bfloat16), "mp", up).astype(jnp.float32)
         got_b = lax.ppermute(send_b.astype(jnp.bfloat16), "mp", down).astype(jnp.float32)
         own_a = chunk(z + far + 1 - r)
@@ -32,7 +34,8 @@
         if r <= far:
             send_a = got_a + own_a
             send_b = got_b + own_b
-    return own_a + got_a + got_b
+    out = own_a + got_a + got_b
+    return out if sync is None else (out, sync)
 
 
 def _ring_reduce_scatter(part_z, part_y):
@@ -49,16 +52,21 @@
     down = [(i, ((i // nlo - 1) % nz) * nlo + i % nlo) for i in range(nmp)]
     pair = [(i, i ^ 1) for i in range(nmp)]
 
-    out_y = lax.psum_scatter(part_y, "mp", scatter_dimension=0, tiled=True)
+    py = part_y.reshape(nz, nlo, sub, halfc)
+    keep = lax.dynamic_index_in_dim(py, lo, axis=1, keepdims=False)
+    give = lax.dynamic_index_in_dim(py, 1 - lo, axis=1, keepdims=False)
+    got_y = lax.ppermute(give, "mp", pair)
 
     pz = part_z.reshape(nz, rows, halfc)
-    acc_z = _z_reduce_scatter(pz, z, nz, up, down)
+    acc_z, got_y = _z_reduce_scatter(pz, z, nz, up, down, sync=got_y)
+    acc_y = keep.astype(jnp.float32) + got_y.astype(jnp.float32)
     mine = lax.dynamic_slice_in_dim(acc_z, lo * sub, sub, axis=0)
     other = lax.dynamic_slice_in_dim(acc_z, (1 - lo) * sub, sub, axis=0)
     got = lax.ppermute(other.astype(jnp.bfloat16), "mp", pair)
     out_z = mine + got.astype(jnp.float32)
 
-    return jnp.concatenate([out_z.astype(jnp.bfloat16), out_y], axis=1)
+    out_y = _z_reduce_scatter(acc_y.astype(jnp.bfloat16), z, nz, up, down)
+    return jnp.concatenate([out_z, out_y], axis=1).astype(jnp.bfloat16)
 
 
 def shards(

time: 156 us -> 131 us (0.84); the launches traced: 154 us -> 130 us
  waiting for transfers between devices: 64 us -> 44 us
  starting transfers between devices: 30 us -> 45.1 us
  between operations: 14.4 us -> 1.07 us
  matrix products: 19.4 us -> 15.4 us
    ppermute x1, waiting for transfers between devices: 18.1 us -> 3.15 us  [_ring_reduce_scatter(): got = lax.ppermute(other.astype(jnp.bfloat16), 'mp', pair)]
    ppermute x4 -> x8, starting transfers between devices: 15.6 us -> 27.8 us  [_z_reduce_scatter(): lax.ppermute(send_b.astype(jnp.bfloat16), 'mp', down).astype(jnp.float32)]
    ppermute x0 -> x1, waiting for transfers between devices: none -> 8.07 us  [_ring_reduce_scatter(): got_y = lax.ppermute(give, 'mp', pair)]
    ppermute x3, waiting for transfers between devices: 8.07 us -> 0.01 us  [shards(): got = lax.ppermute(blk.astype(jnp.bfloat16), 'dp', _shift(ndp, s))]
    ppermute x4 -> x8, waiting for transfers between devices: 11.2 us -> 6.33 us  [_z_reduce_scatter(): lax.ppermute(send_a.astype(jnp.bfloat16), 'mp', up).astype(jnp.float32)]
    convert_element_type x3 -> x4, other arithmetic: 4.46 us -> 1.39 us  [_z_reduce_scatter(): send_a.astype(jnp.bfloat16)]
    convert_element_type x1 -> x2, other arithmetic: 0.03 us -> 2.73 us  [the longest x1 1.63 us: _ring_reduce_scatter(): out_y = _z_reduce_scatter(acc_y.astype(jnp.bfloat16), z, nz, up, down)]
    unnamed x28 -> x24, local copies, waits for them, and re-layouts: 7.58 us -> 5.31 us
  transfers between devices with their start and end apart: 19 -> 27, of which waited for: 9 -> 9; matrix products, arithmetic and copies ran while one was open for 19% -> 18% of each run, Pallas kernels for 0% -> 0%
where the time goes in v6:
time: 131 us; the launch traced here: 130 us
  starting transfers between devices  45.1 us (34%)
  waiting for transfers between devices  44 us (34%)
  matrix products  15.4 us (12%)
  other arithmetic  14.3 us (11%)
  local copies, waits for them, and re-layouts  10.5 us (8%)
    ppermute x8, starting transfers between devices, _z_reduce_scatter(): lax.ppermute(send_b.astype(jnp.bfloat16), 'mp', down).astype(jnp.float32)  27.8 us
    ppermute x1, waiting for transfers between devices, shards(): from_left = lax.ppermute(shard, 'dp', _shift(ndp, 1))  20.9 us
    ppermute x1, waiting for transfers between devices, _ring_reduce_scatter(): got_y = lax.ppermute(give, 'mp', pair)  8.07 us
    ppermute x8, waiting for transfers between devices, _z_reduce_scatter(): lax.ppermute(send_a.astype(jnp.bfloat16), 'mp', up).astype(jnp.float32)  6.33 us
    dot_general x5, matrix products, shards(): p1 = jnp.dot(xs, piece[:, :2 * ff], preferred_element_type=jnp.float32)  5.58 us
    unnamed x24, local copies, waits for them, and re-layouts  5.31 us
    ppermute x3, starting transfers between devices, shards(): got = lax.ppermute(blk.astype(jnp.bfloat16), 'dp', _shift(ndp, s))  5.18 us
    dot_general x5, matrix products, shards(): p2 = jnp.dot(gs, piece[:, 2 * ff:], preferred_element_type=jnp.float32)  4.26 us
  transfers between devices with their start and end apart: 27, of which 9 were waited for; matrix products, arithmetic and copies ran while one was open for 18% of the time, Pallas kernels for 0%

profile of v6, /device:TPU:8, one launch (start us, length us, event | category | flops | bytes accessed | tf_op | source)
XLA Modules:
  0.0 130.3 jit_solution(3511243578081321126)
XLA Ops:
  0.6 1.2 copy.14
  1.9 1.2 copy.15
  3.1 1.1 pad_maximum_fusion.1
  4.3 1.5 %collective-permute-start = (bf16[512,1152]{0,1:T(8,128)(2,1)}, bf16[512,1152]{0,1:T(8,128)(2,1)S(1)}, u32[]{:S(2)}, u32[]{:S(2)}) collective-permute-start(bf16[512,1152]{0,1:T(8,128)(2,1)} %pad_maximum_fusion.1), channel_id=1, source_target_pairs={{0,16},{16,32},{32,48},{48,0},{1,17},{17,33},{33,49},{49,1},{2,18}... | collective-permute-start | bytes 3538952 | tf_op jit(solution)/shard_map/ppermute | solution.py:95
  5.8 1.7 %collective-permute-start.1 = (bf16[512,1152]{0,1:T(8,128)(2,1)}, bf16[512,1152]{0,1:T(8,128)(2,1)}, u32[]{:S(2)}, u32[]{:S(2)}) collective-permute-start(bf16[512,1152]{0,1:T(8,128)(2,1)} %pad_maximum_fusion.1), channel_id=1, source_target_pairs={{0,48},{16,0},{32,16},{48,32},{1,49},{17,1},{33,17},{49,33},{2,50}... | collective-permute-start | bytes 3538952 | tf_op jit(solution)/shard_map/ppermute | solution.py:96
  7.5 0.4 broadcast_in_dim.12
  7.9 0.1 fusion.52
  8.0 1.7 %copy-done.10 = bf16[1,1024,2048]{2,1,0:T(8,128)(2,1)S(1)} copy-done((bf16[1,1024,2048]{2,1,0:T(8,128)(2,1)S(1)}, bf16[1,1024,2048]{2,1,0:T(8,128)(2,1)}, u32[]{:S(2)}) %copy-start.10) | copy-done | bytes 4194328
  9.7 1.0 fusion.16
  10.7 1.2 copy-done.1
  11.9 0.6 fusion.10
  12.5 20.9 %collective-permute-done = bf16[512,1152]{0,1:T(8,128)(2,1)S(1)} collective-permute-done((bf16[512,1152]{0,1:T(8,128)(2,1)}, bf16[512,1152]{0,1:T(8,128)(2,1)S(1)}, u32[]{:S(2)}, u32[]{:S(2)}) %collective-permute-start) | collective-permute-done | bytes 1179680 | tf_op jit(solution)/shard_map/ppermute | solution.py:95
  33.4 0.4 collective-permute-start.2
  33.8 1.1 slice.87
  34.9 3.2 %collective-permute-start.3 = (bf16[256,1152]{0,1:T(8,128)(2,1)S(1)}, bf16[256,1152]{0,1:T(8,128)(2,1)S(1)}, u32[]{:S(2)}, u32[]{:S(2)}) collective-permute-start(bf16[256,1152]{0,1:T(8,128)(2,1)S(1)} %slice.87), channel_id=1, source_target_pairs={{0,48},{16,0},{32,16},{48,32},{1,49},{17,1},{33,17},{49,33},{2,50}... | collective-permute-start | bytes 1769480 | tf_op jit(solution)/shard_map/ppermute | solution.py:98
  38.1 2.1 %fusion.12 = f32[1024,768]{0,1:T(8,128)S(1)} fusion(bf16[1,1024,2048]{2,1,0:T(8,128)(2,1)S(1)} %copy-done.10, s32[]{:T(128)S(6)} %select_n.163, bf16[512,1152]{0,1:T(8,128)(2,1)} %collective-permute-done.1), kind=kOutput, calls=%fused_computation.24 | convolution fusion | flops 805306368 | bytes 4980740 | tf_op jit(solution)/shard_map/dot_general | solution.py:114
  40.3 1.6 %fusion.6 = f32[1024,384]{0,1:T(8,128)S(1)} fusion(bf16[1,1024,2048]{2,1,0:T(8,128)(2,1)S(1)} %copy-done.1, s32[]{:T(128)S(6)} %select_n.163, bf16[512,1152]{0,1:T(8,128)(2,1)} %collective-permute-done.1), kind=kOutput, calls=%fused_computation.18 | convolution fusion | flops 402653184 | bytes 3014660 | tf_op jit(solution)/shard_map/dot_general | solution.py:115
  41.9 1.0 fusion.14
  42.9 0.1 slice_dynamic-update-slice_fusion.1
  43.0 1.2 slice_dynamic-update-slice_fusion
  44.3 0.6 fusion.8
  44.9 4.0 %collective-permute-done.2 = bf16[256,1152]{0,1:T(8,128)(2,1)S(1)} collective-permute-done((bf16[256,1152]{0,1:T(8,128)(2,1)S(1)}, bf16[256,1152]{0,1:T(8,128)(2,1)S(1)}, u32[]{:S(2)}, u32[]{:S(2)}) %collective-permute-start.2) | collective-permute-done | bytes 589856 | tf_op jit(solution)/shard_map/ppermute | solution.py:97
  48.9 0.6 fusion.46
  49.6 0.8 add_add_fusion
  50.4 1.8 %fusion = f32[384,2048]{1,0:T(8,128)S(1)} fusion(bf16[1,1024,2048]{2,1,0:T(8,128)(2,1)S(1)} %copy-done.1, f32[1024,768]{0,1:T(8,128)S(1)} %add_add_fusion), kind=kOutput, calls=%fused_computation | convolution fusion | flops 1612972032 | bytes 10485760 | tf_op jit(solution)/shard_map/dot_general | solution.py:130
  52.2 0.4 fusion.40
  52.6 1.0 multiply_convert_fusion.1
  53.7 0.1 pad_maximum_fusion
  53.9 1.8 %convolution_convert_fusion.1 = bf16[1024,1024]{1,0:T(8,128)(2,1)S(1)} fusion(bf16[2048,768]{0,1:T(8,128)(2,1)S(1)} %slice_dynamic-update-slice_fusion.2, bf16[1024,384]{0,1:T(8,128)(2,1)S(1)} %get-tuple-element.20, bf16[1024,384]{0,1:T(8,128)(2,1)S(1)} %get-tuple-element.19), kind=kOutput, calls=%fused_computation.6 | convolution fusion | flops 1614807040 | bytes 5242880 | tf_op jit(solution)/shard_map/dot_general | solution.py:142
  55.8 1.8 %convolution_convert_fusion = bf16[1024,1024]{1,0:T(8,128)(2,1)S(1)} fusion(bf16[1024,768]{0,1:T(8,128)(2,1)S(1)} %pad_maximum_fusion, bf16[2048,768]{0,1:T(8,128)(2,1)S(1)} %slice_dynamic-update-slice_fusion.2), kind=kOutput, calls=%fused_computation.5 | convolution fusion | flops 1611661312 | bytes 5242880 | tf_op jit(solution)/shard_map/dot_general | solution.py:146
  57.6 1.1 dynamic-slice_convert_fusion.2
  58.7 1.1 collective-permute-start.4
  59.9 4.0 %collective-permute-start.5 = (bf16[384,512]{1,0:T(8,128)(2,1)}, bf16[384,512]{1,0:T(8,128)(2,1)}, u32[]{:S(2)}, u32[]{:S(2)}) collective-permute-start(bf16[384,512]{1,0:T(8,128)(2,1)} %get-tuple-element.23), channel_id=1, source_target_pairs={{0,32},{16,48},{32,0},{48,16},{1,33},{17,49},{33,1},{49,17},{2,34}... | collective-permute-start | bytes 1179656 | tf_op jit(solution)/shard_map/ppermute | solution.py:137
  63.9 5.9 %collective-permute-start.11 = (bf16[128,512]{1,0:T(8,128)(2,1)S(1)}, bf16[128,512]{1,0:T(8,128)(2,1)S(1)}, u32[]{:S(2)}, u32[]{:S(2)}) collective-permute-start(bf16[128,512]{1,0:T(8,128)(2,1)S(1)} %get-tuple-element.38), channel_id=1, source_target_pairs={{0,14},{1,15},{2,0},{3,1},{4,2},{5,3},{6,4},{7,5},{8,6},{9,7},{10,... | collective-permute-start | bytes 393224 | tf_op jit(solution)/shard_map/ppermute | solution.py:28
  69.9 1.1 dynamic-slice_bitcast_fusion
  71.0 1.4 %collective-permute-done.11 = bf16[128,512]{1,0:T(8,128)(2,1)S(1)} collective-permute-done((bf16[128,512]{1,0:T(8,128)(2,1)S(1)}, bf16[128,512]{1,0:T(8,128)(2,1)S(1)}, u32[]{:S(2)}, u32[]{:S(2)}) %collective-permute-start.11) | collective-permute-done | bytes 131104 | tf_op jit(solution)/shard_map/ppermute | solution.py:28
  72.4 0.4 collective-permute-start.13
  72.8 3.2 %collective-permute-done.9 = bf16[128,512]{1,0:T(8,128)(2,1)S(1)} collective-permute-done((bf16[128,512]{1,0:T(8,128)(2,1)S(1)}, bf16[128,512]{1,0:T(8,128)(2,1)S(1)}, u32[]{:S(2)}, u32[]{:S(2)}) %collective-permute-start.9) | collective-permute-done | bytes 131104 | tf_op jit(solution)/shard_map/ppermute | solution.py:27
  76.1 1.1 fusion.33
  77.3 3.2 %collective-permute-start.12 = (bf16[128,1024]{1,0:T(8,128)(2,1)S(1)}, bf16[128,1024]{1,0:T(8,128)(2,1)S(1)}, u32[]{:S(2)}, u32[]{:S(2)}) collective-permute-start(bf16[128,1024]{1,0:T(8,128)(2,1)S(1)} %get-tuple-element.28), channel_id=1, source_target_pairs={{0,14},{1,15},{2,0},{3,1},{4,2},{5,3},{6,4},{7,5},{8,6},{9,7},{10,... | collective-permute-start | bytes 786440 | tf_op jit(solution)/shard_map/ppermute | solution.py:28
  80.5 2.6 %fusion.69 = (f32[1,384,512]{2,1,0:T(8,128)}, f32[384,512]{1,0:T(8,128)S(1)}) fusion(f32[1,384,512]{2,1,0:T(8,128)S(1)} %copy-done.2, bf16[384,512]{1,0:T(8,128)(2,1)} %collective-permute-done.6, bf16[384,512]{1,0:T(8,128)(2,1)} %collective-permute-done.5, bf16[384,512]{1,0:T(8,128)(2,1)S(1)} %collective-permute-done.4, f32[384,2048]{1,0:T(8,128)} %copy-done.7, ...), kind=kLoop, calls=%fused_computation.113 | loop fusion | flops 1966080 | bytes 4325380 | tf_op jit(solution)/shard_map/broadcast_in_dim | solution.py:168
  83.1 1.5 %fusion.68 = (f32[1,384,512]{2,1,0:T(8,128)}, bf16[384,512]{1,0:T(8,128)(2,1)S(1)}) fusion(f32[384,512]{1,0:T(8,128)S(1)} %get-tuple-element.16, f32[1,384,512]{2,1,0:T(8,128)S(1)} %copy-done.8, f32[384,512]{1,0:T(8,128)S(1)} %copy-done.3, f32[1,384,512]{2,1,0:T(8,128)S(1)} %copy-done.2, f32[1,384,512]{2,1,0:T(8,128)S(1)} %copy-done), kind=kLoop, calls=%fused_computation.112 | loop fusion | flops 3342336 | bytes 5111808 | tf_op jit(solution)/shard_map/broadcast_in_dim | solution.py:168
  84.6 0.2 collective-permute-done.10
  84.8 1.2 convert_add_fusion.4
  86.1 8.1 %collective-permute-done.13 = bf16[8,64,1024]{2,1,0:T(8,128)(2,1)} collective-permute-done((bf16[8,64,1024]{2,1,0:T(8,128)(2,1)}, bf16[8,64,1024]{2,1,0:T(8,128)(2,1)}, u32[]{:S(2)}, u32[]{:S(2)}) %collective-permute-start.13) | collective-permute-done | bytes 1048608 | tf_op jit(solution)/shard_map/ppermute | solution.py:58
  94.1 1.6 %fusion.2 = bf16[8,64,1024]{2,1,0:T(8,128)(2,1)S(1)} fusion(bf16[8,64,1024]{2,1,0:T(8,128)(2,1)} %collective-permute-done.13, bf16[8,2,64,1024]{3,2,1,0:T(8,128)(2,1)S(1)} %bitcast.145, s32[]{:T(128)S(6)} %select_n.190), kind=kLoop, calls=%fused_computation.4 | loop fusion | flops 2097152 | bytes 3145732 | tf_op jit(solution)/shard_map/convert_element_type | solution.py:68
  95.8 0.1 collective-permute-start.19
  95.9 3.7 %collective-permute-start.23 = (bf16[64,512]{1,0:T(8,128)(2,1)S(1)}, bf16[64,512]{1,0:T(8,128)(2,1)S(1)}, u32[]{:S(2)}, u32[]{:S(2)}) collective-permute-start(bf16[64,512]{1,0:T(8,128)(2,1)S(1)} %get-tuple-element.41), channel_id=1, source_target_pairs={{0,14},{1,15},{2,0},{3,1},{4,2},{5,3},{6,4},{7,5},{8,6},{9,7},{10,... | collective-permute-start | bytes 196616 | tf_op jit(solution)/shard_map/ppermute | solution.py:28
  99.6 3.2 %collective-permute-start.16 = (bf16[128,1024]{1,0:T(8,128)(2,1)S(1)}, bf16[128,1024]{1,0:T(8,128)(2,1)S(1)}, u32[]{:S(2)}, u32[]{:S(2)}) collective-permute-start(bf16[128,1024]{1,0:T(8,128)(2,1)S(1)} %get-tuple-element.13), channel_id=1, source_target_pairs={{0,14},{1,15},{2,0},{3,1},{4,2},{5,3},{6,4},{7,5},{8,6},{9,7},{10,... | collective-permute-start | bytes 786440 | tf_op jit(solution)/shard_map/ppermute | solution.py:28
  103.0 3.2 %collective-permute-start.24 = (bf16[64,1024]{1,0:T(8,128)(2,1)S(1)}, bf16[64,1024]{1,0:T(8,128)(2,1)S(1)}, u32[]{:S(2)}, u32[]{:S(2)}) collective-permute-start(bf16[64,1024]{1,0:T(8,128)(2,1)S(1)} %get-tuple-element.37), channel_id=1, source_target_pairs={{0,14},{1,15},{2,0},{3,1},{4,2},{5,3},{6,4},{7,5},{8,6},{9,7},{10,... | collective-permute-start | bytes 393224 | tf_op jit(solution)/shard_map/ppermute | solution.py:28
  106.2 0.1 add_convert_fusion
  106.3 2.4 %collective-permute-start.8 = (bf16[384,512]{1,0:T(8,128)(2,1)S(1)}, bf16[384,512]{1,0:T(8,128)(2,1)S(1)}, u32[]{:S(2)}, u32[]{:S(2)}) collective-permute-start(bf16[384,512]{1,0:T(8,128)(2,1)S(1)} %add_convert_fusion), channel_id=1, source_target_pairs={{0,128},{64,192},{128,0},{192,64},{1,129},{65,193},{129,1},{193,65... | collective-permute-start | bytes 1179656 | tf_op jit(solution)/shard_map/ppermute | solution.py:163
  108.7 1.6 %collective-permute-done.20 = bf16[64,1024]{1,0:T(8,128)(2,1)S(1)} collective-permute-done((bf16[64,1024]{1,0:T(8,128)(2,1)S(1)}, bf16[64,1024]{1,0:T(8,128)(2,1)S(1)}, u32[]{:S(2)}, u32[]{:S(2)}) %collective-permute-start.20) | collective-permute-done | bytes 131104 | tf_op jit(solution)/shard_map/ppermute | solution.py:27
  110.4 1.5 %collective-permute-start.21 = (bf16[64,1024]{1,0:T(8,128)(2,1)S(1)}, bf16[64,1024]{1,0:T(8,128)(2,1)S(1)}, u32[]{:S(2)}, u32[]{:S(2)}) collective-permute-start(bf16[64,1024]{1,0:T(8,128)(2,1)S(1)} %get-tuple-element.34), channel_id=1, source_target_pairs={{0,2},{1,3},{2,4},{3,5},{4,6},{5,7},{6,8},{7,9},{8,10},{9,11},{10,... | collective-permute-start | bytes 393224 | tf_op jit(solution)/shard_map/ppermute | solution.py:27
  111.9 2.1 %collective-permute-start.25 = (bf16[64,1024]{1,0:T(8,128)(2,1)S(1)}, bf16[64,1024]{1,0:T(8,128)(2,1)S(1)}, u32[]{:S(2)}, u32[]{:S(2)}) collective-permute-start(bf16[64,1024]{1,0:T(8,128)(2,1)S(1)} %get-tuple-element.35), channel_id=1, source_target_pairs={{0,14},{1,15},{2,0},{3,1},{4,2},{5,3},{6,4},{7,5},{8,6},{9,7},{10,... | collective-permute-start | bytes 393224 | tf_op jit(solution)/shard_map/ppermute | solution.py:28
  114.0 1.2 fusion.32
  115.3 3.2 %collective-permute-start.17 = (bf16[128,1024]{1,0:T(8,128)(2,1)S(1)}, bf16[128,1024]{1,0:T(8,128)(2,1)S(1)}, u32[]{:S(2)}, u32[]{:S(2)}) collective-permute-start(bf16[128,1024]{1,0:T(8,128)(2,1)S(1)} %get-tuple-element.25), channel_id=1, source_target_pairs={{0,14},{1,15},{2,0},{3,1},{4,2},{5,3},{6,4},{7,5},{8,6},{9,7},{10,... | collective-permute-start | bytes 786440 | tf_op jit(solution)/shard_map/ppermute | solution.py:28
  118.6 1.4 %multiply_subtract_fusion = (f32[384,512]{1,0:T(8,128)}, f32[384,512]{1,0:T(8,128)}) fusion(f32[384,512]{1,0:T(8,128)S(1)} %copy-done.3, bf16[384,512]{1,0:T(8,128)(2,1)S(1)} %collective-permute-done.8, bf16[384,512]{1,0:T(8,128)(2,1)S(1)} %add_convert_fusion, f32[384,512]{1,0:T(8,128)S(1)} %copy-done.9), kind=kLoop, calls=%fused_computation.47 | loop fusion | flops 1966080 | bytes 3932160 | tf_op jit(solution)/shard_map/sub | solution.py:167
  120.2 3.2 %collective-permute-start.26 = (bf16[64,1024]{1,0:T(8,128)(2,1)S(1)}, bf16[64,1024]{1,0:T(8,128)(2,1)S(1)}, u32[]{:S(2)}, u32[]{:S(2)}) collective-permute-start(bf16[64,1024]{1,0:T(8,128)(2,1)S(1)} %get-tuple-element.33), channel_id=1, source_target_pairs={{0,14},{1,15},{2,0},{3,1},{4,2},{5,3},{6,4},{7,5},{8,6},{9,7},{10,... | collective-permute-start | bytes 393224 | tf_op jit(solution)/shard_map/ppermute | solution.py:28
  123.4 1.1 fusion.35
  124.5 0.6 collective-permute-start.18
  125.1 1.3 collective-permute-done.22
  126.4 3.1 %collective-permute-done.18 = bf16[64,1024]{1,0:T(8,128)(2,1)S(1)} collective-permute-done((bf16[64,1024]{1,0:T(8,128)(2,1)S(1)}, bf16[64,1024]{1,0:T(8,128)(2,1)S(1)}, u32[]{:S(2)}, u32[]{:S(2)}) %collective-permute-start.18) | collective-permute-done | bytes 131104 | tf_op jit(solution)/shard_map/ppermute | solution.py:65
  129.6 0.7 pad_maximum_fusion.4
  (60 shorter events, 1.0 us)
Async XLA Ops:
  0.6 2.4 %copy-start = (f32[1,384,512]{2,1,0:T(8,128)S(1)}, f32[1,384,512]{2,1,0:T(8,128)}, u32[]{:S(2)}) copy-start(f32[1,384,512]{2,1,0:T(8,128)} %param.13) | copy-start | bytes 2359300
  4.3 29.1 %collective-permute-start = (bf16[512,1152]{0,1:T(8,128)(2,1)}, bf16[512,1152]{0,1:T(8,128)(2,1)S(1)}, u32[]{:S(2)}, u32[]{:S(2)}) collective-permute-start(bf16[512,1152]{0,1:T(8,128)(2,1)} %pad_maximum_fusion.1), channel_id=1, source_target_pairs={{0,16},{16,32},{32,48},{48,0},{1,17},{17,33},{33,49},{49,1},{2,18}... | collective-permute-start | bytes 3538952 | tf_op jit(solution)/shard_map/ppermute | solution.py:95
  5.8 28.0 %collective-permute-start.1 = (bf16[512,1152]{0,1:T(8,128)(2,1)}, bf16[512,1152]{0,1:T(8,128)(2,1)}, u32[]{:S(2)}, u32[]{:S(2)}) collective-permute-start(bf16[512,1152]{0,1:T(8,128)(2,1)} %pad_maximum_fusion.1), channel_id=1, source_target_pairs={{0,48},{16,0},{32,16},{48,32},{1,49},{17,1},{33,17},{49,33},{2,50}... | collective-permute-start | bytes 3538952 | tf_op jit(solution)/shard_map/ppermute | solution.py:96
  7.5 2.2 %copy-start.10 = (bf16[1,1024,2048]{2,1,0:T(8,128)(2,1)S(1)}, bf16[1,1024,2048]{2,1,0:T(8,128)(2,1)}, u32[]{:S(2)}) copy-start(bf16[1,1024,2048]{2,1,0:T(8,128)(2,1)} %param.9) | copy-start | bytes 12582916
  9.7 2.2 %copy-start.1 = (bf16[1,1024,2048]{2,1,0:T(8,128)(2,1)S(1)}, bf16[1,1024,2048]{2,1,0:T(8,128)(2,1)}, u32[]{:S(2)}) copy-start(bf16[1,1024,2048]{2,1,0:T(8,128)(2,1)} %param.10) | copy-start | bytes 12582916
  33.4 15.5 %collective-permute-start.2 = (bf16[256,1152]{0,1:T(8,128)(2,1)S(1)}, bf16[256,1152]{0,1:T(8,128)(2,1)S(1)}, u32[]{:S(2)}, u32[]{:S(2)}) collective-permute-start(bf16[256,1152]{0,1:T(8,128)(2,1)S(1)} %slice.85), channel_id=1, source_target_pairs={{0,16},{16,32},{32,48},{48,0},{1,17},{17,33},{33,49},{49,1},{2,18}... | collective-permute-start | bytes 1769480 | tf_op jit(solution)/shard_map/ppermute | solution.py:97
  34.9 14.6 %collective-permute-start.3 = (bf16[256,1152]{0,1:T(8,128)(2,1)S(1)}, bf16[256,1152]{0,1:T(8,128)(2,1)S(1)}, u32[]{:S(2)}, u32[]{:S(2)}) collective-permute-start(bf16[256,1152]{0,1:T(8,128)(2,1)S(1)} %slice.87), channel_id=1, source_target_pairs={{0,48},{16,0},{32,16},{48,32},{1,49},{17,1},{33,17},{49,33},{2,50}... | collective-permute-start | bytes 1769480 | tf_op jit(solution)/shard_map/ppermute | solution.py:98
  52.2 5.4 %copy-start.7 = (f32[384,2048]{1,0:T(8,128)}, f32[384,2048]{1,0:T(8,128)S(1)}, u32[]{:S(2)}) copy-start(f32[384,2048]{1,0:T(8,128)S(1)} %fusion) | copy-start | bytes 9437188
  55.8 14.1 %copy-start.4 = (bf16[1024,1024]{1,0:T(8,128)(2,1)}, bf16[1024,1024]{1,0:T(8,128)(2,1)S(1)}, u32[]{:S(2)}) copy-start(bf16[1024,1024]{1,0:T(8,128)(2,1)S(1)} %convolution_convert_fusion.1) | copy-start | bytes 6291460
  57.6 13.3 %copy-start.6 = (bf16[1024,1024]{1,0:T(8,128)(2,1)}, bf16[1024,1024]{1,0:T(8,128)(2,1)S(1)}, u32[]{:S(2)}) copy-start(bf16[1024,1024]{1,0:T(8,128)(2,1)S(1)} %convolution_convert_fusion) | copy-start | bytes 6291460
  58.7 18.6 %collective-permute-start.4 = (bf16[384,512]{1,0:T(8,128)(2,1)S(1)}, bf16[384,512]{1,0:T(8,128)(2,1)S(1)}, u32[]{:S(2)}, u32[]{:S(2)}) collective-permute-start(bf16[384,512]{1,0:T(8,128)(2,1)S(1)} %get-tuple-element.21), channel_id=1, source_target_pairs={{0,16},{16,32},{32,48},{48,0},{1,17},{17,33},{33,49},{49,1},{2,18}... | collective-permute-start | bytes 1179656 | tf_op jit(solution)/shard_map/ppermute | solution.py:137
  59.9 20.6 %collective-permute-start.5 = (bf16[384,512]{1,0:T(8,128)(2,1)}, bf16[384,512]{1,0:T(8,128)(2,1)}, u32[]{:S(2)}, u32[]{:S(2)}) collective-permute-start(bf16[384,512]{1,0:T(8,128)(2,1)} %get-tuple-element.23), channel_id=1, source_target_pairs={{0,32},{16,48},{32,0},{48,16},{1,33},{17,49},{33,1},{49,17},{2,34}... | collective-permute-start | bytes 1179656 | tf_op jit(solution)/shard_map/ppermute | solution.py:137
  63.9 16.6 %collective-permute-start.6 = (bf16[384,512]{1,0:T(8,128)(2,1)S(1)}, bf16[384,512]{1,0:T(8,128)(2,1)}, u32[]{:S(2)}, u32[]{:S(2)}) collective-permute-start(bf16[384,512]{1,0:T(8,128)(2,1)S(1)} %get-tuple-element.22), channel_id=1, source_target_pairs={{0,48},{16,0},{32,16},{48,32},{1,49},{17,1},{33,17},{49,33},{2,50}... | collective-permute-start | bytes 1179656 | tf_op jit(solution)/shard_map/ppermute | solution.py:137
  63.9 16.6 %copy-start.2 = (f32[1,384,512]{2,1,0:T(8,128)S(1)}, f32[1,384,512]{2,1,0:T(8,128)}, u32[]{:S(2)}) copy-start(f32[1,384,512]{2,1,0:T(8,128)} %param.15) | copy-start | bytes 2359300
  63.9 8.5 %collective-permute-start.11 = (bf16[128,512]{1,0:T(8,128)(2,1)S(1)}, bf16[128,512]{1,0:T(8,128)(2,1)S(1)}, u32[]{:S(2)}, u32[]{:S(2)}) collective-permute-start(bf16[128,512]{1,0:T(8,128)(2,1)S(1)} %get-tuple-element.38), channel_id=1, source_target_pairs={{0,14},{1,15},{2,0},{3,1},{4,2},{5,3},{6,4},{7,5},{8,6},{9,7},{10,... | collective-permute-start | bytes 393224 | tf_op jit(solution)/shard_map/ppermute | solution.py:28
  69.9 6.2 %collective-permute-start.9 = (bf16[128,512]{1,0:T(8,128)(2,1)S(1)}, bf16[128,512]{1,0:T(8,128)(2,1)S(1)}, u32[]{:S(2)}, u32[]{:S(2)}) collective-permute-start(bf16[128,512]{1,0:T(8,128)(2,1)S(1)} %get-tuple-element.39), channel_id=1, source_target_pairs={{0,2},{1,3},{2,4},{3,5},{4,6},{5,7},{6,8},{7,9},{8,10},{9,11},{10,... | collective-permute-start | bytes 393224 | tf_op jit(solution)/shard_map/ppermute | solution.py:27
  72.4 21.7 %collective-permute-start.13 = (bf16[8,64,1024]{2,1,0:T(8,128)(2,1)}, bf16[8,64,1024]{2,1,0:T(8,128)(2,1)}, u32[]{:S(2)}, u32[]{:S(2)}) collective-permute-start(bf16[8,64,1024]{2,1,0:T(8,128)(2,1)} %dynamic-slice_bitcast_fusion), channel_id=1, source_target_pairs={{0,1},{1,0},{2,3},{3,2},{4,5},{5,4},{6,7},{7,6},{8,9},{9,8},{10,11... | collective-permute-start | bytes 3145736 | tf_op jit(solution)/shard_map/ppermute | solution.py:58
  77.2 7.7 %collective-permute-start.10 = (bf16[128,1024]{1,0:T(8,128)(2,1)S(1)}, bf16[128,1024]{1,0:T(8,128)(2,1)S(1)}, u32[]{:S(2)}, u32[]{:S(2)}) collective-permute-start(bf16[128,1024]{1,0:T(8,128)(2,1)S(1)} %get-tuple-element.29), channel_id=1, source_target_pairs={{0,2},{1,3},{2,4},{3,5},{4,6},{5,7},{6,8},{7,9},{8,10},{9,11},{10,... | collective-permute-start | bytes 786440 | tf_op jit(solution)/shard_map/ppermute | solution.py:27
  77.3 5.8 %copy-start.3 = (f32[384,512]{1,0:T(8,128)S(1)}, f32[384,512]{1,0:T(8,128)}, u32[]{:S(2)}) copy-start(f32[384,512]{1,0:T(8,128)} %param.16) | copy-start | bytes 2359300
  77.3 5.8 %copy-start.8 = (f32[1,384,512]{2,1,0:T(8,128)S(1)}, f32[1,384,512]{2,1,0:T(8,128)}, u32[]{:S(2)}) copy-start(f32[1,384,512]{2,1,0:T(8,128)} %param.14) | copy-start | bytes 2359300
  77.3 7.5 %collective-permute-start.12 = (bf16[128,1024]{1,0:T(8,128)(2,1)S(1)}, bf16[128,1024]{1,0:T(8,128)(2,1)S(1)}, u32[]{:S(2)}, u32[]{:S(2)}) collective-permute-start(bf16[128,1024]{1,0:T(8,128)(2,1)S(1)} %get-tuple-element.28), channel_id=1, source_target_pairs={{0,14},{1,15},{2,0},{3,1},{4,2},{5,3},{6,4},{7,5},{8,6},{9,7},{10,... | collective-permute-start | bytes 786440 | tf_op jit(solution)/shard_map/ppermute | solution.py:28
  83.1 11.1 %copy-start.5 = (bf16[1024,1024]{1,0:T(8,128)(2,1)S(1)}, bf16[1024,1024]{1,0:T(8,128)(2,1)}, u32[]{:S(2)}) copy-start(bf16[1024,1024]{1,0:T(8,128)(2,1)} %copy-done.4) | copy-start | bytes 6291460
  84.6 21.6 %collective-permute-start.7 = (bf16[384,512]{1,0:T(8,128)(2,1)S(1)}, bf16[384,512]{1,0:T(8,128)(2,1)S(1)}, u32[]{:S(2)}, u32[]{:S(2)}) collective-permute-start(bf16[384,512]{1,0:T(8,128)(2,1)S(1)} %get-tuple-element.31), channel_id=1, source_target_pairs={{0,64},{64,0},{128,192},{192,128},{1,65},{65,1},{129,193},{193,129... | collective-permute-start | bytes 1179656 | tf_op jit(solution)/shard_map/ppermute | solution.py:163
  95.8 7.1 %collective-permute-start.19 = (bf16[64,512]{1,0:T(8,128)(2,1)S(1)}, bf16[64,512]{1,0:T(8,128)(2,1)S(1)}, u32[]{:S(2)}, u32[]{:S(2)}) collective-permute-start(bf16[64,512]{1,0:T(8,128)(2,1)S(1)} %get-tuple-element.40), channel_id=1, source_target_pairs={{0,2},{1,3},{2,4},{3,5},{4,6},{5,7},{6,8},{7,9},{8,10},{9,11},{10,... | collective-permute-start | bytes 196616 | tf_op jit(solution)/shard_map/ppermute | solution.py:27
  95.9 7.0 %collective-permute-start.23 = (bf16[64,512]{1,0:T(8,128)(2,1)S(1)}, bf16[64,512]{1,0:T(8,128)(2,1)S(1)}, u32[]{:S(2)}, u32[]{:S(2)}) collective-permute-start(bf16[64,512]{1,0:T(8,128)(2,1)S(1)} %get-tuple-element.41), channel_id=1, source_target_pairs={{0,14},{1,15},{2,0},{3,1},{4,2},{5,3},{6,4},{7,5},{8,6},{9,7},{10,... | collective-permute-start | bytes 196616 | tf_op jit(solution)/shard_map/ppermute | solution.py:28
  99.6 18.9 %copy-start.9 = (f32[384,512]{1,0:T(8,128)S(1)}, f32[384,512]{1,0:T(8,128)}, u32[]{:S(2)}) copy-start(f32[384,512]{1,0:T(8,128)} %param.17) | copy-start | bytes 2359300
  99.6 14.4 %collective-permute-start.14 = (bf16[128,1024]{1,0:T(8,128)(2,1)S(1)}, bf16[128,1024]{1,0:T(8,128)(2,1)S(1)}, u32[]{:S(2)}, u32[]{:S(2)}) collective-permute-start(bf16[128,1024]{1,0:T(8,128)(2,1)S(1)} %get-tuple-element.12), channel_id=1, source_target_pairs={{0,2},{1,3},{2,4},{3,5},{4,6},{5,7},{6,8},{7,9},{8,10},{9,11},{10,... | collective-permute-start | bytes 786440 | tf_op jit(solution)/shard_map/ppermute | solution.py:27
  99.6 14.4 %collective-permute-start.16 = (bf16[128,1024]{1,0:T(8,128)(2,1)S(1)}, bf16[128,1024]{1,0:T(8,128)(2,1)S(1)}, u32[]{:S(2)}, u32[]{:S(2)}) collective-permute-start(bf16[128,1024]{1,0:T(8,128)(2,1)S(1)} %get-tuple-element.13), channel_id=1, source_target_pairs={{0,14},{1,15},{2,0},{3,1},{4,2},{5,3},{6,4},{7,5},{8,6},{9,7},{10,... | collective-permute-start | bytes 786440 | tf_op jit(solution)/shard_map/ppermute | solution.py:28
  102.9 7.4 %collective-permute-start.20 = (bf16[64,1024]{1,0:T(8,128)(2,1)S(1)}, bf16[64,1024]{1,0:T(8,128)(2,1)S(1)}, u32[]{:S(2)}, u32[]{:S(2)}) collective-permute-start(bf16[64,1024]{1,0:T(8,128)(2,1)S(1)} %get-tuple-element.36), channel_id=1, source_target_pairs={{0,2},{1,3},{2,4},{3,5},{4,6},{5,7},{6,8},{7,9},{8,10},{9,11},{10,... | collective-permute-start | bytes 393224 | tf_op jit(solution)/shard_map/ppermute | solution.py:27
  103.0 7.3 %collective-permute-start.24 = (bf16[64,1024]{1,0:T(8,128)(2,1)S(1)}, bf16[64,1024]{1,0:T(8,128)(2,1)S(1)}, u32[]{:S(2)}, u32[]{:S(2)}) collective-permute-start(bf16[64,1024]{1,0:T(8,128)(2,1)S(1)} %get-tuple-element.37), channel_id=1, source_target_pairs={{0,14},{1,15},{2,0},{3,1},{4,2},{5,3},{6,4},{7,5},{8,6},{9,7},{10,... | collective-permute-start | bytes 393224 | tf_op jit(solution)/shard_map/ppermute | solution.py:28
  106.3 12.2 %collective-permute-start.8 = (bf16[384,512]{1,0:T(8,128)(2,1)S(1)}, bf16[384,512]{1,0:T(8,128)(2,1)S(1)}, u32[]{:S(2)}, u32[]{:S(2)}) collective-permute-start(bf16[384,512]{1,0:T(8,128)(2,1)S(1)} %add_convert_fusion), channel_id=1, source_target_pairs={{0,128},{64,192},{128,0},{192,64},{1,129},{65,193},{129,1},{193,65... | collective-permute-start | bytes 1179656 | tf_op jit(solution)/shard_map/ppermute | solution.py:163
  110.4 9.6 %collective-permute-start.21 = (bf16[64,1024]{1,0:T(8,128)(2,1)S(1)}, bf16[64,1024]{1,0:T(8,128)(2,1)S(1)}, u32[]{:S(2)}, u32[]{:S(2)}) collective-permute-start(bf16[64,1024]{1,0:T(8,128)(2,1)S(1)} %get-tuple-element.34), channel_id=1, source_target_pairs={{0,2},{1,3},{2,4},{3,5},{4,6},{5,7},{6,8},{7,9},{8,10},{9,11},{10,... | collective-permute-start | bytes 393224 | tf_op jit(solution)/shard_map/ppermute | solution.py:27
  111.9 8.1 %collective-permute-start.25 = (bf16[64,1024]{1,0:T(8,128)(2,1)S(1)}, bf16[64,1024]{1,0:T(8,128)(2,1)S(1)}, u32[]{:S(2)}, u32[]{:S(2)}) collective-permute-start(bf16[64,1024]{1,0:T(8,128)(2,1)S(1)} %get-tuple-element.35), channel_id=1, source_target_pairs={{0,14},{1,15},{2,0},{3,1},{4,2},{5,3},{6,4},{7,5},{8,6},{9,7},{10,... | collective-permute-start | bytes 393224 | tf_op jit(solution)/shard_map/ppermute | solution.py:28
  115.2 8.2 %collective-permute-start.15 = (bf16[128,1024]{1,0:T(8,128)(2,1)S(1)}, bf16[128,1024]{1,0:T(8,128)(2,1)S(1)}, u32[]{:S(2)}, u32[]{:S(2)}) collective-permute-start(bf16[128,1024]{1,0:T(8,128)(2,1)S(1)} %get-tuple-element.24), channel_id=1, source_target_pairs={{0,2},{1,3},{2,4},{3,5},{4,6},{5,7},{6,8},{7,9},{8,10},{9,11},{10,... | collective-permute-start | bytes 786440 | tf_op jit(solution)/shard_map/ppermute | solution.py:27
  115.3 8.1 %collective-permute-start.17 = (bf16[128,1024]{1,0:T(8,128)(2,1)S(1)}, bf16[128,1024]{1,0:T(8,128)(2,1)S(1)}, u32[]{:S(2)}, u32[]{:S(2)}) collective-permute-start(bf16[128,1024]{1,0:T(8,128)(2,1)S(1)} %get-tuple-element.25), channel_id=1, source_target_pairs={{0,14},{1,15},{2,0},{3,1},{4,2},{5,3},{6,4},{7,5},{8,6},{9,7},{10,... | collective-permute-start | bytes 786440 | tf_op jit(solution)/shard_map/ppermute | solution.py:28
  120.1 6.3 %collective-permute-start.22 = (bf16[64,1024]{1,0:T(8,128)(2,1)S(1)}, bf16[64,1024]{1,0:T(8,128)(2,1)S(1)}, u32[]{:S(2)}, u32[]{:S(2)}) collective-permute-start(bf16[64,1024]{1,0:T(8,128)(2,1)S(1)} %get-tuple-element.32), channel_id=1, source_target_pairs={{0,2},{1,3},{2,4},{3,5},{4,6},{5,7},{6,8},{7,9},{8,10},{9,11},{10,... | collective-permute-start | bytes 393224 | tf_op jit(solution)/shard_map/ppermute | solution.py:27
  120.2 6.2 %collective-permute-start.26 = (bf16[64,1024]{1,0:T(8,128)(2,1)S(1)}, bf16[64,1024]{1,0:T(8,128)(2,1)S(1)}, u32[]{:S(2)}, u32[]{:S(2)}) collective-permute-start(bf16[64,1024]{1,0:T(8,128)(2,1)S(1)} %get-tuple-element.33), channel_id=1, source_target_pairs={{0,14},{1,15},{2,0},{3,1},{4,2},{5,3},{6,4},{7,5},{8,6},{9,7},{10,... | collective-permute-start | bytes 393224 | tf_op jit(solution)/shard_map/ppermute | solution.py:28
  124.5 5.1 %collective-permute-start.18 = (bf16[64,1024]{1,0:T(8,128)(2,1)S(1)}, bf16[64,1024]{1,0:T(8,128)(2,1)S(1)}, u32[]{:S(2)}, u32[]{:S(2)}) collective-permute-start(bf16[64,1024]{1,0:T(8,128)(2,1)S(1)} %dynamic-slice_convert_fusion.3), channel_id=1, source_target_pairs={{0,1},{1,0},{2,3},{3,2},{4,5},{5,4},{6,7},{7,6},{8,9},{9,8},{10,11... | collective-permute-start | bytes 393224 | tf_op jit(solution)/shard_map/ppermute | solution.py:65

commit v7 on v3

--- a/solution.py
+++ b/solution.py
@@ -107,15 +107,10 @@
         grad_hidden * up_pre * gate_sigmoid * (1.0 + gate_pre * (1.0 - gate_sigmoid))
     ).astype(jnp.bfloat16)
 
-    full_grad = lax.dot_general(
-        hidden, upstream, (((0,), (0,)), ((), ())), preferred_element_type=jnp.float32
-    )
-    cols = full_grad.shape[1] // ndp
-    grad_down = lax.dynamic_slice_in_dim(full_grad, j * cols, cols, axis=1)
-    for s in range(1, ndp):
-        blk = lax.dynamic_slice_in_dim(full_grad, ((j + s) % ndp) * cols, cols, axis=1)
-        got = lax.ppermute(blk.astype(jnp.bfloat16), "dp", _shift(ndp, s))
-        grad_down = grad_down + got.astype(jnp.float32)
+    full_grad = jnp.dot(hidden.T, upstream, preferred_element_type=jnp.float32)
+    grad_down = lax.psum_scatter(
+        full_grad.astype(jnp.bfloat16), "dp", scatter_dimension=1, tiled=True
+    ).astype(jnp.float32)
 
     both = jnp.concatenate([grad_gate, grad_up], axis=1)
     partial_sum = lax.dot_general(

time: 130 us -> 157 us (1.21)
  between operations: 0.96 us -> 14.2 us
  starting transfers between devices: 30.6 us -> 22.1 us
  waiting for transfers between devices: 56.7 us -> 63.5 us
  other arithmetic: 12 us -> 18 us
  matrix products: 18.5 us -> 24.1 us
  local copies, waits for them, and re-layouts: 11.2 us -> 13.6 us
    ppermute x4, waiting for transfers between devices: 3.9 us -> 25.6 us  [_ring_reduce_scatter(): lax.ppermute(send_b.astype(jnp.bfloat16), 'mp', down).astype(jnp.float32)]
    ppermute x3 -> x0, waiting for transfers between devices: 9.54 us -> none  [shards(): got = lax.ppermute(blk.astype(jnp.bfloat16), 'dp', _shift(ndp, s))]
    ppermute x4, starting transfers between devices: 15.6 us -> 6.95 us  [_ring_reduce_scatter(): lax.ppermute(send_b.astype(jnp.bfloat16), 'mp', down).astype(jnp.float32)]
    dot_general x5, matrix products: 4.26 us -> 11.7 us  [shards(): p2 = jnp.dot(gs, piece[:, 2 * ff:], preferred_element_type=jnp.float32)]
    convert_element_type x3, other arithmetic: 2.12 us -> 7.58 us  [_ring_reduce_scatter(): send_a.astype(jnp.bfloat16)]
    ppermute x3 -> x0, starting transfers between devices: 4.99 us -> none  [shards(): got = lax.ppermute(blk.astype(jnp.bfloat16), 'dp', _shift(ndp, s))]
    ppermute x4, waiting for transfers between devices: 12.5 us -> 7.68 us  [_ring_reduce_scatter(): lax.ppermute(send_a.astype(jnp.bfloat16), 'mp', up).astype(jnp.float32)]
    ppermute x4, starting transfers between devices: 0.25 us -> 5.07 us  [_ring_reduce_scatter(): lax.ppermute(send_a.astype(jnp.bfloat16), 'mp', up).astype(jnp.float32)]
  transfers between devices with their start and end apart: 18 -> 16, of which waited for: 8 -> 12; matrix products, arithmetic and copies ran while one was open for 18% -> 24% of each run, Pallas kernels for 0% -> 0%
where the time goes in v7:
time: 157 us; the launch traced here: 156 us
  waiting for transfers between devices  63.5 us (40%)
  matrix products  24.1 us (15%)
  starting transfers between devices  22.1 us (14%)
  other arithmetic  18 us (11%)
  between operations  14.2 us (9%)
  local copies, waits for them, and re-layouts  13.6 us (9%)
    ppermute x4, waiting for transfers between devices, _ring_reduce_scatter(): lax.ppermute(send_b.astype(jnp.bfloat16), 'mp', down).astype(jnp.float32)  25.6 us
    ppermute x1, waiting for transfers between devices, shards(): from_left = lax.ppermute(shard, 'dp', _shift(ndp, 1))  19.5 us
    dot_general x5, matrix products, shards(): p2 = jnp.dot(gs, piece[:, 2 * ff:], preferred_element_type=jnp.float32)  11.7 us
    unnamed x24, local copies, waits for them, and re-layouts  9.03 us
    ppermute x4, waiting for transfers between devices, _ring_reduce_scatter(): lax.ppermute(send_a.astype(jnp.bfloat16), 'mp', up).astype(jnp.float32)  7.68 us
    convert_element_type x3, other arithmetic, _ring_reduce_scatter(): send_a.astype(jnp.bfloat16)  7.58 us
    ppermute x4, starting transfers between devices, _ring_reduce_scatter(): lax.ppermute(send_b.astype(jnp.bfloat16), 'mp', down).astype(jnp.float32)  6.95 us
    dot_general x5, matrix products, shards(): p1 = jnp.dot(xs, piece[:, :2 * ff], preferred_element_type=jnp.float32)  5.58 us
  transfers between devices with their start and end apart: 16, of which 12 were waited for; matrix products, arithmetic and copies ran while one was open for 24% of the time, Pallas kernels for 0%

profile of v7, /device:TPU:8, one launch (start us, length us, event | category | flops | bytes accessed | tf_op | source)
XLA Modules:
  0.0 155.6 jit_solution(4627201237307177726)
XLA Ops:
  7.2 0.0 reduce-scatter.2.cloned.1.call-start
  7.2 1.2 copy.14
  8.4 1.2 copy.15
  9.6 1.2 fusion.54
  10.7 1.1 pad_maximum_fusion
  11.9 1.5 collective-permute-start
  13.4 1.7 %collective-permute-start.1 = (bf16[512,1152]{0,1:T(8,128)(2,1)}, bf16[512,1152]{0,1:T(8,128)(2,1)S(1)}, u32[]{:S(2)}, u32[]{:S(2)}) collective-permute-start(bf16[512,1152]{0,1:T(8,128)(2,1)} %pad_maximum_fusion), channel_id=1, source_target_pairs={{0,48},{16,0},{32,16},{48,32},{1,49},{17,1},{33,17},{49,33},{2,50}... | collective-permute-start | bytes 3538952 | tf_op jit(solution)/shard_map/ppermute | solution.py:76
  15.1 0.4 broadcast_in_dim.14
  15.5 0.1 fusion.51
  15.6 1.7 %copy-done.10 = bf16[1,1024,2048]{2,1,0:T(8,128)(2,1)S(1)} copy-done((bf16[1,1024,2048]{2,1,0:T(8,128)(2,1)S(1)}, bf16[1,1024,2048]{2,1,0:T(8,128)(2,1)}, u32[]{:S(2)}) %copy-start.10) | copy-done | bytes 4194328
  17.3 1.0 fusion.19
  18.3 0.1 copy-done
  18.4 1.3 copy-done.2
  19.7 1.8 %fusion.13 = f32[1024,384]{0,1:T(8,128)} fusion(bf16[1,1024,2048]{2,1,0:T(8,128)(2,1)S(1)} %copy-done.2, s32[]{:T(128)S(6)} %select_n.112, f32[1,384,512]{2,1,0:T(8,128)S(1)} %copy-done), kind=kOutput, calls=%fused_computation.20 | convolution fusion | flops 402849792 | bytes 3407876 | tf_op jit(solution)/shard_map/dot_general | solution.py:95
  21.6 19.5 %collective-permute-done = bf16[512,1152]{0,1:T(8,128)(2,1)} collective-permute-done((bf16[512,1152]{0,1:T(8,128)(2,1)}, bf16[512,1152]{0,1:T(8,128)(2,1)}, u32[]{:S(2)}, u32[]{:S(2)}) %collective-permute-start) | collective-permute-done | bytes 1179680 | tf_op jit(solution)/shard_map/ppermute | solution.py:75
  41.1 1.1 slice.67
  42.2 0.4 collective-permute-start.2
  42.6 3.2 %collective-permute-start.3 = (bf16[256,1152]{0,1:T(8,128)(2,1)S(1)}, bf16[256,1152]{0,1:T(8,128)(2,1)S(1)}, u32[]{:S(2)}, u32[]{:S(2)}) collective-permute-start(bf16[256,1152]{0,1:T(8,128)(2,1)S(1)} %slice.69), channel_id=1, source_target_pairs={{0,48},{16,0},{32,16},{48,32},{1,49},{17,1},{33,17},{49,33},{2,50}... | collective-permute-start | bytes 1769480 | tf_op jit(solution)/shard_map/ppermute | solution.py:78
  45.8 2.1 %fusion.17 = f32[1024,768]{0,1:T(8,128)S(1)} fusion(bf16[1,1024,2048]{2,1,0:T(8,128)(2,1)S(1)} %copy-done.10, s32[]{:T(128)S(6)} %select_n.114, bf16[512,1152]{0,1:T(8,128)(2,1)} %collective-permute-done), kind=kOutput, calls=%fused_computation.24 | convolution fusion | flops 805306368 | bytes 4980740 | tf_op jit(solution)/shard_map/dot_general | solution.py:94
  48.0 2.8 %fusion.11 = f32[1024,384]{0,1:T(8,128)} fusion(bf16[1,1024,2048]{2,1,0:T(8,128)(2,1)S(1)} %copy-done.2, s32[]{:T(128)S(6)} %select_n.114, bf16[512,1152]{0,1:T(8,128)(2,1)} %collective-permute-done), kind=kOutput, calls=%fused_computation.18 | convolution fusion | flops 402653184 | bytes 3014660 | tf_op jit(solution)/shard_map/dot_general | solution.py:95
  50.7 1.0 fusion.15
  51.8 1.2 slice_dynamic-update-slice_fusion.1
  53.0 0.1 slice_dynamic-update-slice_fusion
  53.1 2.2 %fusion.9 = f32[1024,384]{0,1:T(8,128)} fusion(bf16[1,1024,2048]{2,1,0:T(8,128)(2,1)S(1)} %copy-done.2, s32[]{:T(128)S(6)} %select_n.116, bf16[512,1152]{0,1:T(8,128)(2,1)S(1)} %collective-permute-done.1), kind=kOutput, calls=%fused_computation.16 | convolution fusion | flops 402653184 | bytes 3014660 | tf_op jit(solution)/shard_map/dot_general | solution.py:95
  55.3 2.4 %collective-permute-done.2 = bf16[256,1152]{0,1:T(8,128)(2,1)S(1)} collective-permute-done((bf16[256,1152]{0,1:T(8,128)(2,1)S(1)}, bf16[256,1152]{0,1:T(8,128)(2,1)S(1)}, u32[]{:S(2)}, u32[]{:S(2)}) %collective-permute-start.2) | collective-permute-done | bytes 589856 | tf_op jit(solution)/shard_map/ppermute | solution.py:77
  57.7 0.6 fusion.45
  58.3 0.0 collective-permute-done.3
  58.3 0.8 add_add_fusion
  59.1 1.6 %copy-done.3 = f32[1024,768]{0,1:T(8,128)} copy-done((f32[1024,768]{0,1:T(8,128)}, f32[1024,768]{0,1:T(8,128)S(1)}, u32[]{:S(2)}) %copy-start.3) | copy-done | bytes 3145752
  60.8 3.0 %fusion.2 = bf16[384,2048]{1,0:T(8,128)(2,1)} fusion(bf16[1,1024,2048]{2,1,0:T(8,128)(2,1)S(1)} %copy-done.2, f32[1024,768]{0,1:T(8,128)S(1)} %add_add_fusion), kind=kOutput, calls=%fused_computation.4 | convolution fusion | flops 1613758464 | bytes 8912896 | tf_op jit(solution)/shard_map/dot_general | solution.py:110
  63.7 0.0 reduce-scatter.2.cloned.1.call-update
  63.8 1.6 %fusion.39 = f32[1024,384]{0,1:T(8,128)S(1)} fusion(bf16[1,1024,2048]{2,1,0:T(8,128)(2,1)} %param.10, s32[]{:T(128)S(6)} %select_n.118, bf16[256,1152]{0,1:T(8,128)(2,1)S(1)} %collective-permute-done.2), kind=kOutput, calls=%fused_computation.62 | convolution fusion | flops 201326592 | bytes 2293764 | tf_op jit(solution)/shard_map/dot_general | solution.py:95
  65.4 0.8 slice_dynamic-update-slice_fusion.3
  66.2 0.8 slice_dynamic-update-slice_fusion.2
  67.0 3.4 %multiply_convert_fusion.1 = (bf16[1024,384]{0,1:T(8,128)(2,1)S(1)}, bf16[1024,384]{0,1:T(8,128)(2,1)S(1)}) fusion(f32[1024,768]{0,1:T(8,128)S(1)} %copy-done.4, bf16[256,1152]{0,1:T(8,128)(2,1)S(1)} %collective-permute-done.3, bf16[1,1024,2048]{2,1,0:T(8,128)(2,1)} %param.10, s32[]{:T(128)S(6)} %select_n.119, f32[1024,384]{0,1:T(8,128)S(1)} %fusion.39, ...), kind=kOutput, calls=%fused_computation.9 | convolution fusion | flops 208011264 | bytes 11730948 | tf_op jit(solution)/shard_map/dot_general | solution.py:95
  70.4 3.8 %convolution_convert_fusion = bf16[1024,2048]{1,0:T(8,128)(2,1)S(1)} fusion(bf16[2048,768]{0,1:T(8,128)(2,1)S(1)} %copy-done.6, bf16[1024,384]{0,1:T(8,128)(2,1)S(1)} %get-tuple-element.8, bf16[1024,384]{0,1:T(8,128)(2,1)S(1)} %get-tuple-element.7), kind=kOutput, calls=%fused_computation.2 | convolution fusion | flops 3226468352 | bytes 8912896 | tf_op jit(solution)/shard_map/dot_general | solution.py:116
  74.2 1.9 %copy-done.1 = bf16[1024,2048]{1,0:T(8,128)(2,1)} copy-done((bf16[1024,2048]{1,0:T(8,128)(2,1)}, bf16[1024,2048]{1,0:T(8,128)(2,1)S(1)}, u32[]{:S(2)}) %copy-start.1) | copy-done | bytes 4194328
  76.2 5.9 %collective-permute-start.10 = (bf16[128,1024]{1,0:T(8,128)(2,1)S(1)}, bf16[128,1024]{1,0:T(8,128)(2,1)S(1)}, u32[]{:S(2)}, u32[]{:S(2)}) collective-permute-start(bf16[128,1024]{1,0:T(8,128)(2,1)S(1)} %get-tuple-element.16), channel_id=1, source_target_pairs={{0,14},{1,15},{2,0},{3,1},{4,2},{5,3},{6,4},{7,5},{8,6},{9,7},{10,... | collective-permute-start | bytes 786440 | tf_op jit(solution)/shard_map/ppermute | solution.py:35
  82.2 3.9 %collective-permute-done.10 = bf16[128,1024]{1,0:T(8,128)(2,1)S(1)} collective-permute-done((bf16[128,1024]{1,0:T(8,128)(2,1)S(1)}, bf16[128,1024]{1,0:T(8,128)(2,1)S(1)}, u32[]{:S(2)}, u32[]{:S(2)}) %collective-permute-start.10) | collective-permute-done | bytes 262176 | tf_op jit(solution)/shard_map/ppermute | solution.py:35
  86.1 3.7 %collective-permute-done.6 = bf16[128,1024]{1,0:T(8,128)(2,1)S(1)} collective-permute-done((bf16[128,1024]{1,0:T(8,128)(2,1)S(1)}, bf16[128,1024]{1,0:T(8,128)(2,1)S(1)}, u32[]{:S(2)}, u32[]{:S(2)}) %collective-permute-start.6) | collective-permute-done | bytes 262176 | tf_op jit(solution)/shard_map/ppermute | solution.py:34
  89.7 2.2 %add_convert_fusion.5 = (bf16[128,2048]{1,0:T(8,128)(2,1)S(1)}, bf16[128,2048]{1,0:T(8,128)(2,1)}) fusion(bf16[1024,2048]{1,0:T(8,128)(2,1)} %copy-done.1, s32[]{:T(128)S(6)} %select_n.126, bf16[128,1024]{1,0:T(8,128)(2,1)S(1)} %collective-permute-done.6, s32[]{:T(128)S(6)} %select_n.132, bf16[128,1024]{1,0:T(8,128)(2,1)S(1)} %collective-permute-done.10), kind=kLoop, calls=%fused_computation.34 | loop fusion | flops 2097152 | bytes 2621448 | tf_op jit(solution)/shard_map/convert_element_type | solution.py:34
  91.9 0.0 collective-permute-start.11
  91.9 2.0 %collective-permute-start.7 = (bf16[128,2048]{1,0:T(8,128)(2,1)S(1)}, bf16[128,2048]{1,0:T(8,128)(2,1)}, u32[]{:S(2)}, u32[]{:S(2)}) collective-permute-start(bf16[128,2048]{1,0:T(8,128)(2,1)S(1)} %get-tuple-element.13), channel_id=1, source_target_pairs={{0,2},{1,3},{2,4},{3,5},{4,6},{5,7},{6,8},{7,9},{8,10},{9,11},{10,... | collective-permute-start | bytes 1572872 | tf_op jit(solution)/shard_map/ppermute | solution.py:34
  93.9 9.1 %collective-permute-done.11 = bf16[128,2048]{1,0:T(8,128)(2,1)} collective-permute-done((bf16[128,2048]{1,0:T(8,128)(2,1)}, bf16[128,2048]{1,0:T(8,128)(2,1)}, u32[]{:S(2)}, u32[]{:S(2)}) %collective-permute-start.11) | collective-permute-done | bytes 524320 | tf_op jit(solution)/shard_map/ppermute | solution.py:35
  103.1 1.0 collective-permute-done.7
  104.1 2.7 %add_convert_fusion.4 = (bf16[128,2048]{1,0:T(8,128)(2,1)S(1)}, bf16[128,2048]{1,0:T(8,128)(2,1)}) fusion(bf16[128,2048]{1,0:T(8,128)(2,1)} %collective-permute-done.7, bf16[1024,2048]{1,0:T(8,128)(2,1)} %copy-done.1, s32[]{:T(128)S(6)} %select_n.128, s32[]{:T(128)S(6)} %select_n.134, bf16[128,2048]{1,0:T(8,128)(2,1)} %collective-permute-done.11), kind=kLoop, calls=%fused_computation.33 | loop fusion | flops 2097152 | bytes 3145736 | tf_op jit(solution)/shard_map/convert_element_type | solution.py:34
  106.8 0.5 collective-permute-start.12
  107.3 1.5 collective-permute-start.8
  108.8 8.2 %collective-permute-done.12 = bf16[128,2048]{1,0:T(8,128)(2,1)} collective-permute-done((bf16[128,2048]{1,0:T(8,128)(2,1)}, bf16[128,2048]{1,0:T(8,128)(2,1)}, u32[]{:S(2)}, u32[]{:S(2)}) %collective-permute-start.12) | collective-permute-done | bytes 524320 | tf_op jit(solution)/shard_map/ppermute | solution.py:35
  117.0 1.5 collective-permute-done.8
  118.5 2.7 %add_convert_fusion.3 = (bf16[128,2048]{1,0:T(8,128)(2,1)S(1)}, bf16[128,2048]{1,0:T(8,128)(2,1)}) fusion(bf16[128,2048]{1,0:T(8,128)(2,1)} %collective-permute-done.8, bf16[1024,2048]{1,0:T(8,128)(2,1)} %copy-done.1, s32[]{:T(128)S(6)} %select_n.130, s32[]{:T(128)S(6)} %select_n.136, bf16[128,2048]{1,0:T(8,128)(2,1)} %collective-permute-done.12), kind=kLoop, calls=%fused_computation.32 | loop fusion | flops 2097152 | bytes 3145736 | tf_op jit(solution)/shard_map/convert_element_type | solution.py:34
  121.2 0.5 collective-permute-start.13
  121.7 1.5 collective-permute-start.9
  123.2 3.1 %fusion.53 = (f32[1,384,512]{2,1,0:T(8,128)}, bf16[384,512]{1,0:T(8,128)(2,1)S(1)}, f32[1,384,512]{2,1,0:T(8,128)}) fusion(bf16[384,512]{1,0:T(8,128)(2,1)} %reduce-scatter.2.cloned.1.call-done, f32[1,384,512]{2,1,0:T(8,128)S(1)} %copy-done.9, f32[384,512]{1,0:T(8,128)S(1)} %copy-done.7, f32[1,384,512]{2,1,0:T(8,128)} %param.14, f32[1,384,512]{2,1,0:T(8,128)S(1)} %copy-done), kind=kLoop, calls=%fused_computation.76 | loop fusion | flops 3538944 | bytes 5505024 | tf_op jit(solution)/shard_map/broadcast_in_dim | solution.py:138
  126.3 4.4 %collective-permute-done.13 = bf16[128,2048]{1,0:T(8,128)(2,1)} collective-permute-done((bf16[128,2048]{1,0:T(8,128)(2,1)}, bf16[128,2048]{1,0:T(8,128)(2,1)}, u32[]{:S(2)}, u32[]{:S(2)}) %collective-permute-start.13) | collective-permute-done | bytes 524320 | tf_op jit(solution)/shard_map/ppermute | solution.py:35
  130.7 1.5 collective-permute-done.9
  132.2 1.6 %convert_add_fusion = f32[128,2048]{1,0:T(8,128)S(1)} fusion(bf16[128,2048]{1,0:T(8,128)(2,1)} %collective-permute-done.13, bf16[128,2048]{1,0:T(8,128)(2,1)} %collective-permute-done.9, bf16[1024,2048]{1,0:T(8,128)(2,1)} %copy-done.1, s32[]{:T(128)S(6)} %select_n.122), kind=kLoop, calls=%fused_computation.28 | loop fusion | flops 1310720 | bytes 2621444 | tf_op jit(solution)/shard_map/add | solution.py:44
  133.8 0.6 collective-permute-start.14
  134.4 0.1 add_convert_fusion.6
  134.5 2.6 %collective-permute-start.5 = (bf16[384,512]{1,0:T(8,128)(2,1)S(1)}, bf16[384,512]{1,0:T(8,128)(2,1)S(1)}, u32[]{:S(2)}, u32[]{:S(2)}) collective-permute-start(bf16[384,512]{1,0:T(8,128)(2,1)S(1)} %add_convert_fusion.6), channel_id=1, source_target_pairs={{0,128},{64,192},{128,0},{192,64},{1,129},{65,193},{129,1},{193,65... | collective-permute-start | bytes 1179656 | tf_op jit(solution)/shard_map/ppermute | solution.py:133
  137.1 3.8 %collective-permute-done.14 = bf16[64,2048]{1,0:T(8,128)(2,1)S(1)} collective-permute-done((bf16[64,2048]{1,0:T(8,128)(2,1)S(1)}, bf16[64,2048]{1,0:T(8,128)(2,1)S(1)}, u32[]{:S(2)}, u32[]{:S(2)}) %collective-permute-start.14) | collective-permute-done | bytes 262176 | tf_op jit(solution)/shard_map/ppermute | solution.py:48
  141.0 0.7 fusion.61
  141.7 4.5 %collective-permute-done.5 = bf16[384,512]{1,0:T(8,128)(2,1)S(1)} collective-permute-done((bf16[384,512]{1,0:T(8,128)(2,1)S(1)}, bf16[384,512]{1,0:T(8,128)(2,1)S(1)}, u32[]{:S(2)}, u32[]{:S(2)}) %collective-permute-start.5) | collective-permute-done | bytes 393248 | tf_op jit(solution)/shard_map/ppermute | solution.py:133
  146.2 2.5 %multiply_subtract_fusion = (f32[384,512]{1,0:T(8,128)}, f32[384,512]{1,0:T(8,128)}) fusion(f32[384,512]{1,0:T(8,128)S(1)} %copy-done.7, bf16[384,512]{1,0:T(8,128)(2,1)S(1)} %collective-permute-done.5, bf16[384,512]{1,0:T(8,128)(2,1)S(1)} %add_convert_fusion.6, f32[384,512]{1,0:T(8,128)} %param.17), kind=kLoop, calls=%fused_computation.52 | loop fusion | flops 1966080 | bytes 3932160 | tf_op jit(solution)/shard_map/sub | solution.py:137
  (25 shorter events, 0.2 us)
Async XLA Ops:
  7.2 116.1 %reduce-scatter.2.cloned.1.call-start = ((), (), s32[]{:S(2)}) async-start(), calls=%async_computation.1 | async-start | bytes 1966080 | tf_op jit(solution)/shard_map/reduce_scatter | solution.py:111
  11.9 29.2 %collective-permute-start = (bf16[512,1152]{0,1:T(8,128)(2,1)}, bf16[512,1152]{0,1:T(8,128)(2,1)}, u32[]{:S(2)}, u32[]{:S(2)}) collective-permute-start(bf16[512,1152]{0,1:T(8,128)(2,1)} %pad_maximum_fusion), channel_id=1, source_target_pairs={{0,16},{16,32},{32,48},{48,0},{1,17},{17,33},{33,49},{49,1},{2,18}... | collective-permute-start | bytes 3538952 | tf_op jit(solution)/shard_map/ppermute | solution.py:75
  13.4 29.2 %collective-permute-start.1 = (bf16[512,1152]{0,1:T(8,128)(2,1)}, bf16[512,1152]{0,1:T(8,128)(2,1)S(1)}, u32[]{:S(2)}, u32[]{:S(2)}) collective-permute-start(bf16[512,1152]{0,1:T(8,128)(2,1)} %pad_maximum_fusion), channel_id=1, source_target_pairs={{0,48},{16,0},{32,16},{48,32},{1,49},{17,1},{33,17},{49,33},{2,50}... | collective-permute-start | bytes 3538952 | tf_op jit(solution)/shard_map/ppermute | solution.py:76
  15.1 2.2 %copy-start.10 = (bf16[1,1024,2048]{2,1,0:T(8,128)(2,1)S(1)}, bf16[1,1024,2048]{2,1,0:T(8,128)(2,1)}, u32[]{:S(2)}) copy-start(bf16[1,1024,2048]{2,1,0:T(8,128)(2,1)} %param.9) | copy-start | bytes 12582916
  17.3 1.1 copy-start
  17.3 2.4 %copy-start.2 = (bf16[1,1024,2048]{2,1,0:T(8,128)(2,1)S(1)}, bf16[1,1024,2048]{2,1,0:T(8,128)(2,1)}, u32[]{:S(2)}) copy-start(bf16[1,1024,2048]{2,1,0:T(8,128)(2,1)} %param.10) | copy-start | bytes 12582916
  42.2 15.5 %collective-permute-start.2 = (bf16[256,1152]{0,1:T(8,128)(2,1)S(1)}, bf16[256,1152]{0,1:T(8,128)(2,1)S(1)}, u32[]{:S(2)}, u32[]{:S(2)}) collective-permute-start(bf16[256,1152]{0,1:T(8,128)(2,1)S(1)} %slice.67), channel_id=1, source_target_pairs={{0,16},{16,32},{32,48},{48,0},{1,17},{17,33},{33,49},{49,1},{2,18}... | collective-permute-start | bytes 1769480 | tf_op jit(solution)/shard_map/ppermute | solution.py:77
  42.6 15.7 %collective-permute-start.3 = (bf16[256,1152]{0,1:T(8,128)(2,1)S(1)}, bf16[256,1152]{0,1:T(8,128)(2,1)S(1)}, u32[]{:S(2)}, u32[]{:S(2)}) collective-permute-start(bf16[256,1152]{0,1:T(8,128)(2,1)S(1)} %slice.69), channel_id=1, source_target_pairs={{0,48},{16,0},{32,16},{48,32},{1,49},{17,1},{33,17},{49,33},{2,50}... | collective-permute-start | bytes 1769480 | tf_op jit(solution)/shard_map/ppermute | solution.py:78
  53.1 5.2 %copy-start.5 = (bf16[2048,768]{0,1:T(8,128)(2,1)}, bf16[2048,768]{0,1:T(8,128)(2,1)S(1)}, u32[]{:S(2)}) copy-start(bf16[2048,768]{0,1:T(8,128)(2,1)S(1)} %slice_dynamic-update-slice_fusion) | copy-start | bytes 9437188
  59.1 1.6 %copy-start.3 = (f32[1024,768]{0,1:T(8,128)}, f32[1024,768]{0,1:T(8,128)S(1)}, u32[]{:S(2)}) copy-start(f32[1024,768]{0,1:T(8,128)S(1)} %add_add_fusion) | copy-start | bytes 9437188
  63.7 3.3 %copy-start.8 = (f32[1024,384]{0,1:T(8,128)S(1)}, f32[1024,384]{0,1:T(8,128)}, u32[]{:S(2)}) copy-start(f32[1024,384]{0,1:T(8,128)} %fusion.13) | copy-start | bytes 4718596
  63.8 3.3 %copy-start.4 = (f32[1024,768]{0,1:T(8,128)S(1)}, f32[1024,768]{0,1:T(8,128)}, u32[]{:S(2)}) copy-start(f32[1024,768]{0,1:T(8,128)} %copy-done.3) | copy-start | bytes 9437188
  67.0 3.4 %copy-start.6 = (bf16[2048,768]{0,1:T(8,128)(2,1)S(1)}, bf16[2048,768]{0,1:T(8,128)(2,1)}, u32[]{:S(2)}) copy-start(bf16[2048,768]{0,1:T(8,128)(2,1)} %slice_dynamic-update-slice_fusion.2) | copy-start | bytes 9437188
  74.2 2.0 %copy-start.1 = (bf16[1024,2048]{1,0:T(8,128)(2,1)}, bf16[1024,2048]{1,0:T(8,128)(2,1)S(1)}, u32[]{:S(2)}) copy-start(bf16[1024,2048]{1,0:T(8,128)(2,1)S(1)} %convolution_convert_fusion) | copy-start | bytes 12582916
  76.2 9.8 %collective-permute-start.10 = (bf16[128,1024]{1,0:T(8,128)(2,1)S(1)}, bf16[128,1024]{1,0:T(8,128)(2,1)S(1)}, u32[]{:S(2)}, u32[]{:S(2)}) collective-permute-start(bf16[128,1024]{1,0:T(8,128)(2,1)S(1)} %get-tuple-element.16), channel_id=1, source_target_pairs={{0,14},{1,15},{2,0},{3,1},{4,2},{5,3},{6,4},{7,5},{8,6},{9,7},{10,... | collective-permute-start | bytes 786440 | tf_op jit(solution)/shard_map/ppermute | solution.py:35
  82.2 7.6 %collective-permute-start.6 = (bf16[128,1024]{1,0:T(8,128)(2,1)S(1)}, bf16[128,1024]{1,0:T(8,128)(2,1)S(1)}, u32[]{:S(2)}, u32[]{:S(2)}) collective-permute-start(bf16[128,1024]{1,0:T(8,128)(2,1)S(1)} %get-tuple-element.15), channel_id=1, source_target_pairs={{0,2},{1,3},{2,4},{3,5},{4,6},{5,7},{6,8},{7,9},{8,10},{9,11},{10,... | collective-permute-start | bytes 786440 | tf_op jit(solution)/shard_map/ppermute | solution.py:34
  91.9 11.2 %collective-permute-start.11 = (bf16[128,2048]{1,0:T(8,128)(2,1)}, bf16[128,2048]{1,0:T(8,128)(2,1)}, u32[]{:S(2)}, u32[]{:S(2)}) collective-permute-start(bf16[128,2048]{1,0:T(8,128)(2,1)} %get-tuple-element.14), channel_id=1, source_target_pairs={{0,14},{1,15},{2,0},{3,1},{4,2},{5,3},{6,4},{7,5},{8,6},{9,7},{10,... | collective-permute-start | bytes 1572872 | tf_op jit(solution)/shard_map/ppermute | solution.py:35
  91.9 12.1 %collective-permute-start.7 = (bf16[128,2048]{1,0:T(8,128)(2,1)S(1)}, bf16[128,2048]{1,0:T(8,128)(2,1)}, u32[]{:S(2)}, u32[]{:S(2)}) collective-permute-start(bf16[128,2048]{1,0:T(8,128)(2,1)S(1)} %get-tuple-element.13), channel_id=1, source_target_pairs={{0,2},{1,3},{2,4},{3,5},{4,6},{5,7},{6,8},{7,9},{8,10},{9,11},{10,... | collective-permute-start | bytes 1572872 | tf_op jit(solution)/shard_map/ppermute | solution.py:34
  93.9 29.3 %copy-start.7 = (f32[384,512]{1,0:T(8,128)S(1)}, f32[384,512]{1,0:T(8,128)}, u32[]{:S(2)}) copy-start(f32[384,512]{1,0:T(8,128)} %param.16) | copy-start | bytes 2359300
  93.9 29.3 %copy-start.9 = (f32[1,384,512]{2,1,0:T(8,128)S(1)}, f32[1,384,512]{2,1,0:T(8,128)}, u32[]{:S(2)}) copy-start(f32[1,384,512]{2,1,0:T(8,128)} %param.15) | copy-start | bytes 2359300
  106.8 10.2 %collective-permute-start.12 = (bf16[128,2048]{1,0:T(8,128)(2,1)}, bf16[128,2048]{1,0:T(8,128)(2,1)}, u32[]{:S(2)}, u32[]{:S(2)}) collective-permute-start(bf16[128,2048]{1,0:T(8,128)(2,1)} %get-tuple-element.12), channel_id=1, source_target_pairs={{0,14},{1,15},{2,0},{3,1},{4,2},{5,3},{6,4},{7,5},{8,6},{9,7},{10,... | collective-permute-start | bytes 1572872 | tf_op jit(solution)/shard_map/ppermute | solution.py:35
  107.3 11.2 %collective-permute-start.8 = (bf16[128,2048]{1,0:T(8,128)(2,1)S(1)}, bf16[128,2048]{1,0:T(8,128)(2,1)}, u32[]{:S(2)}, u32[]{:S(2)}) collective-permute-start(bf16[128,2048]{1,0:T(8,128)(2,1)S(1)} %get-tuple-element.11), channel_id=1, source_target_pairs={{0,2},{1,3},{2,4},{3,5},{4,6},{5,7},{6,8},{7,9},{8,10},{9,11},{10,... | collective-permute-start | bytes 1572872 | tf_op jit(solution)/shard_map/ppermute | solution.py:34
  121.2 9.5 %collective-permute-start.13 = (bf16[128,2048]{1,0:T(8,128)(2,1)}, bf16[128,2048]{1,0:T(8,128)(2,1)}, u32[]{:S(2)}, u32[]{:S(2)}) collective-permute-start(bf16[128,2048]{1,0:T(8,128)(2,1)} %get-tuple-element.10), channel_id=1, source_target_pairs={{0,14},{1,15},{2,0},{3,1},{4,2},{5,3},{6,4},{7,5},{8,6},{9,7},{10,... | collective-permute-start | bytes 1572872 | tf_op jit(solution)/shard_map/ppermute | solution.py:35
  121.7 10.5 %collective-permute-start.9 = (bf16[128,2048]{1,0:T(8,128)(2,1)S(1)}, bf16[128,2048]{1,0:T(8,128)(2,1)}, u32[]{:S(2)}, u32[]{:S(2)}) collective-permute-start(bf16[128,2048]{1,0:T(8,128)(2,1)S(1)} %get-tuple-element.9), channel_id=1, source_target_pairs={{0,2},{1,3},{2,4},{3,5},{4,6},{5,7},{6,8},{7,9},{8,10},{9,11},{10,... | collective-permute-start | bytes 1572872 | tf_op jit(solution)/shard_map/ppermute | solution.py:34
  126.3 8.1 %collective-permute-start.4 = (bf16[384,512]{1,0:T(8,128)(2,1)S(1)}, bf16[384,512]{1,0:T(8,128)(2,1)S(1)}, u32[]{:S(2)}, u32[]{:S(2)}) collective-permute-start(bf16[384,512]{1,0:T(8,128)(2,1)S(1)} %get-tuple-element.18), channel_id=1, source_target_pairs={{0,64},{64,0},{128,192},{192,128},{1,65},{65,1},{129,193},{193,129... | collective-permute-start | bytes 1179656 | tf_op jit(solution)/shard_map/ppermute | solution.py:133
  133.8 7.2 %collective-permute-start.14 = (bf16[64,2048]{1,0:T(8,128)(2,1)S(1)}, bf16[64,2048]{1,0:T(8,128)(2,1)S(1)}, u32[]{:S(2)}, u32[]{:S(2)}) collective-permute-start(bf16[64,2048]{1,0:T(8,128)(2,1)S(1)} %dynamic-slice_convert_fusion), channel_id=1, source_target_pairs={{0,1},{1,0},{2,3},{3,2},{4,5},{5,4},{6,7},{7,6},{8,9},{9,8},{10,11... | collective-permute-start | bytes 786440 | tf_op jit(solution)/shard_map/ppermute | solution.py:48
  134.5 11.7 %collective-permute-start.5 = (bf16[384,512]{1,0:T(8,128)(2,1)S(1)}, bf16[384,512]{1,0:T(8,128)(2,1)S(1)}, u32[]{:S(2)}, u32[]{:S(2)}) collective-permute-start(bf16[384,512]{1,0:T(8,128)(2,1)S(1)} %add_convert_fusion.6), channel_id=1, source_target_pairs={{0,128},{64,192},{128,0},{192,64},{1,129},{65,193},{129,1},{193,65... | collective-permute-start | bytes 1179656 | tf_op jit(solution)/shard_map/ppermute | solution.py:133
Sparse Core Ops, SparseCore 0:
  63.9 30.6 reduce-scatter.1

commit v8 on v4

--- a/solution.py
+++ b/solution.py
@@ -47,23 +47,15 @@
     halfc = part.shape[1] // 2
     up = [(i, ((i // nlo + 1) % nz) * nlo + i % nlo) for i in range(nmp)]
     down = [(i, ((i // nlo - 1) % nz) * nlo + i % nlo) for i in range(nmp)]
-    pair = [(i, i ^ 1) for i in range(nmp)]
-
-    py = part[:, halfc:].reshape(nz, nlo, sub, halfc)
-    keep = lax.dynamic_index_in_dim(py, lo, axis=1, keepdims=False)
-    give = lax.dynamic_index_in_dim(py, 1 - lo, axis=1, keepdims=False)
-    got_y = lax.ppermute(give, "mp", pair)
-    acc_y = keep.astype(jnp.float32) + got_y.astype(jnp.float32)
-
-    pz = part[:, :halfc].reshape(nz, rows, halfc)
-    acc_z = _z_reduce_scatter(pz, z, nz, up, down)
-    mine = lax.dynamic_slice_in_dim(acc_z, lo * sub, sub, axis=0)
-    other = lax.dynamic_slice_in_dim(acc_z, (1 - lo) * sub, sub, axis=0)
-    got = lax.ppermute(other.astype(jnp.bfloat16), "mp", pair)
-    out_z = mine + got.astype(jnp.float32)
-
-    out_y = _z_reduce_scatter(acc_y.astype(jnp.bfloat16), z, nz, up, down)
-    return jnp.concatenate([out_z, out_y], axis=1).astype(jnp.bfloat16)
+    pa = part[:, :halfc].reshape(nz, rows, halfc)
+    pb = part[:, halfc:].reshape(nz, rows, halfc)
+    acc = jnp.concatenate(
+        [_z_reduce_scatter(pa, z, nz, up, down), _z_reduce_scatter(pb, z, nz, up, down)], axis=1
+    )
+    mine = lax.dynamic_slice_in_dim(acc, lo * sub, sub, axis=0)
+    other = lax.dynamic_slice_in_dim(acc, (1 - lo) * sub, sub, axis=0)
+    got = lax.ppermute(other.astype(jnp.bfloat16), "mp", [(i, i ^ 1) for i in range(nmp)])
+    return (mine + got.astype(jnp.float32)).astype(jnp.bfloat16)
 
 
 def shards(

time: 130 us -> 128 us (0.985)
  waiting for transfers between devices: 48 us -> 53.2 us
  local copies, waits for them, and re-layouts: 12.6 us -> 8.98 us
  starting transfers between devices: 40.9 us -> 38.8 us
  other arithmetic: 10.7 us -> 9.15 us
    ppermute x2 -> x1, waiting for transfers between devices: 1.44 us -> 6.33 us  [_ring_reduce_scatter(): lax.ppermute(other.astype(jnp.bfloat16), 'mp', [(i, i ^ 1) for i in range...]
    ppermute x8, waiting for transfers between devices: 10.7 us -> 5.98 us  [_z_reduce_scatter(): lax.ppermute(send_a.astype(jnp.bfloat16), 'mp', up).astype(jnp.float32)]
    ppermute x2, waiting for transfers between devices: 0.01 us -> 4.47 us  [shards(): lax.ppermute(mine, 'outer', perm).astype(jnp.float32)]
    ppermute x8, starting transfers between devices: 25 us -> 21.4 us  [_z_reduce_scatter(): lax.ppermute(send_b.astype(jnp.bfloat16), 'mp', down).astype(jnp.float32)]
    ppermute x8, waiting for transfers between devices: 0.63 us -> 3.49 us  [_z_reduce_scatter(): lax.ppermute(send_b.astype(jnp.bfloat16), 'mp', down).astype(jnp.float32)]
    ppermute x8, starting transfers between devices: 0.99 us -> 3.53 us  [_z_reduce_scatter(): lax.ppermute(send_a.astype(jnp.bfloat16), 'mp', up).astype(jnp.float32)]
    ppermute x3, waiting for transfers between devices: 10.4 us -> 8.09 us  [shards(): got = lax.ppermute(blk.astype(jnp.bfloat16), 'dp', _shift(ndp, s))]
    broadcast_in_dim x0 -> x1, other arithmetic: none -> 1.7 us  [shards(): input_grad[None]]
  transfers between devices with their start and end apart: 27 -> 26, of which waited for: 12 -> 11; matrix products, arithmetic and copies ran while one was open for 18% -> 15% of each run, Pallas kernels for 0% -> 0%
where the time goes in v8:
time: 128 us; the launch traced here: 127 us
  waiting for transfers between devices  53.2 us (42%)
  starting transfers between devices  38.8 us (30%)
  matrix products  16 us (12%)
  other arithmetic  9.15 us (7%)
  local copies, waits for them, and re-layouts  8.98 us (7%)
    ppermute x8, starting transfers between devices, _z_reduce_scatter(): lax.ppermute(send_b.astype(jnp.bfloat16), 'mp', down).astype(jnp.float32)  21.4 us
    ppermute x1, waiting for transfers between devices, shards(): from_left = lax.ppermute(shard, 'dp', _shift(ndp, 1))  20.9 us
    ppermute x3, waiting for transfers between devices, shards(): got = lax.ppermute(blk.astype(jnp.bfloat16), 'dp', _shift(ndp, s))  8.09 us
    ppermute x1, waiting for transfers between devices, _ring_reduce_scatter(): lax.ppermute(other.astype(jnp.bfloat16), 'mp', [(i, i ^ 1) for i in range...  6.33 us
    ppermute x8, waiting for transfers between devices, _z_reduce_scatter(): lax.ppermute(send_a.astype(jnp.bfloat16), 'mp', up).astype(jnp.float32)  5.98 us
    dot_general x5, matrix products, shards(): p1 = jnp.dot(xs, piece[:, :2 * ff], preferred_element_type=jnp.float32)  5.88 us
    unnamed x16, local copies, waits for them, and re-layouts  5.29 us
    ppermute x2, waiting for transfers between devices, shards(): lax.ppermute(mine, 'outer', perm).astype(jnp.float32)  4.47 us
  transfers between devices with their start and end apart: 26, of which 11 were waited for; matrix products, arithmetic and copies ran while one was open for 15% of the time, Pallas kernels for 0%

profile of v8, /device:TPU:8, one launch (start us, length us, event | category | flops | bytes accessed | tf_op | source)
XLA Modules:
  0.0 127.2 jit_solution(16970039372125678786)
XLA Ops:
  0.6 1.2 copy.14
  1.9 1.2 copy.15
  3.1 1.1 pad_maximum_fusion
  4.3 1.5 %collective-permute-start = (bf16[512,1152]{0,1:T(8,128)(2,1)}, bf16[512,1152]{0,1:T(8,128)(2,1)S(1)}, u32[]{:S(2)}, u32[]{:S(2)}) collective-permute-start(bf16[512,1152]{0,1:T(8,128)(2,1)} %pad_maximum_fusion), channel_id=1, source_target_pairs={{0,16},{16,32},{32,48},{48,0},{1,17},{17,33},{33,49},{49,1},{2,18}... | collective-permute-start | bytes 3538952 | tf_op jit(solution)/shard_map/ppermute | solution.py:84
  5.7 1.7 %collective-permute-start.1 = (bf16[512,1152]{0,1:T(8,128)(2,1)}, bf16[512,1152]{0,1:T(8,128)(2,1)}, u32[]{:S(2)}, u32[]{:S(2)}) collective-permute-start(bf16[512,1152]{0,1:T(8,128)(2,1)} %pad_maximum_fusion), channel_id=1, source_target_pairs={{0,48},{16,0},{32,16},{48,32},{1,49},{17,1},{33,17},{49,33},{2,50}... | collective-permute-start | bytes 3538952 | tf_op jit(solution)/shard_map/ppermute | solution.py:85
  7.5 0.4 broadcast_in_dim.14
  7.9 0.1 fusion.66
  8.0 1.7 %copy-done.6 = bf16[1,1024,2048]{2,1,0:T(8,128)(2,1)S(1)} copy-done((bf16[1,1024,2048]{2,1,0:T(8,128)(2,1)S(1)}, bf16[1,1024,2048]{2,1,0:T(8,128)(2,1)}, u32[]{:S(2)}) %copy-start.6) | copy-done | bytes 4194328
  9.7 1.0 fusion.16
  10.7 1.2 copy-done.1
  11.9 0.6 fusion.10
  12.5 20.9 %collective-permute-done = bf16[512,1152]{0,1:T(8,128)(2,1)S(1)} collective-permute-done((bf16[512,1152]{0,1:T(8,128)(2,1)}, bf16[512,1152]{0,1:T(8,128)(2,1)S(1)}, u32[]{:S(2)}, u32[]{:S(2)}) %collective-permute-start) | collective-permute-done | bytes 1179680 | tf_op jit(solution)/shard_map/ppermute | solution.py:84
  33.4 0.4 collective-permute-start.2
  33.8 1.1 slice.87
  34.9 3.2 %collective-permute-start.3 = (bf16[256,1152]{0,1:T(8,128)(2,1)S(1)}, bf16[256,1152]{0,1:T(8,128)(2,1)S(1)}, u32[]{:S(2)}, u32[]{:S(2)}) collective-permute-start(bf16[256,1152]{0,1:T(8,128)(2,1)S(1)} %slice.87), channel_id=1, source_target_pairs={{0,48},{16,0},{32,16},{48,32},{1,49},{17,1},{33,17},{49,33},{2,50}... | collective-permute-start | bytes 1769480 | tf_op jit(solution)/shard_map/ppermute | solution.py:87
  38.1 2.2 %fusion.12 = f32[1024,768]{0,1:T(8,128)S(1)} fusion(bf16[1,1024,2048]{2,1,0:T(8,128)(2,1)S(1)} %copy-done.6, s32[]{:T(128)S(6)} %select_n.155, bf16[512,1152]{0,1:T(8,128)(2,1)} %collective-permute-done.1), kind=kOutput, calls=%fused_computation.25 | convolution fusion | flops 805306368 | bytes 4980740 | tf_op jit(solution)/shard_map/dot_general | solution.py:103
  40.3 1.6 %fusion.6 = f32[1024,384]{0,1:T(8,128)S(1)} fusion(bf16[1,1024,2048]{2,1,0:T(8,128)(2,1)S(1)} %copy-done.1, s32[]{:T(128)S(6)} %select_n.155, bf16[512,1152]{0,1:T(8,128)(2,1)} %collective-permute-done.1), kind=kOutput, calls=%fused_computation.19 | convolution fusion | flops 402653184 | bytes 3014660 | tf_op jit(solution)/shard_map/dot_general | solution.py:104
  41.9 0.6 fusion.8
  42.6 1.2 slice_dynamic-update-slice_fusion
  43.9 1.0 fusion.14
  44.9 4.0 %collective-permute-done.2 = bf16[256,1152]{0,1:T(8,128)(2,1)S(1)} collective-permute-done((bf16[256,1152]{0,1:T(8,128)(2,1)S(1)}, bf16[256,1152]{0,1:T(8,128)(2,1)S(1)}, u32[]{:S(2)}, u32[]{:S(2)}) %collective-permute-start.2) | collective-permute-done | bytes 589856 | tf_op jit(solution)/shard_map/ppermute | solution.py:86
  49.0 0.4 fusion.54
  49.4 0.6 fusion.60
  50.1 1.1 add_add_fusion
  51.1 1.2 multiply_convert_fusion.1
  52.3 3.8 %convolution_convert_fusion = bf16[1024,2048]{1,0:T(8,128)(2,1)S(1)} fusion(bf16[2048,768]{0,1:T(8,128)(2,1)S(1)} %slice_dynamic-update-slice_fusion.2, bf16[1024,384]{0,1:T(8,128)(2,1)S(1)} %get-tuple-element.10, bf16[1024,384]{0,1:T(8,128)(2,1)S(1)} %get-tuple-element.9), kind=kOutput, calls=%fused_computation.2 | convolution fusion | flops 3226468352 | bytes 8912896 | tf_op jit(solution)/shard_map/dot_general | solution.py:130
  56.1 0.5 fusion.93
  56.7 2.0 %collective-permute-start.17 = (bf16[128,512]{1,0:T(8,128)(2,1)S(1)}, bf16[128,512]{1,0:T(8,128)(2,1)S(1)}, u32[]{:S(2)}, u32[]{:S(2)}) collective-permute-start(bf16[128,512]{1,0:T(8,128)(2,1)S(1)} %get-tuple-element.30), channel_id=1, source_target_pairs={{0,2},{1,3},{2,4},{3,5},{4,6},{5,7},{6,8},{7,9},{8,10},{9,11},{10,... | collective-permute-start | bytes 393224 | tf_op jit(solution)/shard_map/ppermute | solution.py:25
  58.7 4.0 %collective-permute-start.21 = (bf16[128,512]{1,0:T(8,128)(2,1)S(1)}, bf16[128,512]{1,0:T(8,128)(2,1)S(1)}, u32[]{:S(2)}, u32[]{:S(2)}) collective-permute-start(bf16[128,512]{1,0:T(8,128)(2,1)S(1)} %get-tuple-element.31), channel_id=1, source_target_pairs={{0,14},{1,15},{2,0},{3,1},{4,2},{5,3},{6,4},{7,5},{8,6},{9,7},{10,... | collective-permute-start | bytes 393224 | tf_op jit(solution)/shard_map/ppermute | solution.py:26
  62.8 2.0 %collective-permute-start.13 = (bf16[128,512]{1,0:T(8,128)(2,1)S(1)}, bf16[128,512]{1,0:T(8,128)(2,1)S(1)}, u32[]{:S(2)}, u32[]{:S(2)}) collective-permute-start(bf16[128,512]{1,0:T(8,128)(2,1)S(1)} %get-tuple-element.33), channel_id=1, source_target_pairs={{0,14},{1,15},{2,0},{3,1},{4,2},{5,3},{6,4},{7,5},{8,6},{9,7},{10,... | collective-permute-start | bytes 393224 | tf_op jit(solution)/shard_map/ppermute | solution.py:26
  64.9 1.9 %fusion = f32[384,2048]{1,0:T(8,128)S(1)} fusion(bf16[1,1024,2048]{2,1,0:T(8,128)(2,1)S(1)} %copy-done.1, f32[1024,768]{0,1:T(8,128)S(1)} %add_add_fusion), kind=kOutput, calls=%fused_computation | convolution fusion | flops 1612972032 | bytes 10485760 | tf_op jit(solution)/shard_map/dot_general | solution.py:119
  67.0 3.2 %collective-permute-start.22 = (bf16[128,1024]{1,0:T(8,128)(2,1)S(1)}, bf16[128,1024]{1,0:T(8,128)(2,1)S(1)}, u32[]{:S(2)}, u32[]{:S(2)}) collective-permute-start(bf16[128,1024]{1,0:T(8,128)(2,1)S(1)} %get-tuple-element.21), channel_id=1, source_target_pairs={{0,14},{1,15},{2,0},{3,1},{4,2},{5,3},{6,4},{7,5},{8,6},{9,7},{10,... | collective-permute-start | bytes 786440 | tf_op jit(solution)/shard_map/ppermute | solution.py:26
  70.2 2.2 %collective-permute-done.9 = bf16[128,512]{1,0:T(8,128)(2,1)S(1)} collective-permute-done((bf16[128,512]{1,0:T(8,128)(2,1)S(1)}, bf16[128,512]{1,0:T(8,128)(2,1)S(1)}, u32[]{:S(2)}, u32[]{:S(2)}) %collective-permute-start.9) | collective-permute-done | bytes 131104 | tf_op jit(solution)/shard_map/ppermute | solution.py:25
  72.6 3.2 %collective-permute-start.14 = (bf16[128,1024]{1,0:T(8,128)(2,1)S(1)}, bf16[128,1024]{1,0:T(8,128)(2,1)S(1)}, u32[]{:S(2)}, u32[]{:S(2)}) collective-permute-start(bf16[128,1024]{1,0:T(8,128)(2,1)S(1)} %get-tuple-element.27), channel_id=1, source_target_pairs={{0,14},{1,15},{2,0},{3,1},{4,2},{5,3},{6,4},{7,5},{8,6},{9,7},{10,... | collective-permute-start | bytes 786440 | tf_op jit(solution)/shard_map/ppermute | solution.py:26
  75.8 0.2 dynamic-slice_convert_fusion.2
  76.0 0.7 collective-permute-start.4
  76.7 1.1 collective-permute-done.18
  77.8 3.0 %collective-permute-start.5 = (bf16[384,512]{1,0:T(8,128)(2,1)S(1)}, bf16[384,512]{1,0:T(8,128)(2,1)S(1)}, u32[]{:S(2)}, u32[]{:S(2)}) collective-permute-start(bf16[384,512]{1,0:T(8,128)(2,1)S(1)} %get-tuple-element.15), channel_id=1, source_target_pairs={{0,32},{16,48},{32,0},{48,16},{1,33},{17,49},{33,1},{49,17},{2,34}... | collective-permute-start | bytes 1179656 | tf_op jit(solution)/shard_map/ppermute | solution.py:126
  80.8 0.2 collective-permute-start.6
  80.9 0.2 fusion.40
  81.2 3.2 %collective-permute-start.23 = (bf16[128,1024]{1,0:T(8,128)(2,1)S(1)}, bf16[128,1024]{1,0:T(8,128)(2,1)S(1)}, u32[]{:S(2)}, u32[]{:S(2)}) collective-permute-start(bf16[128,1024]{1,0:T(8,128)(2,1)S(1)} %get-tuple-element.19), channel_id=1, source_target_pairs={{0,14},{1,15},{2,0},{3,1},{4,2},{5,3},{6,4},{7,5},{8,6},{9,7},{10,... | collective-permute-start | bytes 786440 | tf_op jit(solution)/shard_map/ppermute | solution.py:26
  84.5 0.2 fusion.47
  84.7 3.2 %collective-permute-done.4 = bf16[384,512]{1,0:T(8,128)(2,1)S(1)} collective-permute-done((bf16[384,512]{1,0:T(8,128)(2,1)S(1)}, bf16[384,512]{1,0:T(8,128)(2,1)S(1)}, u32[]{:S(2)}, u32[]{:S(2)}) %collective-permute-start.4) | collective-permute-done | bytes 393248 | tf_op jit(solution)/shard_map/ppermute | solution.py:126
  87.8 4.2 %collective-permute-done.5 = bf16[384,512]{1,0:T(8,128)(2,1)S(1)} collective-permute-done((bf16[384,512]{1,0:T(8,128)(2,1)S(1)}, bf16[384,512]{1,0:T(8,128)(2,1)S(1)}, u32[]{:S(2)}, u32[]{:S(2)}) %collective-permute-start.5) | collective-permute-done | bytes 393248 | tf_op jit(solution)/shard_map/ppermute | solution.py:126
  92.0 0.3 collective-permute-start.15
  92.3 0.7 collective-permute-done.6
  93.0 1.2 fusion.76
  94.3 0.2 fusion.39
  94.5 1.1 collective-permute-start.20
  95.6 2.2 %collective-permute-start.24 = (bf16[128,1024]{1,0:T(8,128)(2,1)S(1)}, bf16[128,1024]{1,0:T(8,128)(2,1)S(1)}, u32[]{:S(2)}, u32[]{:S(2)}) collective-permute-start(bf16[128,1024]{1,0:T(8,128)(2,1)S(1)} %get-tuple-element.17), channel_id=1, source_target_pairs={{0,14},{1,15},{2,0},{3,1},{4,2},{5,3},{6,4},{7,5},{8,6},{9,7},{10,... | collective-permute-start | bytes 786440 | tf_op jit(solution)/shard_map/ppermute | solution.py:26
  97.8 3.5 %collective-permute-done.15 = bf16[128,1024]{1,0:T(8,128)(2,1)S(1)} collective-permute-done((bf16[128,1024]{1,0:T(8,128)(2,1)S(1)}, bf16[128,1024]{1,0:T(8,128)(2,1)S(1)}, u32[]{:S(2)}, u32[]{:S(2)}) %collective-permute-start.15) | collective-permute-done | bytes 262176 | tf_op jit(solution)/shard_map/ppermute | solution.py:26
  101.3 0.2 fusion.46
  101.6 3.2 %collective-permute-start.16 = (bf16[128,1024]{1,0:T(8,128)(2,1)S(1)}, bf16[128,1024]{1,0:T(8,128)(2,1)S(1)}, u32[]{:S(2)}, u32[]{:S(2)}) collective-permute-start(bf16[128,1024]{1,0:T(8,128)(2,1)S(1)} %get-tuple-element.23), channel_id=1, source_target_pairs={{0,14},{1,15},{2,0},{3,1},{4,2},{5,3},{6,4},{7,5},{8,6},{9,7},{10,... | collective-permute-start | bytes 786440 | tf_op jit(solution)/shard_map/ppermute | solution.py:26
  104.8 1.5 %fusion.75 = (f32[1,384,512]{2,1,0:T(8,128)}, bf16[384,512]{1,0:T(8,128)(2,1)S(1)}) fusion(f32[384,512]{1,0:T(8,128)S(1)} %get-tuple-element.6, f32[1,384,512]{2,1,0:T(8,128)S(1)} %copy-done.4, f32[384,512]{1,0:T(8,128)S(1)} %copy-done.3, f32[1,384,512]{2,1,0:T(8,128)S(1)} %copy-done.2, f32[1,384,512]{2,1,0:T(8,128)S(1)} %copy-done), kind=kLoop, calls=%fused_computation.117 | loop fusion | flops 3342336 | bytes 5111808 | tf_op jit(solution)/shard_map/broadcast_in_dim | solution.py:152
  106.4 0.1 fusion.42
  106.5 2.7 %collective-permute-done.12 = bf16[128,1024]{1,0:T(8,128)(2,1)S(1)} collective-permute-done((bf16[128,1024]{1,0:T(8,128)(2,1)S(1)}, bf16[128,1024]{1,0:T(8,128)(2,1)S(1)}, u32[]{:S(2)}, u32[]{:S(2)}) %collective-permute-start.12) | collective-permute-done | bytes 262176 | tf_op jit(solution)/shard_map/ppermute | solution.py:25
  109.1 0.1 fusion.49
  109.3 0.7 fusion.32
  110.0 0.4 collective-permute-start.25
  110.6 2.7 %collective-permute-start.8 = (bf16[384,512]{1,0:T(8,128)(2,1)S(1)}, bf16[384,512]{1,0:T(8,128)(2,1)S(1)}, u32[]{:S(2)}, u32[]{:S(2)}) collective-permute-start(bf16[384,512]{1,0:T(8,128)(2,1)S(1)} %add_convert_fusion), channel_id=1, source_target_pairs={{0,128},{64,192},{128,0},{192,64},{1,129},{65,193},{129,1},{193,65... | collective-permute-start | bytes 1179656 | tf_op jit(solution)/shard_map/ppermute | solution.py:147
  113.2 6.3 %collective-permute-done.25 = bf16[64,2048]{1,0:T(8,128)(2,1)} collective-permute-done((bf16[64,2048]{1,0:T(8,128)(2,1)}, bf16[64,2048]{1,0:T(8,128)(2,1)}, u32[]{:S(2)}, u32[]{:S(2)}) %collective-permute-start.25) | collective-permute-done | bytes 262176 | tf_op jit(solution)/shard_map/ppermute | solution.py:57
  119.6 1.7 %fusion.74 = bf16[1,64,2048]{2,1,0:T(8,128)(2,1)} fusion(bf16[64,2048]{1,0:T(8,128)(2,1)} %collective-permute-done.25, s32[]{:T(128)S(6)} %select_n.179, f32[128,1024]{1,0:T(8,128)S(1)} %fusion.42, f32[128,1024]{1,0:T(8,128)S(1)} %fusion.49), kind=kLoop, calls=%fused_computation.114 | loop fusion | flops 524288 | bytes 1572868 | tf_op jit(solution)/shard_map/broadcast_in_dim | solution.py:152
  121.3 4.5 %collective-permute-done.8 = bf16[384,512]{1,0:T(8,128)(2,1)S(1)} collective-permute-done((bf16[384,512]{1,0:T(8,128)(2,1)S(1)}, bf16[384,512]{1,0:T(8,128)(2,1)S(1)}, u32[]{:S(2)}, u32[]{:S(2)}) %collective-permute-start.8) | collective-permute-done | bytes 393248 | tf_op jit(solution)/shard_map/ppermute | solution.py:147
  125.7 1.4 %multiply_subtract_fusion = (f32[384,512]{1,0:T(8,128)}, f32[384,512]{1,0:T(8,128)}) fusion(f32[384,512]{1,0:T(8,128)S(1)} %copy-done.3, bf16[384,512]{1,0:T(8,128)(2,1)S(1)} %collective-permute-done.8, bf16[384,512]{1,0:T(8,128)(2,1)S(1)} %add_convert_fusion, f32[384,512]{1,0:T(8,128)S(1)} %copy-done.5), kind=kLoop, calls=%fused_computation.47 | loop fusion | flops 1966080 | bytes 3932160 | tf_op jit(solution)/shard_map/sub | solution.py:151
  (45 shorter events, 1.1 us)
Async XLA Ops:
  0.6 2.4 %copy-start = (f32[1,384,512]{2,1,0:T(8,128)S(1)}, f32[1,384,512]{2,1,0:T(8,128)}, u32[]{:S(2)}) copy-start(f32[1,384,512]{2,1,0:T(8,128)} %param.13) | copy-start | bytes 2359300
  4.3 29.1 %collective-permute-start = (bf16[512,1152]{0,1:T(8,128)(2,1)}, bf16[512,1152]{0,1:T(8,128)(2,1)S(1)}, u32[]{:S(2)}, u32[]{:S(2)}) collective-permute-start(bf16[512,1152]{0,1:T(8,128)(2,1)} %pad_maximum_fusion), channel_id=1, source_target_pairs={{0,16},{16,32},{32,48},{48,0},{1,17},{17,33},{33,49},{49,1},{2,18}... | collective-permute-start | bytes 3538952 | tf_op jit(solution)/shard_map/ppermute | solution.py:84
  5.7 28.0 %collective-permute-start.1 = (bf16[512,1152]{0,1:T(8,128)(2,1)}, bf16[512,1152]{0,1:T(8,128)(2,1)}, u32[]{:S(2)}, u32[]{:S(2)}) collective-permute-start(bf16[512,1152]{0,1:T(8,128)(2,1)} %pad_maximum_fusion), channel_id=1, source_target_pairs={{0,48},{16,0},{32,16},{48,32},{1,49},{17,1},{33,17},{49,33},{2,50}... | collective-permute-start | bytes 3538952 | tf_op jit(solution)/shard_map/ppermute | solution.py:85
  7.5 2.2 %copy-start.6 = (bf16[1,1024,2048]{2,1,0:T(8,128)(2,1)S(1)}, bf16[1,1024,2048]{2,1,0:T(8,128)(2,1)}, u32[]{:S(2)}) copy-start(bf16[1,1024,2048]{2,1,0:T(8,128)(2,1)} %param.9) | copy-start | bytes 12582916
  9.7 2.2 %copy-start.1 = (bf16[1,1024,2048]{2,1,0:T(8,128)(2,1)S(1)}, bf16[1,1024,2048]{2,1,0:T(8,128)(2,1)}, u32[]{:S(2)}) copy-start(bf16[1,1024,2048]{2,1,0:T(8,128)(2,1)} %param.10) | copy-start | bytes 12582916
  33.4 15.5 %collective-permute-start.2 = (bf16[256,1152]{0,1:T(8,128)(2,1)S(1)}, bf16[256,1152]{0,1:T(8,128)(2,1)S(1)}, u32[]{:S(2)}, u32[]{:S(2)}) collective-permute-start(bf16[256,1152]{0,1:T(8,128)(2,1)S(1)} %slice.85), channel_id=1, source_target_pairs={{0,16},{16,32},{32,48},{48,0},{1,17},{17,33},{33,49},{49,1},{2,18}... | collective-permute-start | bytes 1769480 | tf_op jit(solution)/shard_map/ppermute | solution.py:86
  34.9 15.1 %collective-permute-start.3 = (bf16[256,1152]{0,1:T(8,128)(2,1)S(1)}, bf16[256,1152]{0,1:T(8,128)(2,1)S(1)}, u32[]{:S(2)}, u32[]{:S(2)}) collective-permute-start(bf16[256,1152]{0,1:T(8,128)(2,1)S(1)} %slice.87), channel_id=1, source_target_pairs={{0,48},{16,0},{32,16},{48,32},{1,49},{17,1},{33,17},{49,33},{2,50}... | collective-permute-start | bytes 1769480 | tf_op jit(solution)/shard_map/ppermute | solution.py:87
  56.7 10.0 %collective-permute-start.17 = (bf16[128,512]{1,0:T(8,128)(2,1)S(1)}, bf16[128,512]{1,0:T(8,128)(2,1)S(1)}, u32[]{:S(2)}, u32[]{:S(2)}) collective-permute-start(bf16[128,512]{1,0:T(8,128)(2,1)S(1)} %get-tuple-element.30), channel_id=1, source_target_pairs={{0,2},{1,3},{2,4},{3,5},{4,6},{5,7},{6,8},{7,9},{8,10},{9,11},{10,... | collective-permute-start | bytes 393224 | tf_op jit(solution)/shard_map/ppermute | solution.py:25
  58.7 8.1 %collective-permute-start.21 = (bf16[128,512]{1,0:T(8,128)(2,1)S(1)}, bf16[128,512]{1,0:T(8,128)(2,1)S(1)}, u32[]{:S(2)}, u32[]{:S(2)}) collective-permute-start(bf16[128,512]{1,0:T(8,128)(2,1)S(1)} %get-tuple-element.31), channel_id=1, source_target_pairs={{0,14},{1,15},{2,0},{3,1},{4,2},{5,3},{6,4},{7,5},{8,6},{9,7},{10,... | collective-permute-start | bytes 393224 | tf_op jit(solution)/shard_map/ppermute | solution.py:26
  62.8 7.4 %collective-permute-start.13 = (bf16[128,512]{1,0:T(8,128)(2,1)S(1)}, bf16[128,512]{1,0:T(8,128)(2,1)S(1)}, u32[]{:S(2)}, u32[]{:S(2)}) collective-permute-start(bf16[128,512]{1,0:T(8,128)(2,1)S(1)} %get-tuple-element.33), channel_id=1, source_target_pairs={{0,14},{1,15},{2,0},{3,1},{4,2},{5,3},{6,4},{7,5},{8,6},{9,7},{10,... | collective-permute-start | bytes 393224 | tf_op jit(solution)/shard_map/ppermute | solution.py:26
  64.8 7.6 %collective-permute-start.9 = (bf16[128,512]{1,0:T(8,128)(2,1)S(1)}, bf16[128,512]{1,0:T(8,128)(2,1)S(1)}, u32[]{:S(2)}, u32[]{:S(2)}) collective-permute-start(bf16[128,512]{1,0:T(8,128)(2,1)S(1)} %get-tuple-element.32), channel_id=1, source_target_pairs={{0,2},{1,3},{2,4},{3,5},{4,6},{5,7},{6,8},{7,9},{8,10},{9,11},{10,... | collective-permute-start | bytes 393224 | tf_op jit(solution)/shard_map/ppermute | solution.py:25
  66.9 10.9 %collective-permute-start.18 = (bf16[128,1024]{1,0:T(8,128)(2,1)S(1)}, bf16[128,1024]{1,0:T(8,128)(2,1)S(1)}, u32[]{:S(2)}, u32[]{:S(2)}) collective-permute-start(bf16[128,1024]{1,0:T(8,128)(2,1)S(1)} %get-tuple-element.20), channel_id=1, source_target_pairs={{0,2},{1,3},{2,4},{3,5},{4,6},{5,7},{6,8},{7,9},{8,10},{9,11},{10,... | collective-permute-start | bytes 786440 | tf_op jit(solution)/shard_map/ppermute | solution.py:25
  67.0 13.8 %collective-permute-start.22 = (bf16[128,1024]{1,0:T(8,128)(2,1)S(1)}, bf16[128,1024]{1,0:T(8,128)(2,1)S(1)}, u32[]{:S(2)}, u32[]{:S(2)}) collective-permute-start(bf16[128,1024]{1,0:T(8,128)(2,1)S(1)} %get-tuple-element.21), channel_id=1, source_target_pairs={{0,14},{1,15},{2,0},{3,1},{4,2},{5,3},{6,4},{7,5},{8,6},{9,7},{10,... | collective-permute-start | bytes 786440 | tf_op jit(solution)/shard_map/ppermute | solution.py:26
  72.5 8.6 %collective-permute-start.10 = (bf16[128,1024]{1,0:T(8,128)(2,1)S(1)}, bf16[128,1024]{1,0:T(8,128)(2,1)S(1)}, u32[]{:S(2)}, u32[]{:S(2)}) collective-permute-start(bf16[128,1024]{1,0:T(8,128)(2,1)S(1)} %get-tuple-element.26), channel_id=1, source_target_pairs={{0,2},{1,3},{2,4},{3,5},{4,6},{5,7},{6,8},{7,9},{8,10},{9,11},{10,... | collective-permute-start | bytes 786440 | tf_op jit(solution)/shard_map/ppermute | solution.py:25
  72.6 8.6 %collective-permute-start.14 = (bf16[128,1024]{1,0:T(8,128)(2,1)S(1)}, bf16[128,1024]{1,0:T(8,128)(2,1)S(1)}, u32[]{:S(2)}, u32[]{:S(2)}) collective-permute-start(bf16[128,1024]{1,0:T(8,128)(2,1)S(1)} %get-tuple-element.27), channel_id=1, source_target_pairs={{0,14},{1,15},{2,0},{3,1},{4,2},{5,3},{6,4},{7,5},{8,6},{9,7},{10,... | collective-permute-start | bytes 786440 | tf_op jit(solution)/shard_map/ppermute | solution.py:26
  76.0 17.1 %copy-start.2 = (f32[1,384,512]{2,1,0:T(8,128)S(1)}, f32[1,384,512]{2,1,0:T(8,128)}, u32[]{:S(2)}) copy-start(f32[1,384,512]{2,1,0:T(8,128)} %param.15) | copy-start | bytes 2359300
  76.0 11.8 %collective-permute-start.4 = (bf16[384,512]{1,0:T(8,128)(2,1)S(1)}, bf16[384,512]{1,0:T(8,128)(2,1)S(1)}, u32[]{:S(2)}, u32[]{:S(2)}) collective-permute-start(bf16[384,512]{1,0:T(8,128)(2,1)S(1)} %get-tuple-element.13), channel_id=1, source_target_pairs={{0,16},{16,32},{32,48},{48,0},{1,17},{17,33},{33,49},{49,1},{2,18}... | collective-permute-start | bytes 1179656 | tf_op jit(solution)/shard_map/ppermute | solution.py:126
  77.8 14.2 %collective-permute-start.5 = (bf16[384,512]{1,0:T(8,128)(2,1)S(1)}, bf16[384,512]{1,0:T(8,128)(2,1)S(1)}, u32[]{:S(2)}, u32[]{:S(2)}) collective-permute-start(bf16[384,512]{1,0:T(8,128)(2,1)S(1)} %get-tuple-element.15), channel_id=1, source_target_pairs={{0,32},{16,48},{32,0},{48,16},{1,33},{17,49},{33,1},{49,17},{2,34}... | collective-permute-start | bytes 1179656 | tf_op jit(solution)/shard_map/ppermute | solution.py:126
  80.8 12.3 %collective-permute-start.6 = (bf16[384,512]{1,0:T(8,128)(2,1)S(1)}, bf16[384,512]{1,0:T(8,128)(2,1)S(1)}, u32[]{:S(2)}, u32[]{:S(2)}) collective-permute-start(bf16[384,512]{1,0:T(8,128)(2,1)S(1)} %get-tuple-element.14), channel_id=1, source_target_pairs={{0,48},{16,0},{32,16},{48,32},{1,49},{17,1},{33,17},{49,33},{2,50}... | collective-permute-start | bytes 1179656 | tf_op jit(solution)/shard_map/ppermute | solution.py:126
  81.1 13.1 %collective-permute-start.19 = (bf16[128,1024]{1,0:T(8,128)(2,1)S(1)}, bf16[128,1024]{1,0:T(8,128)(2,1)S(1)}, u32[]{:S(2)}, u32[]{:S(2)}) collective-permute-start(bf16[128,1024]{1,0:T(8,128)(2,1)S(1)} %get-tuple-element.18), channel_id=1, source_target_pairs={{0,2},{1,3},{2,4},{3,5},{4,6},{5,7},{6,8},{7,9},{8,10},{9,11},{10,... | collective-permute-start | bytes 786440 | tf_op jit(solution)/shard_map/ppermute | solution.py:25
  81.2 13.0 %collective-permute-start.23 = (bf16[128,1024]{1,0:T(8,128)(2,1)S(1)}, bf16[128,1024]{1,0:T(8,128)(2,1)S(1)}, u32[]{:S(2)}, u32[]{:S(2)}) collective-permute-start(bf16[128,1024]{1,0:T(8,128)(2,1)S(1)} %get-tuple-element.19), channel_id=1, source_target_pairs={{0,14},{1,15},{2,0},{3,1},{4,2},{5,3},{6,4},{7,5},{8,6},{9,7},{10,... | collective-permute-start | bytes 786440 | tf_op jit(solution)/shard_map/ppermute | solution.py:26
  87.8 10.0 %collective-permute-start.11 = (bf16[128,1024]{1,0:T(8,128)(2,1)S(1)}, bf16[128,1024]{1,0:T(8,128)(2,1)S(1)}, u32[]{:S(2)}, u32[]{:S(2)}) collective-permute-start(bf16[128,1024]{1,0:T(8,128)(2,1)S(1)} %get-tuple-element.24), channel_id=1, source_target_pairs={{0,2},{1,3},{2,4},{3,5},{4,6},{5,7},{6,8},{7,9},{8,10},{9,11},{10,... | collective-permute-start | bytes 786440 | tf_op jit(solution)/shard_map/ppermute | solution.py:25
  92.0 9.2 %collective-permute-start.15 = (bf16[128,1024]{1,0:T(8,128)(2,1)S(1)}, bf16[128,1024]{1,0:T(8,128)(2,1)S(1)}, u32[]{:S(2)}, u32[]{:S(2)}) collective-permute-start(bf16[128,1024]{1,0:T(8,128)(2,1)S(1)} %get-tuple-element.25), channel_id=1, source_target_pairs={{0,14},{1,15},{2,0},{3,1},{4,2},{5,3},{6,4},{7,5},{8,6},{9,7},{10,... | collective-permute-start | bytes 786440 | tf_op jit(solution)/shard_map/ppermute | solution.py:26
  94.3 10.5 %copy-start.3 = (f32[384,512]{1,0:T(8,128)S(1)}, f32[384,512]{1,0:T(8,128)}, u32[]{:S(2)}) copy-start(f32[384,512]{1,0:T(8,128)} %param.16) | copy-start | bytes 2359300
  94.3 10.5 %copy-start.4 = (f32[1,384,512]{2,1,0:T(8,128)S(1)}, f32[1,384,512]{2,1,0:T(8,128)}, u32[]{:S(2)}) copy-start(f32[1,384,512]{2,1,0:T(8,128)} %param.14) | copy-start | bytes 2359300
  94.5 11.9 %collective-permute-start.20 = (bf16[128,1024]{1,0:T(8,128)(2,1)S(1)}, bf16[128,1024]{1,0:T(8,128)(2,1)S(1)}, u32[]{:S(2)}, u32[]{:S(2)}) collective-permute-start(bf16[128,1024]{1,0:T(8,128)(2,1)S(1)} %get-tuple-element.16), channel_id=1, source_target_pairs={{0,2},{1,3},{2,4},{3,5},{4,6},{5,7},{6,8},{7,9},{8,10},{9,11},{10,... | collective-permute-start | bytes 786440 | tf_op jit(solution)/shard_map/ppermute | solution.py:25
  95.6 10.8 %collective-permute-start.24 = (bf16[128,1024]{1,0:T(8,128)(2,1)S(1)}, bf16[128,1024]{1,0:T(8,128)(2,1)S(1)}, u32[]{:S(2)}, u32[]{:S(2)}) collective-permute-start(bf16[128,1024]{1,0:T(8,128)(2,1)S(1)} %get-tuple-element.17), channel_id=1, source_target_pairs={{0,14},{1,15},{2,0},{3,1},{4,2},{5,3},{6,4},{7,5},{8,6},{9,7},{10,... | collective-permute-start | bytes 786440 | tf_op jit(solution)/shard_map/ppermute | solution.py:26
  101.5 7.7 %collective-permute-start.12 = (bf16[128,1024]{1,0:T(8,128)(2,1)S(1)}, bf16[128,1024]{1,0:T(8,128)(2,1)S(1)}, u32[]{:S(2)}, u32[]{:S(2)}) collective-permute-start(bf16[128,1024]{1,0:T(8,128)(2,1)S(1)} %get-tuple-element.22), channel_id=1, source_target_pairs={{0,2},{1,3},{2,4},{3,5},{4,6},{5,7},{6,8},{7,9},{8,10},{9,11},{10,... | collective-permute-start | bytes 786440 | tf_op jit(solution)/shard_map/ppermute | solution.py:25
  101.6 7.6 %collective-permute-start.16 = (bf16[128,1024]{1,0:T(8,128)(2,1)S(1)}, bf16[128,1024]{1,0:T(8,128)(2,1)S(1)}, u32[]{:S(2)}, u32[]{:S(2)}) collective-permute-start(bf16[128,1024]{1,0:T(8,128)(2,1)S(1)} %get-tuple-element.23), channel_id=1, source_target_pairs={{0,14},{1,15},{2,0},{3,1},{4,2},{5,3},{6,4},{7,5},{8,6},{9,7},{10,... | collective-permute-start | bytes 786440 | tf_op jit(solution)/shard_map/ppermute | solution.py:26
  106.3 4.1 %collective-permute-start.7 = (bf16[384,512]{1,0:T(8,128)(2,1)S(1)}, bf16[384,512]{1,0:T(8,128)(2,1)S(1)}, u32[]{:S(2)}, u32[]{:S(2)}) collective-permute-start(bf16[384,512]{1,0:T(8,128)(2,1)S(1)} %get-tuple-element.29), channel_id=1, source_target_pairs={{0,64},{64,0},{128,192},{192,128},{1,65},{65,1},{129,193},{193,129... | collective-permute-start | bytes 1179656 | tf_op jit(solution)/shard_map/ppermute | solution.py:147
  109.3 16.5 %copy-start.5 = (f32[384,512]{1,0:T(8,128)S(1)}, f32[384,512]{1,0:T(8,128)}, u32[]{:S(2)}) copy-start(f32[384,512]{1,0:T(8,128)} %param.17) | copy-start | bytes 2359300
  110.0 9.6 %collective-permute-start.25 = (bf16[64,2048]{1,0:T(8,128)(2,1)}, bf16[64,2048]{1,0:T(8,128)(2,1)}, u32[]{:S(2)}, u32[]{:S(2)}) collective-permute-start(bf16[64,2048]{1,0:T(8,128)(2,1)} %fusion.32), channel_id=1, source_target_pairs={{0,1},{1,0},{2,3},{3,2},{4,5},{5,4},{6,7},{7,6},{8,9},{9,8},{10,11... | collective-permute-start | bytes 786440 | tf_op jit(solution)/shard_map/ppermute | solution.py:57
  110.6 15.2 %collective-permute-start.8 = (bf16[384,512]{1,0:T(8,128)(2,1)S(1)}, bf16[384,512]{1,0:T(8,128)(2,1)S(1)}, u32[]{:S(2)}, u32[]{:S(2)}) collective-permute-start(bf16[384,512]{1,0:T(8,128)(2,1)S(1)} %add_convert_fusion), channel_id=1, source_target_pairs={{0,128},{64,192},{128,0},{192,64},{1,129},{65,193},{129,1},{193,65... | collective-permute-start | bytes 1179656 | tf_op jit(solution)/shard_map/ppermute | solution.py:147

commit v9 on v8

--- a/solution.py
+++ b/solution.py
@@ -35,7 +35,7 @@
     return own_a + got_a + got_b
 
 
-def _ring_reduce_scatter(part):
+def _ring_reduce_scatter(part, sync):
     nmp = lax.axis_size("mp")
     m = lax.axis_index("mp")
     nlo = 2
@@ -54,8 +54,9 @@
     )
     mine = lax.dynamic_slice_in_dim(acc, lo * sub, sub, axis=0)
     other = lax.dynamic_slice_in_dim(acc, (1 - lo) * sub, sub, axis=0)
+    other, sync = lax.optimization_barrier((other, sync))
     got = lax.ppermute(other.astype(jnp.bfloat16), "mp", [(i, i ^ 1) for i in range(nmp)])
-    return (mine + got.astype(jnp.float32)).astype(jnp.bfloat16)
+    return (mine + got.astype(jnp.float32)).astype(jnp.bfloat16), sync
 
 
 def shards(
@@ -130,7 +131,6 @@
     partial_sum = lax.dot_general(
         both, weights_full, (((1,), (1,)), ((), ())), preferred_element_type=jnp.float32
     )
-    input_grad = _ring_reduce_scatter(partial_sum.astype(jnp.bfloat16))
 
     first_new = 0.9 * first_moment[0] + 0.1 * grad_down
     second_new = 0.999 * second_moment[0] + 0.001 * grad_down * grad_down
@@ -146,6 +146,7 @@
         mine = total.astype(jnp.bfloat16)
         total = mine.astype(jnp.float32) + lax.ppermute(mine, "outer", perm).astype(jnp.float32)
         step *= 2
+    input_grad, total = _ring_reduce_scatter(partial_sum.astype(jnp.bfloat16), total)
     mean_drift = total / nout
     momentum_out = 0.9 * outer_momentum + mean_drift
     new_params = anchor - 0.7 * (mean_drift + 0.9 * momentum_out)

time: 128 us -> 122 us (0.953)
  waiting for transfers between devices: 53.2 us -> 49.4 us
  other arithmetic: 9.15 us -> 7.64 us
    ppermute x2, waiting for transfers between devices: 4.47 us -> 2.02 us  [shards(): lax.ppermute(mine, 'outer', perm).astype(jnp.float32)]
    ppermute x8, starting transfers between devices: 21.4 us -> 19.5 us  [_z_reduce_scatter(): lax.ppermute(send_b.astype(jnp.bfloat16), 'mp', down).astype(jnp.float32)]
    ppermute x8, starting transfers between devices: 3.53 us -> 5.49 us  [_z_reduce_scatter(): lax.ppermute(send_a.astype(jnp.bfloat16), 'mp', up).astype(jnp.float32)]
    ppermute x1, waiting for transfers between devices: 6.33 us -> 4.47 us  [_ring_reduce_scatter(): lax.ppermute(other.astype(jnp.bfloat16), 'mp', [(i, i ^ 1) for i in range...]
    ppermute x8, waiting for transfers between devices: 5.98 us -> 4.66 us  [_z_reduce_scatter(): lax.ppermute(send_a.astype(jnp.bfloat16), 'mp', up).astype(jnp.float32)]
  transfers between devices with their start and end apart: 26 -> 26, of which waited for: 11 -> 12; matrix products, arithmetic and copies ran while one was open for 15% -> 15% of each run, Pallas kernels for 0% -> 0%
where the time goes in v9:
time: 122 us
  waiting for transfers between devices  49.4 us (40%)
  starting transfers between devices  38.6 us (32%)
  matrix products  16 us (13%)
  local copies, waits for them, and re-layouts  8.98 us (7%)
  other arithmetic  7.64 us (6%)
    ppermute x1, waiting for transfers between devices, shards(): from_left = lax.ppermute(shard, 'dp', _shift(ndp, 1))  20.9 us
    ppermute x8, starting transfers between devices, _z_reduce_scatter(): lax.ppermute(send_b.astype(jnp.bfloat16), 'mp', down).astype(jnp.float32)  19.5 us
    ppermute x3, waiting for transfers between devices, shards(): got = lax.ppermute(blk.astype(jnp.bfloat16), 'dp', _shift(ndp, s))  8.68 us
    dot_general x5, matrix products, shards(): p1 = jnp.dot(xs, piece[:, :2 * ff], preferred_element_type=jnp.float32)  5.88 us
    ppermute x8, starting transfers between devices, _z_reduce_scatter(): lax.ppermute(send_a.astype(jnp.bfloat16), 'mp', up).astype(jnp.float32)  5.49 us
    unnamed x16, local copies, waits for them, and re-layouts  5.29 us
    ppermute x8, waiting for transfers between devices, _z_reduce_scatter(): lax.ppermute(send_b.astype(jnp.bfloat16), 'mp', down).astype(jnp.float32)  4.68 us
    ppermute x8, waiting for transfers between devices, _z_reduce_scatter(): lax.ppermute(send_a.astype(jnp.bfloat16), 'mp', up).astype(jnp.float32)  4.66 us
  transfers between devices with their start and end apart: 26, of which 12 were waited for; matrix products, arithmetic and copies ran while one was open for 15% of the time, Pallas kernels for 0%

profile of v9, /device:TPU:8, one launch (start us, length us, event | category | flops | bytes accessed | tf_op | source)
XLA Modules:
  0.0 121.7 jit_solution(16588277076501185745)
XLA Ops:
  0.6 1.2 %copy.14 = bf16[1,512,384]{1,2,0:T(8,128)(2,1)S(1)} copy(bf16[1,512,384]{2,1,0:T(8,128)(2,1)} %param.11) | data formatting | bytes 786432 | tf_op args[2]
  1.9 1.2 copy.15
  3.1 1.1 pad_maximum_fusion
  4.3 1.5 %collective-permute-start = (bf16[512,1152]{0,1:T(8,128)(2,1)}, bf16[512,1152]{0,1:T(8,128)(2,1)S(1)}, u32[]{:S(2)}, u32[]{:S(2)}) collective-permute-start(bf16[512,1152]{0,1:T(8,128)(2,1)} %pad_maximum_fusion), channel_id=1, source_target_pairs={{0,16},{16,32},{32,48},{48,0},{1,17},{17,33},{33,49},{49,1},{2,18}... | collective-permute-start | bytes 3538952 | tf_op jit(solution)/shard_map/ppermute | solution.py:85
  5.7 1.7 %collective-permute-start.1 = (bf16[512,1152]{0,1:T(8,128)(2,1)}, bf16[512,1152]{0,1:T(8,128)(2,1)}, u32[]{:S(2)}, u32[]{:S(2)}) collective-permute-start(bf16[512,1152]{0,1:T(8,128)(2,1)} %pad_maximum_fusion), channel_id=1, source_target_pairs={{0,48},{16,0},{32,16},{48,32},{1,49},{17,1},{33,17},{49,33},{2,50}... | collective-permute-start | bytes 3538952 | tf_op jit(solution)/shard_map/ppermute | solution.py:86
  7.5 0.4 broadcast_in_dim.12
  8.0 1.7 %copy-done.6 = bf16[1,1024,2048]{2,1,0:T(8,128)(2,1)S(1)} copy-done((bf16[1,1024,2048]{2,1,0:T(8,128)(2,1)S(1)}, bf16[1,1024,2048]{2,1,0:T(8,128)(2,1)}, u32[]{:S(2)}) %copy-start.6) | copy-done | bytes 4194328
  9.7 1.0 fusion.10
  10.7 1.2 copy-done.1
  11.9 0.6 fusion.16
  12.5 20.9 %collective-permute-done = bf16[512,1152]{0,1:T(8,128)(2,1)S(1)} collective-permute-done((bf16[512,1152]{0,1:T(8,128)(2,1)}, bf16[512,1152]{0,1:T(8,128)(2,1)S(1)}, u32[]{:S(2)}, u32[]{:S(2)}) %collective-permute-start) | collective-permute-done | bytes 1179680 | tf_op jit(solution)/shard_map/ppermute | solution.py:85
  33.4 0.4 collective-permute-start.2
  33.8 1.1 slice.87
  34.9 3.2 %collective-permute-start.3 = (bf16[256,1152]{0,1:T(8,128)(2,1)S(1)}, bf16[256,1152]{0,1:T(8,128)(2,1)S(1)}, u32[]{:S(2)}, u32[]{:S(2)}) collective-permute-start(bf16[256,1152]{0,1:T(8,128)(2,1)S(1)} %slice.87), channel_id=1, source_target_pairs={{0,48},{16,0},{32,16},{48,32},{1,49},{17,1},{33,17},{49,33},{2,50}... | collective-permute-start | bytes 1769480 | tf_op jit(solution)/shard_map/ppermute | solution.py:88
  38.1 2.2 %fusion.6 = f32[1024,768]{0,1:T(8,128)S(1)} fusion(bf16[1,1024,2048]{2,1,0:T(8,128)(2,1)S(1)} %copy-done.6, s32[]{:T(128)S(6)} %select_n.155, bf16[512,1152]{0,1:T(8,128)(2,1)} %collective-permute-done.1), kind=kOutput, calls=%fused_computation.19 | convolution fusion | flops 805306368 | bytes 4980740 | tf_op jit(solution)/shard_map/dot_general | solution.py:104
  40.3 1.6 %fusion.12 = f32[1024,384]{0,1:T(8,128)S(1)} fusion(bf16[1,1024,2048]{2,1,0:T(8,128)(2,1)S(1)} %copy-done.1, s32[]{:T(128)S(6)} %select_n.155, bf16[512,1152]{0,1:T(8,128)(2,1)} %collective-permute-done.1), kind=kOutput, calls=%fused_computation.25 | convolution fusion | flops 402653184 | bytes 3014660 | tf_op jit(solution)/shard_map/dot_general | solution.py:105
  41.9 0.6 fusion.14
  42.6 1.2 %slice_dynamic-update-slice_fusion = bf16[2048,768]{0,1:T(8,128)(2,1)S(1)} fusion(bf16[2048,768]{0,1:T(8,128)(2,1)S(1)} %slice_dynamic-update-slice_fusion.1, s32[]{:T(128)S(6)} %select_n.155, bf16[512,1152]{0,1:T(8,128)(2,1)} %collective-permute-done.1), kind=kLoop, calls=%fused_computation.55 | loop fusion | bytes 1572868 | tf_op jit(solution)/shard_map/dynamic_update_slice | solution.py:108
  43.9 1.0 fusion.8
  44.9 4.0 %collective-permute-done.2 = bf16[256,1152]{0,1:T(8,128)(2,1)S(1)} collective-permute-done((bf16[256,1152]{0,1:T(8,128)(2,1)S(1)}, bf16[256,1152]{0,1:T(8,128)(2,1)S(1)}, u32[]{:S(2)}, u32[]{:S(2)}) %collective-permute-start.2) | collective-permute-done | bytes 589856 | tf_op jit(solution)/shard_map/ppermute | solution.py:87
  49.0 0.4 fusion.59
  49.4 0.6 fusion.53
  50.1 1.1 add_add_fusion
  51.1 1.2 multiply_convert_fusion.2
  52.3 3.8 %convolution_convert_fusion = bf16[1024,2048]{1,0:T(8,128)(2,1)S(1)} fusion(bf16[2048,768]{0,1:T(8,128)(2,1)S(1)} %slice_dynamic-update-slice_fusion.2, bf16[1024,384]{0,1:T(8,128)(2,1)S(1)} %get-tuple-element.14, bf16[1024,384]{0,1:T(8,128)(2,1)S(1)} %get-tuple-element.13), kind=kOutput, calls=%fused_computation.2 | convolution fusion | flops 3226468352 | bytes 8912896 | tf_op jit(solution)/shard_map/dot_general | solution.py:131
  56.1 0.5 fusion.92
  56.7 2.0 %collective-permute-start.12 = (bf16[128,512]{1,0:T(8,128)(2,1)S(1)}, bf16[128,512]{1,0:T(8,128)(2,1)S(1)}, u32[]{:S(2)}, u32[]{:S(2)}) collective-permute-start(bf16[128,512]{1,0:T(8,128)(2,1)S(1)} %get-tuple-element.34), channel_id=1, source_target_pairs={{0,2},{1,3},{2,4},{3,5},{4,6},{5,7},{6,8},{7,9},{8,10},{9,11},{10,... | collective-permute-start | bytes 393224 | tf_op jit(solution)/shard_map/ppermute | solution.py:25
  58.7 4.0 %collective-permute-start.16 = (bf16[128,512]{1,0:T(8,128)(2,1)S(1)}, bf16[128,512]{1,0:T(8,128)(2,1)S(1)}, u32[]{:S(2)}, u32[]{:S(2)}) collective-permute-start(bf16[128,512]{1,0:T(8,128)(2,1)S(1)} %get-tuple-element.35), channel_id=1, source_target_pairs={{0,14},{1,15},{2,0},{3,1},{4,2},{5,3},{6,4},{7,5},{8,6},{9,7},{10,... | collective-permute-start | bytes 393224 | tf_op jit(solution)/shard_map/ppermute | solution.py:26
  62.9 3.2 %collective-permute-start.8 = (bf16[128,512]{1,0:T(8,128)(2,1)S(1)}, bf16[128,512]{1,0:T(8,128)(2,1)S(1)}, u32[]{:S(2)}, u32[]{:S(2)}) collective-permute-start(bf16[128,512]{1,0:T(8,128)(2,1)S(1)} %get-tuple-element.37), channel_id=1, source_target_pairs={{0,14},{1,15},{2,0},{3,1},{4,2},{5,3},{6,4},{7,5},{8,6},{9,7},{10,... | collective-permute-start | bytes 393224 | tf_op jit(solution)/shard_map/ppermute | solution.py:26
  66.1 1.9 %fusion = f32[384,2048]{1,0:T(8,128)S(1)} fusion(bf16[1,1024,2048]{2,1,0:T(8,128)(2,1)S(1)} %copy-done.1, f32[1024,768]{0,1:T(8,128)S(1)} %add_add_fusion), kind=kOutput, calls=%fused_computation | convolution fusion | flops 1612972032 | bytes 10485760 | tf_op jit(solution)/shard_map/dot_general | solution.py:120
  68.2 3.2 %collective-permute-start.17 = (bf16[128,1024]{1,0:T(8,128)(2,1)S(1)}, bf16[128,1024]{1,0:T(8,128)(2,1)S(1)}, u32[]{:S(2)}, u32[]{:S(2)}) collective-permute-start(bf16[128,1024]{1,0:T(8,128)(2,1)S(1)} %get-tuple-element.25), channel_id=1, source_target_pairs={{0,14},{1,15},{2,0},{3,1},{4,2},{5,3},{6,4},{7,5},{8,6},{9,7},{10,... | collective-permute-start | bytes 786440 | tf_op jit(solution)/shard_map/ppermute | solution.py:26
  71.6 3.2 %collective-permute-start.9 = (bf16[128,1024]{1,0:T(8,128)(2,1)S(1)}, bf16[128,1024]{1,0:T(8,128)(2,1)S(1)}, u32[]{:S(2)}, u32[]{:S(2)}) collective-permute-start(bf16[128,1024]{1,0:T(8,128)(2,1)S(1)} %get-tuple-element.31), channel_id=1, source_target_pairs={{0,14},{1,15},{2,0},{3,1},{4,2},{5,3},{6,4},{7,5},{8,6},{9,7},{10,... | collective-permute-start | bytes 786440 | tf_op jit(solution)/shard_map/ppermute | solution.py:26
  74.8 0.2 dynamic-slice_convert_fusion.2
  75.0 0.7 collective-permute-start.20
  75.7 1.9 %collective-permute-done.13 = bf16[128,1024]{1,0:T(8,128)(2,1)S(1)} collective-permute-done((bf16[128,1024]{1,0:T(8,128)(2,1)S(1)}, bf16[128,1024]{1,0:T(8,128)(2,1)S(1)}, u32[]{:S(2)}, u32[]{:S(2)}) %collective-permute-start.13) | collective-permute-done | bytes 262176 | tf_op jit(solution)/shard_map/ppermute | solution.py:25
  77.6 2.1 %collective-permute-start.21 = (bf16[384,512]{1,0:T(8,128)(2,1)S(1)}, bf16[384,512]{1,0:T(8,128)(2,1)S(1)}, u32[]{:S(2)}, u32[]{:S(2)}) collective-permute-start(bf16[384,512]{1,0:T(8,128)(2,1)S(1)} %get-tuple-element.19), channel_id=1, source_target_pairs={{0,32},{16,48},{32,0},{48,16},{1,33},{17,49},{33,1},{49,17},{2,34}... | collective-permute-start | bytes 1179656 | tf_op jit(solution)/shard_map/ppermute | solution.py:127
  79.8 1.0 collective-permute-start.22
  80.8 0.2 fusion.39
  81.0 0.9 collective-permute-start.14
  81.9 2.5 %collective-permute-start.18 = (bf16[128,1024]{1,0:T(8,128)(2,1)S(1)}, bf16[128,1024]{1,0:T(8,128)(2,1)S(1)}, u32[]{:S(2)}, u32[]{:S(2)}) collective-permute-start(bf16[128,1024]{1,0:T(8,128)(2,1)S(1)} %get-tuple-element.23), channel_id=1, source_target_pairs={{0,14},{1,15},{2,0},{3,1},{4,2},{5,3},{6,4},{7,5},{8,6},{9,7},{10,... | collective-permute-start | bytes 786440 | tf_op jit(solution)/shard_map/ppermute | solution.py:26
  84.4 0.2 fusion.46
  84.6 3.7 %collective-permute-done.20 = bf16[384,512]{1,0:T(8,128)(2,1)S(1)} collective-permute-done((bf16[384,512]{1,0:T(8,128)(2,1)S(1)}, bf16[384,512]{1,0:T(8,128)(2,1)S(1)}, u32[]{:S(2)}, u32[]{:S(2)}) %collective-permute-start.20) | collective-permute-done | bytes 393248 | tf_op jit(solution)/shard_map/ppermute | solution.py:127
  88.3 4.7 %collective-permute-done.21 = bf16[384,512]{1,0:T(8,128)(2,1)S(1)} collective-permute-done((bf16[384,512]{1,0:T(8,128)(2,1)S(1)}, bf16[384,512]{1,0:T(8,128)(2,1)S(1)}, u32[]{:S(2)}, u32[]{:S(2)}) %collective-permute-start.21) | collective-permute-done | bytes 393248 | tf_op jit(solution)/shard_map/ppermute | solution.py:127
  93.0 0.2 collective-permute-done.22
  93.3 1.2 %fusion.75 = (f32[1,384,512]{2,1,0:T(8,128)}, f32[384,512]{1,0:T(8,128)S(1)}) fusion(f32[1,384,512]{2,1,0:T(8,128)S(1)} %copy-done.2, bf16[384,512]{1,0:T(8,128)(2,1)S(1)} %collective-permute-done.22, bf16[384,512]{1,0:T(8,128)(2,1)S(1)} %collective-permute-done.21, bf16[384,512]{1,0:T(8,128)(2,1)S(1)} %collective-permute-done.20, f32[384,2048]{1,0:T(8,128)S(1)} %fusion, ...), kind=kLoop, calls=%fused_computation.117 | loop fusion | flops 1966080 | bytes 4325380 | tf_op jit(solution)/shard_map/broadcast_in_dim | solution.py:153
  94.5 1.5 %fusion.74 = (f32[1,384,512]{2,1,0:T(8,128)}, bf16[384,512]{1,0:T(8,128)(2,1)S(1)}) fusion(f32[384,512]{1,0:T(8,128)S(1)} %get-tuple-element.10, f32[1,384,512]{2,1,0:T(8,128)S(1)} %copy-done.4, f32[384,512]{1,0:T(8,128)S(1)} %copy-done.3, f32[1,384,512]{2,1,0:T(8,128)S(1)} %copy-done.2, f32[1,384,512]{2,1,0:T(8,128)S(1)} %copy-done), kind=kLoop, calls=%fused_computation.116 | loop fusion | flops 3342336 | bytes 5111808 | tf_op jit(solution)/shard_map/broadcast_in_dim | solution.py:153
  96.1 0.2 fusion.38
  96.3 1.4 %collective-permute-start.15 = (bf16[128,1024]{1,0:T(8,128)(2,1)S(1)}, bf16[128,1024]{1,0:T(8,128)(2,1)S(1)}, u32[]{:S(2)}, u32[]{:S(2)}) collective-permute-start(bf16[128,1024]{1,0:T(8,128)(2,1)S(1)} %get-tuple-element.20), channel_id=1, source_target_pairs={{0,2},{1,3},{2,4},{3,5},{4,6},{5,7},{6,8},{7,9},{8,10},{9,11},{10,... | collective-permute-start | bytes 786440 | tf_op jit(solution)/shard_map/ppermute | solution.py:25
  97.7 2.2 %collective-permute-start.19 = (bf16[128,1024]{1,0:T(8,128)(2,1)S(1)}, bf16[128,1024]{1,0:T(8,128)(2,1)S(1)}, u32[]{:S(2)}, u32[]{:S(2)}) collective-permute-start(bf16[128,1024]{1,0:T(8,128)(2,1)S(1)} %get-tuple-element.21), channel_id=1, source_target_pairs={{0,14},{1,15},{2,0},{3,1},{4,2},{5,3},{6,4},{7,5},{8,6},{9,7},{10,... | collective-permute-start | bytes 786440 | tf_op jit(solution)/shard_map/ppermute | solution.py:26
  99.9 0.7 collective-permute-done.6
  100.6 0.2 fusion.45
  100.8 1.1 collective-permute-start.11
  101.9 1.0 collective-permute-start.7
  103.0 2.4 %collective-permute-start.24 = (bf16[384,512]{1,0:T(8,128)(2,1)S(1)}, bf16[384,512]{1,0:T(8,128)(2,1)S(1)}, u32[]{:S(2)}, u32[]{:S(2)}) collective-permute-start(bf16[384,512]{1,0:T(8,128)(2,1)S(1)} %add_convert_fusion), channel_id=1, source_target_pairs={{0,128},{64,192},{128,0},{192,64},{1,129},{65,193},{129,1},{193,65... | collective-permute-start | bytes 1179656 | tf_op jit(solution)/shard_map/ppermute | solution.py:147
  105.4 1.5 %collective-permute-done.15 = bf16[128,1024]{1,0:T(8,128)(2,1)S(1)} collective-permute-done((bf16[128,1024]{1,0:T(8,128)(2,1)S(1)}, bf16[128,1024]{1,0:T(8,128)(2,1)S(1)}, u32[]{:S(2)}, u32[]{:S(2)}) %collective-permute-start.15) | collective-permute-done | bytes 262176 | tf_op jit(solution)/shard_map/ppermute | solution.py:25
  106.9 0.1 fusion.41
  107.1 4.7 %collective-permute-done.11 = bf16[128,1024]{1,0:T(8,128)(2,1)S(1)} collective-permute-done((bf16[128,1024]{1,0:T(8,128)(2,1)S(1)}, bf16[128,1024]{1,0:T(8,128)(2,1)S(1)}, u32[]{:S(2)}, u32[]{:S(2)}) %collective-permute-start.11) | collective-permute-done | bytes 262176 | tf_op jit(solution)/shard_map/ppermute | solution.py:26
  111.7 0.5 collective-permute-done.7
  112.2 0.1 fusion.48
  112.4 2.0 %collective-permute-done.24 = bf16[384,512]{1,0:T(8,128)(2,1)S(1)} collective-permute-done((bf16[384,512]{1,0:T(8,128)(2,1)S(1)}, bf16[384,512]{1,0:T(8,128)(2,1)S(1)}, u32[]{:S(2)}, u32[]{:S(2)}) %collective-permute-start.24) | collective-permute-done | bytes 393248 | tf_op jit(solution)/shard_map/ppermute | solution.py:147
  114.5 0.6 collective-permute-start.25
  115.1 1.4 %multiply_subtract_fusion = (f32[384,512]{1,0:T(8,128)}, f32[384,512]{1,0:T(8,128)}) fusion(f32[384,512]{1,0:T(8,128)S(1)} %copy-done.3, f32[384,512]{1,0:T(8,128)S(1)} %convert_add_fusion, f32[384,512]{1,0:T(8,128)S(1)} %copy-done.5), kind=kLoop, calls=%fused_computation.47 | loop fusion | flops 1376256 | bytes 3932160 | tf_op jit(solution)/shard_map/sub | solution.py:152
  116.5 4.5 %collective-permute-done.25 = bf16[64,2048]{1,0:T(8,128)(2,1)S(1)} collective-permute-done((bf16[64,2048]{1,0:T(8,128)(2,1)S(1)}, bf16[64,2048]{1,0:T(8,128)(2,1)S(1)}, u32[]{:S(2)}, u32[]{:S(2)}) %collective-permute-start.25) | collective-permute-done | bytes 262176 | tf_op jit(solution)/shard_map/ppermute | solution.py:58
  121.0 0.7 fusion.73
  (46 shorter events, 1.2 us)
Async XLA Ops:
  0.6 2.4 %copy-start = (f32[1,384,512]{2,1,0:T(8,128)S(1)}, f32[1,384,512]{2,1,0:T(8,128)}, u32[]{:S(2)}) copy-start(f32[1,384,512]{2,1,0:T(8,128)} %param.13) | copy-start | bytes 2359300
  4.3 29.1 %collective-permute-start = (bf16[512,1152]{0,1:T(8,128)(2,1)}, bf16[512,1152]{0,1:T(8,128)(2,1)S(1)}, u32[]{:S(2)}, u32[]{:S(2)}) collective-permute-start(bf16[512,1152]{0,1:T(8,128)(2,1)} %pad_maximum_fusion), channel_id=1, source_target_pairs={{0,16},{16,32},{32,48},{48,0},{1,17},{17,33},{33,49},{49,1},{2,18}... | collective-permute-start | bytes 3538952 | tf_op jit(solution)/shard_map/ppermute | solution.py:85
  5.7 28.0 %collective-permute-start.1 = (bf16[512,1152]{0,1:T(8,128)(2,1)}, bf16[512,1152]{0,1:T(8,128)(2,1)}, u32[]{:S(2)}, u32[]{:S(2)}) collective-permute-start(bf16[512,1152]{0,1:T(8,128)(2,1)} %pad_maximum_fusion), channel_id=1, source_target_pairs={{0,48},{16,0},{32,16},{48,32},{1,49},{17,1},{33,17},{49,33},{2,50}... | collective-permute-start | bytes 3538952 | tf_op jit(solution)/shard_map/ppermute | solution.py:86
  7.5 2.2 %copy-start.6 = (bf16[1,1024,2048]{2,1,0:T(8,128)(2,1)S(1)}, bf16[1,1024,2048]{2,1,0:T(8,128)(2,1)}, u32[]{:S(2)}) copy-start(bf16[1,1024,2048]{2,1,0:T(8,128)(2,1)} %param.9) | copy-start | bytes 12582916
  9.7 2.2 %copy-start.1 = (bf16[1,1024,2048]{2,1,0:T(8,128)(2,1)S(1)}, bf16[1,1024,2048]{2,1,0:T(8,128)(2,1)}, u32[]{:S(2)}) copy-start(bf16[1,1024,2048]{2,1,0:T(8,128)(2,1)} %param.10) | copy-start | bytes 12582916
  33.4 15.5 %collective-permute-start.2 = (bf16[256,1152]{0,1:T(8,128)(2,1)S(1)}, bf16[256,1152]{0,1:T(8,128)(2,1)S(1)}, u32[]{:S(2)}, u32[]{:S(2)}) collective-permute-start(bf16[256,1152]{0,1:T(8,128)(2,1)S(1)} %slice.85), channel_id=1, source_target_pairs={{0,16},{16,32},{32,48},{48,0},{1,17},{17,33},{33,49},{49,1},{2,18}... | collective-permute-start | bytes 1769480 | tf_op jit(solution)/shard_map/ppermute | solution.py:87
  34.9 15.1 %collective-permute-start.3 = (bf16[256,1152]{0,1:T(8,128)(2,1)S(1)}, bf16[256,1152]{0,1:T(8,128)(2,1)S(1)}, u32[]{:S(2)}, u32[]{:S(2)}) collective-permute-start(bf16[256,1152]{0,1:T(8,128)(2,1)S(1)} %slice.87), channel_id=1, source_target_pairs={{0,48},{16,0},{32,16},{48,32},{1,49},{17,1},{33,17},{49,33},{2,50}... | collective-permute-start | bytes 1769480 | tf_op jit(solution)/shard_map/ppermute | solution.py:88
  56.7 11.3 %collective-permute-start.12 = (bf16[128,512]{1,0:T(8,128)(2,1)S(1)}, bf16[128,512]{1,0:T(8,128)(2,1)S(1)}, u32[]{:S(2)}, u32[]{:S(2)}) collective-permute-start(bf16[128,512]{1,0:T(8,128)(2,1)S(1)} %get-tuple-element.34), channel_id=1, source_target_pairs={{0,2},{1,3},{2,4},{3,5},{4,6},{5,7},{6,8},{7,9},{8,10},{9,11},{10,... | collective-permute-start | bytes 393224 | tf_op jit(solution)/shard_map/ppermute | solution.py:25
  58.7 9.3 %collective-permute-start.16 = (bf16[128,512]{1,0:T(8,128)(2,1)S(1)}, bf16[128,512]{1,0:T(8,128)(2,1)S(1)}, u32[]{:S(2)}, u32[]{:S(2)}) collective-permute-start(bf16[128,512]{1,0:T(8,128)(2,1)S(1)} %get-tuple-element.35), channel_id=1, source_target_pairs={{0,14},{1,15},{2,0},{3,1},{4,2},{5,3},{6,4},{7,5},{8,6},{9,7},{10,... | collective-permute-start | bytes 393224 | tf_op jit(solution)/shard_map/ppermute | solution.py:26
  62.8 8.6 %collective-permute-start.4 = (bf16[128,512]{1,0:T(8,128)(2,1)S(1)}, bf16[128,512]{1,0:T(8,128)(2,1)S(1)}, u32[]{:S(2)}, u32[]{:S(2)}) collective-permute-start(bf16[128,512]{1,0:T(8,128)(2,1)S(1)} %get-tuple-element.36), channel_id=1, source_target_pairs={{0,2},{1,3},{2,4},{3,5},{4,6},{5,7},{6,8},{7,9},{8,10},{9,11},{10,... | collective-permute-start | bytes 393224 | tf_op jit(solution)/shard_map/ppermute | solution.py:25
  62.9 8.5 %collective-permute-start.8 = (bf16[128,512]{1,0:T(8,128)(2,1)S(1)}, bf16[128,512]{1,0:T(8,128)(2,1)S(1)}, u32[]{:S(2)}, u32[]{:S(2)}) collective-permute-start(bf16[128,512]{1,0:T(8,128)(2,1)S(1)} %get-tuple-element.37), channel_id=1, source_target_pairs={{0,14},{1,15},{2,0},{3,1},{4,2},{5,3},{6,4},{7,5},{8,6},{9,7},{10,... | collective-permute-start | bytes 393224 | tf_op jit(solution)/shard_map/ppermute | solution.py:26
  68.1 9.5 %collective-permute-start.13 = (bf16[128,1024]{1,0:T(8,128)(2,1)S(1)}, bf16[128,1024]{1,0:T(8,128)(2,1)S(1)}, u32[]{:S(2)}, u32[]{:S(2)}) collective-permute-start(bf16[128,1024]{1,0:T(8,128)(2,1)S(1)} %get-tuple-element.24), channel_id=1, source_target_pairs={{0,2},{1,3},{2,4},{3,5},{4,6},{5,7},{6,8},{7,9},{8,10},{9,11},{10,... | collective-permute-start | bytes 786440 | tf_op jit(solution)/shard_map/ppermute | solution.py:25
  68.2 11.6 %collective-permute-start.17 = (bf16[128,1024]{1,0:T(8,128)(2,1)S(1)}, bf16[128,1024]{1,0:T(8,128)(2,1)S(1)}, u32[]{:S(2)}, u32[]{:S(2)}) collective-permute-start(bf16[128,1024]{1,0:T(8,128)(2,1)S(1)} %get-tuple-element.25), channel_id=1, source_target_pairs={{0,14},{1,15},{2,0},{3,1},{4,2},{5,3},{6,4},{7,5},{8,6},{9,7},{10,... | collective-permute-start | bytes 786440 | tf_op jit(solution)/shard_map/ppermute | solution.py:26
  71.5 9.5 %collective-permute-start.5 = (bf16[128,1024]{1,0:T(8,128)(2,1)S(1)}, bf16[128,1024]{1,0:T(8,128)(2,1)S(1)}, u32[]{:S(2)}, u32[]{:S(2)}) collective-permute-start(bf16[128,1024]{1,0:T(8,128)(2,1)S(1)} %get-tuple-element.30), channel_id=1, source_target_pairs={{0,2},{1,3},{2,4},{3,5},{4,6},{5,7},{6,8},{7,9},{8,10},{9,11},{10,... | collective-permute-start | bytes 786440 | tf_op jit(solution)/shard_map/ppermute | solution.py:25
  71.6 10.3 %collective-permute-start.9 = (bf16[128,1024]{1,0:T(8,128)(2,1)S(1)}, bf16[128,1024]{1,0:T(8,128)(2,1)S(1)}, u32[]{:S(2)}, u32[]{:S(2)}) collective-permute-start(bf16[128,1024]{1,0:T(8,128)(2,1)S(1)} %get-tuple-element.31), channel_id=1, source_target_pairs={{0,14},{1,15},{2,0},{3,1},{4,2},{5,3},{6,4},{7,5},{8,6},{9,7},{10,... | collective-permute-start | bytes 786440 | tf_op jit(solution)/shard_map/ppermute | solution.py:26
  75.0 18.3 %copy-start.2 = (f32[1,384,512]{2,1,0:T(8,128)S(1)}, f32[1,384,512]{2,1,0:T(8,128)}, u32[]{:S(2)}) copy-start(f32[1,384,512]{2,1,0:T(8,128)} %param.15) | copy-start | bytes 2359300
  75.0 13.3 %collective-permute-start.20 = (bf16[384,512]{1,0:T(8,128)(2,1)S(1)}, bf16[384,512]{1,0:T(8,128)(2,1)S(1)}, u32[]{:S(2)}, u32[]{:S(2)}) collective-permute-start(bf16[384,512]{1,0:T(8,128)(2,1)S(1)} %get-tuple-element.17), channel_id=1, source_target_pairs={{0,16},{16,32},{32,48},{48,0},{1,17},{17,33},{33,49},{49,1},{2,18}... | collective-permute-start | bytes 1179656 | tf_op jit(solution)/shard_map/ppermute | solution.py:127
  77.6 15.4 %collective-permute-start.21 = (bf16[384,512]{1,0:T(8,128)(2,1)S(1)}, bf16[384,512]{1,0:T(8,128)(2,1)S(1)}, u32[]{:S(2)}, u32[]{:S(2)}) collective-permute-start(bf16[384,512]{1,0:T(8,128)(2,1)S(1)} %get-tuple-element.19), channel_id=1, source_target_pairs={{0,32},{16,48},{32,0},{48,16},{1,33},{17,49},{33,1},{49,17},{2,34}... | collective-permute-start | bytes 1179656 | tf_op jit(solution)/shard_map/ppermute | solution.py:127
  79.8 13.5 %collective-permute-start.22 = (bf16[384,512]{1,0:T(8,128)(2,1)S(1)}, bf16[384,512]{1,0:T(8,128)(2,1)S(1)}, u32[]{:S(2)}, u32[]{:S(2)}) collective-permute-start(bf16[384,512]{1,0:T(8,128)(2,1)S(1)} %get-tuple-element.18), channel_id=1, source_target_pairs={{0,48},{16,0},{32,16},{48,32},{1,49},{17,1},{33,17},{49,33},{2,50}... | collective-permute-start | bytes 1179656 | tf_op jit(solution)/shard_map/ppermute | solution.py:127
  81.0 15.0 %collective-permute-start.14 = (bf16[128,1024]{1,0:T(8,128)(2,1)S(1)}, bf16[128,1024]{1,0:T(8,128)(2,1)S(1)}, u32[]{:S(2)}, u32[]{:S(2)}) collective-permute-start(bf16[128,1024]{1,0:T(8,128)(2,1)S(1)} %get-tuple-element.22), channel_id=1, source_target_pairs={{0,2},{1,3},{2,4},{3,5},{4,6},{5,7},{6,8},{7,9},{8,10},{9,11},{10,... | collective-permute-start | bytes 786440 | tf_op jit(solution)/shard_map/ppermute | solution.py:25
  81.9 14.2 %collective-permute-start.18 = (bf16[128,1024]{1,0:T(8,128)(2,1)S(1)}, bf16[128,1024]{1,0:T(8,128)(2,1)S(1)}, u32[]{:S(2)}, u32[]{:S(2)}) collective-permute-start(bf16[128,1024]{1,0:T(8,128)(2,1)S(1)} %get-tuple-element.23), channel_id=1, source_target_pairs={{0,14},{1,15},{2,0},{3,1},{4,2},{5,3},{6,4},{7,5},{8,6},{9,7},{10,... | collective-permute-start | bytes 786440 | tf_op jit(solution)/shard_map/ppermute | solution.py:26
  88.3 11.6 %collective-permute-start.10 = (bf16[128,1024]{1,0:T(8,128)(2,1)S(1)}, bf16[128,1024]{1,0:T(8,128)(2,1)S(1)}, u32[]{:S(2)}, u32[]{:S(2)}) collective-permute-start(bf16[128,1024]{1,0:T(8,128)(2,1)S(1)} %get-tuple-element.29), channel_id=1, source_target_pairs={{0,14},{1,15},{2,0},{3,1},{4,2},{5,3},{6,4},{7,5},{8,6},{9,7},{10,... | collective-permute-start | bytes 786440 | tf_op jit(solution)/shard_map/ppermute | solution.py:26
  93.0 1.5 %copy-start.3 = (f32[384,512]{1,0:T(8,128)S(1)}, f32[384,512]{1,0:T(8,128)}, u32[]{:S(2)}) copy-start(f32[384,512]{1,0:T(8,128)} %param.16) | copy-start | bytes 2359300
  93.0 1.5 %copy-start.4 = (f32[1,384,512]{2,1,0:T(8,128)S(1)}, f32[1,384,512]{2,1,0:T(8,128)}, u32[]{:S(2)}) copy-start(f32[1,384,512]{2,1,0:T(8,128)} %param.14) | copy-start | bytes 2359300
  93.0 7.6 %collective-permute-start.6 = (bf16[128,1024]{1,0:T(8,128)(2,1)S(1)}, bf16[128,1024]{1,0:T(8,128)(2,1)S(1)}, u32[]{:S(2)}, u32[]{:S(2)}) collective-permute-start(bf16[128,1024]{1,0:T(8,128)(2,1)S(1)} %get-tuple-element.28), channel_id=1, source_target_pairs={{0,2},{1,3},{2,4},{3,5},{4,6},{5,7},{6,8},{7,9},{8,10},{9,11},{10,... | collective-permute-start | bytes 786440 | tf_op jit(solution)/shard_map/ppermute | solution.py:25
  96.0 6.9 %collective-permute-start.23 = (bf16[384,512]{1,0:T(8,128)(2,1)S(1)}, bf16[384,512]{1,0:T(8,128)(2,1)S(1)}, u32[]{:S(2)}, u32[]{:S(2)}) collective-permute-start(bf16[384,512]{1,0:T(8,128)(2,1)S(1)} %get-tuple-element.33), channel_id=1, source_target_pairs={{0,64},{64,0},{128,192},{192,128},{1,65},{65,1},{129,193},{193,129... | collective-permute-start | bytes 1179656 | tf_op jit(solution)/shard_map/ppermute | solution.py:147
  96.3 10.6 %collective-permute-start.15 = (bf16[128,1024]{1,0:T(8,128)(2,1)S(1)}, bf16[128,1024]{1,0:T(8,128)(2,1)S(1)}, u32[]{:S(2)}, u32[]{:S(2)}) collective-permute-start(bf16[128,1024]{1,0:T(8,128)(2,1)S(1)} %get-tuple-element.20), channel_id=1, source_target_pairs={{0,2},{1,3},{2,4},{3,5},{4,6},{5,7},{6,8},{7,9},{8,10},{9,11},{10,... | collective-permute-start | bytes 786440 | tf_op jit(solution)/shard_map/ppermute | solution.py:25
  97.7 9.3 %collective-permute-start.19 = (bf16[128,1024]{1,0:T(8,128)(2,1)S(1)}, bf16[128,1024]{1,0:T(8,128)(2,1)S(1)}, u32[]{:S(2)}, u32[]{:S(2)}) collective-permute-start(bf16[128,1024]{1,0:T(8,128)(2,1)S(1)} %get-tuple-element.21), channel_id=1, source_target_pairs={{0,14},{1,15},{2,0},{3,1},{4,2},{5,3},{6,4},{7,5},{8,6},{9,7},{10,... | collective-permute-start | bytes 786440 | tf_op jit(solution)/shard_map/ppermute | solution.py:26
  100.8 10.9 %collective-permute-start.11 = (bf16[128,1024]{1,0:T(8,128)(2,1)S(1)}, bf16[128,1024]{1,0:T(8,128)(2,1)S(1)}, u32[]{:S(2)}, u32[]{:S(2)}) collective-permute-start(bf16[128,1024]{1,0:T(8,128)(2,1)S(1)} %get-tuple-element.27), channel_id=1, source_target_pairs={{0,14},{1,15},{2,0},{3,1},{4,2},{5,3},{6,4},{7,5},{8,6},{9,7},{10,... | collective-permute-start | bytes 786440 | tf_op jit(solution)/shard_map/ppermute | solution.py:26
  101.9 10.3 %collective-permute-start.7 = (bf16[128,1024]{1,0:T(8,128)(2,1)S(1)}, bf16[128,1024]{1,0:T(8,128)(2,1)S(1)}, u32[]{:S(2)}, u32[]{:S(2)}) collective-permute-start(bf16[128,1024]{1,0:T(8,128)(2,1)S(1)} %get-tuple-element.26), channel_id=1, source_target_pairs={{0,2},{1,3},{2,4},{3,5},{4,6},{5,7},{6,8},{7,9},{8,10},{9,11},{10,... | collective-permute-start | bytes 786440 | tf_op jit(solution)/shard_map/ppermute | solution.py:25
  103.0 11.4 %collective-permute-start.24 = (bf16[384,512]{1,0:T(8,128)(2,1)S(1)}, bf16[384,512]{1,0:T(8,128)(2,1)S(1)}, u32[]{:S(2)}, u32[]{:S(2)}) collective-permute-start(bf16[384,512]{1,0:T(8,128)(2,1)S(1)} %add_convert_fusion), channel_id=1, source_target_pairs={{0,128},{64,192},{128,0},{192,64},{1,129},{65,193},{129,1},{193,65... | collective-permute-start | bytes 1179656 | tf_op jit(solution)/shard_map/ppermute | solution.py:147
  107.0 8.0 %copy-start.5 = (f32[384,512]{1,0:T(8,128)S(1)}, f32[384,512]{1,0:T(8,128)}, u32[]{:S(2)}) copy-start(f32[384,512]{1,0:T(8,128)} %param.17) | copy-start | bytes 2359300
  114.5 6.5 %collective-permute-start.25 = (bf16[64,2048]{1,0:T(8,128)(2,1)S(1)}, bf16[64,2048]{1,0:T(8,128)(2,1)S(1)}, u32[]{:S(2)}, u32[]{:S(2)}) collective-permute-start(bf16[64,2048]{1,0:T(8,128)(2,1)S(1)} %fusion.34), channel_id=1, source_target_pairs={{0,1},{1,0},{2,3},{3,2},{4,5},{5,4},{6,7},{7,6},{8,9},{9,8},{10,11... | collective-permute-start | bytes 786440 | tf_op jit(solution)/shard_map/ppermute | solution.py:58

commit v10 on v9

--- a/solution.py
+++ b/solution.py
@@ -121,11 +121,9 @@
         hidden, upstream, (((0,), (0,)), ((), ())), preferred_element_type=jnp.float32
     )
     cols = full_grad.shape[1] // ndp
-    grad_down = lax.dynamic_slice_in_dim(full_grad, j * cols, cols, axis=1)
-    for s in range(1, ndp):
-        blk = lax.dynamic_slice_in_dim(full_grad, ((j + s) % ndp) * cols, cols, axis=1)
-        got = lax.ppermute(blk.astype(jnp.bfloat16), "dp", _shift(ndp, s))
-        grad_down = grad_down + got.astype(jnp.float32)
+    blocks = full_grad.astype(jnp.bfloat16).reshape(full_grad.shape[0], ndp, cols)
+    got = lax.all_to_all(blocks, "dp", 1, 1, tiled=True)
+    grad_down = jnp.sum(got.astype(jnp.float32), axis=1)
 
     both = jnp.concatenate([grad_gate, grad_up], axis=1)
     partial_sum = lax.dot_general(

time: 122 us -> 138 us (1.13); the launches traced: 122 us -> 136 us
  other arithmetic: 7.64 us -> 20.6 us
  waiting for transfers between devices: 49.4 us -> 44.6 us
  starting transfers between devices: 38.6 us -> 42.8 us
  local copies, waits for them, and re-layouts: 8.98 us -> 10.9 us
    convert_element_type x6, other arithmetic: 0.96 us -> 10.7 us  [_z_reduce_scatter(): send_a.astype(jnp.bfloat16)]
    ppermute x3 -> x0, waiting for transfers between devices: 8.68 us -> none  [shards(): got = lax.ppermute(blk.astype(jnp.bfloat16), 'dp', _shift(ndp, s))]
    ppermute x8, starting transfers between devices: 19.5 us -> 25.6 us  [_z_reduce_scatter(): lax.ppermute(send_b.astype(jnp.bfloat16), 'mp', down).astype(jnp.float32)]
    all_to_all x0 -> x1, starting transfers between devices: none -> 4.37 us  [shards(): got = lax.all_to_all(blocks, 'dp', 1, 1, tiled=True)]
    ppermute x2, waiting for transfers between devices: 2.02 us -> 6.18 us  [shards(): lax.ppermute(mine, 'outer', perm).astype(jnp.float32)]
    ppermute x3 -> x0, starting transfers between devices: 3.91 us -> none  [shards(): got = lax.ppermute(blk.astype(jnp.bfloat16), 'dp', _shift(ndp, s))]
    ppermute x8, waiting for transfers between devices: 4.68 us -> 1.35 us  [_z_reduce_scatter(): lax.ppermute(send_b.astype(jnp.bfloat16), 'mp', down).astype(jnp.float32)]
    ppermute x8, starting transfers between devices: 5.49 us -> 2.59 us  [_z_reduce_scatter(): lax.ppermute(send_a.astype(jnp.bfloat16), 'mp', up).astype(jnp.float32)]
  transfers between devices with their start and end apart: 26 -> 24, of which waited for: 12 -> 9; matrix products, arithmetic and copies ran while one was open for 15% -> 25% of each run, Pallas kernels for 0% -> 0%
where the time goes in v10:
time: 138 us; the launch traced here: 136 us
  waiting for transfers between devices  44.6 us (32%)
  starting transfers between devices  42.8 us (31%)
  other arithmetic  20.6 us (15%)
  matrix products  15.9 us (12%)
  local copies, waits for them, and re-layouts  10.9 us (8%)
    ppermute x8, starting transfers between devices, _z_reduce_scatter(): lax.ppermute(send_b.astype(jnp.bfloat16), 'mp', down).astype(jnp.float32)  25.6 us
    ppermute x1, waiting for transfers between devices, shards(): from_left = lax.ppermute(shard, 'dp', _shift(ndp, 1))  21 us
    convert_element_type x6, other arithmetic, _z_reduce_scatter(): send_a.astype(jnp.bfloat16)  10.7 us
    ppermute x8, waiting for transfers between devices, _z_reduce_scatter(): lax.ppermute(send_a.astype(jnp.bfloat16), 'mp', up).astype(jnp.float32)  6.86 us
    ppermute x2, waiting for transfers between devices, shards(): lax.ppermute(mine, 'outer', perm).astype(jnp.float32)  6.18 us
    dot_general x5, matrix products, shards(): p1 = jnp.dot(xs, piece[:, :2 * ff], preferred_element_type=jnp.float32)  5.84 us
    unnamed x18, local copies, waits for them, and re-layouts  5.43 us
    ppermute x1, waiting for transfers between devices, shards(): far_a = lax.ppermute(from_left[:half], 'dp', _shift(ndp, 1))  5.06 us
  transfers between devices with their start and end apart: 24, of which 9 were waited for; matrix products, arithmetic and copies ran while one was open for 25% of the time, Pallas kernels for 0%

profile of v10, /device:TPU:8, one launch (start us, length us, event | category | flops | bytes accessed | tf_op | source)
XLA Modules:
  0.0 135.8 jit_solution(9210873279008362886)
XLA Ops:
  0.6 1.2 copy.16
  1.9 1.2 copy.17
  3.1 1.1 pad_maximum_fusion
  4.2 1.5 %collective-permute-start = (bf16[512,1152]{0,1:T(8,128)(2,1)}, bf16[512,1152]{0,1:T(8,128)(2,1)}, u32[]{:S(2)}, u32[]{:S(2)}) collective-permute-start(bf16[512,1152]{0,1:T(8,128)(2,1)} %pad_maximum_fusion), channel_id=1, source_target_pairs={{0,16},{16,32},{32,48},{48,0},{1,17},{17,33},{33,49},{49,1},{2,18}... | collective-permute-start | bytes 3538952 | tf_op jit(solution)/shard_map/ppermute | solution.py:85
  5.7 1.7 %collective-permute-start.1 = (bf16[512,1152]{0,1:T(8,128)(2,1)}, bf16[512,1152]{0,1:T(8,128)(2,1)S(1)}, u32[]{:S(2)}, u32[]{:S(2)}) collective-permute-start(bf16[512,1152]{0,1:T(8,128)(2,1)} %pad_maximum_fusion), channel_id=1, source_target_pairs={{0,48},{16,0},{32,16},{48,32},{1,49},{17,1},{33,17},{49,33},{2,50}... | collective-permute-start | bytes 3538952 | tf_op jit(solution)/shard_map/ppermute | solution.py:86
  7.5 0.4 broadcast_in_dim.8
  8.0 1.7 %copy-done.7 = bf16[1,1024,2048]{2,1,0:T(8,128)(2,1)S(1)} copy-done((bf16[1,1024,2048]{2,1,0:T(8,128)(2,1)S(1)}, bf16[1,1024,2048]{2,1,0:T(8,128)(2,1)}, u32[]{:S(2)}) %copy-start.7) | copy-done | bytes 4194328
  9.7 1.0 fusion.13
  10.7 1.2 copy-done.2
  11.9 0.6 fusion.19
  12.5 21.0 %collective-permute-done = bf16[512,1152]{0,1:T(8,128)(2,1)} collective-permute-done((bf16[512,1152]{0,1:T(8,128)(2,1)}, bf16[512,1152]{0,1:T(8,128)(2,1)}, u32[]{:S(2)}, u32[]{:S(2)}) %collective-permute-start) | collective-permute-done | bytes 1179680 | tf_op jit(solution)/shard_map/ppermute | solution.py:85
  33.5 1.1 slice.85
  34.6 0.4 collective-permute-start.2
  35.0 3.2 %collective-permute-start.3 = (bf16[256,1152]{0,1:T(8,128)(2,1)S(1)}, bf16[256,1152]{0,1:T(8,128)(2,1)S(1)}, u32[]{:S(2)}, u32[]{:S(2)}) collective-permute-start(bf16[256,1152]{0,1:T(8,128)(2,1)S(1)} %slice.87), channel_id=1, source_target_pairs={{0,48},{16,0},{32,16},{48,32},{1,49},{17,1},{33,17},{49,33},{2,50}... | collective-permute-start | bytes 1769480 | tf_op jit(solution)/shard_map/ppermute | solution.py:88
  38.2 2.2 %fusion.11 = f32[1024,768]{0,1:T(8,128)S(1)} fusion(bf16[1,1024,2048]{2,1,0:T(8,128)(2,1)S(1)} %copy-done.7, s32[]{:T(128)S(6)} %select_n.139, bf16[512,1152]{0,1:T(8,128)(2,1)} %collective-permute-done), kind=kOutput, calls=%fused_computation.25 | convolution fusion | flops 805306368 | bytes 4980740 | tf_op jit(solution)/shard_map/dot_general | solution.py:104
  40.4 1.6 %fusion.17 = f32[1024,384]{0,1:T(8,128)S(1)} fusion(bf16[1,1024,2048]{2,1,0:T(8,128)(2,1)S(1)} %copy-done.2, s32[]{:T(128)S(6)} %select_n.139, bf16[512,1152]{0,1:T(8,128)(2,1)} %collective-permute-done), kind=kOutput, calls=%fused_computation.31 | convolution fusion | flops 402653184 | bytes 3014660 | tf_op jit(solution)/shard_map/dot_general | solution.py:105
  42.0 0.6 fusion.15
  42.6 1.2 slice_dynamic-update-slice_fusion.1
  44.0 1.0 fusion.9
  45.0 5.1 %collective-permute-done.2 = bf16[256,1152]{0,1:T(8,128)(2,1)S(1)} collective-permute-done((bf16[256,1152]{0,1:T(8,128)(2,1)S(1)}, bf16[256,1152]{0,1:T(8,128)(2,1)S(1)}, u32[]{:S(2)}, u32[]{:S(2)}) %collective-permute-start.2) | collective-permute-done | bytes 589856 | tf_op jit(solution)/shard_map/ppermute | solution.py:87
  50.1 0.4 fusion.68
  50.5 0.6 fusion.62
  51.2 1.0 add_add_fusion
  52.2 1.1 multiply_convert_fusion.2
  53.3 3.8 %convolution_convert_fusion = bf16[1024,2048]{1,0:T(8,128)(2,1)S(1)} fusion(bf16[2048,768]{0,1:T(8,128)(2,1)S(1)} %slice_dynamic-update-slice_fusion.2, bf16[1024,384]{0,1:T(8,128)(2,1)S(1)} %get-tuple-element.12, bf16[1024,384]{0,1:T(8,128)(2,1)S(1)} %get-tuple-element.11), kind=kOutput, calls=%fused_computation.2 | convolution fusion | flops 3226468352 | bytes 8912896 | tf_op jit(solution)/shard_map/dot_general | solution.py:129
  57.2 0.5 fusion.99
  57.7 2.0 %collective-permute-start.12 = (bf16[128,512]{1,0:T(8,128)(2,1)S(1)}, bf16[128,512]{1,0:T(8,128)(2,1)S(1)}, u32[]{:S(2)}, u32[]{:S(2)}) collective-permute-start(bf16[128,512]{1,0:T(8,128)(2,1)S(1)} %get-tuple-element.29), channel_id=1, source_target_pairs={{0,2},{1,3},{2,4},{3,5},{4,6},{5,7},{6,8},{7,9},{8,10},{9,11},{10,... | collective-permute-start | bytes 393224 | tf_op jit(solution)/shard_map/ppermute | solution.py:25
  59.7 4.0 %collective-permute-start.16 = (bf16[128,512]{1,0:T(8,128)(2,1)S(1)}, bf16[128,512]{1,0:T(8,128)(2,1)S(1)}, u32[]{:S(2)}, u32[]{:S(2)}) collective-permute-start(bf16[128,512]{1,0:T(8,128)(2,1)S(1)} %get-tuple-element.30), channel_id=1, source_target_pairs={{0,14},{1,15},{2,0},{3,1},{4,2},{5,3},{6,4},{7,5},{8,6},{9,7},{10,... | collective-permute-start | bytes 393224 | tf_op jit(solution)/shard_map/ppermute | solution.py:26
  63.7 0.7 fusion.101
  64.5 3.2 %collective-permute-start.8 = (bf16[128,512]{1,0:T(8,128)(2,1)}, bf16[128,512]{1,0:T(8,128)(2,1)}, u32[]{:S(2)}, u32[]{:S(2)}) collective-permute-start(bf16[128,512]{1,0:T(8,128)(2,1)} %get-tuple-element.32), channel_id=1, source_target_pairs={{0,14},{1,15},{2,0},{3,1},{4,2},{5,3},{6,4},{7,5},{8,6},{9,7},{10,... | collective-permute-start | bytes 393224 | tf_op jit(solution)/shard_map/ppermute | solution.py:26
  67.7 0.8 fusion.49
  68.5 3.2 %collective-permute-start.17 = (bf16[128,1024]{1,0:T(8,128)(2,1)S(1)}, bf16[128,1024]{1,0:T(8,128)(2,1)}, u32[]{:S(2)}, u32[]{:S(2)}) collective-permute-start(bf16[128,1024]{1,0:T(8,128)(2,1)S(1)} %get-tuple-element.20), channel_id=1, source_target_pairs={{0,14},{1,15},{2,0},{3,1},{4,2},{5,3},{6,4},{7,5},{8,6},{9,7},{10,... | collective-permute-start | bytes 786440 | tf_op jit(solution)/shard_map/ppermute | solution.py:26
  71.7 1.9 %fusion.2 = bf16[384,2048]{1,0:T(8,128)(2,1)S(1)} fusion(bf16[1,1024,2048]{2,1,0:T(8,128)(2,1)S(1)} %copy-done.2, f32[1024,768]{0,1:T(8,128)S(1)} %add_add_fusion), kind=kOutput, calls=%fused_computation.5 | convolution fusion | flops 1613758464 | bytes 8912896 | tf_op jit(solution)/shard_map/dot_general | solution.py:120
  73.6 1.3 copy.21
  74.9 4.4 %all-to-all-start = ((bf16[384,4,512]{2,0,1:T(8,128)(2,1)}), bf16[384,4,512]{2,0,1:T(8,128)(2,1)}, u32[]{:S(2)}, u32[]{:S(2)}) async-start(bf16[384,4,512]{2,0,1:T(8,128)(2,1)} %bitcast.144), calls=%async_computation | async-start | bytes 3145728 | tf_op jit(solution)/shard_map/all_to_all | solution.py:125
  79.3 1.8 %fusion.56 = (bf16[128,1024]{1,0:T(8,128)(2,1)}, bf16[128,1024]{1,0:T(8,128)(2,1)}) fusion(bf16[8,128,1024]{2,1,0:T(8,128)(2,1)S(1)} %bitcast.135, s32[]{:T(128)S(6)} %select_n.151, bf16[128,512]{1,0:T(8,128)(2,1)S(1)} %collective-permute-done.4, s32[]{:T(128)S(6)} %select_n.157, bf16[128,512]{1,0:T(8,128)(2,1)} %collective-permute-done.8), kind=kLoop, calls=%fused_computation.95 | loop fusion | flops 1048576 | bytes 1310728 | tf_op jit(solution)/shard_map/convert_element_type | solution.py:25
  81.1 3.2 %collective-permute-start.9 = (bf16[128,1024]{1,0:T(8,128)(2,1)}, bf16[128,1024]{1,0:T(8,128)(2,1)}, u32[]{:S(2)}, u32[]{:S(2)}) collective-permute-start(bf16[128,1024]{1,0:T(8,128)(2,1)} %get-tuple-element.26), channel_id=1, source_target_pairs={{0,14},{1,15},{2,0},{3,1},{4,2},{5,3},{6,4},{7,5},{8,6},{9,7},{10,... | collective-permute-start | bytes 786440 | tf_op jit(solution)/shard_map/ppermute | solution.py:26
  84.4 2.0 %fusion.48 = (bf16[128,1024]{1,0:T(8,128)(2,1)}, bf16[128,1024]{1,0:T(8,128)(2,1)S(1)}) fusion(bf16[128,1024]{1,0:T(8,128)(2,1)S(1)} %collective-permute-done.13, bf16[8,128,1024]{2,1,0:T(8,128)(2,1)} %bitcast.141, s32[]{:T(128)S(6)} %select_n.153, s32[]{:T(128)S(6)} %select_n.159, bf16[128,1024]{1,0:T(8,128)(2,1)} %collective-permute-done.17), kind=kLoop, calls=%fused_computation.79 | loop fusion | flops 1048576 | bytes 1572872 | tf_op jit(solution)/shard_map/convert_element_type | solution.py:25
  86.4 3.2 %collective-permute-start.18 = (bf16[128,1024]{1,0:T(8,128)(2,1)S(1)}, bf16[128,1024]{1,0:T(8,128)(2,1)}, u32[]{:S(2)}, u32[]{:S(2)}) collective-permute-start(bf16[128,1024]{1,0:T(8,128)(2,1)S(1)} %get-tuple-element.18), channel_id=1, source_target_pairs={{0,14},{1,15},{2,0},{3,1},{4,2},{5,3},{6,4},{7,5},{8,6},{9,7},{10,... | collective-permute-start | bytes 786440 | tf_op jit(solution)/shard_map/ppermute | solution.py:26
  89.6 1.9 %collective-permute-done.5 = bf16[128,1024]{1,0:T(8,128)(2,1)} collective-permute-done((bf16[128,1024]{1,0:T(8,128)(2,1)}, bf16[128,1024]{1,0:T(8,128)(2,1)}, u32[]{:S(2)}, u32[]{:S(2)}) %collective-permute-start.5) | collective-permute-done | bytes 262176 | tf_op jit(solution)/shard_map/ppermute | solution.py:25
  91.5 2.0 %fusion.55 = (bf16[128,1024]{1,0:T(8,128)(2,1)}, bf16[128,1024]{1,0:T(8,128)(2,1)}) fusion(bf16[128,1024]{1,0:T(8,128)(2,1)} %collective-permute-done.5, bf16[8,128,1024]{2,1,0:T(8,128)(2,1)S(1)} %bitcast.136, s32[]{:T(128)S(6)} %select_n.153, s32[]{:T(128)S(6)} %select_n.159, bf16[128,1024]{1,0:T(8,128)(2,1)} %collective-permute-done.9), kind=kLoop, calls=%fused_computation.93 | loop fusion | flops 1048576 | bytes 1572872 | tf_op jit(solution)/shard_map/convert_element_type | solution.py:25
  93.6 3.5 %collective-permute-start.10 = (bf16[128,1024]{1,0:T(8,128)(2,1)}, bf16[128,1024]{1,0:T(8,128)(2,1)}, u32[]{:S(2)}, u32[]{:S(2)}) collective-permute-start(bf16[128,1024]{1,0:T(8,128)(2,1)} %get-tuple-element.24), channel_id=1, source_target_pairs={{0,14},{1,15},{2,0},{3,1},{4,2},{5,3},{6,4},{7,5},{8,6},{9,7},{10,... | collective-permute-start | bytes 786440 | tf_op jit(solution)/shard_map/ppermute | solution.py:26
  97.1 2.1 %fusion.47 = (bf16[128,1024]{1,0:T(8,128)(2,1)}, bf16[128,1024]{1,0:T(8,128)(2,1)}) fusion(bf16[128,1024]{1,0:T(8,128)(2,1)S(1)} %collective-permute-done.14, bf16[8,128,1024]{2,1,0:T(8,128)(2,1)} %bitcast.142, s32[]{:T(128)S(6)} %select_n.155, s32[]{:T(128)S(6)} %select_n.161, bf16[128,1024]{1,0:T(8,128)(2,1)} %collective-permute-done.18), kind=kLoop, calls=%fused_computation.77 | loop fusion | flops 1048576 | bytes 1572872 | tf_op jit(solution)/shard_map/convert_element_type | solution.py:25
  99.2 0.6 collective-permute-start.15
  99.8 2.9 %collective-permute-start.19 = (bf16[128,1024]{1,0:T(8,128)(2,1)}, bf16[128,1024]{1,0:T(8,128)(2,1)S(1)}, u32[]{:S(2)}, u32[]{:S(2)}) collective-permute-start(bf16[128,1024]{1,0:T(8,128)(2,1)} %get-tuple-element.16), channel_id=1, source_target_pairs={{0,14},{1,15},{2,0},{3,1},{4,2},{5,3},{6,4},{7,5},{8,6},{9,7},{10,... | collective-permute-start | bytes 786440 | tf_op jit(solution)/shard_map/ppermute | solution.py:26
  102.6 0.9 collective-permute-done.10
  103.6 1.4 %collective-permute-done.6 = bf16[128,1024]{1,0:T(8,128)(2,1)} collective-permute-done((bf16[128,1024]{1,0:T(8,128)(2,1)}, bf16[128,1024]{1,0:T(8,128)(2,1)}, u32[]{:S(2)}, u32[]{:S(2)}) %collective-permute-start.6) | collective-permute-done | bytes 262176 | tf_op jit(solution)/shard_map/ppermute | solution.py:25
  105.0 2.0 %fusion.54 = (bf16[128,1024]{1,0:T(8,128)(2,1)}, bf16[128,1024]{1,0:T(8,128)(2,1)}) fusion(bf16[128,1024]{1,0:T(8,128)(2,1)} %collective-permute-done.6, bf16[8,128,1024]{2,1,0:T(8,128)(2,1)S(1)} %bitcast.137, s32[]{:T(128)S(6)} %select_n.155, s32[]{:T(128)S(6)} %select_n.161, bf16[128,1024]{1,0:T(8,128)(2,1)} %collective-permute-done.10), kind=kLoop, calls=%fused_computation.91 | loop fusion | flops 1048576 | bytes 1572872 | tf_op jit(solution)/shard_map/convert_element_type | solution.py:25
  107.0 2.3 %collective-permute-start.11 = (bf16[128,1024]{1,0:T(8,128)(2,1)}, bf16[128,1024]{1,0:T(8,128)(2,1)}, u32[]{:S(2)}, u32[]{:S(2)}) collective-permute-start(bf16[128,1024]{1,0:T(8,128)(2,1)} %get-tuple-element.22), channel_id=1, source_target_pairs={{0,14},{1,15},{2,0},{3,1},{4,2},{5,3},{6,4},{7,5},{8,6},{9,7},{10,... | collective-permute-start | bytes 786440 | tf_op jit(solution)/shard_map/ppermute | solution.py:26
  109.3 1.9 %convert_reduce_fusion = f32[384,512]{1,0:T(8,128)S(1)} fusion(bf16[384,4,512]{2,0,1:T(8,128)(2,1)} %all-to-all-done), kind=kLoop, calls=%fused_computation.3 | loop fusion | flops 1376256 | bytes 2359296 | tf_op jit(solution)/shard_map/reduce_sum | solution.py:126
  111.2 0.1 copy-done.5
  111.4 0.7 fusion.37
  112.2 1.1 fusion.50
  113.3 0.4 collective-permute-done.11
  113.7 3.5 %collective-permute-done.7 = bf16[128,1024]{1,0:T(8,128)(2,1)} collective-permute-done((bf16[128,1024]{1,0:T(8,128)(2,1)}, bf16[128,1024]{1,0:T(8,128)(2,1)}, u32[]{:S(2)}, u32[]{:S(2)}) %collective-permute-start.7) | collective-permute-done | bytes 262176 | tf_op jit(solution)/shard_map/ppermute | solution.py:25
  117.2 1.1 fusion.57
  118.4 2.4 %collective-permute-start.21 = (bf16[384,512]{1,0:T(8,128)(2,1)S(1)}, bf16[384,512]{1,0:T(8,128)(2,1)S(1)}, u32[]{:S(2)}, u32[]{:S(2)}) collective-permute-start(bf16[384,512]{1,0:T(8,128)(2,1)S(1)} %add_convert_fusion), channel_id=1, source_target_pairs={{0,128},{64,192},{128,0},{192,64},{1,129},{65,193},{129,1},{193,65... | collective-permute-start | bytes 1179656 | tf_op jit(solution)/shard_map/ppermute | solution.py:145
  120.9 1.4 %fusion.33 = (f32[1,384,512]{2,1,0:T(8,128)}, f32[1,384,512]{2,1,0:T(8,128)}) fusion(f32[384,512]{1,0:T(8,128)S(1)} %convert_reduce_fusion, f32[1,384,512]{2,1,0:T(8,128)S(1)} %copy-done.3, f32[1,384,512]{2,1,0:T(8,128)S(1)} %copy-done.4), kind=kLoop, calls=%fused_computation.47 | loop fusion | flops 1376256 | bytes 3932160 | tf_op jit(solution)/shard_map/add | solution.py:134
  122.3 6.2 %collective-permute-done.21 = bf16[384,512]{1,0:T(8,128)(2,1)S(1)} collective-permute-done((bf16[384,512]{1,0:T(8,128)(2,1)S(1)}, bf16[384,512]{1,0:T(8,128)(2,1)S(1)}, u32[]{:S(2)}, u32[]{:S(2)}) %collective-permute-start.21) | collective-permute-done | bytes 393248 | tf_op jit(solution)/shard_map/ppermute | solution.py:145
  128.5 0.1 convert_add_fusion
  128.6 0.9 collective-permute-start.22
  129.5 1.4 %multiply_subtract_fusion = (f32[384,512]{1,0:T(8,128)}, f32[384,512]{1,0:T(8,128)}) fusion(f32[384,512]{1,0:T(8,128)S(1)} %copy-done.5, f32[384,512]{1,0:T(8,128)S(1)} %convert_add_fusion, f32[384,512]{1,0:T(8,128)S(1)} %copy-done.6), kind=kLoop, calls=%fused_computation.58 | loop fusion | flops 1376256 | bytes 3932160 | tf_op jit(solution)/shard_map/sub | solution.py:150
  130.9 4.1 %collective-permute-done.22 = bf16[64,2048]{1,0:T(8,128)(2,1)S(1)} collective-permute-done((bf16[64,2048]{1,0:T(8,128)(2,1)S(1)}, bf16[64,2048]{1,0:T(8,128)(2,1)S(1)}, u32[]{:S(2)}, u32[]{:S(2)}) %collective-permute-start.22) | collective-permute-done | bytes 262176 | tf_op jit(solution)/shard_map/ppermute | solution.py:58
  135.0 0.8 fusion.82
  (45 shorter events, 0.7 us)
Async XLA Ops:
  0.6 2.4 %copy-start.1 = (f32[1,384,512]{2,1,0:T(8,128)S(1)}, f32[1,384,512]{2,1,0:T(8,128)}, u32[]{:S(2)}) copy-start(f32[1,384,512]{2,1,0:T(8,128)} %param.13) | copy-start | bytes 2359300
  4.2 29.2 %collective-permute-start = (bf16[512,1152]{0,1:T(8,128)(2,1)}, bf16[512,1152]{0,1:T(8,128)(2,1)}, u32[]{:S(2)}, u32[]{:S(2)}) collective-permute-start(bf16[512,1152]{0,1:T(8,128)(2,1)} %pad_maximum_fusion), channel_id=1, source_target_pairs={{0,16},{16,32},{32,48},{48,0},{1,17},{17,33},{33,49},{49,1},{2,18}... | collective-permute-start | bytes 3538952 | tf_op jit(solution)/shard_map/ppermute | solution.py:85
  5.7 29.2 %collective-permute-start.1 = (bf16[512,1152]{0,1:T(8,128)(2,1)}, bf16[512,1152]{0,1:T(8,128)(2,1)S(1)}, u32[]{:S(2)}, u32[]{:S(2)}) collective-permute-start(bf16[512,1152]{0,1:T(8,128)(2,1)} %pad_maximum_fusion), channel_id=1, source_target_pairs={{0,48},{16,0},{32,16},{48,32},{1,49},{17,1},{33,17},{49,33},{2,50}... | collective-permute-start | bytes 3538952 | tf_op jit(solution)/shard_map/ppermute | solution.py:86
  7.5 2.2 %copy-start.7 = (bf16[1,1024,2048]{2,1,0:T(8,128)(2,1)S(1)}, bf16[1,1024,2048]{2,1,0:T(8,128)(2,1)}, u32[]{:S(2)}) copy-start(bf16[1,1024,2048]{2,1,0:T(8,128)(2,1)} %param.9) | copy-start | bytes 12582916
  9.7 2.2 %copy-start.2 = (bf16[1,1024,2048]{2,1,0:T(8,128)(2,1)S(1)}, bf16[1,1024,2048]{2,1,0:T(8,128)(2,1)}, u32[]{:S(2)}) copy-start(bf16[1,1024,2048]{2,1,0:T(8,128)(2,1)} %param.10) | copy-start | bytes 12582916
  34.6 15.5 %collective-permute-start.2 = (bf16[256,1152]{0,1:T(8,128)(2,1)S(1)}, bf16[256,1152]{0,1:T(8,128)(2,1)S(1)}, u32[]{:S(2)}, u32[]{:S(2)}) collective-permute-start(bf16[256,1152]{0,1:T(8,128)(2,1)S(1)} %slice.85), channel_id=1, source_target_pairs={{0,16},{16,32},{32,48},{48,0},{1,17},{17,33},{33,49},{49,1},{2,18}... | collective-permute-start | bytes 1769480 | tf_op jit(solution)/shard_map/ppermute | solution.py:87
  35.0 16.2 %collective-permute-start.3 = (bf16[256,1152]{0,1:T(8,128)(2,1)S(1)}, bf16[256,1152]{0,1:T(8,128)(2,1)S(1)}, u32[]{:S(2)}, u32[]{:S(2)}) collective-permute-start(bf16[256,1152]{0,1:T(8,128)(2,1)S(1)} %slice.87), channel_id=1, source_target_pairs={{0,48},{16,0},{32,16},{48,32},{1,49},{17,1},{33,17},{49,33},{2,50}... | collective-permute-start | bytes 1769480 | tf_op jit(solution)/shard_map/ppermute | solution.py:88
  57.6 16.0 %copy-start = (bf16[1024,1024]{1,0:T(8,128)(2,1)}, bf16[1024,1024]{1,0:T(8,128)(2,1)S(1)}, u32[]{:S(2)}) copy-start(bf16[1024,1024]{1,0:T(8,128)(2,1)S(1)} %get-tuple-element.13) | copy-start | bytes 6291460
  57.7 10.0 %collective-permute-start.12 = (bf16[128,512]{1,0:T(8,128)(2,1)S(1)}, bf16[128,512]{1,0:T(8,128)(2,1)S(1)}, u32[]{:S(2)}, u32[]{:S(2)}) collective-permute-start(bf16[128,512]{1,0:T(8,128)(2,1)S(1)} %get-tuple-element.29), channel_id=1, source_target_pairs={{0,2},{1,3},{2,4},{3,5},{4,6},{5,7},{6,8},{7,9},{8,10},{9,11},{10,... | collective-permute-start | bytes 393224 | tf_op jit(solution)/shard_map/ppermute | solution.py:25
  59.7 8.0 %collective-permute-start.16 = (bf16[128,512]{1,0:T(8,128)(2,1)S(1)}, bf16[128,512]{1,0:T(8,128)(2,1)S(1)}, u32[]{:S(2)}, u32[]{:S(2)}) collective-permute-start(bf16[128,512]{1,0:T(8,128)(2,1)S(1)} %get-tuple-element.30), channel_id=1, source_target_pairs={{0,14},{1,15},{2,0},{3,1},{4,2},{5,3},{6,4},{7,5},{8,6},{9,7},{10,... | collective-permute-start | bytes 393224 | tf_op jit(solution)/shard_map/ppermute | solution.py:26
  64.5 14.9 %collective-permute-start.4 = (bf16[128,512]{1,0:T(8,128)(2,1)}, bf16[128,512]{1,0:T(8,128)(2,1)S(1)}, u32[]{:S(2)}, u32[]{:S(2)}) collective-permute-start(bf16[128,512]{1,0:T(8,128)(2,1)} %get-tuple-element.31), channel_id=1, source_target_pairs={{0,2},{1,3},{2,4},{3,5},{4,6},{5,7},{6,8},{7,9},{8,10},{9,11},{10,... | collective-permute-start | bytes 393224 | tf_op jit(solution)/shard_map/ppermute | solution.py:25
  64.5 14.9 %collective-permute-start.8 = (bf16[128,512]{1,0:T(8,128)(2,1)}, bf16[128,512]{1,0:T(8,128)(2,1)}, u32[]{:S(2)}, u32[]{:S(2)}) collective-permute-start(bf16[128,512]{1,0:T(8,128)(2,1)} %get-tuple-element.32), channel_id=1, source_target_pairs={{0,14},{1,15},{2,0},{3,1},{4,2},{5,3},{6,4},{7,5},{8,6},{9,7},{10,... | collective-permute-start | bytes 393224 | tf_op jit(solution)/shard_map/ppermute | solution.py:26
  68.5 15.9 %collective-permute-start.13 = (bf16[128,1024]{1,0:T(8,128)(2,1)}, bf16[128,1024]{1,0:T(8,128)(2,1)S(1)}, u32[]{:S(2)}, u32[]{:S(2)}) collective-permute-start(bf16[128,1024]{1,0:T(8,128)(2,1)} %get-tuple-element.19), channel_id=1, source_target_pairs={{0,2},{1,3},{2,4},{3,5},{4,6},{5,7},{6,8},{7,9},{8,10},{9,11},{10,... | collective-permute-start | bytes 786440 | tf_op jit(solution)/shard_map/ppermute | solution.py:25
  68.5 15.9 %collective-permute-start.17 = (bf16[128,1024]{1,0:T(8,128)(2,1)S(1)}, bf16[128,1024]{1,0:T(8,128)(2,1)}, u32[]{:S(2)}, u32[]{:S(2)}) collective-permute-start(bf16[128,1024]{1,0:T(8,128)(2,1)S(1)} %get-tuple-element.20), channel_id=1, source_target_pairs={{0,14},{1,15},{2,0},{3,1},{4,2},{5,3},{6,4},{7,5},{8,6},{9,7},{10,... | collective-permute-start | bytes 786440 | tf_op jit(solution)/shard_map/ppermute | solution.py:26
  74.9 34.4 %all-to-all-start = ((bf16[384,4,512]{2,0,1:T(8,128)(2,1)}), bf16[384,4,512]{2,0,1:T(8,128)(2,1)}, u32[]{:S(2)}, u32[]{:S(2)}) async-start(bf16[384,4,512]{2,0,1:T(8,128)(2,1)} %bitcast.144), calls=%async_computation | async-start | bytes 3145728 | tf_op jit(solution)/shard_map/all_to_all | solution.py:125
  81.1 10.4 %collective-permute-start.5 = (bf16[128,1024]{1,0:T(8,128)(2,1)}, bf16[128,1024]{1,0:T(8,128)(2,1)}, u32[]{:S(2)}, u32[]{:S(2)}) collective-permute-start(bf16[128,1024]{1,0:T(8,128)(2,1)} %get-tuple-element.25), channel_id=1, source_target_pairs={{0,2},{1,3},{2,4},{3,5},{4,6},{5,7},{6,8},{7,9},{8,10},{9,11},{10,... | collective-permute-start | bytes 786440 | tf_op jit(solution)/shard_map/ppermute | solution.py:25
  81.1 10.4 %collective-permute-start.9 = (bf16[128,1024]{1,0:T(8,128)(2,1)}, bf16[128,1024]{1,0:T(8,128)(2,1)}, u32[]{:S(2)}, u32[]{:S(2)}) collective-permute-start(bf16[128,1024]{1,0:T(8,128)(2,1)} %get-tuple-element.26), channel_id=1, source_target_pairs={{0,14},{1,15},{2,0},{3,1},{4,2},{5,3},{6,4},{7,5},{8,6},{9,7},{10,... | collective-permute-start | bytes 786440 | tf_op jit(solution)/shard_map/ppermute | solution.py:26
  86.4 10.7 %collective-permute-start.14 = (bf16[128,1024]{1,0:T(8,128)(2,1)}, bf16[128,1024]{1,0:T(8,128)(2,1)S(1)}, u32[]{:S(2)}, u32[]{:S(2)}) collective-permute-start(bf16[128,1024]{1,0:T(8,128)(2,1)} %get-tuple-element.17), channel_id=1, source_target_pairs={{0,2},{1,3},{2,4},{3,5},{4,6},{5,7},{6,8},{7,9},{8,10},{9,11},{10,... | collective-permute-start | bytes 786440 | tf_op jit(solution)/shard_map/ppermute | solution.py:25
  86.4 10.7 %collective-permute-start.18 = (bf16[128,1024]{1,0:T(8,128)(2,1)S(1)}, bf16[128,1024]{1,0:T(8,128)(2,1)}, u32[]{:S(2)}, u32[]{:S(2)}) collective-permute-start(bf16[128,1024]{1,0:T(8,128)(2,1)S(1)} %get-tuple-element.18), channel_id=1, source_target_pairs={{0,14},{1,15},{2,0},{3,1},{4,2},{5,3},{6,4},{7,5},{8,6},{9,7},{10,... | collective-permute-start | bytes 786440 | tf_op jit(solution)/shard_map/ppermute | solution.py:26
  93.6 10.0 %collective-permute-start.10 = (bf16[128,1024]{1,0:T(8,128)(2,1)}, bf16[128,1024]{1,0:T(8,128)(2,1)}, u32[]{:S(2)}, u32[]{:S(2)}) collective-permute-start(bf16[128,1024]{1,0:T(8,128)(2,1)} %get-tuple-element.24), channel_id=1, source_target_pairs={{0,14},{1,15},{2,0},{3,1},{4,2},{5,3},{6,4},{7,5},{8,6},{9,7},{10,... | collective-permute-start | bytes 786440 | tf_op jit(solution)/shard_map/ppermute | solution.py:26
  97.1 7.9 %collective-permute-start.6 = (bf16[128,1024]{1,0:T(8,128)(2,1)}, bf16[128,1024]{1,0:T(8,128)(2,1)}, u32[]{:S(2)}, u32[]{:S(2)}) collective-permute-start(bf16[128,1024]{1,0:T(8,128)(2,1)} %get-tuple-element.23), channel_id=1, source_target_pairs={{0,2},{1,3},{2,4},{3,5},{4,6},{5,7},{6,8},{7,9},{8,10},{9,11},{10,... | collective-permute-start | bytes 786440 | tf_op jit(solution)/shard_map/ppermute | solution.py:25
  99.2 13.0 %collective-permute-start.15 = (bf16[128,1024]{1,0:T(8,128)(2,1)}, bf16[128,1024]{1,0:T(8,128)(2,1)S(1)}, u32[]{:S(2)}, u32[]{:S(2)}) collective-permute-start(bf16[128,1024]{1,0:T(8,128)(2,1)} %get-tuple-element.15), channel_id=1, source_target_pairs={{0,2},{1,3},{2,4},{3,5},{4,6},{5,7},{6,8},{7,9},{8,10},{9,11},{10,... | collective-permute-start | bytes 786440 | tf_op jit(solution)/shard_map/ppermute | solution.py:25
  99.8 12.4 %collective-permute-start.19 = (bf16[128,1024]{1,0:T(8,128)(2,1)}, bf16[128,1024]{1,0:T(8,128)(2,1)S(1)}, u32[]{:S(2)}, u32[]{:S(2)}) collective-permute-start(bf16[128,1024]{1,0:T(8,128)(2,1)} %get-tuple-element.16), channel_id=1, source_target_pairs={{0,14},{1,15},{2,0},{3,1},{4,2},{5,3},{6,4},{7,5},{8,6},{9,7},{10,... | collective-permute-start | bytes 786440 | tf_op jit(solution)/shard_map/ppermute | solution.py:26
  107.0 6.7 %collective-permute-start.11 = (bf16[128,1024]{1,0:T(8,128)(2,1)}, bf16[128,1024]{1,0:T(8,128)(2,1)}, u32[]{:S(2)}, u32[]{:S(2)}) collective-permute-start(bf16[128,1024]{1,0:T(8,128)(2,1)} %get-tuple-element.22), channel_id=1, source_target_pairs={{0,14},{1,15},{2,0},{3,1},{4,2},{5,3},{6,4},{7,5},{8,6},{9,7},{10,... | collective-permute-start | bytes 786440 | tf_op jit(solution)/shard_map/ppermute | solution.py:26
  109.3 7.9 %collective-permute-start.7 = (bf16[128,1024]{1,0:T(8,128)(2,1)}, bf16[128,1024]{1,0:T(8,128)(2,1)}, u32[]{:S(2)}, u32[]{:S(2)}) collective-permute-start(bf16[128,1024]{1,0:T(8,128)(2,1)} %get-tuple-element.21), channel_id=1, source_target_pairs={{0,2},{1,3},{2,4},{3,5},{4,6},{5,7},{6,8},{7,9},{8,10},{9,11},{10,... | collective-permute-start | bytes 786440 | tf_op jit(solution)/shard_map/ppermute | solution.py:25
  109.3 1.9 %copy-start.3 = (f32[1,384,512]{2,1,0:T(8,128)S(1)}, f32[1,384,512]{2,1,0:T(8,128)}, u32[]{:S(2)}) copy-start(f32[1,384,512]{2,1,0:T(8,128)} %param.15) | copy-start | bytes 2359300
  109.3 1.9 %copy-start.4 = (f32[1,384,512]{2,1,0:T(8,128)S(1)}, f32[1,384,512]{2,1,0:T(8,128)}, u32[]{:S(2)}) copy-start(f32[1,384,512]{2,1,0:T(8,128)} %param.14) | copy-start | bytes 2359300
  109.3 2.1 %copy-start.5 = (f32[384,512]{1,0:T(8,128)S(1)}, f32[384,512]{1,0:T(8,128)}, u32[]{:S(2)}) copy-start(f32[384,512]{1,0:T(8,128)} %param.16) | copy-start | bytes 2359300
  112.1 6.2 %collective-permute-start.20 = (bf16[384,512]{1,0:T(8,128)(2,1)S(1)}, bf16[384,512]{1,0:T(8,128)(2,1)S(1)}, u32[]{:S(2)}, u32[]{:S(2)}) collective-permute-start(bf16[384,512]{1,0:T(8,128)(2,1)S(1)} %fusion.37), channel_id=1, source_target_pairs={{0,64},{64,0},{128,192},{192,128},{1,65},{65,1},{129,193},{193,129... | collective-permute-start | bytes 1179656 | tf_op jit(solution)/shard_map/ppermute | solution.py:145
  118.4 10.0 %collective-permute-start.21 = (bf16[384,512]{1,0:T(8,128)(2,1)S(1)}, bf16[384,512]{1,0:T(8,128)(2,1)S(1)}, u32[]{:S(2)}, u32[]{:S(2)}) collective-permute-start(bf16[384,512]{1,0:T(8,128)(2,1)S(1)} %add_convert_fusion), channel_id=1, source_target_pairs={{0,128},{64,192},{128,0},{192,64},{1,129},{65,193},{129,1},{193,65... | collective-permute-start | bytes 1179656 | tf_op jit(solution)/shard_map/ppermute | solution.py:145
  120.8 8.6 %copy-start.6 = (f32[384,512]{1,0:T(8,128)S(1)}, f32[384,512]{1,0:T(8,128)}, u32[]{:S(2)}) copy-start(f32[384,512]{1,0:T(8,128)} %param.17) | copy-start | bytes 2359300
  128.6 6.5 %collective-permute-start.22 = (bf16[64,2048]{1,0:T(8,128)(2,1)S(1)}, bf16[64,2048]{1,0:T(8,128)(2,1)S(1)}, u32[]{:S(2)}, u32[]{:S(2)}) collective-permute-start(bf16[64,2048]{1,0:T(8,128)(2,1)S(1)} %fusion.43), channel_id=1, source_target_pairs={{0,1},{1,0},{2,3},{3,2},{4,5},{5,4},{6,7},{7,6},{8,9},{9,8},{10,11... | collective-permute-start | bytes 786440 | tf_op jit(solution)/shard_map/ppermute | solution.py:58

commit v11 on v9

--- a/solution.py
+++ b/solution.py
@@ -47,16 +47,18 @@
     halfc = part.shape[1] // 2
     up = [(i, ((i // nlo + 1) % nz) * nlo + i % nlo) for i in range(nmp)]
     down = [(i, ((i // nlo - 1) % nz) * nlo + i % nlo) for i in range(nmp)]
-    pa = part[:, :halfc].reshape(nz, rows, halfc)
-    pb = part[:, halfc:].reshape(nz, rows, halfc)
-    acc = jnp.concatenate(
-        [_z_reduce_scatter(pa, z, nz, up, down), _z_reduce_scatter(pb, z, nz, up, down)], axis=1
-    )
-    mine = lax.dynamic_slice_in_dim(acc, lo * sub, sub, axis=0)
-    other = lax.dynamic_slice_in_dim(acc, (1 - lo) * sub, sub, axis=0)
-    other, sync = lax.optimization_barrier((other, sync))
-    got = lax.ppermute(other.astype(jnp.bfloat16), "mp", [(i, i ^ 1) for i in range(nmp)])
-    return (mine + got.astype(jnp.float32)).astype(jnp.bfloat16), sync
+    pair = [(i, i ^ 1) for i in range(nmp)]
+    outs = []
+    for h in range(2):
+        ph = part[:, h * halfc : (h + 1) * halfc].reshape(nz, rows, halfc)
+        acc = _z_reduce_scatter(ph, z, nz, up, down)
+        mine = lax.dynamic_slice_in_dim(acc, lo * sub, sub, axis=0)
+        other = lax.dynamic_slice_in_dim(acc, (1 - lo) * sub, sub, axis=0)
+        if h == 1:
+            other, sync = lax.optimization_barrier((other, sync))
+        got = lax.ppermute(other.astype(jnp.bfloat16), "mp", pair)
+        outs.append(mine + got.astype(jnp.float32))
+    return jnp.concatenate(outs, axis=1).astype(jnp.bfloat16), sync
 
 
 def shards(

time: 122 us -> 124 us (1.016)
    ppermute x1 -> x2, waiting for transfers between devices: 4.47 us -> 7.84 us  [_ring_reduce_scatter(): got = lax.ppermute(other.astype(jnp.bfloat16), 'mp', pair)]
    ppermute x2, waiting for transfers between devices: 2.02 us -> 0.01 us  [shards(): lax.ppermute(mine, 'outer', perm).astype(jnp.float32)]
  transfers between devices with their start and end apart: 26 -> 27, of which waited for: 12 -> 12; matrix products, arithmetic and copies ran while one was open for 15% -> 15% of each run, Pallas kernels for 0% -> 0%
where the time goes in v11:
time: 124 us; the launch traced here: 123 us
  waiting for transfers between devices  50.2 us (40%)
  starting transfers between devices  39.3 us (32%)
  matrix products  16 us (13%)
  local copies, waits for them, and re-layouts  9.03 us (7%)
  other arithmetic  7.62 us (6%)
    ppermute x1, waiting for transfers between devices, shards(): from_left = lax.ppermute(shard, 'dp', _shift(ndp, 1))  20.9 us
    ppermute x8, starting transfers between devices, _z_reduce_scatter(): lax.ppermute(send_b.astype(jnp.bfloat16), 'mp', down).astype(jnp.float32)  19.5 us
    ppermute x3, waiting for transfers between devices, shards(): got = lax.ppermute(blk.astype(jnp.bfloat16), 'dp', _shift(ndp, s))  8.7 us
    ppermute x2, waiting for transfers between devices, _ring_reduce_scatter(): got = lax.ppermute(other.astype(jnp.bfloat16), 'mp', pair)  7.84 us
    dot_general x5, matrix products, shards(): p1 = jnp.dot(xs, piece[:, :2 * ff], preferred_element_type=jnp.float32)  5.89 us
    ppermute x8, starting transfers between devices, _z_reduce_scatter(): lax.ppermute(send_a.astype(jnp.bfloat16), 'mp', up).astype(jnp.float32)  5.5 us
    unnamed x16, local copies, waits for them, and re-layouts  5.29 us
    ppermute x8, waiting for transfers between devices, _z_reduce_scatter(): lax.ppermute(send_a.astype(jnp.bfloat16), 'mp', up).astype(jnp.float32)  4.69 us
  transfers between devices with their start and end apart: 27, of which 12 were waited for; matrix products, arithmetic and copies ran while one was open for 15% of the time, Pallas kernels for 0%

profile of v11, /device:TPU:8, one launch (start us, length us, event | category | flops | bytes accessed | tf_op | source)
XLA Modules:
  0.0 123.3 jit_solution(8941689130030663114)
XLA Ops:
  0.6 1.2 %copy.14 = bf16[1,512,384]{1,2,0:T(8,128)(2,1)S(1)} copy(bf16[1,512,384]{2,1,0:T(8,128)(2,1)} %param.11) | data formatting | bytes 786432 | tf_op args[2]
  1.9 1.2 copy.15
  3.1 1.1 pad_maximum_fusion
  4.2 1.5 %collective-permute-start = (bf16[512,1152]{0,1:T(8,128)(2,1)}, bf16[512,1152]{0,1:T(8,128)(2,1)S(1)}, u32[]{:S(2)}, u32[]{:S(2)}) collective-permute-start(bf16[512,1152]{0,1:T(8,128)(2,1)} %pad_maximum_fusion), channel_id=1, source_target_pairs={{0,16},{16,32},{32,48},{48,0},{1,17},{17,33},{33,49},{49,1},{2,18}... | collective-permute-start | bytes 3538952 | tf_op jit(solution)/shard_map/ppermute | solution.py:87
  5.7 1.7 %collective-permute-start.1 = (bf16[512,1152]{0,1:T(8,128)(2,1)}, bf16[512,1152]{0,1:T(8,128)(2,1)}, u32[]{:S(2)}, u32[]{:S(2)}) collective-permute-start(bf16[512,1152]{0,1:T(8,128)(2,1)} %pad_maximum_fusion), channel_id=1, source_target_pairs={{0,48},{16,0},{32,16},{48,32},{1,49},{17,1},{33,17},{49,33},{2,50}... | collective-permute-start | bytes 3538952 | tf_op jit(solution)/shard_map/ppermute | solution.py:88
  7.5 0.4 broadcast_in_dim.10
  8.0 1.7 %copy-done.6 = bf16[1,1024,2048]{2,1,0:T(8,128)(2,1)S(1)} copy-done((bf16[1,1024,2048]{2,1,0:T(8,128)(2,1)S(1)}, bf16[1,1024,2048]{2,1,0:T(8,128)(2,1)}, u32[]{:S(2)}) %copy-start.6) | copy-done | bytes 4194328
  9.7 1.0 fusion.10
  10.7 1.2 copy-done.1
  11.9 0.6 fusion.16
  12.5 20.9 %collective-permute-done = bf16[512,1152]{0,1:T(8,128)(2,1)S(1)} collective-permute-done((bf16[512,1152]{0,1:T(8,128)(2,1)}, bf16[512,1152]{0,1:T(8,128)(2,1)S(1)}, u32[]{:S(2)}, u32[]{:S(2)}) %collective-permute-start) | collective-permute-done | bytes 1179680 | tf_op jit(solution)/shard_map/ppermute | solution.py:87
  33.4 0.4 collective-permute-start.2
  33.8 1.1 slice.87
  34.9 3.2 %collective-permute-start.3 = (bf16[256,1152]{0,1:T(8,128)(2,1)S(1)}, bf16[256,1152]{0,1:T(8,128)(2,1)S(1)}, u32[]{:S(2)}, u32[]{:S(2)}) collective-permute-start(bf16[256,1152]{0,1:T(8,128)(2,1)S(1)} %slice.87), channel_id=1, source_target_pairs={{0,48},{16,0},{32,16},{48,32},{1,49},{17,1},{33,17},{49,33},{2,50}... | collective-permute-start | bytes 1769480 | tf_op jit(solution)/shard_map/ppermute | solution.py:90
  38.1 2.2 %fusion.6 = f32[1024,768]{0,1:T(8,128)S(1)} fusion(bf16[1,1024,2048]{2,1,0:T(8,128)(2,1)S(1)} %copy-done.6, s32[]{:T(128)S(6)} %select_n.157, bf16[512,1152]{0,1:T(8,128)(2,1)} %collective-permute-done.1), kind=kOutput, calls=%fused_computation.15 | convolution fusion | flops 805306368 | bytes 4980740 | tf_op jit(solution)/shard_map/dot_general | solution.py:106
  40.3 1.6 %fusion.12 = f32[1024,384]{0,1:T(8,128)S(1)} fusion(bf16[1,1024,2048]{2,1,0:T(8,128)(2,1)S(1)} %copy-done.1, s32[]{:T(128)S(6)} %select_n.157, bf16[512,1152]{0,1:T(8,128)(2,1)} %collective-permute-done.1), kind=kOutput, calls=%fused_computation.21 | convolution fusion | flops 402653184 | bytes 3014660 | tf_op jit(solution)/shard_map/dot_general | solution.py:107
  41.9 0.6 fusion.14
  42.6 1.2 slice_dynamic-update-slice_fusion
  43.9 1.0 fusion.8
  44.9 4.0 %collective-permute-done.2 = bf16[256,1152]{0,1:T(8,128)(2,1)S(1)} collective-permute-done((bf16[256,1152]{0,1:T(8,128)(2,1)S(1)}, bf16[256,1152]{0,1:T(8,128)(2,1)S(1)}, u32[]{:S(2)}, u32[]{:S(2)}) %collective-permute-start.2) | collective-permute-done | bytes 589856 | tf_op jit(solution)/shard_map/ppermute | solution.py:89
  49.0 0.4 fusion.55
  49.4 0.6 fusion.49
  50.1 1.1 add_add_fusion
  51.1 1.1 multiply_convert_fusion.2
  52.3 3.8 %convolution_convert_fusion = bf16[1024,2048]{1,0:T(8,128)(2,1)S(1)} fusion(bf16[2048,768]{0,1:T(8,128)(2,1)S(1)} %slice_dynamic-update-slice_fusion.2, bf16[1024,384]{0,1:T(8,128)(2,1)S(1)} %get-tuple-element.14, bf16[1024,384]{0,1:T(8,128)(2,1)S(1)} %get-tuple-element.13), kind=kOutput, calls=%fused_computation.2 | convolution fusion | flops 3226468352 | bytes 8912896 | tf_op jit(solution)/shard_map/dot_general | solution.py:133
  56.1 0.5 fusion.89
  56.7 2.0 %collective-permute-start.17 = (bf16[128,512]{1,0:T(8,128)(2,1)S(1)}, bf16[128,512]{1,0:T(8,128)(2,1)S(1)}, u32[]{:S(2)}, u32[]{:S(2)}) collective-permute-start(bf16[128,512]{1,0:T(8,128)(2,1)S(1)} %get-tuple-element.34), channel_id=1, source_target_pairs={{0,2},{1,3},{2,4},{3,5},{4,6},{5,7},{6,8},{7,9},{8,10},{9,11},{10,... | collective-permute-start | bytes 393224 | tf_op jit(solution)/shard_map/ppermute | solution.py:25
  58.7 4.0 %collective-permute-start.21 = (bf16[128,512]{1,0:T(8,128)(2,1)S(1)}, bf16[128,512]{1,0:T(8,128)(2,1)S(1)}, u32[]{:S(2)}, u32[]{:S(2)}) collective-permute-start(bf16[128,512]{1,0:T(8,128)(2,1)S(1)} %get-tuple-element.35), channel_id=1, source_target_pairs={{0,14},{1,15},{2,0},{3,1},{4,2},{5,3},{6,4},{7,5},{8,6},{9,7},{10,... | collective-permute-start | bytes 393224 | tf_op jit(solution)/shard_map/ppermute | solution.py:26
  62.9 3.2 %collective-permute-start.8 = (bf16[128,512]{1,0:T(8,128)(2,1)S(1)}, bf16[128,512]{1,0:T(8,128)(2,1)S(1)}, u32[]{:S(2)}, u32[]{:S(2)}) collective-permute-start(bf16[128,512]{1,0:T(8,128)(2,1)S(1)} %get-tuple-element.37), channel_id=1, source_target_pairs={{0,14},{1,15},{2,0},{3,1},{4,2},{5,3},{6,4},{7,5},{8,6},{9,7},{10,... | collective-permute-start | bytes 393224 | tf_op jit(solution)/shard_map/ppermute | solution.py:26
  66.1 1.9 %fusion = f32[384,2048]{1,0:T(8,128)S(1)} fusion(bf16[1,1024,2048]{2,1,0:T(8,128)(2,1)S(1)} %copy-done.1, f32[1024,768]{0,1:T(8,128)S(1)} %add_add_fusion), kind=kOutput, calls=%fused_computation | convolution fusion | flops 1612972032 | bytes 10485760 | tf_op jit(solution)/shard_map/dot_general | solution.py:122
  68.2 3.2 %collective-permute-start.22 = (bf16[128,1024]{1,0:T(8,128)(2,1)S(1)}, bf16[128,1024]{1,0:T(8,128)(2,1)S(1)}, u32[]{:S(2)}, u32[]{:S(2)}) collective-permute-start(bf16[128,1024]{1,0:T(8,128)(2,1)S(1)} %get-tuple-element.25), channel_id=1, source_target_pairs={{0,14},{1,15},{2,0},{3,1},{4,2},{5,3},{6,4},{7,5},{8,6},{9,7},{10,... | collective-permute-start | bytes 786440 | tf_op jit(solution)/shard_map/ppermute | solution.py:26
  71.6 3.2 %collective-permute-start.9 = (bf16[128,1024]{1,0:T(8,128)(2,1)S(1)}, bf16[128,1024]{1,0:T(8,128)(2,1)S(1)}, u32[]{:S(2)}, u32[]{:S(2)}) collective-permute-start(bf16[128,1024]{1,0:T(8,128)(2,1)S(1)} %get-tuple-element.31), channel_id=1, source_target_pairs={{0,14},{1,15},{2,0},{3,1},{4,2},{5,3},{6,4},{7,5},{8,6},{9,7},{10,... | collective-permute-start | bytes 786440 | tf_op jit(solution)/shard_map/ppermute | solution.py:26
  74.8 0.2 dynamic-slice_convert_fusion.2
  75.0 0.7 collective-permute-start.12
  75.7 1.9 %collective-permute-done.18 = bf16[128,1024]{1,0:T(8,128)(2,1)S(1)} collective-permute-done((bf16[128,1024]{1,0:T(8,128)(2,1)S(1)}, bf16[128,1024]{1,0:T(8,128)(2,1)S(1)}, u32[]{:S(2)}, u32[]{:S(2)}) %collective-permute-start.18) | collective-permute-done | bytes 262176 | tf_op jit(solution)/shard_map/ppermute | solution.py:25
  77.6 2.1 %collective-permute-start.13 = (bf16[384,512]{1,0:T(8,128)(2,1)S(1)}, bf16[384,512]{1,0:T(8,128)(2,1)S(1)}, u32[]{:S(2)}, u32[]{:S(2)}) collective-permute-start(bf16[384,512]{1,0:T(8,128)(2,1)S(1)} %get-tuple-element.19), channel_id=1, source_target_pairs={{0,32},{16,48},{32,0},{48,16},{1,33},{17,49},{33,1},{49,17},{2,34}... | collective-permute-start | bytes 1179656 | tf_op jit(solution)/shard_map/ppermute | solution.py:129
  79.8 1.0 collective-permute-start.14
  80.8 0.2 fusion.35
  81.0 0.9 collective-permute-start.19
  81.9 2.5 %collective-permute-start.23 = (bf16[128,1024]{1,0:T(8,128)(2,1)S(1)}, bf16[128,1024]{1,0:T(8,128)(2,1)S(1)}, u32[]{:S(2)}, u32[]{:S(2)}) collective-permute-start(bf16[128,1024]{1,0:T(8,128)(2,1)S(1)} %get-tuple-element.23), channel_id=1, source_target_pairs={{0,14},{1,15},{2,0},{3,1},{4,2},{5,3},{6,4},{7,5},{8,6},{9,7},{10,... | collective-permute-start | bytes 786440 | tf_op jit(solution)/shard_map/ppermute | solution.py:26
  84.3 0.2 fusion.42
  84.5 3.7 %collective-permute-done.12 = bf16[384,512]{1,0:T(8,128)(2,1)S(1)} collective-permute-done((bf16[384,512]{1,0:T(8,128)(2,1)S(1)}, bf16[384,512]{1,0:T(8,128)(2,1)S(1)}, u32[]{:S(2)}, u32[]{:S(2)}) %collective-permute-start.12) | collective-permute-done | bytes 393248 | tf_op jit(solution)/shard_map/ppermute | solution.py:129
  88.3 4.7 %collective-permute-done.13 = bf16[384,512]{1,0:T(8,128)(2,1)S(1)} collective-permute-done((bf16[384,512]{1,0:T(8,128)(2,1)S(1)}, bf16[384,512]{1,0:T(8,128)(2,1)S(1)}, u32[]{:S(2)}, u32[]{:S(2)}) %collective-permute-start.13) | collective-permute-done | bytes 393248 | tf_op jit(solution)/shard_map/ppermute | solution.py:129
  93.0 0.2 collective-permute-done.14
  93.3 1.2 fusion.70
  94.5 1.5 %fusion.69 = (f32[1,384,512]{2,1,0:T(8,128)}, bf16[384,512]{1,0:T(8,128)(2,1)S(1)}) fusion(f32[384,512]{1,0:T(8,128)S(1)} %get-tuple-element.10, f32[1,384,512]{2,1,0:T(8,128)S(1)} %copy-done.4, f32[384,512]{1,0:T(8,128)S(1)} %copy-done.3, f32[1,384,512]{2,1,0:T(8,128)S(1)} %copy-done.2, f32[1,384,512]{2,1,0:T(8,128)S(1)} %copy-done), kind=kLoop, calls=%fused_computation.111 | loop fusion | flops 3342336 | bytes 5111808 | tf_op jit(solution)/shard_map/broadcast_in_dim | solution.py:155
  96.0 0.2 fusion.34
  96.2 1.4 %collective-permute-start.20 = (bf16[128,1024]{1,0:T(8,128)(2,1)S(1)}, bf16[128,1024]{1,0:T(8,128)(2,1)S(1)}, u32[]{:S(2)}, u32[]{:S(2)}) collective-permute-start(bf16[128,1024]{1,0:T(8,128)(2,1)S(1)} %get-tuple-element.20), channel_id=1, source_target_pairs={{0,2},{1,3},{2,4},{3,5},{4,6},{5,7},{6,8},{7,9},{8,10},{9,11},{10,... | collective-permute-start | bytes 786440 | tf_op jit(solution)/shard_map/ppermute | solution.py:25
  97.6 2.2 %collective-permute-start.24 = (bf16[128,1024]{1,0:T(8,128)(2,1)S(1)}, bf16[128,1024]{1,0:T(8,128)(2,1)S(1)}, u32[]{:S(2)}, u32[]{:S(2)}) collective-permute-start(bf16[128,1024]{1,0:T(8,128)(2,1)S(1)} %get-tuple-element.21), channel_id=1, source_target_pairs={{0,14},{1,15},{2,0},{3,1},{4,2},{5,3},{6,4},{7,5},{8,6},{9,7},{10,... | collective-permute-start | bytes 786440 | tf_op jit(solution)/shard_map/ppermute | solution.py:26
  99.8 0.8 collective-permute-done.6
  100.6 0.2 fusion.41
  100.8 1.1 collective-permute-start.11
  101.9 1.0 collective-permute-start.7
  103.0 2.4 %collective-permute-start.16 = (bf16[384,512]{1,0:T(8,128)(2,1)S(1)}, bf16[384,512]{1,0:T(8,128)(2,1)S(1)}, u32[]{:S(2)}, u32[]{:S(2)}) collective-permute-start(bf16[384,512]{1,0:T(8,128)(2,1)S(1)} %add_convert_fusion), channel_id=1, source_target_pairs={{0,128},{64,192},{128,0},{192,64},{1,129},{65,193},{129,1},{193,65... | collective-permute-start | bytes 1179656 | tf_op jit(solution)/shard_map/ppermute | solution.py:149
  105.4 1.5 %collective-permute-done.20 = bf16[128,1024]{1,0:T(8,128)(2,1)S(1)} collective-permute-done((bf16[128,1024]{1,0:T(8,128)(2,1)S(1)}, bf16[128,1024]{1,0:T(8,128)(2,1)S(1)}, u32[]{:S(2)}, u32[]{:S(2)}) %collective-permute-start.20) | collective-permute-done | bytes 262176 | tf_op jit(solution)/shard_map/ppermute | solution.py:25
  106.9 0.1 fusion.37
  107.1 0.5 collective-permute-start.25
  107.6 4.1 %collective-permute-done.11 = bf16[128,1024]{1,0:T(8,128)(2,1)S(1)} collective-permute-done((bf16[128,1024]{1,0:T(8,128)(2,1)S(1)}, bf16[128,1024]{1,0:T(8,128)(2,1)S(1)}, u32[]{:S(2)}, u32[]{:S(2)}) %collective-permute-start.11) | collective-permute-done | bytes 262176 | tf_op jit(solution)/shard_map/ppermute | solution.py:26
  111.7 0.5 collective-permute-done.7
  112.3 5.0 %collective-permute-done.25 = bf16[64,1024]{1,0:T(8,128)(2,1)S(1)} collective-permute-done((bf16[64,1024]{1,0:T(8,128)(2,1)S(1)}, bf16[64,1024]{1,0:T(8,128)(2,1)S(1)}, u32[]{:S(2)}, u32[]{:S(2)}) %collective-permute-start.25) | collective-permute-done | bytes 131104 | tf_op jit(solution)/shard_map/ppermute | solution.py:59
  117.5 0.8 collective-permute-start.26
  118.2 1.4 %multiply_subtract_fusion = (f32[384,512]{1,0:T(8,128)}, f32[384,512]{1,0:T(8,128)}) fusion(f32[384,512]{1,0:T(8,128)S(1)} %copy-done.3, f32[384,512]{1,0:T(8,128)S(1)} %convert_add_fusion, f32[384,512]{1,0:T(8,128)S(1)} %copy-done.5), kind=kLoop, calls=%fused_computation.43 | loop fusion | flops 1376256 | bytes 3932160 | tf_op jit(solution)/shard_map/sub | solution.py:154
  119.6 2.9 %collective-permute-done.26 = bf16[64,1024]{1,0:T(8,128)(2,1)S(1)} collective-permute-done((bf16[64,1024]{1,0:T(8,128)(2,1)S(1)}, bf16[64,1024]{1,0:T(8,128)(2,1)S(1)}, u32[]{:S(2)}, u32[]{:S(2)}) %collective-permute-start.26) | collective-permute-done | bytes 131104 | tf_op jit(solution)/shard_map/ppermute | solution.py:59
  122.5 0.7 pad_maximum_fusion.3
  (51 shorter events, 1.4 us)
Async XLA Ops:
  0.6 2.4 %copy-start = (f32[1,384,512]{2,1,0:T(8,128)S(1)}, f32[1,384,512]{2,1,0:T(8,128)}, u32[]{:S(2)}) copy-start(f32[1,384,512]{2,1,0:T(8,128)} %param.13) | copy-start | bytes 2359300
  4.2 29.1 %collective-permute-start = (bf16[512,1152]{0,1:T(8,128)(2,1)}, bf16[512,1152]{0,1:T(8,128)(2,1)S(1)}, u32[]{:S(2)}, u32[]{:S(2)}) collective-permute-start(bf16[512,1152]{0,1:T(8,128)(2,1)} %pad_maximum_fusion), channel_id=1, source_target_pairs={{0,16},{16,32},{32,48},{48,0},{1,17},{17,33},{33,49},{49,1},{2,18}... | collective-permute-start | bytes 3538952 | tf_op jit(solution)/shard_map/ppermute | solution.py:87
  5.7 28.0 %collective-permute-start.1 = (bf16[512,1152]{0,1:T(8,128)(2,1)}, bf16[512,1152]{0,1:T(8,128)(2,1)}, u32[]{:S(2)}, u32[]{:S(2)}) collective-permute-start(bf16[512,1152]{0,1:T(8,128)(2,1)} %pad_maximum_fusion), channel_id=1, source_target_pairs={{0,48},{16,0},{32,16},{48,32},{1,49},{17,1},{33,17},{49,33},{2,50}... | collective-permute-start | bytes 3538952 | tf_op jit(solution)/shard_map/ppermute | solution.py:88
  7.5 2.2 %copy-start.6 = (bf16[1,1024,2048]{2,1,0:T(8,128)(2,1)S(1)}, bf16[1,1024,2048]{2,1,0:T(8,128)(2,1)}, u32[]{:S(2)}) copy-start(bf16[1,1024,2048]{2,1,0:T(8,128)(2,1)} %param.9) | copy-start | bytes 12582916
  9.7 2.2 %copy-start.1 = (bf16[1,1024,2048]{2,1,0:T(8,128)(2,1)S(1)}, bf16[1,1024,2048]{2,1,0:T(8,128)(2,1)}, u32[]{:S(2)}) copy-start(bf16[1,1024,2048]{2,1,0:T(8,128)(2,1)} %param.10) | copy-start | bytes 12582916
  33.4 15.5 %collective-permute-start.2 = (bf16[256,1152]{0,1:T(8,128)(2,1)S(1)}, bf16[256,1152]{0,1:T(8,128)(2,1)S(1)}, u32[]{:S(2)}, u32[]{:S(2)}) collective-permute-start(bf16[256,1152]{0,1:T(8,128)(2,1)S(1)} %slice.85), channel_id=1, source_target_pairs={{0,16},{16,32},{32,48},{48,0},{1,17},{17,33},{33,49},{49,1},{2,18}... | collective-permute-start | bytes 1769480 | tf_op jit(solution)/shard_map/ppermute | solution.py:89
  34.9 15.1 %collective-permute-start.3 = (bf16[256,1152]{0,1:T(8,128)(2,1)S(1)}, bf16[256,1152]{0,1:T(8,128)(2,1)S(1)}, u32[]{:S(2)}, u32[]{:S(2)}) collective-permute-start(bf16[256,1152]{0,1:T(8,128)(2,1)S(1)} %slice.87), channel_id=1, source_target_pairs={{0,48},{16,0},{32,16},{48,32},{1,49},{17,1},{33,17},{49,33},{2,50}... | collective-permute-start | bytes 1769480 | tf_op jit(solution)/shard_map/ppermute | solution.py:90
  56.7 11.3 %collective-permute-start.17 = (bf16[128,512]{1,0:T(8,128)(2,1)S(1)}, bf16[128,512]{1,0:T(8,128)(2,1)S(1)}, u32[]{:S(2)}, u32[]{:S(2)}) collective-permute-start(bf16[128,512]{1,0:T(8,128)(2,1)S(1)} %get-tuple-element.34), channel_id=1, source_target_pairs={{0,2},{1,3},{2,4},{3,5},{4,6},{5,7},{6,8},{7,9},{8,10},{9,11},{10,... | collective-permute-start | bytes 393224 | tf_op jit(solution)/shard_map/ppermute | solution.py:25
  58.7 9.3 %collective-permute-start.21 = (bf16[128,512]{1,0:T(8,128)(2,1)S(1)}, bf16[128,512]{1,0:T(8,128)(2,1)S(1)}, u32[]{:S(2)}, u32[]{:S(2)}) collective-permute-start(bf16[128,512]{1,0:T(8,128)(2,1)S(1)} %get-tuple-element.35), channel_id=1, source_target_pairs={{0,14},{1,15},{2,0},{3,1},{4,2},{5,3},{6,4},{7,5},{8,6},{9,7},{10,... | collective-permute-start | bytes 393224 | tf_op jit(solution)/shard_map/ppermute | solution.py:26
  62.8 8.6 %collective-permute-start.4 = (bf16[128,512]{1,0:T(8,128)(2,1)S(1)}, bf16[128,512]{1,0:T(8,128)(2,1)S(1)}, u32[]{:S(2)}, u32[]{:S(2)}) collective-permute-start(bf16[128,512]{1,0:T(8,128)(2,1)S(1)} %get-tuple-element.36), channel_id=1, source_target_pairs={{0,2},{1,3},{2,4},{3,5},{4,6},{5,7},{6,8},{7,9},{8,10},{9,11},{10,... | collective-permute-start | bytes 393224 | tf_op jit(solution)/shard_map/ppermute | solution.py:25
  62.9 8.6 %collective-permute-start.8 = (bf16[128,512]{1,0:T(8,128)(2,1)S(1)}, bf16[128,512]{1,0:T(8,128)(2,1)S(1)}, u32[]{:S(2)}, u32[]{:S(2)}) collective-permute-start(bf16[128,512]{1,0:T(8,128)(2,1)S(1)} %get-tuple-element.37), channel_id=1, source_target_pairs={{0,14},{1,15},{2,0},{3,1},{4,2},{5,3},{6,4},{7,5},{8,6},{9,7},{10,... | collective-permute-start | bytes 393224 | tf_op jit(solution)/shard_map/ppermute | solution.py:26
  68.1 9.5 %collective-permute-start.18 = (bf16[128,1024]{1,0:T(8,128)(2,1)S(1)}, bf16[128,1024]{1,0:T(8,128)(2,1)S(1)}, u32[]{:S(2)}, u32[]{:S(2)}) collective-permute-start(bf16[128,1024]{1,0:T(8,128)(2,1)S(1)} %get-tuple-element.24), channel_id=1, source_target_pairs={{0,2},{1,3},{2,4},{3,5},{4,6},{5,7},{6,8},{7,9},{8,10},{9,11},{10,... | collective-permute-start | bytes 786440 | tf_op jit(solution)/shard_map/ppermute | solution.py:25
  68.2 11.6 %collective-permute-start.22 = (bf16[128,1024]{1,0:T(8,128)(2,1)S(1)}, bf16[128,1024]{1,0:T(8,128)(2,1)S(1)}, u32[]{:S(2)}, u32[]{:S(2)}) collective-permute-start(bf16[128,1024]{1,0:T(8,128)(2,1)S(1)} %get-tuple-element.25), channel_id=1, source_target_pairs={{0,14},{1,15},{2,0},{3,1},{4,2},{5,3},{6,4},{7,5},{8,6},{9,7},{10,... | collective-permute-start | bytes 786440 | tf_op jit(solution)/shard_map/ppermute | solution.py:26
  71.5 9.5 %collective-permute-start.5 = (bf16[128,1024]{1,0:T(8,128)(2,1)S(1)}, bf16[128,1024]{1,0:T(8,128)(2,1)S(1)}, u32[]{:S(2)}, u32[]{:S(2)}) collective-permute-start(bf16[128,1024]{1,0:T(8,128)(2,1)S(1)} %get-tuple-element.30), channel_id=1, source_target_pairs={{0,2},{1,3},{2,4},{3,5},{4,6},{5,7},{6,8},{7,9},{8,10},{9,11},{10,... | collective-permute-start | bytes 786440 | tf_op jit(solution)/shard_map/ppermute | solution.py:25
  71.6 10.3 %collective-permute-start.9 = (bf16[128,1024]{1,0:T(8,128)(2,1)S(1)}, bf16[128,1024]{1,0:T(8,128)(2,1)S(1)}, u32[]{:S(2)}, u32[]{:S(2)}) collective-permute-start(bf16[128,1024]{1,0:T(8,128)(2,1)S(1)} %get-tuple-element.31), channel_id=1, source_target_pairs={{0,14},{1,15},{2,0},{3,1},{4,2},{5,3},{6,4},{7,5},{8,6},{9,7},{10,... | collective-permute-start | bytes 786440 | tf_op jit(solution)/shard_map/ppermute | solution.py:26
  75.0 18.3 %copy-start.2 = (f32[1,384,512]{2,1,0:T(8,128)S(1)}, f32[1,384,512]{2,1,0:T(8,128)}, u32[]{:S(2)}) copy-start(f32[1,384,512]{2,1,0:T(8,128)} %param.15) | copy-start | bytes 2359300
  75.0 13.3 %collective-permute-start.12 = (bf16[384,512]{1,0:T(8,128)(2,1)S(1)}, bf16[384,512]{1,0:T(8,128)(2,1)S(1)}, u32[]{:S(2)}, u32[]{:S(2)}) collective-permute-start(bf16[384,512]{1,0:T(8,128)(2,1)S(1)} %get-tuple-element.17), channel_id=1, source_target_pairs={{0,16},{16,32},{32,48},{48,0},{1,17},{17,33},{33,49},{49,1},{2,18}... | collective-permute-start | bytes 1179656 | tf_op jit(solution)/shard_map/ppermute | solution.py:129
  77.6 15.4 %collective-permute-start.13 = (bf16[384,512]{1,0:T(8,128)(2,1)S(1)}, bf16[384,512]{1,0:T(8,128)(2,1)S(1)}, u32[]{:S(2)}, u32[]{:S(2)}) collective-permute-start(bf16[384,512]{1,0:T(8,128)(2,1)S(1)} %get-tuple-element.19), channel_id=1, source_target_pairs={{0,32},{16,48},{32,0},{48,16},{1,33},{17,49},{33,1},{49,17},{2,34}... | collective-permute-start | bytes 1179656 | tf_op jit(solution)/shard_map/ppermute | solution.py:129
  79.8 13.5 %collective-permute-start.14 = (bf16[384,512]{1,0:T(8,128)(2,1)S(1)}, bf16[384,512]{1,0:T(8,128)(2,1)S(1)}, u32[]{:S(2)}, u32[]{:S(2)}) collective-permute-start(bf16[384,512]{1,0:T(8,128)(2,1)S(1)} %get-tuple-element.18), channel_id=1, source_target_pairs={{0,48},{16,0},{32,16},{48,32},{1,49},{17,1},{33,17},{49,33},{2,50}... | collective-permute-start | bytes 1179656 | tf_op jit(solution)/shard_map/ppermute | solution.py:129
  81.0 15.0 %collective-permute-start.19 = (bf16[128,1024]{1,0:T(8,128)(2,1)S(1)}, bf16[128,1024]{1,0:T(8,128)(2,1)S(1)}, u32[]{:S(2)}, u32[]{:S(2)}) collective-permute-start(bf16[128,1024]{1,0:T(8,128)(2,1)S(1)} %get-tuple-element.22), channel_id=1, source_target_pairs={{0,2},{1,3},{2,4},{3,5},{4,6},{5,7},{6,8},{7,9},{8,10},{9,11},{10,... | collective-permute-start | bytes 786440 | tf_op jit(solution)/shard_map/ppermute | solution.py:25
  81.9 14.2 %collective-permute-start.23 = (bf16[128,1024]{1,0:T(8,128)(2,1)S(1)}, bf16[128,1024]{1,0:T(8,128)(2,1)S(1)}, u32[]{:S(2)}, u32[]{:S(2)}) collective-permute-start(bf16[128,1024]{1,0:T(8,128)(2,1)S(1)} %get-tuple-element.23), channel_id=1, source_target_pairs={{0,14},{1,15},{2,0},{3,1},{4,2},{5,3},{6,4},{7,5},{8,6},{9,7},{10,... | collective-permute-start | bytes 786440 | tf_op jit(solution)/shard_map/ppermute | solution.py:26
  88.3 11.6 %collective-permute-start.10 = (bf16[128,1024]{1,0:T(8,128)(2,1)S(1)}, bf16[128,1024]{1,0:T(8,128)(2,1)S(1)}, u32[]{:S(2)}, u32[]{:S(2)}) collective-permute-start(bf16[128,1024]{1,0:T(8,128)(2,1)S(1)} %get-tuple-element.29), channel_id=1, source_target_pairs={{0,14},{1,15},{2,0},{3,1},{4,2},{5,3},{6,4},{7,5},{8,6},{9,7},{10,... | collective-permute-start | bytes 786440 | tf_op jit(solution)/shard_map/ppermute | solution.py:26
  93.0 1.5 %copy-start.3 = (f32[384,512]{1,0:T(8,128)S(1)}, f32[384,512]{1,0:T(8,128)}, u32[]{:S(2)}) copy-start(f32[384,512]{1,0:T(8,128)} %param.16) | copy-start | bytes 2359300
  93.0 1.5 %copy-start.4 = (f32[1,384,512]{2,1,0:T(8,128)S(1)}, f32[1,384,512]{2,1,0:T(8,128)}, u32[]{:S(2)}) copy-start(f32[1,384,512]{2,1,0:T(8,128)} %param.14) | copy-start | bytes 2359300
  93.0 7.6 %collective-permute-start.6 = (bf16[128,1024]{1,0:T(8,128)(2,1)S(1)}, bf16[128,1024]{1,0:T(8,128)(2,1)S(1)}, u32[]{:S(2)}, u32[]{:S(2)}) collective-permute-start(bf16[128,1024]{1,0:T(8,128)(2,1)S(1)} %get-tuple-element.28), channel_id=1, source_target_pairs={{0,2},{1,3},{2,4},{3,5},{4,6},{5,7},{6,8},{7,9},{8,10},{9,11},{10,... | collective-permute-start | bytes 786440 | tf_op jit(solution)/shard_map/ppermute | solution.py:25
  96.0 6.9 %collective-permute-start.15 = (bf16[384,512]{1,0:T(8,128)(2,1)S(1)}, bf16[384,512]{1,0:T(8,128)(2,1)S(1)}, u32[]{:S(2)}, u32[]{:S(2)}) collective-permute-start(bf16[384,512]{1,0:T(8,128)(2,1)S(1)} %get-tuple-element.33), channel_id=1, source_target_pairs={{0,64},{64,0},{128,192},{192,128},{1,65},{65,1},{129,193},{193,129... | collective-permute-start | bytes 1179656 | tf_op jit(solution)/shard_map/ppermute | solution.py:149
  96.2 10.6 %collective-permute-start.20 = (bf16[128,1024]{1,0:T(8,128)(2,1)S(1)}, bf16[128,1024]{1,0:T(8,128)(2,1)S(1)}, u32[]{:S(2)}, u32[]{:S(2)}) collective-permute-start(bf16[128,1024]{1,0:T(8,128)(2,1)S(1)} %get-tuple-element.20), channel_id=1, source_target_pairs={{0,2},{1,3},{2,4},{3,5},{4,6},{5,7},{6,8},{7,9},{8,10},{9,11},{10,... | collective-permute-start | bytes 786440 | tf_op jit(solution)/shard_map/ppermute | solution.py:25
  97.6 9.3 %collective-permute-start.24 = (bf16[128,1024]{1,0:T(8,128)(2,1)S(1)}, bf16[128,1024]{1,0:T(8,128)(2,1)S(1)}, u32[]{:S(2)}, u32[]{:S(2)}) collective-permute-start(bf16[128,1024]{1,0:T(8,128)(2,1)S(1)} %get-tuple-element.21), channel_id=1, source_target_pairs={{0,14},{1,15},{2,0},{3,1},{4,2},{5,3},{6,4},{7,5},{8,6},{9,7},{10,... | collective-permute-start | bytes 786440 | tf_op jit(solution)/shard_map/ppermute | solution.py:26
  100.8 10.9 %collective-permute-start.11 = (bf16[128,1024]{1,0:T(8,128)(2,1)S(1)}, bf16[128,1024]{1,0:T(8,128)(2,1)S(1)}, u32[]{:S(2)}, u32[]{:S(2)}) collective-permute-start(bf16[128,1024]{1,0:T(8,128)(2,1)S(1)} %get-tuple-element.27), channel_id=1, source_target_pairs={{0,14},{1,15},{2,0},{3,1},{4,2},{5,3},{6,4},{7,5},{8,6},{9,7},{10,... | collective-permute-start | bytes 786440 | tf_op jit(solution)/shard_map/ppermute | solution.py:26
  101.9 10.3 %collective-permute-start.7 = (bf16[128,1024]{1,0:T(8,128)(2,1)S(1)}, bf16[128,1024]{1,0:T(8,128)(2,1)S(1)}, u32[]{:S(2)}, u32[]{:S(2)}) collective-permute-start(bf16[128,1024]{1,0:T(8,128)(2,1)S(1)} %get-tuple-element.26), channel_id=1, source_target_pairs={{0,2},{1,3},{2,4},{3,5},{4,6},{5,7},{6,8},{7,9},{8,10},{9,11},{10,... | collective-permute-start | bytes 786440 | tf_op jit(solution)/shard_map/ppermute | solution.py:25
  103.0 14.3 %collective-permute-start.16 = (bf16[384,512]{1,0:T(8,128)(2,1)S(1)}, bf16[384,512]{1,0:T(8,128)(2,1)S(1)}, u32[]{:S(2)}, u32[]{:S(2)}) collective-permute-start(bf16[384,512]{1,0:T(8,128)(2,1)S(1)} %add_convert_fusion), channel_id=1, source_target_pairs={{0,128},{64,192},{128,0},{192,64},{1,129},{65,193},{129,1},{193,65... | collective-permute-start | bytes 1179656 | tf_op jit(solution)/shard_map/ppermute | solution.py:149
  107.0 11.2 %copy-start.5 = (f32[384,512]{1,0:T(8,128)S(1)}, f32[384,512]{1,0:T(8,128)}, u32[]{:S(2)}) copy-start(f32[384,512]{1,0:T(8,128)} %param.17) | copy-start | bytes 2359300
  107.1 10.2 %collective-permute-start.25 = (bf16[64,1024]{1,0:T(8,128)(2,1)S(1)}, bf16[64,1024]{1,0:T(8,128)(2,1)S(1)}, u32[]{:S(2)}, u32[]{:S(2)}) collective-permute-start(bf16[64,1024]{1,0:T(8,128)(2,1)S(1)} %dynamic-slice_convert_fusion.3), channel_id=1, source_target_pairs={{0,1},{1,0},{2,3},{3,2},{4,5},{5,4},{6,7},{7,6},{8,9},{9,8},{10,11... | collective-permute-start | bytes 393224 | tf_op jit(solution)/shard_map/ppermute | solution.py:59
  117.5 5.1 %collective-permute-start.26 = (bf16[64,1024]{1,0:T(8,128)(2,1)S(1)}, bf16[64,1024]{1,0:T(8,128)(2,1)S(1)}, u32[]{:S(2)}, u32[]{:S(2)}) collective-permute-start(bf16[64,1024]{1,0:T(8,128)(2,1)S(1)} %constant_dynamic-slice_fusion), channel_id=1, source_target_pairs={{0,1},{1,0},{2,3},{3,2},{4,5},{5,4},{6,7},{7,6},{8,9},{9,8},{10,11... | collective-permute-start | bytes 393224 | tf_op jit(solution)/shard_map/ppermute | solution.py:59

commit v12 on v9

--- a/solution.py
+++ b/solution.py
@@ -79,33 +79,49 @@
     ff = master.shape[0]
 
     assert ndp == 4
-    shard = jnp.concatenate([gate_weight[0], up_weight[0], down_half.T], axis=1)
-    rows = shard.shape[0]
+    rows = gate_weight.shape[1]
+    dcols = down_half.shape[1]
+    shard = jnp.concatenate(
+        [gate_weight[0], up_weight[0], down_half.reshape(rows, -1)], axis=1
+    )
     half = rows // 2
     from_left = lax.ppermute(shard, "dp", _shift(ndp, 1))
     from_right = lax.ppermute(shard, "dp", _shift(ndp, -1))
     far_a = lax.ppermute(from_left[:half], "dp", _shift(ndp, 1))
     far_b = lax.ppermute(from_right[half:], "dp", _shift(ndp, -1))
-    pieces = [
-        (j * rows, shard),
-        (((j - 1) % ndp) * rows, from_left),
-        (((j + 1) % ndp) * rows, from_right),
-        (((j + 2) % ndp) * rows, far_a),
-        (((j + 2) % ndp) * rows + half, far_b),
+
+    def down_of(piece):
+        return piece[:, 2 * ff :].reshape(-1, dcols)
+
+    far = (j + 2) % ndp
+    gu_pieces = [
+        (j * rows, shard[:, : 2 * ff]),
+        (((j - 1) % ndp) * rows, from_left[:, : 2 * ff]),
+        (((j + 1) % ndp) * rows, from_right[:, : 2 * ff]),
+        (far * rows, far_a[:, : 2 * ff]),
+        (far * rows + half, far_b[:, : 2 * ff]),
+    ]
+    down_pieces = [
+        (j * rows, down_half),
+        (((j - 1) % ndp) * rows, down_of(from_left)),
+        (((j + 1) % ndp) * rows, down_of(from_right)),
+        (far * rows, jnp.concatenate([down_of(far_a), down_of(far_b)], axis=0)),
     ]
 
     gu_pre = None
     grad_hidden = None
     weights_full = jnp.zeros((rows * ndp, 2 * ff), jnp.bfloat16)
-    for start, piece in pieces:
-        size = piece.shape[0]
-        xs = lax.dynamic_slice_in_dim(inputs, start, size, axis=1)
-        gs = lax.dynamic_slice_in_dim(upstream, start, size, axis=1)
-        p1 = jnp.dot(xs, piece[:, : 2 * ff], preferred_element_type=jnp.float32)
-        p2 = jnp.dot(gs, piece[:, 2 * ff :], preferred_element_type=jnp.float32)
+    for start, piece in gu_pieces:
+        xs = lax.dynamic_slice_in_dim(inputs, start, piece.shape[0], axis=1)
+        p1 = jnp.dot(xs, piece, preferred_element_type=jnp.float32)
         gu_pre = p1 if gu_pre is None else gu_pre + p1
+        weights_full = lax.dynamic_update_slice(weights_full, piece, (start, 0))
+    for start, piece in down_pieces:
+        gs = lax.dynamic_slice_in_dim(upstream, start, piece.shape[1], axis=1)
+        p2 = lax.dot_general(
+            gs, piece, (((1,), (1,)), ((), ())), preferred_element_type=jnp.float32
+        )
         grad_hidden = p2 if grad_hidden is None else grad_hidden + p2
-        weights_full = lax.dynamic_update_slice(weights_full, piece[:, : 2 * ff], (start, 0))
 
     gate_pre = gu_pre[:, :ff]
     up_pre = gu_pre[:, ff:]

time: 122 us -> 137 us (1.12)
  matrix products: 16 us -> 30.9 us
  waiting for transfers between devices: 49.4 us -> 43.7 us
  local copies, waits for them, and re-layouts: 8.98 us -> 13.2 us
  other arithmetic: 7.64 us -> 9.89 us
    dot_general x10 -> x9, matrix products: 10.3 us -> 25.3 us  [the longest x5 14.9 us: shards(): p1 = jnp.dot(xs, piece, preferred_element_type=jnp.float32)]
    ppermute x1, waiting for transfers between devices: 4 us -> 0.01 us  [shards(): far_a = lax.ppermute(from_left[:half], 'dp', _shift(ndp, 1))]
    ppermute x1, waiting for transfers between devices: 20.9 us -> 17.9 us  [shards(): from_left = lax.ppermute(shard, 'dp', _shift(ndp, 1))]
    unnamed x16 -> x40, local copies, waits for them, and re-layouts: 5.29 us -> 2.55 us
    dynamic_update_slice x4, local copies, waits for them, and re-layouts: 1.41 us -> 3.98 us  [shards(): weights_full = lax.dynamic_update_slice(weights_full, piece, (start, 0))]
    ppermute x8, waiting for transfers between devices: 4.66 us -> 6.84 us  [_z_reduce_scatter(): lax.ppermute(send_a.astype(jnp.bfloat16), 'mp', up).astype(jnp.float32)]
    ppermute x3, starting transfers between devices: 3.91 us -> 1.8 us  [shards(): got = lax.ppermute(blk.astype(jnp.bfloat16), 'dp', _shift(ndp, s))]
    ppermute x8, starting transfers between devices: 19.5 us -> 21.5 us  [_z_reduce_scatter(): lax.ppermute(send_b.astype(jnp.bfloat16), 'mp', down).astype(jnp.float32)]
  transfers between devices with their start and end apart: 26 -> 26, of which waited for: 12 -> 9; matrix products, arithmetic and copies ran while one was open for 15% -> 24% of each run, Pallas kernels for 0% -> 0%
where the time goes in v12:
time: 137 us
  waiting for transfers between devices  43.7 us (32%)
  starting transfers between devices  38.1 us (28%)
  matrix products  30.9 us (23%)
  local copies, waits for them, and re-layouts  13.2 us (10%)
  other arithmetic  9.89 us (7%)
    ppermute x8, starting transfers between devices, _z_reduce_scatter(): lax.ppermute(send_b.astype(jnp.bfloat16), 'mp', down).astype(jnp.float32)  21.5 us
    ppermute x1, waiting for transfers between devices, shards(): from_left = lax.ppermute(shard, 'dp', _shift(ndp, 1))  17.9 us
    dot_general x5, matrix products, shards(): p1 = jnp.dot(xs, piece, preferred_element_type=jnp.float32)  14.9 us
    dot_general x4, matrix products, shards(): lax.dot_general(gs, piece, (((1,), (1,)), ((), ())), preferred_element_ty...  10.4 us
    ppermute x3, waiting for transfers between devices, shards(): got = lax.ppermute(blk.astype(jnp.bfloat16), 'dp', _shift(ndp, s))  7.85 us
    ppermute x8, waiting for transfers between devices, _z_reduce_scatter(): lax.ppermute(send_a.astype(jnp.bfloat16), 'mp', up).astype(jnp.float32)  6.84 us
    ppermute x8, starting transfers between devices, _z_reduce_scatter(): lax.ppermute(send_a.astype(jnp.bfloat16), 'mp', up).astype(jnp.float32)  5.42 us
    ppermute x1, waiting for transfers between devices, _ring_reduce_scatter(): lax.ppermute(other.astype(jnp.bfloat16), 'mp', [(i, i ^ 1) for i in range...  4.8 us
  transfers between devices with their start and end apart: 26, of which 9 were waited for; matrix products, arithmetic and copies ran while one was open for 24% of the time, Pallas kernels for 0%

profile of v12, /device:TPU:8, one launch (start us, length us, event | category | flops | bytes accessed | tf_op | source)
XLA Modules:
  0.0 136.9 jit_solution(322544661337302642)
XLA Ops:
  0.6 1.2 convert_element_type.239
  1.8 0.3 convert_element_type.241
  2.1 2.3 %pad_maximum_fusion = bf16[512,1152]{1,0:T(8,128)(2,1)} fusion(bf16[512,384]{1,0:T(8,128)(2,1)S(1)} %convert_element_type.241, bf16[512,384]{1,0:T(8,128)(2,1)} %bitcast.133, bf16[512,384]{1,0:T(8,128)(2,1)} %bitcast.136), kind=kLoop, calls=%fused_computation.18 | loop fusion | flops 3538944 | bytes 2359296 | tf_op jit(solution)/shard_map/concatenate | solution.py:84
  4.4 1.5 %collective-permute-start = (bf16[512,1152]{1,0:T(8,128)(2,1)}, bf16[512,1152]{1,0:T(8,128)(2,1)S(1)}, u32[]{:S(2)}, u32[]{:S(2)}) collective-permute-start(bf16[512,1152]{1,0:T(8,128)(2,1)} %pad_maximum_fusion), channel_id=1, source_target_pairs={{0,16},{16,32},{32,48},{48,0},{1,17},{17,33},{33,49},{49,1},{2,18}... | collective-permute-start | bytes 3538952 | tf_op jit(solution)/shard_map/ppermute | solution.py:88
  5.9 1.7 %collective-permute-start.1 = (bf16[512,1152]{1,0:T(8,128)(2,1)}, bf16[512,1152]{1,0:T(8,128)(2,1)S(1)}, u32[]{:S(2)}, u32[]{:S(2)}) collective-permute-start(bf16[512,1152]{1,0:T(8,128)(2,1)} %pad_maximum_fusion), channel_id=1, source_target_pairs={{0,48},{16,0},{32,16},{48,32},{1,49},{17,1},{33,17},{49,33},{2,50}... | collective-permute-start | bytes 3538952 | tf_op jit(solution)/shard_map/ppermute | solution.py:89
  8.0 4.7 %fusion.10 = f32[1024,768]{0,1:T(8,128)} fusion(bf16[1,1024,2048]{2,1,0:T(8,128)(2,1)} %param.9, s32[]{:T(128)S(6)} %select_n.152, bf16[512,384]{1,0:T(8,128)(2,1)S(1)} %bitcast.135, bf16[512,384]{1,0:T(8,128)(2,1)S(1)} %bitcast.138), kind=kOutput, calls=%fused_computation.23 | convolution fusion | flops 806879232 | bytes 4980740 | tf_op jit(solution)/shard_map/dot_general | solution.py:116
  12.6 3.0 %fusion.20 = f32[1024,384]{0,1:T(8,128)} fusion(bf16[1,1024,2048]{2,1,0:T(8,128)(2,1)} %param.10, s32[]{:T(128)S(6)} %select_n.152, bf16[1,384,512]{2,1,0:T(8,128)(2,1)S(1)} %convert_element_type.239), kind=kOutput, calls=%fused_computation.31 | convolution fusion | flops 402653184 | bytes 3014660 | tf_op jit(solution)/shard_map/dot_general | solution.py:121
  15.7 17.9 %collective-permute-done = bf16[512,1152]{1,0:T(8,128)(2,1)S(1)} collective-permute-done((bf16[512,1152]{1,0:T(8,128)(2,1)}, bf16[512,1152]{1,0:T(8,128)(2,1)S(1)}, u32[]{:S(2)}, u32[]{:S(2)}) %collective-permute-start) | collective-permute-done | bytes 1179680 | tf_op jit(solution)/shard_map/ppermute | solution.py:88
  33.5 0.9 slice.80
  34.5 0.3 collective-permute-start.2
  34.8 0.9 slice.82
  35.7 3.0 %collective-permute-start.3 = (bf16[256,1152]{1,0:T(8,128)(2,1)}, bf16[256,1152]{1,0:T(8,128)(2,1)}, u32[]{:S(2)}, u32[]{:S(2)}) collective-permute-start(bf16[256,1152]{1,0:T(8,128)(2,1)} %slice.82), channel_id=1, source_target_pairs={{0,48},{16,0},{32,16},{48,32},{1,49},{17,1},{33,17},{49,33},{2,50}... | collective-permute-start | bytes 1769480 | tf_op jit(solution)/shard_map/ppermute | solution.py:91
  38.7 0.3 reshape.78
  39.1 0.3 reshape.77
  39.4 3.2 %fusion.16 = f32[1024,384]{0,1:T(8,128)} fusion(bf16[384,512]{1,0:T(8,128)(2,1)S(1)} %reshape.78, bf16[1,1024,2048]{2,1,0:T(8,128)(2,1)} %param.10, s32[]{:T(128)S(6)} %select_n.156), kind=kOutput, calls=%fused_computation.27 | convolution fusion | flops 402653184 | bytes 3014660 | tf_op jit(solution)/shard_map/dot_general | solution.py:121
  42.6 3.0 %fusion.18 = f32[1024,384]{0,1:T(8,128)} fusion(bf16[384,512]{1,0:T(8,128)(2,1)S(1)} %reshape.77, bf16[1,1024,2048]{2,1,0:T(8,128)(2,1)} %param.10, s32[]{:T(128)S(6)} %select_n.154), kind=kOutput, calls=%fused_computation.29 | convolution fusion | flops 402653184 | bytes 3014660 | tf_op jit(solution)/shard_map/dot_general | solution.py:121
  45.6 2.3 %fusion.6 = f32[1024,768]{0,1:T(8,128)S(1)} fusion(bf16[1,1024,2048]{2,1,0:T(8,128)(2,1)S(1)} %copy-done.10, s32[]{:T(128)S(6)} %select_n.156, bf16[512,1152]{1,0:T(8,128)(2,1)} %copy-done.3), kind=kOutput, calls=%fused_computation.19 | convolution fusion | flops 805306368 | bytes 4980740 | tf_op jit(solution)/shard_map/dot_general | solution.py:116
  47.9 1.0 slice_dynamic-update-slice_fusion.1
  48.9 1.0 slice_dynamic-update-slice_fusion
  49.8 2.8 %fusion.8 = f32[1024,768]{0,1:T(8,128)} fusion(bf16[1,1024,2048]{2,1,0:T(8,128)(2,1)S(1)} %copy-done.10, s32[]{:T(128)S(6)} %select_n.154, bf16[512,1152]{1,0:T(8,128)(2,1)S(1)} %copy-done.2), kind=kOutput, calls=%fused_computation.21 | convolution fusion | flops 805306368 | bytes 4980740 | tf_op jit(solution)/shard_map/dot_general | solution.py:116
  52.6 0.9 slice.81
  53.7 0.9 slice.83
  54.7 0.8 reshape.80
  55.5 1.9 %fusion.58 = f32[1024,768]{0,1:T(8,128)S(1)} fusion(bf16[1,1024,2048]{2,1,0:T(8,128)(2,1)} %param.9, s32[]{:T(128)S(6)} %select_n.158, bf16[256,1152]{1,0:T(8,128)(2,1)} %collective-permute-done.2), kind=kOutput, calls=%fused_computation.95 | convolution fusion | flops 402653184 | bytes 4063236 | tf_op jit(solution)/shard_map/dot_general | solution.py:116
  57.5 0.2 copy-done
  57.7 3.2 %add_add_fusion = f32[1024,768]{0,1:T(8,128)S(1)} fusion(f32[1024,768]{0,1:T(8,128)S(1)} %fusion.58, f32[1024,768]{0,1:T(8,128)S(1)} %fusion.6, f32[1024,768]{0,1:T(8,128)} %fusion.10, f32[1024,768]{0,1:T(8,128)S(1)} %copy-done, bf16[1,1024,2048]{2,1,0:T(8,128)(2,1)} %param.9, s32[]{:T(128)S(6)} %select_n.159, bf16[256,1152]{1,0:T(8,128)(2,1)} %collective-permute-done.3), kind=kOutput, calls=%fused_computation.3 | convolution fusion | flops 405798912 | bytes 16646148 | tf_op jit(solution)/shard_map/dot_general | solution.py:116
  61.1 0.5 copy-done.12
  61.6 0.5 copy-done.13
  62.1 0.4 copy-done.14
  62.5 1.3 multiply_convert_fusion.2
  63.8 0.6 copy-done.8
  64.4 1.0 slice_dynamic-update-slice_fusion.3
  65.5 1.0 slice_dynamic-update-slice_fusion.2
  66.5 3.7 %convolution_convert_fusion = bf16[1024,2048]{1,0:T(8,128)(2,1)S(1)} fusion(bf16[2048,768]{1,0:T(8,128)(2,1)S(1)} %slice_dynamic-update-slice_fusion.2, bf16[1024,384]{0,1:T(8,128)(2,1)S(1)} %get-tuple-element.14, bf16[1024,384]{0,1:T(8,128)(2,1)S(1)} %get-tuple-element.13), kind=kOutput, calls=%fused_computation.2 | convolution fusion | flops 3226468352 | bytes 8912896 | tf_op jit(solution)/shard_map/dot_general | solution.py:147
  70.2 0.4 fusion.86
  70.7 2.0 %collective-permute-start.12 = (bf16[128,512]{1,0:T(8,128)(2,1)S(1)}, bf16[128,512]{1,0:T(8,128)(2,1)S(1)}, u32[]{:S(2)}, u32[]{:S(2)}) collective-permute-start(bf16[128,512]{1,0:T(8,128)(2,1)S(1)} %get-tuple-element.34), channel_id=1, source_target_pairs={{0,2},{1,3},{2,4},{3,5},{4,6},{5,7},{6,8},{7,9},{8,10},{9,11},{10,... | collective-permute-start | bytes 393224 | tf_op jit(solution)/shard_map/ppermute | solution.py:25
  72.7 4.0 %collective-permute-start.16 = (bf16[128,512]{1,0:T(8,128)(2,1)S(1)}, bf16[128,512]{1,0:T(8,128)(2,1)S(1)}, u32[]{:S(2)}, u32[]{:S(2)}) collective-permute-start(bf16[128,512]{1,0:T(8,128)(2,1)S(1)} %get-tuple-element.35), channel_id=1, source_target_pairs={{0,14},{1,15},{2,0},{3,1},{4,2},{5,3},{6,4},{7,5},{8,6},{9,7},{10,... | collective-permute-start | bytes 393224 | tf_op jit(solution)/shard_map/ppermute | solution.py:26
  76.9 3.2 %collective-permute-start.8 = (bf16[128,512]{1,0:T(8,128)(2,1)S(1)}, bf16[128,512]{1,0:T(8,128)(2,1)S(1)}, u32[]{:S(2)}, u32[]{:S(2)}) collective-permute-start(bf16[128,512]{1,0:T(8,128)(2,1)S(1)} %get-tuple-element.37), channel_id=1, source_target_pairs={{0,14},{1,15},{2,0},{3,1},{4,2},{5,3},{6,4},{7,5},{8,6},{9,7},{10,... | collective-permute-start | bytes 393224 | tf_op jit(solution)/shard_map/ppermute | solution.py:26
  80.1 1.9 %fusion = f32[384,2048]{1,0:T(8,128)S(1)} fusion(bf16[1,1024,2048]{2,1,0:T(8,128)(2,1)S(1)} %copy-done.11, f32[1024,768]{0,1:T(8,128)S(1)} %add_add_fusion), kind=kOutput, calls=%fused_computation | convolution fusion | flops 1612972032 | bytes 10485760 | tf_op jit(solution)/shard_map/dot_general | solution.py:136
  82.2 3.2 %collective-permute-start.17 = (bf16[128,1024]{1,0:T(8,128)(2,1)S(1)}, bf16[128,1024]{1,0:T(8,128)(2,1)S(1)}, u32[]{:S(2)}, u32[]{:S(2)}) collective-permute-start(bf16[128,1024]{1,0:T(8,128)(2,1)S(1)} %get-tuple-element.25), channel_id=1, source_target_pairs={{0,14},{1,15},{2,0},{3,1},{4,2},{5,3},{6,4},{7,5},{8,6},{9,7},{10,... | collective-permute-start | bytes 786440 | tf_op jit(solution)/shard_map/ppermute | solution.py:26
  85.6 3.2 %collective-permute-start.9 = (bf16[128,1024]{1,0:T(8,128)(2,1)S(1)}, bf16[128,1024]{1,0:T(8,128)(2,1)S(1)}, u32[]{:S(2)}, u32[]{:S(2)}) collective-permute-start(bf16[128,1024]{1,0:T(8,128)(2,1)S(1)} %get-tuple-element.31), channel_id=1, source_target_pairs={{0,14},{1,15},{2,0},{3,1},{4,2},{5,3},{6,4},{7,5},{8,6},{9,7},{10,... | collective-permute-start | bytes 786440 | tf_op jit(solution)/shard_map/ppermute | solution.py:26
  89.1 3.0 %collective-permute-done.13 = bf16[128,1024]{1,0:T(8,128)(2,1)S(1)} collective-permute-done((bf16[128,1024]{1,0:T(8,128)(2,1)S(1)}, bf16[128,1024]{1,0:T(8,128)(2,1)S(1)}, u32[]{:S(2)}, u32[]{:S(2)}) %collective-permute-start.13) | collective-permute-done | bytes 262176 | tf_op jit(solution)/shard_map/ppermute | solution.py:25
  92.0 0.6 collective-permute-start.21
  92.6 1.1 collective-permute-start.22
  94.0 0.9 collective-permute-done.5
  94.8 3.2 %collective-permute-start.18 = (bf16[128,1024]{1,0:T(8,128)(2,1)S(1)}, bf16[128,1024]{1,0:T(8,128)(2,1)S(1)}, u32[]{:S(2)}, u32[]{:S(2)}) collective-permute-start(bf16[128,1024]{1,0:T(8,128)(2,1)S(1)} %get-tuple-element.23), channel_id=1, source_target_pairs={{0,14},{1,15},{2,0},{3,1},{4,2},{5,3},{6,4},{7,5},{8,6},{9,7},{10,... | collective-permute-start | bytes 786440 | tf_op jit(solution)/shard_map/ppermute | solution.py:26
  98.3 7.8 %collective-permute-done.20 = bf16[384,512]{1,0:T(8,128)(2,1)S(1)} collective-permute-done((bf16[384,512]{1,0:T(8,128)(2,1)S(1)}, bf16[384,512]{1,0:T(8,128)(2,1)S(1)}, u32[]{:S(2)}, u32[]{:S(2)}) %collective-permute-start.20) | collective-permute-done | bytes 393248 | tf_op jit(solution)/shard_map/ppermute | solution.py:143
  106.2 0.6 collective-permute-start.10
  106.8 1.4 %collective-permute-start.6 = (bf16[128,1024]{1,0:T(8,128)(2,1)S(1)}, bf16[128,1024]{1,0:T(8,128)(2,1)S(1)}, u32[]{:S(2)}, u32[]{:S(2)}) collective-permute-start(bf16[128,1024]{1,0:T(8,128)(2,1)S(1)} %get-tuple-element.28), channel_id=1, source_target_pairs={{0,2},{1,3},{2,4},{3,5},{4,6},{5,7},{6,8},{7,9},{8,10},{9,11},{10,... | collective-permute-start | bytes 786440 | tf_op jit(solution)/shard_map/ppermute | solution.py:25
  108.2 1.2 fusion.71
  109.5 1.6 %fusion.70 = (f32[1,384,512]{2,1,0:T(8,128)}, bf16[384,512]{1,0:T(8,128)(2,1)S(1)}) fusion(f32[384,512]{1,0:T(8,128)S(1)} %get-tuple-element.10, f32[1,384,512]{2,1,0:T(8,128)S(1)} %copy-done.17, f32[384,512]{1,0:T(8,128)S(1)} %copy-done.9, f32[1,384,512]{2,1,0:T(8,128)S(1)} %copy-done.5, f32[1,384,512]{2,1,0:T(8,128)S(1)} %copy-done.6), kind=kLoop, calls=%fused_computation.111 | loop fusion | flops 3342336 | bytes 5111808 | tf_op jit(solution)/shard_map/broadcast_in_dim | solution.py:169
  111.2 0.4 collective-permute-start.15
  111.6 3.2 %collective-permute-start.19 = (bf16[128,1024]{1,0:T(8,128)(2,1)S(1)}, bf16[128,1024]{1,0:T(8,128)(2,1)S(1)}, u32[]{:S(2)}, u32[]{:S(2)}) collective-permute-start(bf16[128,1024]{1,0:T(8,128)(2,1)S(1)} %get-tuple-element.21), channel_id=1, source_target_pairs={{0,14},{1,15},{2,0},{3,1},{4,2},{5,3},{6,4},{7,5},{8,6},{9,7},{10,... | collective-permute-start | bytes 786440 | tf_op jit(solution)/shard_map/ppermute | solution.py:26
  115.0 0.7 collective-permute-start.11
  115.7 1.4 %collective-permute-start.7 = (bf16[128,1024]{1,0:T(8,128)(2,1)S(1)}, bf16[128,1024]{1,0:T(8,128)(2,1)S(1)}, u32[]{:S(2)}, u32[]{:S(2)}) collective-permute-start(bf16[128,1024]{1,0:T(8,128)(2,1)S(1)} %get-tuple-element.26), channel_id=1, source_target_pairs={{0,2},{1,3},{2,4},{3,5},{4,6},{5,7},{6,8},{7,9},{8,10},{9,11},{10,... | collective-permute-start | bytes 786440 | tf_op jit(solution)/shard_map/ppermute | solution.py:25
  117.2 2.4 %collective-permute-start.24 = (bf16[384,512]{1,0:T(8,128)(2,1)S(1)}, bf16[384,512]{1,0:T(8,128)(2,1)S(1)}, u32[]{:S(2)}, u32[]{:S(2)}) collective-permute-start(bf16[384,512]{1,0:T(8,128)(2,1)S(1)} %add_convert_fusion), channel_id=1, source_target_pairs={{0,128},{64,192},{128,0},{192,64},{1,129},{65,193},{129,1},{193,65... | collective-permute-start | bytes 1179656 | tf_op jit(solution)/shard_map/ppermute | solution.py:163
  119.6 2.3 %collective-permute-done.15 = bf16[128,1024]{1,0:T(8,128)(2,1)S(1)} collective-permute-done((bf16[128,1024]{1,0:T(8,128)(2,1)S(1)}, bf16[128,1024]{1,0:T(8,128)(2,1)S(1)}, u32[]{:S(2)}, u32[]{:S(2)}) %collective-permute-start.15) | collective-permute-done | bytes 262176 | tf_op jit(solution)/shard_map/ppermute | solution.py:25
  122.0 4.4 %collective-permute-done.11 = bf16[128,1024]{1,0:T(8,128)(2,1)S(1)} collective-permute-done((bf16[128,1024]{1,0:T(8,128)(2,1)S(1)}, bf16[128,1024]{1,0:T(8,128)(2,1)S(1)}, u32[]{:S(2)}, u32[]{:S(2)}) %collective-permute-start.11) | collective-permute-done | bytes 262176 | tf_op jit(solution)/shard_map/ppermute | solution.py:26
  126.4 0.7 collective-permute-done.7
  127.3 2.0 %collective-permute-done.24 = bf16[384,512]{1,0:T(8,128)(2,1)S(1)} collective-permute-done((bf16[384,512]{1,0:T(8,128)(2,1)S(1)}, bf16[384,512]{1,0:T(8,128)(2,1)S(1)}, u32[]{:S(2)}, u32[]{:S(2)}) %collective-permute-start.24) | collective-permute-done | bytes 393248 | tf_op jit(solution)/shard_map/ppermute | solution.py:163
  129.4 0.5 collective-permute-start.25
  129.9 1.4 %multiply_subtract_fusion = (f32[384,512]{1,0:T(8,128)}, f32[384,512]{1,0:T(8,128)}) fusion(f32[384,512]{1,0:T(8,128)S(1)} %copy-done.9, f32[384,512]{1,0:T(8,128)S(1)} %convert_add_fusion, f32[384,512]{1,0:T(8,128)S(1)} %copy-done.18), kind=kLoop, calls=%fused_computation.49 | loop fusion | flops 1376256 | bytes 3932160 | tf_op jit(solution)/shard_map/sub | solution.py:168
  131.3 4.8 %collective-permute-done.25 = bf16[64,2048]{1,0:T(8,128)(2,1)S(1)} collective-permute-done((bf16[64,2048]{1,0:T(8,128)(2,1)S(1)}, bf16[64,2048]{1,0:T(8,128)(2,1)S(1)}, u32[]{:S(2)}, u32[]{:S(2)}) %collective-permute-start.25) | collective-permute-done | bytes 262176 | tf_op jit(solution)/shard_map/ppermute | solution.py:58
  136.1 0.7 fusion.69
  (78 shorter events, 2.9 us)
Async XLA Ops:
  4.4 3.5 %copy-start.15 = (bf16[1,512,384]{2,1,0:T(8,128)(2,1)S(1)}, bf16[1,512,384]{2,1,0:T(8,128)(2,1)}, u32[]{:S(2)}) copy-start(bf16[1,512,384]{2,1,0:T(8,128)(2,1)} %param.12) | copy-start | bytes 1179652
  4.4 3.5 %copy-start.16 = (bf16[1,512,384]{2,1,0:T(8,128)(2,1)S(1)}, bf16[1,512,384]{2,1,0:T(8,128)(2,1)}, u32[]{:S(2)}) copy-start(bf16[1,512,384]{2,1,0:T(8,128)(2,1)} %param.11) | copy-start | bytes 1179652
  4.4 29.1 %collective-permute-start = (bf16[512,1152]{1,0:T(8,128)(2,1)}, bf16[512,1152]{1,0:T(8,128)(2,1)S(1)}, u32[]{:S(2)}, u32[]{:S(2)}) collective-permute-start(bf16[512,1152]{1,0:T(8,128)(2,1)} %pad_maximum_fusion), channel_id=1, source_target_pairs={{0,16},{16,32},{32,48},{48,0},{1,17},{17,33},{33,49},{49,1},{2,18}... | collective-permute-start | bytes 3538952 | tf_op jit(solution)/shard_map/ppermute | solution.py:88
  5.9 28.9 %collective-permute-start.1 = (bf16[512,1152]{1,0:T(8,128)(2,1)}, bf16[512,1152]{1,0:T(8,128)(2,1)S(1)}, u32[]{:S(2)}, u32[]{:S(2)}) collective-permute-start(bf16[512,1152]{1,0:T(8,128)(2,1)} %pad_maximum_fusion), channel_id=1, source_target_pairs={{0,48},{16,0},{32,16},{48,32},{1,49},{17,1},{33,17},{49,33},{2,50}... | collective-permute-start | bytes 3538952 | tf_op jit(solution)/shard_map/ppermute | solution.py:89
  7.9 4.7 %copy-start.7 = (bf16[2048,768]{1,0:T(8,128)(2,1)}, bf16[2048,768]{1,0:T(8,128)(2,1)S(1)}, u32[]{:S(2)}) copy-start(bf16[2048,768]{1,0:T(8,128)(2,1)S(1)} %fusion.62) | copy-start | bytes 9437188
  33.5 5.5 %copy-start.1 = (bf16[512,1152]{1,0:T(8,128)(2,1)}, bf16[512,1152]{1,0:T(8,128)(2,1)S(1)}, u32[]{:S(2)}) copy-start(bf16[512,1152]{1,0:T(8,128)(2,1)S(1)} %collective-permute-done) | copy-start | bytes 3538948
  34.5 18.1 %collective-permute-start.2 = (bf16[256,1152]{1,0:T(8,128)(2,1)}, bf16[256,1152]{1,0:T(8,128)(2,1)}, u32[]{:S(2)}, u32[]{:S(2)}) collective-permute-start(bf16[256,1152]{1,0:T(8,128)(2,1)} %slice.80), channel_id=1, source_target_pairs={{0,16},{16,32},{32,48},{48,0},{1,17},{17,33},{33,49},{49,1},{2,18}... | collective-permute-start | bytes 1769480 | tf_op jit(solution)/shard_map/ppermute | solution.py:90
  34.7 7.9 %copy-start.3 = (bf16[512,1152]{1,0:T(8,128)(2,1)}, bf16[512,1152]{1,0:T(8,128)(2,1)S(1)}, u32[]{:S(2)}) copy-start(bf16[512,1152]{1,0:T(8,128)(2,1)S(1)} %collective-permute-done.1) | copy-start | bytes 3538948
  35.7 18.1 %collective-permute-start.3 = (bf16[256,1152]{1,0:T(8,128)(2,1)}, bf16[256,1152]{1,0:T(8,128)(2,1)}, u32[]{:S(2)}, u32[]{:S(2)}) collective-permute-start(bf16[256,1152]{1,0:T(8,128)(2,1)} %slice.82), channel_id=1, source_target_pairs={{0,48},{16,0},{32,16},{48,32},{1,49},{17,1},{33,17},{49,33},{2,50}... | collective-permute-start | bytes 1769480 | tf_op jit(solution)/shard_map/ppermute | solution.py:91
  39.4 6.2 %copy-start.10 = (bf16[1,1024,2048]{2,1,0:T(8,128)(2,1)S(1)}, bf16[1,1024,2048]{2,1,0:T(8,128)(2,1)}, u32[]{:S(2)}) copy-start(bf16[1,1024,2048]{2,1,0:T(8,128)(2,1)} %param.9) | copy-start | bytes 12582916
  45.6 2.3 %copy-start.2 = (bf16[512,1152]{1,0:T(8,128)(2,1)S(1)}, bf16[512,1152]{1,0:T(8,128)(2,1)}, u32[]{:S(2)}) copy-start(bf16[512,1152]{1,0:T(8,128)(2,1)} %copy-done.1) | copy-start | bytes 3538948
  45.6 3.3 %copy-start.4 = (bf16[512,1152]{1,0:T(8,128)(2,1)S(1)}, bf16[512,1152]{1,0:T(8,128)(2,1)}, u32[]{:S(2)}) copy-start(bf16[512,1152]{1,0:T(8,128)(2,1)} %copy-done.3) | copy-start | bytes 3538948
  55.5 2.2 %copy-start = (f32[1024,768]{0,1:T(8,128)S(1)}, f32[1024,768]{0,1:T(8,128)}, u32[]{:S(2)}) copy-start(f32[1024,768]{0,1:T(8,128)} %fusion.8) | copy-start | bytes 9437188
  57.7 3.4 %copy-start.11 = (bf16[1,1024,2048]{2,1,0:T(8,128)(2,1)S(1)}, bf16[1,1024,2048]{2,1,0:T(8,128)(2,1)}, u32[]{:S(2)}) copy-start(bf16[1,1024,2048]{2,1,0:T(8,128)(2,1)} %param.10) | copy-start | bytes 12582916
  57.7 3.9 %copy-start.12 = (f32[1024,384]{0,1:T(8,128)S(1)}, f32[1024,384]{0,1:T(8,128)}, u32[]{:S(2)}) copy-start(f32[1024,384]{0,1:T(8,128)} %fusion.20) | copy-start | bytes 4718596
  57.7 4.4 %copy-start.13 = (f32[1024,384]{0,1:T(8,128)S(1)}, f32[1024,384]{0,1:T(8,128)}, u32[]{:S(2)}) copy-start(f32[1024,384]{0,1:T(8,128)} %fusion.16) | copy-start | bytes 4718596
  57.7 4.8 %copy-start.14 = (f32[1024,384]{0,1:T(8,128)S(1)}, f32[1024,384]{0,1:T(8,128)}, u32[]{:S(2)}) copy-start(f32[1024,384]{0,1:T(8,128)} %fusion.18) | copy-start | bytes 4718596
  57.7 4.8 %copy-start.19 = (bf16[192,512]{1,0:T(8,128)(2,1)S(1)}, bf16[192,512]{1,0:T(8,128)(2,1)}, u32[]{:S(2)}) copy-start(bf16[192,512]{1,0:T(8,128)(2,1)} %reshape.80) | copy-start | bytes 589828
  62.5 1.9 %copy-start.8 = (bf16[2048,768]{1,0:T(8,128)(2,1)S(1)}, bf16[2048,768]{1,0:T(8,128)(2,1)}, u32[]{:S(2)}) copy-start(bf16[2048,768]{1,0:T(8,128)(2,1)} %slice_dynamic-update-slice_fusion) | copy-start | bytes 9437188
  70.7 11.3 %collective-permute-start.12 = (bf16[128,512]{1,0:T(8,128)(2,1)S(1)}, bf16[128,512]{1,0:T(8,128)(2,1)S(1)}, u32[]{:S(2)}, u32[]{:S(2)}) collective-permute-start(bf16[128,512]{1,0:T(8,128)(2,1)S(1)} %get-tuple-element.34), channel_id=1, source_target_pairs={{0,2},{1,3},{2,4},{3,5},{4,6},{5,7},{6,8},{7,9},{8,10},{9,11},{10,... | collective-permute-start | bytes 393224 | tf_op jit(solution)/shard_map/ppermute | solution.py:25
  72.7 9.3 %collective-permute-start.16 = (bf16[128,512]{1,0:T(8,128)(2,1)S(1)}, bf16[128,512]{1,0:T(8,128)(2,1)S(1)}, u32[]{:S(2)}, u32[]{:S(2)}) collective-permute-start(bf16[128,512]{1,0:T(8,128)(2,1)S(1)} %get-tuple-element.35), channel_id=1, source_target_pairs={{0,14},{1,15},{2,0},{3,1},{4,2},{5,3},{6,4},{7,5},{8,6},{9,7},{10,... | collective-permute-start | bytes 393224 | tf_op jit(solution)/shard_map/ppermute | solution.py:26
  76.8 8.6 %collective-permute-start.4 = (bf16[128,512]{1,0:T(8,128)(2,1)S(1)}, bf16[128,512]{1,0:T(8,128)(2,1)S(1)}, u32[]{:S(2)}, u32[]{:S(2)}) collective-permute-start(bf16[128,512]{1,0:T(8,128)(2,1)S(1)} %get-tuple-element.36), channel_id=1, source_target_pairs={{0,2},{1,3},{2,4},{3,5},{4,6},{5,7},{6,8},{7,9},{8,10},{9,11},{10,... | collective-permute-start | bytes 393224 | tf_op jit(solution)/shard_map/ppermute | solution.py:25
  76.9 8.5 %collective-permute-start.8 = (bf16[128,512]{1,0:T(8,128)(2,1)S(1)}, bf16[128,512]{1,0:T(8,128)(2,1)S(1)}, u32[]{:S(2)}, u32[]{:S(2)}) collective-permute-start(bf16[128,512]{1,0:T(8,128)(2,1)S(1)} %get-tuple-element.37), channel_id=1, source_target_pairs={{0,14},{1,15},{2,0},{3,1},{4,2},{5,3},{6,4},{7,5},{8,6},{9,7},{10,... | collective-permute-start | bytes 393224 | tf_op jit(solution)/shard_map/ppermute | solution.py:26
  82.1 9.9 %collective-permute-start.13 = (bf16[128,1024]{1,0:T(8,128)(2,1)S(1)}, bf16[128,1024]{1,0:T(8,128)(2,1)S(1)}, u32[]{:S(2)}, u32[]{:S(2)}) collective-permute-start(bf16[128,1024]{1,0:T(8,128)(2,1)S(1)} %get-tuple-element.24), channel_id=1, source_target_pairs={{0,2},{1,3},{2,4},{3,5},{4,6},{5,7},{6,8},{7,9},{8,10},{9,11},{10,... | collective-permute-start | bytes 786440 | tf_op jit(solution)/shard_map/ppermute | solution.py:25
  82.2 10.4 %collective-permute-start.17 = (bf16[128,1024]{1,0:T(8,128)(2,1)S(1)}, bf16[128,1024]{1,0:T(8,128)(2,1)S(1)}, u32[]{:S(2)}, u32[]{:S(2)}) collective-permute-start(bf16[128,1024]{1,0:T(8,128)(2,1)S(1)} %get-tuple-element.25), channel_id=1, source_target_pairs={{0,14},{1,15},{2,0},{3,1},{4,2},{5,3},{6,4},{7,5},{8,6},{9,7},{10,... | collective-permute-start | bytes 786440 | tf_op jit(solution)/shard_map/ppermute | solution.py:26
  85.5 9.3 %collective-permute-start.5 = (bf16[128,1024]{1,0:T(8,128)(2,1)S(1)}, bf16[128,1024]{1,0:T(8,128)(2,1)S(1)}, u32[]{:S(2)}, u32[]{:S(2)}) collective-permute-start(bf16[128,1024]{1,0:T(8,128)(2,1)S(1)} %get-tuple-element.30), channel_id=1, source_target_pairs={{0,2},{1,3},{2,4},{3,5},{4,6},{5,7},{6,8},{7,9},{8,10},{9,11},{10,... | collective-permute-start | bytes 786440 | tf_op jit(solution)/shard_map/ppermute | solution.py:25
  85.6 22.6 %copy-start.5 = (f32[1,384,512]{2,1,0:T(8,128)S(1)}, f32[1,384,512]{2,1,0:T(8,128)}, u32[]{:S(2)}) copy-start(f32[1,384,512]{2,1,0:T(8,128)} %param.15) | copy-start | bytes 2359300
  85.6 9.2 %collective-permute-start.9 = (bf16[128,1024]{1,0:T(8,128)(2,1)S(1)}, bf16[128,1024]{1,0:T(8,128)(2,1)S(1)}, u32[]{:S(2)}, u32[]{:S(2)}) collective-permute-start(bf16[128,1024]{1,0:T(8,128)(2,1)S(1)} %get-tuple-element.31), channel_id=1, source_target_pairs={{0,14},{1,15},{2,0},{3,1},{4,2},{5,3},{6,4},{7,5},{8,6},{9,7},{10,... | collective-permute-start | bytes 786440 | tf_op jit(solution)/shard_map/ppermute | solution.py:26
  89.0 17.2 %collective-permute-start.20 = (bf16[384,512]{1,0:T(8,128)(2,1)S(1)}, bf16[384,512]{1,0:T(8,128)(2,1)S(1)}, u32[]{:S(2)}, u32[]{:S(2)}) collective-permute-start(bf16[384,512]{1,0:T(8,128)(2,1)S(1)} %get-tuple-element.17), channel_id=1, source_target_pairs={{0,16},{16,32},{32,48},{48,0},{1,17},{17,33},{33,49},{49,1},{2,18}... | collective-permute-start | bytes 1179656 | tf_op jit(solution)/shard_map/ppermute | solution.py:143
  92.0 14.8 %collective-permute-start.21 = (bf16[384,512]{1,0:T(8,128)(2,1)S(1)}, bf16[384,512]{1,0:T(8,128)(2,1)S(1)}, u32[]{:S(2)}, u32[]{:S(2)}) collective-permute-start(bf16[384,512]{1,0:T(8,128)(2,1)S(1)} %get-tuple-element.19), channel_id=1, source_target_pairs={{0,32},{16,48},{32,0},{48,16},{1,33},{17,49},{33,1},{49,17},{2,34}... | collective-permute-start | bytes 1179656 | tf_op jit(solution)/shard_map/ppermute | solution.py:143
  92.6 15.6 %collective-permute-start.22 = (bf16[384,512]{1,0:T(8,128)(2,1)S(1)}, bf16[384,512]{1,0:T(8,128)(2,1)S(1)}, u32[]{:S(2)}, u32[]{:S(2)}) collective-permute-start(bf16[384,512]{1,0:T(8,128)(2,1)S(1)} %get-tuple-element.18), channel_id=1, source_target_pairs={{0,48},{16,0},{32,16},{48,32},{1,49},{17,1},{33,17},{49,33},{2,50}... | collective-permute-start | bytes 1179656 | tf_op jit(solution)/shard_map/ppermute | solution.py:143
  94.8 16.2 %collective-permute-start.14 = (bf16[128,1024]{1,0:T(8,128)(2,1)S(1)}, bf16[128,1024]{1,0:T(8,128)(2,1)S(1)}, u32[]{:S(2)}, u32[]{:S(2)}) collective-permute-start(bf16[128,1024]{1,0:T(8,128)(2,1)S(1)} %get-tuple-element.22), channel_id=1, source_target_pairs={{0,2},{1,3},{2,4},{3,5},{4,6},{5,7},{6,8},{7,9},{8,10},{9,11},{10,... | collective-permute-start | bytes 786440 | tf_op jit(solution)/shard_map/ppermute | solution.py:25
  94.8 16.2 %collective-permute-start.18 = (bf16[128,1024]{1,0:T(8,128)(2,1)S(1)}, bf16[128,1024]{1,0:T(8,128)(2,1)S(1)}, u32[]{:S(2)}, u32[]{:S(2)}) collective-permute-start(bf16[128,1024]{1,0:T(8,128)(2,1)S(1)} %get-tuple-element.23), channel_id=1, source_target_pairs={{0,14},{1,15},{2,0},{3,1},{4,2},{5,3},{6,4},{7,5},{8,6},{9,7},{10,... | collective-permute-start | bytes 786440 | tf_op jit(solution)/shard_map/ppermute | solution.py:26
  98.3 11.2 %copy-start.6 = (f32[1,384,512]{2,1,0:T(8,128)S(1)}, f32[1,384,512]{2,1,0:T(8,128)}, u32[]{:S(2)}) copy-start(f32[1,384,512]{2,1,0:T(8,128)} %param.13) | copy-start | bytes 2359300
  98.3 11.1 %copy-start.9 = (f32[384,512]{1,0:T(8,128)S(1)}, f32[384,512]{1,0:T(8,128)}, u32[]{:S(2)}) copy-start(f32[384,512]{1,0:T(8,128)} %param.16) | copy-start | bytes 2359300
  98.3 11.1 %copy-start.17 = (f32[1,384,512]{2,1,0:T(8,128)S(1)}, f32[1,384,512]{2,1,0:T(8,128)}, u32[]{:S(2)}) copy-start(f32[1,384,512]{2,1,0:T(8,128)} %param.14) | copy-start | bytes 2359300
  106.2 8.6 %collective-permute-start.10 = (bf16[128,1024]{1,0:T(8,128)(2,1)S(1)}, bf16[128,1024]{1,0:T(8,128)(2,1)S(1)}, u32[]{:S(2)}, u32[]{:S(2)}) collective-permute-start(bf16[128,1024]{1,0:T(8,128)(2,1)S(1)} %get-tuple-element.29), channel_id=1, source_target_pairs={{0,14},{1,15},{2,0},{3,1},{4,2},{5,3},{6,4},{7,5},{8,6},{9,7},{10,... | collective-permute-start | bytes 786440 | tf_op jit(solution)/shard_map/ppermute | solution.py:26
  106.8 8.0 %collective-permute-start.6 = (bf16[128,1024]{1,0:T(8,128)(2,1)S(1)}, bf16[128,1024]{1,0:T(8,128)(2,1)S(1)}, u32[]{:S(2)}, u32[]{:S(2)}) collective-permute-start(bf16[128,1024]{1,0:T(8,128)(2,1)S(1)} %get-tuple-element.28), channel_id=1, source_target_pairs={{0,2},{1,3},{2,4},{3,5},{4,6},{5,7},{6,8},{7,9},{8,10},{9,11},{10,... | collective-permute-start | bytes 786440 | tf_op jit(solution)/shard_map/ppermute | solution.py:25
  111.0 6.1 %collective-permute-start.23 = (bf16[384,512]{1,0:T(8,128)(2,1)S(1)}, bf16[384,512]{1,0:T(8,128)(2,1)S(1)}, u32[]{:S(2)}, u32[]{:S(2)}) collective-permute-start(bf16[384,512]{1,0:T(8,128)(2,1)S(1)} %get-tuple-element.33), channel_id=1, source_target_pairs={{0,64},{64,0},{128,192},{192,128},{1,65},{65,1},{129,193},{193,129... | collective-permute-start | bytes 1179656 | tf_op jit(solution)/shard_map/ppermute | solution.py:163
  111.2 10.7 %collective-permute-start.15 = (bf16[128,1024]{1,0:T(8,128)(2,1)S(1)}, bf16[128,1024]{1,0:T(8,128)(2,1)S(1)}, u32[]{:S(2)}, u32[]{:S(2)}) collective-permute-start(bf16[128,1024]{1,0:T(8,128)(2,1)S(1)} %get-tuple-element.20), channel_id=1, source_target_pairs={{0,2},{1,3},{2,4},{3,5},{4,6},{5,7},{6,8},{7,9},{8,10},{9,11},{10,... | collective-permute-start | bytes 786440 | tf_op jit(solution)/shard_map/ppermute | solution.py:25
  111.6 10.3 %collective-permute-start.19 = (bf16[128,1024]{1,0:T(8,128)(2,1)S(1)}, bf16[128,1024]{1,0:T(8,128)(2,1)S(1)}, u32[]{:S(2)}, u32[]{:S(2)}) collective-permute-start(bf16[128,1024]{1,0:T(8,128)(2,1)S(1)} %get-tuple-element.21), channel_id=1, source_target_pairs={{0,14},{1,15},{2,0},{3,1},{4,2},{5,3},{6,4},{7,5},{8,6},{9,7},{10,... | collective-permute-start | bytes 786440 | tf_op jit(solution)/shard_map/ppermute | solution.py:26
  115.0 11.4 %collective-permute-start.11 = (bf16[128,1024]{1,0:T(8,128)(2,1)S(1)}, bf16[128,1024]{1,0:T(8,128)(2,1)S(1)}, u32[]{:S(2)}, u32[]{:S(2)}) collective-permute-start(bf16[128,1024]{1,0:T(8,128)(2,1)S(1)} %get-tuple-element.27), channel_id=1, source_target_pairs={{0,14},{1,15},{2,0},{3,1},{4,2},{5,3},{6,4},{7,5},{8,6},{9,7},{10,... | collective-permute-start | bytes 786440 | tf_op jit(solution)/shard_map/ppermute | solution.py:26
  115.7 11.4 %collective-permute-start.7 = (bf16[128,1024]{1,0:T(8,128)(2,1)S(1)}, bf16[128,1024]{1,0:T(8,128)(2,1)S(1)}, u32[]{:S(2)}, u32[]{:S(2)}) collective-permute-start(bf16[128,1024]{1,0:T(8,128)(2,1)S(1)} %get-tuple-element.26), channel_id=1, source_target_pairs={{0,2},{1,3},{2,4},{3,5},{4,6},{5,7},{6,8},{7,9},{8,10},{9,11},{10,... | collective-permute-start | bytes 786440 | tf_op jit(solution)/shard_map/ppermute | solution.py:25
  117.2 12.0 %collective-permute-start.24 = (bf16[384,512]{1,0:T(8,128)(2,1)S(1)}, bf16[384,512]{1,0:T(8,128)(2,1)S(1)}, u32[]{:S(2)}, u32[]{:S(2)}) collective-permute-start(bf16[384,512]{1,0:T(8,128)(2,1)S(1)} %add_convert_fusion), channel_id=1, source_target_pairs={{0,128},{64,192},{128,0},{192,64},{1,129},{65,193},{129,1},{193,65... | collective-permute-start | bytes 1179656 | tf_op jit(solution)/shard_map/ppermute | solution.py:163
  122.0 7.9 %copy-start.18 = (f32[384,512]{1,0:T(8,128)S(1)}, f32[384,512]{1,0:T(8,128)}, u32[]{:S(2)}) copy-start(f32[384,512]{1,0:T(8,128)} %param.17) | copy-start | bytes 2359300
  129.4 6.8 %collective-permute-start.25 = (bf16[64,2048]{1,0:T(8,128)(2,1)S(1)}, bf16[64,2048]{1,0:T(8,128)(2,1)S(1)}, u32[]{:S(2)}, u32[]{:S(2)}) collective-permute-start(bf16[64,2048]{1,0:T(8,128)(2,1)S(1)} %fusion.39), channel_id=1, source_target_pairs={{0,1},{1,0},{2,3},{3,2},{4,5},{5,4},{6,7},{7,6},{8,9},{9,8},{10,11... | collective-permute-start | bytes 786440 | tf_op jit(solution)/shard_map/ppermute | solution.py:58

commit v13 on v9

--- a/solution.py
+++ b/solution.py
@@ -13,26 +13,22 @@
 
 def _z_reduce_scatter(chunks, z, nz, up, down):
     far = nz // 2
-    halfc = chunks.shape[2] // 2
 
     def chunk(c):
         return lax.dynamic_index_in_dim(chunks, c % nz, axis=0, keepdims=False).astype(jnp.float32)
 
-    first = chunk(z + far)
-    send_a = first[:, :halfc]
-    send_b = first[:, halfc:]
-    for r in range(2, far + 2):
+    send_a = chunk(z + far)
+    send_b = None
+    for r in range(1, far + 1):
         got_a = lax.ppermute(send_a.astype(jnp.bfloat16), "mp", up).astype(jnp.float32)
-        got_b = lax.ppermute(send_b.astype(jnp.bfloat16), "mp", down).astype(jnp.float32)
-        own_a = chunk(z + far + 1 - r)
-        own_b = chunk(z - far - 1 + r)
-        if r == 2:
-            got_a = jnp.concatenate([got_a, jnp.zeros_like(got_a)], axis=1)
-            got_b = jnp.concatenate([jnp.zeros_like(got_b), got_b], axis=1)
-        if r <= far:
-            send_a = got_a + own_a
-            send_b = got_b + own_b
-    return own_a + got_a + got_b
+        got_b = None
+        if send_b is not None:
+            got_b = lax.ppermute(send_b.astype(jnp.bfloat16), "mp", down).astype(jnp.float32)
+        if r < far:
+            send_a = got_a + chunk(z + far - r)
+            own_b = chunk(z - far + r)
+            send_b = own_b if got_b is None else got_b + own_b
+    return got_a + got_b + chunk(z)
 
 
 def _ring_reduce_scatter(part, sync):

time: 122 us -> 124 us (1.016)
  waiting for transfers between devices: 49.4 us -> 51.8 us
    ppermute x8 -> x6, starting transfers between devices: 19.5 us -> 10.4 us  [_z_reduce_scatter(): lax.ppermute(send_b.astype(jnp.bfloat16), 'mp', down).astype(jnp.float32)]
    ppermute x8, starting transfers between devices: 5.49 us -> 12.7 us  [_z_reduce_scatter(): lax.ppermute(send_a.astype(jnp.bfloat16), 'mp', up).astype(jnp.float32)]
    ppermute x8, waiting for transfers between devices: 4.66 us -> 11 us  [_z_reduce_scatter(): lax.ppermute(send_a.astype(jnp.bfloat16), 'mp', up).astype(jnp.float32)]
    ppermute x3, waiting for transfers between devices: 8.68 us -> 5.04 us  [shards(): got = lax.ppermute(blk.astype(jnp.bfloat16), 'dp', _shift(ndp, s))]
    ppermute x3, starting transfers between devices: 3.91 us -> 5.26 us  [shards(): got = lax.ppermute(blk.astype(jnp.bfloat16), 'dp', _shift(ndp, s))]
    ppermute x8 -> x6, waiting for transfers between devices: 4.68 us -> 4.39 us  [_z_reduce_scatter(): lax.ppermute(send_b.astype(jnp.bfloat16), 'mp', down).astype(jnp.float32)]
  transfers between devices with their start and end apart: 26 -> 24, of which waited for: 12 -> 12; matrix products, arithmetic and copies ran while one was open for 15% -> 13% of each run, Pallas kernels for 0% -> 0%
where the time goes in v13:
time: 124 us; the launch traced here: 123 us
  waiting for transfers between devices  51.8 us (42%)
  starting transfers between devices  38.1 us (31%)
  matrix products  15.4 us (12%)
  local copies, waits for them, and re-layouts  9.02 us (7%)
  other arithmetic  7.6 us (6%)
    ppermute x1, waiting for transfers between devices, shards(): from_left = lax.ppermute(shard, 'dp', _shift(ndp, 1))  20.9 us
    ppermute x8, starting transfers between devices, _z_reduce_scatter(): lax.ppermute(send_a.astype(jnp.bfloat16), 'mp', up).astype(jnp.float32)  12.7 us
    ppermute x8, waiting for transfers between devices, _z_reduce_scatter(): lax.ppermute(send_a.astype(jnp.bfloat16), 'mp', up).astype(jnp.float32)  11 us
    ppermute x6, starting transfers between devices, _z_reduce_scatter(): lax.ppermute(send_b.astype(jnp.bfloat16), 'mp', down).astype(jnp.float32)  10.4 us
    dot_general x5, matrix products, shards(): p1 = jnp.dot(xs, piece[:, :2 * ff], preferred_element_type=jnp.float32)  5.59 us
    unnamed x16, local copies, waits for them, and re-layouts  5.28 us
    ppermute x3, starting transfers between devices, shards(): got = lax.ppermute(blk.astype(jnp.bfloat16), 'dp', _shift(ndp, s))  5.26 us
    ppermute x3, waiting for transfers between devices, shards(): got = lax.ppermute(blk.astype(jnp.bfloat16), 'dp', _shift(ndp, s))  5.04 us
  transfers between devices with their start and end apart: 24, of which 12 were waited for; matrix products, arithmetic and copies ran while one was open for 13% of the time, Pallas kernels for 0%

profile of v13, /device:TPU:8, one launch (start us, length us, event | category | flops | bytes accessed | tf_op | source)
XLA Modules:
  0.0 123.0 jit_solution(12214632608906339049)
XLA Ops:
  0.6 1.2 %copy.14 = bf16[1,512,384]{1,2,0:T(8,128)(2,1)S(1)} copy(bf16[1,512,384]{2,1,0:T(8,128)(2,1)} %param.11) | data formatting | bytes 786432 | tf_op args[2]
  1.9 1.2 copy.15
  3.1 1.1 pad_maximum_fusion
  4.2 1.5 %collective-permute-start = (bf16[512,1152]{0,1:T(8,128)(2,1)}, bf16[512,1152]{0,1:T(8,128)(2,1)S(1)}, u32[]{:S(2)}, u32[]{:S(2)}) collective-permute-start(bf16[512,1152]{0,1:T(8,128)(2,1)} %pad_maximum_fusion), channel_id=1, source_target_pairs={{0,16},{16,32},{32,48},{48,0},{1,17},{17,33},{33,49},{49,1},{2,18}... | collective-permute-start | bytes 3538952 | tf_op jit(solution)/shard_map/ppermute | solution.py:81
  5.7 1.7 %collective-permute-start.1 = (bf16[512,1152]{0,1:T(8,128)(2,1)}, bf16[512,1152]{0,1:T(8,128)(2,1)}, u32[]{:S(2)}, u32[]{:S(2)}) collective-permute-start(bf16[512,1152]{0,1:T(8,128)(2,1)} %pad_maximum_fusion), channel_id=1, source_target_pairs={{0,48},{16,0},{32,16},{48,32},{1,49},{17,1},{33,17},{49,33},{2,50}... | collective-permute-start | bytes 3538952 | tf_op jit(solution)/shard_map/ppermute | solution.py:82
  7.5 0.4 broadcast_in_dim.12
  7.9 0.1 fusion.61
  8.0 1.7 %copy-done.6 = bf16[1,1024,2048]{2,1,0:T(8,128)(2,1)S(1)} copy-done((bf16[1,1024,2048]{2,1,0:T(8,128)(2,1)S(1)}, bf16[1,1024,2048]{2,1,0:T(8,128)(2,1)}, u32[]{:S(2)}) %copy-start.6) | copy-done | bytes 4194328
  9.7 1.0 fusion.10
  10.7 1.2 copy-done.1
  11.9 0.6 fusion.16
  12.5 20.9 %collective-permute-done = bf16[512,1152]{0,1:T(8,128)(2,1)S(1)} collective-permute-done((bf16[512,1152]{0,1:T(8,128)(2,1)}, bf16[512,1152]{0,1:T(8,128)(2,1)S(1)}, u32[]{:S(2)}, u32[]{:S(2)}) %collective-permute-start) | collective-permute-done | bytes 1179680 | tf_op jit(solution)/shard_map/ppermute | solution.py:81
  33.4 0.4 collective-permute-start.2
  33.8 1.1 slice.67
  34.9 3.2 %collective-permute-start.3 = (bf16[256,1152]{0,1:T(8,128)(2,1)S(1)}, bf16[256,1152]{0,1:T(8,128)(2,1)S(1)}, u32[]{:S(2)}, u32[]{:S(2)}) collective-permute-start(bf16[256,1152]{0,1:T(8,128)(2,1)S(1)} %slice.67), channel_id=1, source_target_pairs={{0,48},{16,0},{32,16},{48,32},{1,49},{17,1},{33,17},{49,33},{2,50}... | collective-permute-start | bytes 1769480 | tf_op jit(solution)/shard_map/ppermute | solution.py:84
  38.1 2.1 %fusion.6 = f32[1024,768]{0,1:T(8,128)S(1)} fusion(bf16[1,1024,2048]{2,1,0:T(8,128)(2,1)S(1)} %copy-done.6, s32[]{:T(128)S(6)} %select_n.155, bf16[512,1152]{0,1:T(8,128)(2,1)} %collective-permute-done.1), kind=kOutput, calls=%fused_computation.19 | convolution fusion | flops 805306368 | bytes 4980740 | tf_op jit(solution)/shard_map/dot_general | solution.py:100
  40.3 1.6 %fusion.12 = f32[1024,384]{0,1:T(8,128)S(1)} fusion(bf16[1,1024,2048]{2,1,0:T(8,128)(2,1)S(1)} %copy-done.1, s32[]{:T(128)S(6)} %select_n.155, bf16[512,1152]{0,1:T(8,128)(2,1)} %collective-permute-done.1), kind=kOutput, calls=%fused_computation.25 | convolution fusion | flops 402653184 | bytes 3014660 | tf_op jit(solution)/shard_map/dot_general | solution.py:101
  41.9 1.0 fusion.8
  43.0 1.2 %slice_dynamic-update-slice_fusion = bf16[2048,768]{0,1:T(8,128)(2,1)S(1)} fusion(bf16[2048,768]{0,1:T(8,128)(2,1)S(1)} %slice_dynamic-update-slice_fusion.1, s32[]{:T(128)S(6)} %select_n.155, bf16[512,1152]{0,1:T(8,128)(2,1)} %collective-permute-done.1), kind=kLoop, calls=%fused_computation.55 | loop fusion | bytes 1572868 | tf_op jit(solution)/shard_map/dynamic_update_slice | solution.py:104
  44.3 0.6 fusion.14
  44.9 4.0 %collective-permute-done.2 = bf16[256,1152]{0,1:T(8,128)(2,1)S(1)} collective-permute-done((bf16[256,1152]{0,1:T(8,128)(2,1)S(1)}, bf16[256,1152]{0,1:T(8,128)(2,1)S(1)}, u32[]{:S(2)}, u32[]{:S(2)}) %collective-permute-start.2) | collective-permute-done | bytes 589856 | tf_op jit(solution)/shard_map/ppermute | solution.py:83
  48.9 0.6 fusion.49
  49.5 0.8 add_add_fusion
  50.4 1.8 %fusion = f32[384,2048]{1,0:T(8,128)S(1)} fusion(bf16[1,1024,2048]{2,1,0:T(8,128)(2,1)S(1)} %copy-done.1, f32[1024,768]{0,1:T(8,128)S(1)} %add_add_fusion), kind=kOutput, calls=%fused_computation | convolution fusion | flops 1612972032 | bytes 10485760 | tf_op jit(solution)/shard_map/dot_general | solution.py:116
  52.2 0.4 fusion.55
  52.7 1.0 multiply_convert_fusion.2
  53.7 3.8 %convolution_convert_fusion = bf16[1024,2048]{1,0:T(8,128)(2,1)S(1)} fusion(bf16[2048,768]{0,1:T(8,128)(2,1)S(1)} %slice_dynamic-update-slice_fusion.2, bf16[1024,384]{0,1:T(8,128)(2,1)S(1)} %get-tuple-element.14, bf16[1024,384]{0,1:T(8,128)(2,1)S(1)} %get-tuple-element.13), kind=kOutput, calls=%fused_computation.2 | convolution fusion | flops 3226468352 | bytes 8912896 | tf_op jit(solution)/shard_map/dot_general | solution.py:127
  57.5 0.5 fusion.88
  58.1 2.0 %collective-permute-start.11 = (bf16[128,1024]{1,0:T(8,128)(2,1)S(1)}, bf16[128,1024]{1,0:T(8,128)(2,1)S(1)}, u32[]{:S(2)}, u32[]{:S(2)}) collective-permute-start(bf16[128,1024]{1,0:T(8,128)(2,1)S(1)} %get-tuple-element.24), channel_id=1, source_target_pairs={{0,2},{1,3},{2,4},{3,5},{4,6},{5,7},{6,8},{7,9},{8,10},{9,11},{10,... | collective-permute-start | bytes 786440 | tf_op jit(solution)/shard_map/ppermute | solution.py:23
  60.1 2.0 %collective-permute-start.4 = (bf16[128,1024]{1,0:T(8,128)(2,1)S(1)}, bf16[128,1024]{1,0:T(8,128)(2,1)S(1)}, u32[]{:S(2)}, u32[]{:S(2)}) collective-permute-start(bf16[128,1024]{1,0:T(8,128)(2,1)S(1)} %get-tuple-element.30), channel_id=1, source_target_pairs={{0,2},{1,3},{2,4},{3,5},{4,6},{5,7},{6,8},{7,9},{8,10},{9,11},{10,... | collective-permute-start | bytes 786440 | tf_op jit(solution)/shard_map/ppermute | solution.py:23
  62.2 0.2 dynamic-slice_convert_fusion.2
  62.3 1.2 %collective-permute-start.18 = (bf16[384,512]{1,0:T(8,128)(2,1)S(1)}, bf16[384,512]{1,0:T(8,128)(2,1)S(1)}, u32[]{:S(2)}, u32[]{:S(2)}) collective-permute-start(bf16[384,512]{1,0:T(8,128)(2,1)S(1)} %get-tuple-element.17), channel_id=1, source_target_pairs={{0,16},{16,32},{32,48},{48,0},{1,17},{17,33},{33,49},{49,1},{2,18}... | collective-permute-start | bytes 1179656 | tf_op jit(solution)/shard_map/ppermute | solution.py:123
  63.5 4.0 %collective-permute-start.19 = (bf16[384,512]{1,0:T(8,128)(2,1)S(1)}, bf16[384,512]{1,0:T(8,128)(2,1)S(1)}, u32[]{:S(2)}, u32[]{:S(2)}) collective-permute-start(bf16[384,512]{1,0:T(8,128)(2,1)S(1)} %get-tuple-element.19), channel_id=1, source_target_pairs={{0,32},{16,48},{32,0},{48,16},{1,33},{17,49},{33,1},{49,17},{2,34}... | collective-permute-start | bytes 1179656 | tf_op jit(solution)/shard_map/ppermute | solution.py:123
  67.6 3.7 %collective-permute-done.11 = bf16[128,1024]{1,0:T(8,128)(2,1)S(1)} collective-permute-done((bf16[128,1024]{1,0:T(8,128)(2,1)S(1)}, bf16[128,1024]{1,0:T(8,128)(2,1)S(1)}, u32[]{:S(2)}, u32[]{:S(2)}) %collective-permute-start.11) | collective-permute-done | bytes 262176 | tf_op jit(solution)/shard_map/ppermute | solution.py:23
  71.3 1.8 %collective-permute-start.15 = (bf16[128,1024]{1,0:T(8,128)(2,1)S(1)}, bf16[128,1024]{1,0:T(8,128)(2,1)S(1)}, u32[]{:S(2)}, u32[]{:S(2)}) collective-permute-start(bf16[128,1024]{1,0:T(8,128)(2,1)S(1)} %get-tuple-element.25), channel_id=1, source_target_pairs={{0,14},{1,15},{2,0},{3,1},{4,2},{5,3},{6,4},{7,5},{8,6},{9,7},{10,... | collective-permute-start | bytes 786440 | tf_op jit(solution)/shard_map/ppermute | solution.py:26
  73.2 1.0 collective-permute-done.4
  74.2 1.7 %collective-permute-start.8 = (bf16[128,1024]{1,0:T(8,128)(2,1)S(1)}, bf16[128,1024]{1,0:T(8,128)(2,1)S(1)}, u32[]{:S(2)}, u32[]{:S(2)}) collective-permute-start(bf16[128,1024]{1,0:T(8,128)(2,1)S(1)} %get-tuple-element.31), channel_id=1, source_target_pairs={{0,14},{1,15},{2,0},{3,1},{4,2},{5,3},{6,4},{7,5},{8,6},{9,7},{10,... | collective-permute-start | bytes 786440 | tf_op jit(solution)/shard_map/ppermute | solution.py:26
  76.0 1.1 collective-permute-start.12
  77.2 5.0 %collective-permute-done.19 = bf16[384,512]{1,0:T(8,128)(2,1)S(1)} collective-permute-done((bf16[384,512]{1,0:T(8,128)(2,1)S(1)}, bf16[384,512]{1,0:T(8,128)(2,1)S(1)}, u32[]{:S(2)}, u32[]{:S(2)}) %collective-permute-start.19) | collective-permute-done | bytes 393248 | tf_op jit(solution)/shard_map/ppermute | solution.py:123
  82.2 1.9 %collective-permute-start.5 = (bf16[128,1024]{1,0:T(8,128)(2,1)S(1)}, bf16[128,1024]{1,0:T(8,128)(2,1)S(1)}, u32[]{:S(2)}, u32[]{:S(2)}) collective-permute-start(bf16[128,1024]{1,0:T(8,128)(2,1)S(1)} %fusion.44), channel_id=1, source_target_pairs={{0,2},{1,3},{2,4},{3,5},{4,6},{5,7},{6,8},{7,9},{8,10},{9,11},{10,... | collective-permute-start | bytes 786440 | tf_op jit(solution)/shard_map/ppermute | solution.py:23
  84.1 1.2 fusion.71
  85.3 0.2 fusion.38
  85.6 3.2 %collective-permute-start.13 = (bf16[128,1024]{1,0:T(8,128)(2,1)S(1)}, bf16[128,1024]{1,0:T(8,128)(2,1)S(1)}, u32[]{:S(2)}, u32[]{:S(2)}) collective-permute-start(bf16[128,1024]{1,0:T(8,128)(2,1)S(1)} %get-tuple-element.22), channel_id=1, source_target_pairs={{0,2},{1,3},{2,4},{3,5},{4,6},{5,7},{6,8},{7,9},{8,10},{9,11},{10,... | collective-permute-start | bytes 786440 | tf_op jit(solution)/shard_map/ppermute | solution.py:23
  88.8 0.1 collective-permute-start.16
  88.9 3.8 %collective-permute-done.5 = bf16[128,1024]{1,0:T(8,128)(2,1)S(1)} collective-permute-done((bf16[128,1024]{1,0:T(8,128)(2,1)S(1)}, bf16[128,1024]{1,0:T(8,128)(2,1)S(1)}, u32[]{:S(2)}, u32[]{:S(2)}) %collective-permute-start.5) | collective-permute-done | bytes 262176 | tf_op jit(solution)/shard_map/ppermute | solution.py:23
  92.6 0.2 fusion.43
  92.8 1.3 %collective-permute-start.6 = (bf16[128,1024]{1,0:T(8,128)(2,1)S(1)}, bf16[128,1024]{1,0:T(8,128)(2,1)S(1)}, u32[]{:S(2)}, u32[]{:S(2)}) collective-permute-start(bf16[128,1024]{1,0:T(8,128)(2,1)S(1)} %get-tuple-element.28), channel_id=1, source_target_pairs={{0,2},{1,3},{2,4},{3,5},{4,6},{5,7},{6,8},{7,9},{8,10},{9,11},{10,... | collective-permute-start | bytes 786440 | tf_op jit(solution)/shard_map/ppermute | solution.py:23
  94.2 2.0 %collective-permute-start.9 = (bf16[128,1024]{1,0:T(8,128)(2,1)S(1)}, bf16[128,1024]{1,0:T(8,128)(2,1)S(1)}, u32[]{:S(2)}, u32[]{:S(2)}) collective-permute-start(bf16[128,1024]{1,0:T(8,128)(2,1)S(1)} %get-tuple-element.29), channel_id=1, source_target_pairs={{0,14},{1,15},{2,0},{3,1},{4,2},{5,3},{6,4},{7,5},{8,6},{9,7},{10,... | collective-permute-start | bytes 786440 | tf_op jit(solution)/shard_map/ppermute | solution.py:26
  96.2 1.5 %fusion.70 = (f32[1,384,512]{2,1,0:T(8,128)}, bf16[384,512]{1,0:T(8,128)(2,1)S(1)}) fusion(f32[384,512]{1,0:T(8,128)S(1)} %get-tuple-element.10, f32[1,384,512]{2,1,0:T(8,128)S(1)} %copy-done.4, f32[384,512]{1,0:T(8,128)S(1)} %copy-done.3, f32[1,384,512]{2,1,0:T(8,128)S(1)} %copy-done.2, f32[1,384,512]{2,1,0:T(8,128)S(1)} %copy-done), kind=kLoop, calls=%fused_computation.112 | loop fusion | flops 3342336 | bytes 5111808 | tf_op jit(solution)/shard_map/broadcast_in_dim | solution.py:149
  97.7 0.2 fusion.37
  97.9 1.2 collective-permute-start.14
  99.1 2.1 %collective-permute-start.17 = (bf16[128,1024]{1,0:T(8,128)(2,1)S(1)}, bf16[128,1024]{1,0:T(8,128)(2,1)S(1)}, u32[]{:S(2)}, u32[]{:S(2)}) collective-permute-start(bf16[128,1024]{1,0:T(8,128)(2,1)S(1)} %get-tuple-element.21), channel_id=1, source_target_pairs={{0,14},{1,15},{2,0},{3,1},{4,2},{5,3},{6,4},{7,5},{8,6},{9,7},{10,... | collective-permute-start | bytes 786440 | tf_op jit(solution)/shard_map/ppermute | solution.py:26
  101.3 0.2 fusion.42
  101.5 2.6 %collective-permute-start.10 = (bf16[128,1024]{1,0:T(8,128)(2,1)S(1)}, bf16[128,1024]{1,0:T(8,128)(2,1)S(1)}, u32[]{:S(2)}, u32[]{:S(2)}) collective-permute-start(bf16[128,1024]{1,0:T(8,128)(2,1)S(1)} %get-tuple-element.27), channel_id=1, source_target_pairs={{0,14},{1,15},{2,0},{3,1},{4,2},{5,3},{6,4},{7,5},{8,6},{9,7},{10,... | collective-permute-start | bytes 786440 | tf_op jit(solution)/shard_map/ppermute | solution.py:26
  104.1 2.4 %collective-permute-start.22 = (bf16[384,512]{1,0:T(8,128)(2,1)S(1)}, bf16[384,512]{1,0:T(8,128)(2,1)S(1)}, u32[]{:S(2)}, u32[]{:S(2)}) collective-permute-start(bf16[384,512]{1,0:T(8,128)(2,1)S(1)} %add_convert_fusion), channel_id=1, source_target_pairs={{0,128},{64,192},{128,0},{192,64},{1,129},{65,193},{129,1},{193,65... | collective-permute-start | bytes 1179656 | tf_op jit(solution)/shard_map/ppermute | solution.py:143
  106.5 1.8 %collective-permute-done.14 = bf16[128,1024]{1,0:T(8,128)(2,1)S(1)} collective-permute-done((bf16[128,1024]{1,0:T(8,128)(2,1)S(1)}, bf16[128,1024]{1,0:T(8,128)(2,1)S(1)}, u32[]{:S(2)}, u32[]{:S(2)}) %collective-permute-start.14) | collective-permute-done | bytes 262176 | tf_op jit(solution)/shard_map/ppermute | solution.py:23
  108.3 0.5 collective-permute-done.17
  108.9 3.9 %collective-permute-done.10 = bf16[128,1024]{1,0:T(8,128)(2,1)S(1)} collective-permute-done((bf16[128,1024]{1,0:T(8,128)(2,1)S(1)}, bf16[128,1024]{1,0:T(8,128)(2,1)S(1)}, u32[]{:S(2)}, u32[]{:S(2)}) %collective-permute-start.10) | collective-permute-done | bytes 262176 | tf_op jit(solution)/shard_map/ppermute | solution.py:26
  112.8 0.7 collective-permute-done.7
  113.7 1.9 %collective-permute-done.22 = bf16[384,512]{1,0:T(8,128)(2,1)S(1)} collective-permute-done((bf16[384,512]{1,0:T(8,128)(2,1)S(1)}, bf16[384,512]{1,0:T(8,128)(2,1)S(1)}, u32[]{:S(2)}, u32[]{:S(2)}) %collective-permute-start.22) | collective-permute-done | bytes 393248 | tf_op jit(solution)/shard_map/ppermute | solution.py:143
  115.8 0.5 collective-permute-start.23
  116.3 1.4 %multiply_subtract_fusion = (f32[384,512]{1,0:T(8,128)}, f32[384,512]{1,0:T(8,128)}) fusion(f32[384,512]{1,0:T(8,128)S(1)} %copy-done.3, f32[384,512]{1,0:T(8,128)S(1)} %convert_add_fusion, f32[384,512]{1,0:T(8,128)S(1)} %copy-done.5), kind=kLoop, calls=%fused_computation.47 | loop fusion | flops 1376256 | bytes 3932160 | tf_op jit(solution)/shard_map/sub | solution.py:148
  117.7 4.5 %collective-permute-done.23 = bf16[64,2048]{1,0:T(8,128)(2,1)S(1)} collective-permute-done((bf16[64,2048]{1,0:T(8,128)(2,1)S(1)}, bf16[64,2048]{1,0:T(8,128)(2,1)S(1)}, u32[]{:S(2)}, u32[]{:S(2)}) %collective-permute-start.23) | collective-permute-done | bytes 262176 | tf_op jit(solution)/shard_map/ppermute | solution.py:54
  122.2 0.7 fusion.69
  (41 shorter events, 1.0 us)
Async XLA Ops:
  0.6 2.4 %copy-start = (f32[1,384,512]{2,1,0:T(8,128)S(1)}, f32[1,384,512]{2,1,0:T(8,128)}, u32[]{:S(2)}) copy-start(f32[1,384,512]{2,1,0:T(8,128)} %param.13) | copy-start | bytes 2359300
  4.2 29.1 %collective-permute-start = (bf16[512,1152]{0,1:T(8,128)(2,1)}, bf16[512,1152]{0,1:T(8,128)(2,1)S(1)}, u32[]{:S(2)}, u32[]{:S(2)}) collective-permute-start(bf16[512,1152]{0,1:T(8,128)(2,1)} %pad_maximum_fusion), channel_id=1, source_target_pairs={{0,16},{16,32},{32,48},{48,0},{1,17},{17,33},{33,49},{49,1},{2,18}... | collective-permute-start | bytes 3538952 | tf_op jit(solution)/shard_map/ppermute | solution.py:81
  5.7 28.0 %collective-permute-start.1 = (bf16[512,1152]{0,1:T(8,128)(2,1)}, bf16[512,1152]{0,1:T(8,128)(2,1)}, u32[]{:S(2)}, u32[]{:S(2)}) collective-permute-start(bf16[512,1152]{0,1:T(8,128)(2,1)} %pad_maximum_fusion), channel_id=1, source_target_pairs={{0,48},{16,0},{32,16},{48,32},{1,49},{17,1},{33,17},{49,33},{2,50}... | collective-permute-start | bytes 3538952 | tf_op jit(solution)/shard_map/ppermute | solution.py:82
  7.5 2.2 %copy-start.6 = (bf16[1,1024,2048]{2,1,0:T(8,128)(2,1)S(1)}, bf16[1,1024,2048]{2,1,0:T(8,128)(2,1)}, u32[]{:S(2)}) copy-start(bf16[1,1024,2048]{2,1,0:T(8,128)(2,1)} %param.9) | copy-start | bytes 12582916
  9.7 2.2 %copy-start.1 = (bf16[1,1024,2048]{2,1,0:T(8,128)(2,1)S(1)}, bf16[1,1024,2048]{2,1,0:T(8,128)(2,1)}, u32[]{:S(2)}) copy-start(bf16[1,1024,2048]{2,1,0:T(8,128)(2,1)} %param.10) | copy-start | bytes 12582916
  33.4 15.5 %collective-permute-start.2 = (bf16[256,1152]{0,1:T(8,128)(2,1)S(1)}, bf16[256,1152]{0,1:T(8,128)(2,1)S(1)}, u32[]{:S(2)}, u32[]{:S(2)}) collective-permute-start(bf16[256,1152]{0,1:T(8,128)(2,1)S(1)} %slice.65), channel_id=1, source_target_pairs={{0,16},{16,32},{32,48},{48,0},{1,17},{17,33},{33,49},{49,1},{2,18}... | collective-permute-start | bytes 1769480 | tf_op jit(solution)/shard_map/ppermute | solution.py:83
  34.9 14.6 %collective-permute-start.3 = (bf16[256,1152]{0,1:T(8,128)(2,1)S(1)}, bf16[256,1152]{0,1:T(8,128)(2,1)S(1)}, u32[]{:S(2)}, u32[]{:S(2)}) collective-permute-start(bf16[256,1152]{0,1:T(8,128)(2,1)S(1)} %slice.67), channel_id=1, source_target_pairs={{0,48},{16,0},{32,16},{48,32},{1,49},{17,1},{33,17},{49,33},{2,50}... | collective-permute-start | bytes 1769480 | tf_op jit(solution)/shard_map/ppermute | solution.py:84
  58.1 13.2 %collective-permute-start.11 = (bf16[128,1024]{1,0:T(8,128)(2,1)S(1)}, bf16[128,1024]{1,0:T(8,128)(2,1)S(1)}, u32[]{:S(2)}, u32[]{:S(2)}) collective-permute-start(bf16[128,1024]{1,0:T(8,128)(2,1)S(1)} %get-tuple-element.24), channel_id=1, source_target_pairs={{0,2},{1,3},{2,4},{3,5},{4,6},{5,7},{6,8},{7,9},{8,10},{9,11},{10,... | collective-permute-start | bytes 786440 | tf_op jit(solution)/shard_map/ppermute | solution.py:23
  60.1 24.0 %copy-start.2 = (f32[1,384,512]{2,1,0:T(8,128)S(1)}, f32[1,384,512]{2,1,0:T(8,128)}, u32[]{:S(2)}) copy-start(f32[1,384,512]{2,1,0:T(8,128)} %param.15) | copy-start | bytes 2359300
  60.1 14.0 %collective-permute-start.4 = (bf16[128,1024]{1,0:T(8,128)(2,1)S(1)}, bf16[128,1024]{1,0:T(8,128)(2,1)S(1)}, u32[]{:S(2)}, u32[]{:S(2)}) collective-permute-start(bf16[128,1024]{1,0:T(8,128)(2,1)S(1)} %get-tuple-element.30), channel_id=1, source_target_pairs={{0,2},{1,3},{2,4},{3,5},{4,6},{5,7},{6,8},{7,9},{8,10},{9,11},{10,... | collective-permute-start | bytes 786440 | tf_op jit(solution)/shard_map/ppermute | solution.py:23
  62.3 13.7 %collective-permute-start.18 = (bf16[384,512]{1,0:T(8,128)(2,1)S(1)}, bf16[384,512]{1,0:T(8,128)(2,1)S(1)}, u32[]{:S(2)}, u32[]{:S(2)}) collective-permute-start(bf16[384,512]{1,0:T(8,128)(2,1)S(1)} %get-tuple-element.17), channel_id=1, source_target_pairs={{0,16},{16,32},{32,48},{48,0},{1,17},{17,33},{33,49},{49,1},{2,18}... | collective-permute-start | bytes 1179656 | tf_op jit(solution)/shard_map/ppermute | solution.py:123
  63.5 18.7 %collective-permute-start.19 = (bf16[384,512]{1,0:T(8,128)(2,1)S(1)}, bf16[384,512]{1,0:T(8,128)(2,1)S(1)}, u32[]{:S(2)}, u32[]{:S(2)}) collective-permute-start(bf16[384,512]{1,0:T(8,128)(2,1)S(1)} %get-tuple-element.19), channel_id=1, source_target_pairs={{0,32},{16,48},{32,0},{48,16},{1,33},{17,49},{33,1},{49,17},{2,34}... | collective-permute-start | bytes 1179656 | tf_op jit(solution)/shard_map/ppermute | solution.py:123
  67.6 16.5 %collective-permute-start.20 = (bf16[384,512]{1,0:T(8,128)(2,1)S(1)}, bf16[384,512]{1,0:T(8,128)(2,1)S(1)}, u32[]{:S(2)}, u32[]{:S(2)}) collective-permute-start(bf16[384,512]{1,0:T(8,128)(2,1)S(1)} %get-tuple-element.18), channel_id=1, source_target_pairs={{0,48},{16,0},{32,16},{48,32},{1,49},{17,1},{33,17},{49,33},{2,50}... | collective-permute-start | bytes 1179656 | tf_op jit(solution)/shard_map/ppermute | solution.py:123
  71.3 14.1 %collective-permute-start.15 = (bf16[128,1024]{1,0:T(8,128)(2,1)S(1)}, bf16[128,1024]{1,0:T(8,128)(2,1)S(1)}, u32[]{:S(2)}, u32[]{:S(2)}) collective-permute-start(bf16[128,1024]{1,0:T(8,128)(2,1)S(1)} %get-tuple-element.25), channel_id=1, source_target_pairs={{0,14},{1,15},{2,0},{3,1},{4,2},{5,3},{6,4},{7,5},{8,6},{9,7},{10,... | collective-permute-start | bytes 786440 | tf_op jit(solution)/shard_map/ppermute | solution.py:26
  74.2 14.7 %collective-permute-start.8 = (bf16[128,1024]{1,0:T(8,128)(2,1)S(1)}, bf16[128,1024]{1,0:T(8,128)(2,1)S(1)}, u32[]{:S(2)}, u32[]{:S(2)}) collective-permute-start(bf16[128,1024]{1,0:T(8,128)(2,1)S(1)} %get-tuple-element.31), channel_id=1, source_target_pairs={{0,14},{1,15},{2,0},{3,1},{4,2},{5,3},{6,4},{7,5},{8,6},{9,7},{10,... | collective-permute-start | bytes 786440 | tf_op jit(solution)/shard_map/ppermute | solution.py:26
  76.0 9.3 %collective-permute-start.12 = (bf16[128,1024]{1,0:T(8,128)(2,1)S(1)}, bf16[128,1024]{1,0:T(8,128)(2,1)S(1)}, u32[]{:S(2)}, u32[]{:S(2)}) collective-permute-start(bf16[128,1024]{1,0:T(8,128)(2,1)S(1)} %fusion.39), channel_id=1, source_target_pairs={{0,2},{1,3},{2,4},{3,5},{4,6},{5,7},{6,8},{7,9},{8,10},{9,11},{10,... | collective-permute-start | bytes 786440 | tf_op jit(solution)/shard_map/ppermute | solution.py:23
  82.2 10.5 %collective-permute-start.5 = (bf16[128,1024]{1,0:T(8,128)(2,1)S(1)}, bf16[128,1024]{1,0:T(8,128)(2,1)S(1)}, u32[]{:S(2)}, u32[]{:S(2)}) collective-permute-start(bf16[128,1024]{1,0:T(8,128)(2,1)S(1)} %fusion.44), channel_id=1, source_target_pairs={{0,2},{1,3},{2,4},{3,5},{4,6},{5,7},{6,8},{7,9},{8,10},{9,11},{10,... | collective-permute-start | bytes 786440 | tf_op jit(solution)/shard_map/ppermute | solution.py:23
  85.3 10.8 %copy-start.3 = (f32[384,512]{1,0:T(8,128)S(1)}, f32[384,512]{1,0:T(8,128)}, u32[]{:S(2)}) copy-start(f32[384,512]{1,0:T(8,128)} %param.16) | copy-start | bytes 2359300
  85.3 10.8 %copy-start.4 = (f32[1,384,512]{2,1,0:T(8,128)S(1)}, f32[1,384,512]{2,1,0:T(8,128)}, u32[]{:S(2)}) copy-start(f32[1,384,512]{2,1,0:T(8,128)} %param.14) | copy-start | bytes 2359300
  85.6 12.2 %collective-permute-start.13 = (bf16[128,1024]{1,0:T(8,128)(2,1)S(1)}, bf16[128,1024]{1,0:T(8,128)(2,1)S(1)}, u32[]{:S(2)}, u32[]{:S(2)}) collective-permute-start(bf16[128,1024]{1,0:T(8,128)(2,1)S(1)} %get-tuple-element.22), channel_id=1, source_target_pairs={{0,2},{1,3},{2,4},{3,5},{4,6},{5,7},{6,8},{7,9},{8,10},{9,11},{10,... | collective-permute-start | bytes 786440 | tf_op jit(solution)/shard_map/ppermute | solution.py:23
  88.8 9.0 %collective-permute-start.16 = (bf16[128,1024]{1,0:T(8,128)(2,1)S(1)}, bf16[128,1024]{1,0:T(8,128)(2,1)S(1)}, u32[]{:S(2)}, u32[]{:S(2)}) collective-permute-start(bf16[128,1024]{1,0:T(8,128)(2,1)S(1)} %get-tuple-element.23), channel_id=1, source_target_pairs={{0,14},{1,15},{2,0},{3,1},{4,2},{5,3},{6,4},{7,5},{8,6},{9,7},{10,... | collective-permute-start | bytes 786440 | tf_op jit(solution)/shard_map/ppermute | solution.py:26
  92.8 8.4 %collective-permute-start.6 = (bf16[128,1024]{1,0:T(8,128)(2,1)S(1)}, bf16[128,1024]{1,0:T(8,128)(2,1)S(1)}, u32[]{:S(2)}, u32[]{:S(2)}) collective-permute-start(bf16[128,1024]{1,0:T(8,128)(2,1)S(1)} %get-tuple-element.28), channel_id=1, source_target_pairs={{0,2},{1,3},{2,4},{3,5},{4,6},{5,7},{6,8},{7,9},{8,10},{9,11},{10,... | collective-permute-start | bytes 786440 | tf_op jit(solution)/shard_map/ppermute | solution.py:23
  94.2 7.1 %collective-permute-start.9 = (bf16[128,1024]{1,0:T(8,128)(2,1)S(1)}, bf16[128,1024]{1,0:T(8,128)(2,1)S(1)}, u32[]{:S(2)}, u32[]{:S(2)}) collective-permute-start(bf16[128,1024]{1,0:T(8,128)(2,1)S(1)} %get-tuple-element.29), channel_id=1, source_target_pairs={{0,14},{1,15},{2,0},{3,1},{4,2},{5,3},{6,4},{7,5},{8,6},{9,7},{10,... | collective-permute-start | bytes 786440 | tf_op jit(solution)/shard_map/ppermute | solution.py:26
  97.7 6.3 %collective-permute-start.21 = (bf16[384,512]{1,0:T(8,128)(2,1)S(1)}, bf16[384,512]{1,0:T(8,128)(2,1)S(1)}, u32[]{:S(2)}, u32[]{:S(2)}) collective-permute-start(bf16[384,512]{1,0:T(8,128)(2,1)S(1)} %get-tuple-element.33), channel_id=1, source_target_pairs={{0,64},{64,0},{128,192},{192,128},{1,65},{65,1},{129,193},{193,129... | collective-permute-start | bytes 1179656 | tf_op jit(solution)/shard_map/ppermute | solution.py:143
  97.9 10.4 %collective-permute-start.14 = (bf16[128,1024]{1,0:T(8,128)(2,1)S(1)}, bf16[128,1024]{1,0:T(8,128)(2,1)S(1)}, u32[]{:S(2)}, u32[]{:S(2)}) collective-permute-start(bf16[128,1024]{1,0:T(8,128)(2,1)S(1)} %get-tuple-element.20), channel_id=1, source_target_pairs={{0,2},{1,3},{2,4},{3,5},{4,6},{5,7},{6,8},{7,9},{8,10},{9,11},{10,... | collective-permute-start | bytes 786440 | tf_op jit(solution)/shard_map/ppermute | solution.py:23
  99.1 9.7 %collective-permute-start.17 = (bf16[128,1024]{1,0:T(8,128)(2,1)S(1)}, bf16[128,1024]{1,0:T(8,128)(2,1)S(1)}, u32[]{:S(2)}, u32[]{:S(2)}) collective-permute-start(bf16[128,1024]{1,0:T(8,128)(2,1)S(1)} %get-tuple-element.21), channel_id=1, source_target_pairs={{0,14},{1,15},{2,0},{3,1},{4,2},{5,3},{6,4},{7,5},{8,6},{9,7},{10,... | collective-permute-start | bytes 786440 | tf_op jit(solution)/shard_map/ppermute | solution.py:26
  101.5 11.4 %collective-permute-start.10 = (bf16[128,1024]{1,0:T(8,128)(2,1)S(1)}, bf16[128,1024]{1,0:T(8,128)(2,1)S(1)}, u32[]{:S(2)}, u32[]{:S(2)}) collective-permute-start(bf16[128,1024]{1,0:T(8,128)(2,1)S(1)} %get-tuple-element.27), channel_id=1, source_target_pairs={{0,14},{1,15},{2,0},{3,1},{4,2},{5,3},{6,4},{7,5},{8,6},{9,7},{10,... | collective-permute-start | bytes 786440 | tf_op jit(solution)/shard_map/ppermute | solution.py:26
  104.0 9.5 %collective-permute-start.7 = (bf16[128,1024]{1,0:T(8,128)(2,1)S(1)}, bf16[128,1024]{1,0:T(8,128)(2,1)S(1)}, u32[]{:S(2)}, u32[]{:S(2)}) collective-permute-start(bf16[128,1024]{1,0:T(8,128)(2,1)S(1)} %get-tuple-element.26), channel_id=1, source_target_pairs={{0,2},{1,3},{2,4},{3,5},{4,6},{5,7},{6,8},{7,9},{8,10},{9,11},{10,... | collective-permute-start | bytes 786440 | tf_op jit(solution)/shard_map/ppermute | solution.py:23
  104.1 11.5 %collective-permute-start.22 = (bf16[384,512]{1,0:T(8,128)(2,1)S(1)}, bf16[384,512]{1,0:T(8,128)(2,1)S(1)}, u32[]{:S(2)}, u32[]{:S(2)}) collective-permute-start(bf16[384,512]{1,0:T(8,128)(2,1)S(1)} %add_convert_fusion), channel_id=1, source_target_pairs={{0,128},{64,192},{128,0},{192,64},{1,129},{65,193},{129,1},{193,65... | collective-permute-start | bytes 1179656 | tf_op jit(solution)/shard_map/ppermute | solution.py:143
  108.9 7.4 %copy-start.5 = (f32[384,512]{1,0:T(8,128)S(1)}, f32[384,512]{1,0:T(8,128)}, u32[]{:S(2)}) copy-start(f32[384,512]{1,0:T(8,128)} %param.17) | copy-start | bytes 2359300
  115.8 6.5 %collective-permute-start.23 = (bf16[64,2048]{1,0:T(8,128)(2,1)S(1)}, bf16[64,2048]{1,0:T(8,128)(2,1)S(1)}, u32[]{:S(2)}, u32[]{:S(2)}) collective-permute-start(bf16[64,2048]{1,0:T(8,128)(2,1)S(1)} %fusion.34), channel_id=1, source_target_pairs={{0,1},{1,0},{2,3},{3,2},{4,5},{5,4},{6,7},{7,6},{8,9},{9,8},{10,11... | collective-permute-start | bytes 786440 | tf_op jit(solution)/shard_map/ppermute | solution.py:54

commit v14 on v9

--- a/solution.py
+++ b/solution.py
@@ -122,9 +122,10 @@
     )
     cols = full_grad.shape[1] // ndp
     grad_down = lax.dynamic_slice_in_dim(full_grad, j * cols, cols, axis=1)
+    sent = full_grad.astype(jnp.bfloat16)
     for s in range(1, ndp):
-        blk = lax.dynamic_slice_in_dim(full_grad, ((j + s) % ndp) * cols, cols, axis=1)
-        got = lax.ppermute(blk.astype(jnp.bfloat16), "dp", _shift(ndp, s))
+        blk = lax.dynamic_slice_in_dim(sent, ((j + s) % ndp) * cols, cols, axis=1)
+        got = lax.ppermute(blk, "dp", _shift(ndp, s))
         grad_down = grad_down + got.astype(jnp.float32)
 
     both = jnp.concatenate([grad_gate, grad_up], axis=1)

time: 122 us -> 123 us (level)
  no operation moved by 1% of the time
where the time goes in v14:
time: 123 us; the launch traced here: 122 us
  waiting for transfers between devices  49.5 us (40%)
  starting transfers between devices  38.5 us (31%)
  matrix products  16 us (13%)
  local copies, waits for them, and re-layouts  9.35 us (8%)
  other arithmetic  7.63 us (6%)
    ppermute x1, waiting for transfers between devices, shards(): from_left = lax.ppermute(shard, 'dp', _shift(ndp, 1))  20.9 us
    ppermute x8, starting transfers between devices, _z_reduce_scatter(): lax.ppermute(send_b.astype(jnp.bfloat16), 'mp', down).astype(jnp.float32)  19.9 us
    ppermute x3, waiting for transfers between devices, shards(): got = lax.ppermute(blk, 'dp', _shift(ndp, s))  8.69 us
    dot_general x5, matrix products, shards(): p1 = jnp.dot(xs, piece[:, :2 * ff], preferred_element_type=jnp.float32)  5.89 us
    unnamed x16, local copies, waits for them, and re-layouts  5.69 us
    ppermute x8, starting transfers between devices, _z_reduce_scatter(): lax.ppermute(send_a.astype(jnp.bfloat16), 'mp', up).astype(jnp.float32)  5.04 us
    ppermute x8, waiting for transfers between devices, _z_reduce_scatter(): lax.ppermute(send_a.astype(jnp.bfloat16), 'mp', up).astype(jnp.float32)  4.74 us
    ppermute x8, waiting for transfers between devices, _z_reduce_scatter(): lax.ppermute(send_b.astype(jnp.bfloat16), 'mp', down).astype(jnp.float32)  4.61 us
  transfers between devices with their start and end apart: 26, of which 12 were waited for; matrix products, arithmetic and copies ran while one was open for 15% of the time, Pallas kernels for 0%

profile of v14, /device:TPU:8, one launch (start us, length us, event | category | flops | bytes accessed | tf_op | source)
XLA Modules:
  0.0 122.1 jit_solution(6189614205137249990)
XLA Ops:
  0.6 1.2 %copy.14 = bf16[1,512,384]{1,2,0:T(8,128)(2,1)S(1)} copy(bf16[1,512,384]{2,1,0:T(8,128)(2,1)} %param.11) | data formatting | bytes 786432 | tf_op args[2]
  1.9 1.2 copy.15
  3.1 1.1 pad_maximum_fusion
  4.2 1.5 %collective-permute-start = (bf16[512,1152]{0,1:T(8,128)(2,1)}, bf16[512,1152]{0,1:T(8,128)(2,1)S(1)}, u32[]{:S(2)}, u32[]{:S(2)}) collective-permute-start(bf16[512,1152]{0,1:T(8,128)(2,1)} %pad_maximum_fusion), channel_id=1, source_target_pairs={{0,16},{16,32},{32,48},{48,0},{1,17},{17,33},{33,49},{49,1},{2,18}... | collective-permute-start | bytes 3538952 | tf_op jit(solution)/shard_map/ppermute | solution.py:85
  5.7 1.7 %collective-permute-start.1 = (bf16[512,1152]{0,1:T(8,128)(2,1)}, bf16[512,1152]{0,1:T(8,128)(2,1)}, u32[]{:S(2)}, u32[]{:S(2)}) collective-permute-start(bf16[512,1152]{0,1:T(8,128)(2,1)} %pad_maximum_fusion), channel_id=1, source_target_pairs={{0,48},{16,0},{32,16},{48,32},{1,49},{17,1},{33,17},{49,33},{2,50}... | collective-permute-start | bytes 3538952 | tf_op jit(solution)/shard_map/ppermute | solution.py:86
  7.5 0.4 broadcast_in_dim.12
  8.0 1.7 %copy-done.6 = bf16[1,1024,2048]{2,1,0:T(8,128)(2,1)S(1)} copy-done((bf16[1,1024,2048]{2,1,0:T(8,128)(2,1)S(1)}, bf16[1,1024,2048]{2,1,0:T(8,128)(2,1)}, u32[]{:S(2)}) %copy-start.6) | copy-done | bytes 4194328
  9.7 1.0 fusion.10
  10.7 1.2 copy-done.1
  11.9 0.6 fusion.16
  12.5 20.9 %collective-permute-done = bf16[512,1152]{0,1:T(8,128)(2,1)S(1)} collective-permute-done((bf16[512,1152]{0,1:T(8,128)(2,1)}, bf16[512,1152]{0,1:T(8,128)(2,1)S(1)}, u32[]{:S(2)}, u32[]{:S(2)}) %collective-permute-start) | collective-permute-done | bytes 1179680 | tf_op jit(solution)/shard_map/ppermute | solution.py:85
  33.4 0.4 collective-permute-start.2
  33.8 1.1 slice.87
  34.9 3.2 %collective-permute-start.3 = (bf16[256,1152]{0,1:T(8,128)(2,1)S(1)}, bf16[256,1152]{0,1:T(8,128)(2,1)S(1)}, u32[]{:S(2)}, u32[]{:S(2)}) collective-permute-start(bf16[256,1152]{0,1:T(8,128)(2,1)S(1)} %slice.87), channel_id=1, source_target_pairs={{0,48},{16,0},{32,16},{48,32},{1,49},{17,1},{33,17},{49,33},{2,50}... | collective-permute-start | bytes 1769480 | tf_op jit(solution)/shard_map/ppermute | solution.py:88
  38.1 2.2 %fusion.6 = f32[1024,768]{0,1:T(8,128)S(1)} fusion(bf16[1,1024,2048]{2,1,0:T(8,128)(2,1)S(1)} %copy-done.6, s32[]{:T(128)S(6)} %select_n.155, bf16[512,1152]{0,1:T(8,128)(2,1)} %collective-permute-done.1), kind=kOutput, calls=%fused_computation.19 | convolution fusion | flops 805306368 | bytes 4980740 | tf_op jit(solution)/shard_map/dot_general | solution.py:104
  40.3 1.6 %fusion.12 = f32[1024,384]{0,1:T(8,128)S(1)} fusion(bf16[1,1024,2048]{2,1,0:T(8,128)(2,1)S(1)} %copy-done.1, s32[]{:T(128)S(6)} %select_n.155, bf16[512,1152]{0,1:T(8,128)(2,1)} %collective-permute-done.1), kind=kOutput, calls=%fused_computation.25 | convolution fusion | flops 402653184 | bytes 3014660 | tf_op jit(solution)/shard_map/dot_general | solution.py:105
  41.9 0.6 fusion.14
  42.6 1.2 %slice_dynamic-update-slice_fusion = bf16[2048,768]{0,1:T(8,128)(2,1)S(1)} fusion(bf16[2048,768]{0,1:T(8,128)(2,1)S(1)} %slice_dynamic-update-slice_fusion.1, s32[]{:T(128)S(6)} %select_n.155, bf16[512,1152]{0,1:T(8,128)(2,1)} %collective-permute-done.1), kind=kLoop, calls=%fused_computation.52 | loop fusion | bytes 1572868 | tf_op jit(solution)/shard_map/dynamic_update_slice | solution.py:108
  43.9 1.0 fusion.8
  44.9 4.0 %collective-permute-done.2 = bf16[256,1152]{0,1:T(8,128)(2,1)S(1)} collective-permute-done((bf16[256,1152]{0,1:T(8,128)(2,1)S(1)}, bf16[256,1152]{0,1:T(8,128)(2,1)S(1)}, u32[]{:S(2)}, u32[]{:S(2)}) %collective-permute-start.2) | collective-permute-done | bytes 589856 | tf_op jit(solution)/shard_map/ppermute | solution.py:87
  49.0 0.4 fusion.59
  49.4 0.6 fusion.53
  50.1 1.1 add_add_fusion
  51.1 1.1 multiply_convert_fusion.2
  52.3 3.8 %convolution_convert_fusion = bf16[1024,2048]{1,0:T(8,128)(2,1)S(1)} fusion(bf16[2048,768]{0,1:T(8,128)(2,1)S(1)} %slice_dynamic-update-slice_fusion.2, bf16[1024,384]{0,1:T(8,128)(2,1)S(1)} %get-tuple-element.14, bf16[1024,384]{0,1:T(8,128)(2,1)S(1)} %get-tuple-element.13), kind=kOutput, calls=%fused_computation.2 | convolution fusion | flops 3226468352 | bytes 8912896 | tf_op jit(solution)/shard_map/dot_general | solution.py:132
  56.1 0.5 fusion.92
  56.7 2.0 %collective-permute-start.12 = (bf16[128,512]{1,0:T(8,128)(2,1)S(1)}, bf16[128,512]{1,0:T(8,128)(2,1)S(1)}, u32[]{:S(2)}, u32[]{:S(2)}) collective-permute-start(bf16[128,512]{1,0:T(8,128)(2,1)S(1)} %get-tuple-element.34), channel_id=1, source_target_pairs={{0,2},{1,3},{2,4},{3,5},{4,6},{5,7},{6,8},{7,9},{8,10},{9,11},{10,... | collective-permute-start | bytes 393224 | tf_op jit(solution)/shard_map/ppermute | solution.py:25
  58.7 4.0 %collective-permute-start.16 = (bf16[128,512]{1,0:T(8,128)(2,1)S(1)}, bf16[128,512]{1,0:T(8,128)(2,1)S(1)}, u32[]{:S(2)}, u32[]{:S(2)}) collective-permute-start(bf16[128,512]{1,0:T(8,128)(2,1)S(1)} %get-tuple-element.35), channel_id=1, source_target_pairs={{0,14},{1,15},{2,0},{3,1},{4,2},{5,3},{6,4},{7,5},{8,6},{9,7},{10,... | collective-permute-start | bytes 393224 | tf_op jit(solution)/shard_map/ppermute | solution.py:26
  62.9 3.2 %collective-permute-start.8 = (bf16[128,512]{1,0:T(8,128)(2,1)S(1)}, bf16[128,512]{1,0:T(8,128)(2,1)S(1)}, u32[]{:S(2)}, u32[]{:S(2)}) collective-permute-start(bf16[128,512]{1,0:T(8,128)(2,1)S(1)} %get-tuple-element.37), channel_id=1, source_target_pairs={{0,14},{1,15},{2,0},{3,1},{4,2},{5,3},{6,4},{7,5},{8,6},{9,7},{10,... | collective-permute-start | bytes 393224 | tf_op jit(solution)/shard_map/ppermute | solution.py:26
  66.1 1.9 %fusion.95 = (bf16[384,2048]{1,0:T(8,128)(2,1)S(1)}, f32[384,2048]{1,0:T(8,128)S(1)}) fusion(bf16[1,1024,2048]{2,1,0:T(8,128)(2,1)S(1)} %copy-done.1, f32[1024,768]{0,1:T(8,128)S(1)} %add_add_fusion), kind=kOutput, calls=%fused_computation.136 | convolution fusion | flops 1613758464 | bytes 12058624 | tf_op jit(solution)/shard_map/dot_general | solution.py:120
  68.2 3.2 %collective-permute-start.17 = (bf16[128,1024]{1,0:T(8,128)(2,1)S(1)}, bf16[128,1024]{1,0:T(8,128)(2,1)S(1)}, u32[]{:S(2)}, u32[]{:S(2)}) collective-permute-start(bf16[128,1024]{1,0:T(8,128)(2,1)S(1)} %get-tuple-element.22), channel_id=1, source_target_pairs={{0,14},{1,15},{2,0},{3,1},{4,2},{5,3},{6,4},{7,5},{8,6},{9,7},{10,... | collective-permute-start | bytes 786440 | tf_op jit(solution)/shard_map/ppermute | solution.py:26
  71.6 3.2 %collective-permute-start.9 = (bf16[128,1024]{1,0:T(8,128)(2,1)S(1)}, bf16[128,1024]{1,0:T(8,128)(2,1)S(1)}, u32[]{:S(2)}, u32[]{:S(2)}) collective-permute-start(bf16[128,1024]{1,0:T(8,128)(2,1)S(1)} %get-tuple-element.28), channel_id=1, source_target_pairs={{0,14},{1,15},{2,0},{3,1},{4,2},{5,3},{6,4},{7,5},{8,6},{9,7},{10,... | collective-permute-start | bytes 786440 | tf_op jit(solution)/shard_map/ppermute | solution.py:26
  74.8 0.1 constant_dynamic-slice_fusion.2
  75.0 0.7 collective-permute-start.20
  75.7 2.0 %collective-permute-done.13 = bf16[128,1024]{1,0:T(8,128)(2,1)S(1)} collective-permute-done((bf16[128,1024]{1,0:T(8,128)(2,1)S(1)}, bf16[128,1024]{1,0:T(8,128)(2,1)S(1)}, u32[]{:S(2)}, u32[]{:S(2)}) %collective-permute-start.13) | collective-permute-done | bytes 262176 | tf_op jit(solution)/shard_map/ppermute | solution.py:25
  77.7 2.1 %collective-permute-start.21 = (bf16[384,512]{1,0:T(8,128)(2,1)S(1)}, bf16[384,512]{1,0:T(8,128)(2,1)S(1)}, u32[]{:S(2)}, u32[]{:S(2)}) collective-permute-start(bf16[384,512]{1,0:T(8,128)(2,1)S(1)} %get-tuple-element.33), channel_id=1, source_target_pairs={{0,32},{16,48},{32,0},{48,16},{1,33},{17,49},{33,1},{49,17},{2,34}... | collective-permute-start | bytes 1179656 | tf_op jit(solution)/shard_map/ppermute | solution.py:128
  79.7 1.1 collective-permute-start.22
  80.8 0.2 fusion.39
  81.0 0.9 collective-permute-start.14
  81.9 2.5 %collective-permute-start.18 = (bf16[128,1024]{1,0:T(8,128)(2,1)S(1)}, bf16[128,1024]{1,0:T(8,128)(2,1)S(1)}, u32[]{:S(2)}, u32[]{:S(2)}) collective-permute-start(bf16[128,1024]{1,0:T(8,128)(2,1)S(1)} %get-tuple-element.20), channel_id=1, source_target_pairs={{0,14},{1,15},{2,0},{3,1},{4,2},{5,3},{6,4},{7,5},{8,6},{9,7},{10,... | collective-permute-start | bytes 786440 | tf_op jit(solution)/shard_map/ppermute | solution.py:26
  84.3 0.2 fusion.46
  84.5 3.7 %collective-permute-done.20 = bf16[384,512]{1,0:T(8,128)(2,1)S(1)} collective-permute-done((bf16[384,512]{1,0:T(8,128)(2,1)S(1)}, bf16[384,512]{1,0:T(8,128)(2,1)S(1)}, u32[]{:S(2)}, u32[]{:S(2)}) %collective-permute-start.20) | collective-permute-done | bytes 393248 | tf_op jit(solution)/shard_map/ppermute | solution.py:128
  88.2 4.7 %collective-permute-done.21 = bf16[384,512]{1,0:T(8,128)(2,1)S(1)} collective-permute-done((bf16[384,512]{1,0:T(8,128)(2,1)S(1)}, bf16[384,512]{1,0:T(8,128)(2,1)S(1)}, u32[]{:S(2)}, u32[]{:S(2)}) %collective-permute-start.21) | collective-permute-done | bytes 393248 | tf_op jit(solution)/shard_map/ppermute | solution.py:128
  93.0 0.3 collective-permute-done.22
  93.3 1.2 %fusion.75 = (f32[1,384,512]{2,1,0:T(8,128)}, f32[384,512]{1,0:T(8,128)S(1)}) fusion(f32[1,384,512]{2,1,0:T(8,128)S(1)} %copy-done.2, bf16[384,512]{1,0:T(8,128)(2,1)S(1)} %collective-permute-done.22, bf16[384,512]{1,0:T(8,128)(2,1)S(1)} %collective-permute-done.21, bf16[384,512]{1,0:T(8,128)(2,1)S(1)} %collective-permute-done.20, ...), kind=kLoop, calls=%fused_computation.114 | loop fusion | flops 1966080 | bytes 4325380 | tf_op jit(solution)/shard_map/broadcast_in_dim | solution.py:154
  94.5 0.4 copy-done.4
  94.9 1.5 %fusion.74 = (f32[1,384,512]{2,1,0:T(8,128)}, bf16[384,512]{1,0:T(8,128)(2,1)S(1)}) fusion(f32[384,512]{1,0:T(8,128)S(1)} %get-tuple-element.10, f32[1,384,512]{2,1,0:T(8,128)S(1)} %copy-done.4, f32[384,512]{1,0:T(8,128)S(1)} %copy-done.3, f32[1,384,512]{2,1,0:T(8,128)S(1)} %copy-done.2, f32[1,384,512]{2,1,0:T(8,128)S(1)} %copy-done), kind=kLoop, calls=%fused_computation.113 | loop fusion | flops 3342336 | bytes 5111808 | tf_op jit(solution)/shard_map/broadcast_in_dim | solution.py:154
  96.4 0.2 fusion.38
  96.7 1.3 %collective-permute-start.15 = (bf16[128,1024]{1,0:T(8,128)(2,1)S(1)}, bf16[128,1024]{1,0:T(8,128)(2,1)S(1)}, u32[]{:S(2)}, u32[]{:S(2)}) collective-permute-start(bf16[128,1024]{1,0:T(8,128)(2,1)S(1)} %get-tuple-element.17), channel_id=1, source_target_pairs={{0,2},{1,3},{2,4},{3,5},{4,6},{5,7},{6,8},{7,9},{8,10},{9,11},{10,... | collective-permute-start | bytes 786440 | tf_op jit(solution)/shard_map/ppermute | solution.py:25
  98.0 2.3 %collective-permute-start.19 = (bf16[128,1024]{1,0:T(8,128)(2,1)S(1)}, bf16[128,1024]{1,0:T(8,128)(2,1)S(1)}, u32[]{:S(2)}, u32[]{:S(2)}) collective-permute-start(bf16[128,1024]{1,0:T(8,128)(2,1)S(1)} %get-tuple-element.18), channel_id=1, source_target_pairs={{0,14},{1,15},{2,0},{3,1},{4,2},{5,3},{6,4},{7,5},{8,6},{9,7},{10,... | collective-permute-start | bytes 786440 | tf_op jit(solution)/shard_map/ppermute | solution.py:26
  100.2 0.3 collective-permute-done.6
  100.6 0.2 fusion.45
  100.8 1.5 %collective-permute-start.11 = (bf16[128,1024]{1,0:T(8,128)(2,1)S(1)}, bf16[128,1024]{1,0:T(8,128)(2,1)S(1)}, u32[]{:S(2)}, u32[]{:S(2)}) collective-permute-start(bf16[128,1024]{1,0:T(8,128)(2,1)S(1)} %get-tuple-element.24), channel_id=1, source_target_pairs={{0,14},{1,15},{2,0},{3,1},{4,2},{5,3},{6,4},{7,5},{8,6},{9,7},{10,... | collective-permute-start | bytes 786440 | tf_op jit(solution)/shard_map/ppermute | solution.py:26
  102.3 0.6 collective-permute-start.7
  103.0 2.4 %collective-permute-start.24 = (bf16[384,512]{1,0:T(8,128)(2,1)S(1)}, bf16[384,512]{1,0:T(8,128)(2,1)S(1)}, u32[]{:S(2)}, u32[]{:S(2)}) collective-permute-start(bf16[384,512]{1,0:T(8,128)(2,1)S(1)} %add_convert_fusion), channel_id=1, source_target_pairs={{0,128},{64,192},{128,0},{192,64},{1,129},{65,193},{129,1},{193,65... | collective-permute-start | bytes 1179656 | tf_op jit(solution)/shard_map/ppermute | solution.py:148
  105.4 1.9 %collective-permute-done.15 = bf16[128,1024]{1,0:T(8,128)(2,1)S(1)} collective-permute-done((bf16[128,1024]{1,0:T(8,128)(2,1)S(1)}, bf16[128,1024]{1,0:T(8,128)(2,1)S(1)}, u32[]{:S(2)}, u32[]{:S(2)}) %collective-permute-start.15) | collective-permute-done | bytes 262176 | tf_op jit(solution)/shard_map/ppermute | solution.py:25
  107.3 0.1 fusion.41
  107.4 4.6 %collective-permute-done.11 = bf16[128,1024]{1,0:T(8,128)(2,1)S(1)} collective-permute-done((bf16[128,1024]{1,0:T(8,128)(2,1)S(1)}, bf16[128,1024]{1,0:T(8,128)(2,1)S(1)}, u32[]{:S(2)}, u32[]{:S(2)}) %collective-permute-start.11) | collective-permute-done | bytes 262176 | tf_op jit(solution)/shard_map/ppermute | solution.py:26
  112.0 0.5 collective-permute-done.7
  112.7 2.0 %collective-permute-done.24 = bf16[384,512]{1,0:T(8,128)(2,1)S(1)} collective-permute-done((bf16[384,512]{1,0:T(8,128)(2,1)S(1)}, bf16[384,512]{1,0:T(8,128)(2,1)S(1)}, u32[]{:S(2)}, u32[]{:S(2)}) %collective-permute-start.24) | collective-permute-done | bytes 393248 | tf_op jit(solution)/shard_map/ppermute | solution.py:148
  114.8 0.5 collective-permute-start.25
  115.4 1.4 %multiply_subtract_fusion = (f32[384,512]{1,0:T(8,128)}, f32[384,512]{1,0:T(8,128)}) fusion(f32[384,512]{1,0:T(8,128)S(1)} %copy-done.3, f32[384,512]{1,0:T(8,128)S(1)} %convert_add_fusion, f32[384,512]{1,0:T(8,128)S(1)} %copy-done.5), kind=kLoop, calls=%fused_computation.47 | loop fusion | flops 1376256 | bytes 3932160 | tf_op jit(solution)/shard_map/sub | solution.py:153
  116.8 4.6 %collective-permute-done.25 = bf16[64,2048]{1,0:T(8,128)(2,1)S(1)} collective-permute-done((bf16[64,2048]{1,0:T(8,128)(2,1)S(1)}, bf16[64,2048]{1,0:T(8,128)(2,1)S(1)}, u32[]{:S(2)}, u32[]{:S(2)}) %collective-permute-start.25) | collective-permute-done | bytes 262176 | tf_op jit(solution)/shard_map/ppermute | solution.py:58
  121.4 0.7 fusion.73
  (46 shorter events, 1.3 us)
Async XLA Ops:
  0.6 2.4 %copy-start = (f32[1,384,512]{2,1,0:T(8,128)S(1)}, f32[1,384,512]{2,1,0:T(8,128)}, u32[]{:S(2)}) copy-start(f32[1,384,512]{2,1,0:T(8,128)} %param.13) | copy-start | bytes 2359300
  4.2 29.1 %collective-permute-start = (bf16[512,1152]{0,1:T(8,128)(2,1)}, bf16[512,1152]{0,1:T(8,128)(2,1)S(1)}, u32[]{:S(2)}, u32[]{:S(2)}) collective-permute-start(bf16[512,1152]{0,1:T(8,128)(2,1)} %pad_maximum_fusion), channel_id=1, source_target_pairs={{0,16},{16,32},{32,48},{48,0},{1,17},{17,33},{33,49},{49,1},{2,18}... | collective-permute-start | bytes 3538952 | tf_op jit(solution)/shard_map/ppermute | solution.py:85
  5.7 28.0 %collective-permute-start.1 = (bf16[512,1152]{0,1:T(8,128)(2,1)}, bf16[512,1152]{0,1:T(8,128)(2,1)}, u32[]{:S(2)}, u32[]{:S(2)}) collective-permute-start(bf16[512,1152]{0,1:T(8,128)(2,1)} %pad_maximum_fusion), channel_id=1, source_target_pairs={{0,48},{16,0},{32,16},{48,32},{1,49},{17,1},{33,17},{49,33},{2,50}... | collective-permute-start | bytes 3538952 | tf_op jit(solution)/shard_map/ppermute | solution.py:86
  7.5 2.2 %copy-start.6 = (bf16[1,1024,2048]{2,1,0:T(8,128)(2,1)S(1)}, bf16[1,1024,2048]{2,1,0:T(8,128)(2,1)}, u32[]{:S(2)}) copy-start(bf16[1,1024,2048]{2,1,0:T(8,128)(2,1)} %param.9) | copy-start | bytes 12582916
  9.7 2.2 %copy-start.1 = (bf16[1,1024,2048]{2,1,0:T(8,128)(2,1)S(1)}, bf16[1,1024,2048]{2,1,0:T(8,128)(2,1)}, u32[]{:S(2)}) copy-start(bf16[1,1024,2048]{2,1,0:T(8,128)(2,1)} %param.10) | copy-start | bytes 12582916
  33.4 15.5 %collective-permute-start.2 = (bf16[256,1152]{0,1:T(8,128)(2,1)S(1)}, bf16[256,1152]{0,1:T(8,128)(2,1)S(1)}, u32[]{:S(2)}, u32[]{:S(2)}) collective-permute-start(bf16[256,1152]{0,1:T(8,128)(2,1)S(1)} %slice.85), channel_id=1, source_target_pairs={{0,16},{16,32},{32,48},{48,0},{1,17},{17,33},{33,49},{49,1},{2,18}... | collective-permute-start | bytes 1769480 | tf_op jit(solution)/shard_map/ppermute | solution.py:87
  34.9 15.1 %collective-permute-start.3 = (bf16[256,1152]{0,1:T(8,128)(2,1)S(1)}, bf16[256,1152]{0,1:T(8,128)(2,1)S(1)}, u32[]{:S(2)}, u32[]{:S(2)}) collective-permute-start(bf16[256,1152]{0,1:T(8,128)(2,1)S(1)} %slice.87), channel_id=1, source_target_pairs={{0,48},{16,0},{32,16},{48,32},{1,49},{17,1},{33,17},{49,33},{2,50}... | collective-permute-start | bytes 1769480 | tf_op jit(solution)/shard_map/ppermute | solution.py:88
  56.7 11.3 %collective-permute-start.12 = (bf16[128,512]{1,0:T(8,128)(2,1)S(1)}, bf16[128,512]{1,0:T(8,128)(2,1)S(1)}, u32[]{:S(2)}, u32[]{:S(2)}) collective-permute-start(bf16[128,512]{1,0:T(8,128)(2,1)S(1)} %get-tuple-element.34), channel_id=1, source_target_pairs={{0,2},{1,3},{2,4},{3,5},{4,6},{5,7},{6,8},{7,9},{8,10},{9,11},{10,... | collective-permute-start | bytes 393224 | tf_op jit(solution)/shard_map/ppermute | solution.py:25
  58.7 9.3 %collective-permute-start.16 = (bf16[128,512]{1,0:T(8,128)(2,1)S(1)}, bf16[128,512]{1,0:T(8,128)(2,1)S(1)}, u32[]{:S(2)}, u32[]{:S(2)}) collective-permute-start(bf16[128,512]{1,0:T(8,128)(2,1)S(1)} %get-tuple-element.35), channel_id=1, source_target_pairs={{0,14},{1,15},{2,0},{3,1},{4,2},{5,3},{6,4},{7,5},{8,6},{9,7},{10,... | collective-permute-start | bytes 393224 | tf_op jit(solution)/shard_map/ppermute | solution.py:26
  62.8 8.6 %collective-permute-start.4 = (bf16[128,512]{1,0:T(8,128)(2,1)S(1)}, bf16[128,512]{1,0:T(8,128)(2,1)S(1)}, u32[]{:S(2)}, u32[]{:S(2)}) collective-permute-start(bf16[128,512]{1,0:T(8,128)(2,1)S(1)} %get-tuple-element.36), channel_id=1, source_target_pairs={{0,2},{1,3},{2,4},{3,5},{4,6},{5,7},{6,8},{7,9},{8,10},{9,11},{10,... | collective-permute-start | bytes 393224 | tf_op jit(solution)/shard_map/ppermute | solution.py:25
  62.9 8.6 %collective-permute-start.8 = (bf16[128,512]{1,0:T(8,128)(2,1)S(1)}, bf16[128,512]{1,0:T(8,128)(2,1)S(1)}, u32[]{:S(2)}, u32[]{:S(2)}) collective-permute-start(bf16[128,512]{1,0:T(8,128)(2,1)S(1)} %get-tuple-element.37), channel_id=1, source_target_pairs={{0,14},{1,15},{2,0},{3,1},{4,2},{5,3},{6,4},{7,5},{8,6},{9,7},{10,... | collective-permute-start | bytes 393224 | tf_op jit(solution)/shard_map/ppermute | solution.py:26
  68.1 9.5 %collective-permute-start.13 = (bf16[128,1024]{1,0:T(8,128)(2,1)S(1)}, bf16[128,1024]{1,0:T(8,128)(2,1)S(1)}, u32[]{:S(2)}, u32[]{:S(2)}) collective-permute-start(bf16[128,1024]{1,0:T(8,128)(2,1)S(1)} %get-tuple-element.21), channel_id=1, source_target_pairs={{0,2},{1,3},{2,4},{3,5},{4,6},{5,7},{6,8},{7,9},{8,10},{9,11},{10,... | collective-permute-start | bytes 786440 | tf_op jit(solution)/shard_map/ppermute | solution.py:25
  68.2 11.5 %collective-permute-start.17 = (bf16[128,1024]{1,0:T(8,128)(2,1)S(1)}, bf16[128,1024]{1,0:T(8,128)(2,1)S(1)}, u32[]{:S(2)}, u32[]{:S(2)}) collective-permute-start(bf16[128,1024]{1,0:T(8,128)(2,1)S(1)} %get-tuple-element.22), channel_id=1, source_target_pairs={{0,14},{1,15},{2,0},{3,1},{4,2},{5,3},{6,4},{7,5},{8,6},{9,7},{10,... | collective-permute-start | bytes 786440 | tf_op jit(solution)/shard_map/ppermute | solution.py:26
  71.5 9.5 %collective-permute-start.5 = (bf16[128,1024]{1,0:T(8,128)(2,1)S(1)}, bf16[128,1024]{1,0:T(8,128)(2,1)S(1)}, u32[]{:S(2)}, u32[]{:S(2)}) collective-permute-start(bf16[128,1024]{1,0:T(8,128)(2,1)S(1)} %get-tuple-element.27), channel_id=1, source_target_pairs={{0,2},{1,3},{2,4},{3,5},{4,6},{5,7},{6,8},{7,9},{8,10},{9,11},{10,... | collective-permute-start | bytes 786440 | tf_op jit(solution)/shard_map/ppermute | solution.py:25
  71.6 10.3 %collective-permute-start.9 = (bf16[128,1024]{1,0:T(8,128)(2,1)S(1)}, bf16[128,1024]{1,0:T(8,128)(2,1)S(1)}, u32[]{:S(2)}, u32[]{:S(2)}) collective-permute-start(bf16[128,1024]{1,0:T(8,128)(2,1)S(1)} %get-tuple-element.28), channel_id=1, source_target_pairs={{0,14},{1,15},{2,0},{3,1},{4,2},{5,3},{6,4},{7,5},{8,6},{9,7},{10,... | collective-permute-start | bytes 786440 | tf_op jit(solution)/shard_map/ppermute | solution.py:26
  75.0 18.3 %copy-start.2 = (f32[1,384,512]{2,1,0:T(8,128)S(1)}, f32[1,384,512]{2,1,0:T(8,128)}, u32[]{:S(2)}) copy-start(f32[1,384,512]{2,1,0:T(8,128)} %param.15) | copy-start | bytes 2359300
  75.0 13.3 %collective-permute-start.20 = (bf16[384,512]{1,0:T(8,128)(2,1)S(1)}, bf16[384,512]{1,0:T(8,128)(2,1)S(1)}, u32[]{:S(2)}, u32[]{:S(2)}) collective-permute-start(bf16[384,512]{1,0:T(8,128)(2,1)S(1)} %get-tuple-element.31), channel_id=1, source_target_pairs={{0,16},{16,32},{32,48},{48,0},{1,17},{17,33},{33,49},{49,1},{2,18}... | collective-permute-start | bytes 1179656 | tf_op jit(solution)/shard_map/ppermute | solution.py:128
  77.7 15.3 %collective-permute-start.21 = (bf16[384,512]{1,0:T(8,128)(2,1)S(1)}, bf16[384,512]{1,0:T(8,128)(2,1)S(1)}, u32[]{:S(2)}, u32[]{:S(2)}) collective-permute-start(bf16[384,512]{1,0:T(8,128)(2,1)S(1)} %get-tuple-element.33), channel_id=1, source_target_pairs={{0,32},{16,48},{32,0},{48,16},{1,33},{17,49},{33,1},{49,17},{2,34}... | collective-permute-start | bytes 1179656 | tf_op jit(solution)/shard_map/ppermute | solution.py:128
  79.7 13.5 %collective-permute-start.22 = (bf16[384,512]{1,0:T(8,128)(2,1)S(1)}, bf16[384,512]{1,0:T(8,128)(2,1)S(1)}, u32[]{:S(2)}, u32[]{:S(2)}) collective-permute-start(bf16[384,512]{1,0:T(8,128)(2,1)S(1)} %get-tuple-element.32), channel_id=1, source_target_pairs={{0,48},{16,0},{32,16},{48,32},{1,49},{17,1},{33,17},{49,33},{2,50}... | collective-permute-start | bytes 1179656 | tf_op jit(solution)/shard_map/ppermute | solution.py:128
  81.0 15.4 %collective-permute-start.14 = (bf16[128,1024]{1,0:T(8,128)(2,1)S(1)}, bf16[128,1024]{1,0:T(8,128)(2,1)S(1)}, u32[]{:S(2)}, u32[]{:S(2)}) collective-permute-start(bf16[128,1024]{1,0:T(8,128)(2,1)S(1)} %get-tuple-element.19), channel_id=1, source_target_pairs={{0,2},{1,3},{2,4},{3,5},{4,6},{5,7},{6,8},{7,9},{8,10},{9,11},{10,... | collective-permute-start | bytes 786440 | tf_op jit(solution)/shard_map/ppermute | solution.py:25
  81.9 14.6 %collective-permute-start.18 = (bf16[128,1024]{1,0:T(8,128)(2,1)S(1)}, bf16[128,1024]{1,0:T(8,128)(2,1)S(1)}, u32[]{:S(2)}, u32[]{:S(2)}) collective-permute-start(bf16[128,1024]{1,0:T(8,128)(2,1)S(1)} %get-tuple-element.20), channel_id=1, source_target_pairs={{0,14},{1,15},{2,0},{3,1},{4,2},{5,3},{6,4},{7,5},{8,6},{9,7},{10,... | collective-permute-start | bytes 786440 | tf_op jit(solution)/shard_map/ppermute | solution.py:26
  88.2 12.0 %collective-permute-start.10 = (bf16[128,1024]{1,0:T(8,128)(2,1)S(1)}, bf16[128,1024]{1,0:T(8,128)(2,1)S(1)}, u32[]{:S(2)}, u32[]{:S(2)}) collective-permute-start(bf16[128,1024]{1,0:T(8,128)(2,1)S(1)} %get-tuple-element.26), channel_id=1, source_target_pairs={{0,14},{1,15},{2,0},{3,1},{4,2},{5,3},{6,4},{7,5},{8,6},{9,7},{10,... | collective-permute-start | bytes 786440 | tf_op jit(solution)/shard_map/ppermute | solution.py:26
  93.0 7.6 %collective-permute-start.6 = (bf16[128,1024]{1,0:T(8,128)(2,1)S(1)}, bf16[128,1024]{1,0:T(8,128)(2,1)S(1)}, u32[]{:S(2)}, u32[]{:S(2)}) collective-permute-start(bf16[128,1024]{1,0:T(8,128)(2,1)S(1)} %get-tuple-element.25), channel_id=1, source_target_pairs={{0,2},{1,3},{2,4},{3,5},{4,6},{5,7},{6,8},{7,9},{8,10},{9,11},{10,... | collective-permute-start | bytes 786440 | tf_op jit(solution)/shard_map/ppermute | solution.py:25
  93.3 1.2 %copy-start.3 = (f32[384,512]{1,0:T(8,128)S(1)}, f32[384,512]{1,0:T(8,128)}, u32[]{:S(2)}) copy-start(f32[384,512]{1,0:T(8,128)} %param.16) | copy-start | bytes 2359300
  93.3 1.6 %copy-start.4 = (f32[1,384,512]{2,1,0:T(8,128)S(1)}, f32[1,384,512]{2,1,0:T(8,128)}, u32[]{:S(2)}) copy-start(f32[1,384,512]{2,1,0:T(8,128)} %param.14) | copy-start | bytes 2359300
  96.4 6.4 %collective-permute-start.23 = (bf16[384,512]{1,0:T(8,128)(2,1)S(1)}, bf16[384,512]{1,0:T(8,128)(2,1)S(1)}, u32[]{:S(2)}, u32[]{:S(2)}) collective-permute-start(bf16[384,512]{1,0:T(8,128)(2,1)S(1)} %get-tuple-element.30), channel_id=1, source_target_pairs={{0,64},{64,0},{128,192},{192,128},{1,65},{65,1},{129,193},{193,129... | collective-permute-start | bytes 1179656 | tf_op jit(solution)/shard_map/ppermute | solution.py:148
  96.7 10.7 %collective-permute-start.15 = (bf16[128,1024]{1,0:T(8,128)(2,1)S(1)}, bf16[128,1024]{1,0:T(8,128)(2,1)S(1)}, u32[]{:S(2)}, u32[]{:S(2)}) collective-permute-start(bf16[128,1024]{1,0:T(8,128)(2,1)S(1)} %get-tuple-element.17), channel_id=1, source_target_pairs={{0,2},{1,3},{2,4},{3,5},{4,6},{5,7},{6,8},{7,9},{8,10},{9,11},{10,... | collective-permute-start | bytes 786440 | tf_op jit(solution)/shard_map/ppermute | solution.py:25
  98.0 9.3 %collective-permute-start.19 = (bf16[128,1024]{1,0:T(8,128)(2,1)S(1)}, bf16[128,1024]{1,0:T(8,128)(2,1)S(1)}, u32[]{:S(2)}, u32[]{:S(2)}) collective-permute-start(bf16[128,1024]{1,0:T(8,128)(2,1)S(1)} %get-tuple-element.18), channel_id=1, source_target_pairs={{0,14},{1,15},{2,0},{3,1},{4,2},{5,3},{6,4},{7,5},{8,6},{9,7},{10,... | collective-permute-start | bytes 786440 | tf_op jit(solution)/shard_map/ppermute | solution.py:26
  100.8 11.3 %collective-permute-start.11 = (bf16[128,1024]{1,0:T(8,128)(2,1)S(1)}, bf16[128,1024]{1,0:T(8,128)(2,1)S(1)}, u32[]{:S(2)}, u32[]{:S(2)}) collective-permute-start(bf16[128,1024]{1,0:T(8,128)(2,1)S(1)} %get-tuple-element.24), channel_id=1, source_target_pairs={{0,14},{1,15},{2,0},{3,1},{4,2},{5,3},{6,4},{7,5},{8,6},{9,7},{10,... | collective-permute-start | bytes 786440 | tf_op jit(solution)/shard_map/ppermute | solution.py:26
  102.3 10.3 %collective-permute-start.7 = (bf16[128,1024]{1,0:T(8,128)(2,1)S(1)}, bf16[128,1024]{1,0:T(8,128)(2,1)S(1)}, u32[]{:S(2)}, u32[]{:S(2)}) collective-permute-start(bf16[128,1024]{1,0:T(8,128)(2,1)S(1)} %get-tuple-element.23), channel_id=1, source_target_pairs={{0,2},{1,3},{2,4},{3,5},{4,6},{5,7},{6,8},{7,9},{8,10},{9,11},{10,... | collective-permute-start | bytes 786440 | tf_op jit(solution)/shard_map/ppermute | solution.py:25
  103.0 11.8 %collective-permute-start.24 = (bf16[384,512]{1,0:T(8,128)(2,1)S(1)}, bf16[384,512]{1,0:T(8,128)(2,1)S(1)}, u32[]{:S(2)}, u32[]{:S(2)}) collective-permute-start(bf16[384,512]{1,0:T(8,128)(2,1)S(1)} %add_convert_fusion), channel_id=1, source_target_pairs={{0,128},{64,192},{128,0},{192,64},{1,129},{65,193},{129,1},{193,65... | collective-permute-start | bytes 1179656 | tf_op jit(solution)/shard_map/ppermute | solution.py:148
  107.4 7.9 %copy-start.5 = (f32[384,512]{1,0:T(8,128)S(1)}, f32[384,512]{1,0:T(8,128)}, u32[]{:S(2)}) copy-start(f32[384,512]{1,0:T(8,128)} %param.17) | copy-start | bytes 2359300
  114.8 6.5 %collective-permute-start.25 = (bf16[64,2048]{1,0:T(8,128)(2,1)S(1)}, bf16[64,2048]{1,0:T(8,128)(2,1)S(1)}, u32[]{:S(2)}, u32[]{:S(2)}) collective-permute-start(bf16[64,2048]{1,0:T(8,128)(2,1)S(1)} %fusion.34), channel_id=1, source_target_pairs={{0,1},{1,0},{2,3},{3,2},{4,5},{5,4},{6,7},{7,6},{8,9},{9,8},{10,11... | collective-permute-start | bytes 786440 | tf_op jit(solution)/shard_map/ppermute | solution.py:58

commit v15 on v9

--- a/solution.py
+++ b/solution.py
@@ -82,14 +82,18 @@
     shard = jnp.concatenate([gate_weight[0], up_weight[0], down_half.T], axis=1)
     rows = shard.shape[0]
     half = rows // 2
-    from_left = lax.ppermute(shard, "dp", _shift(ndp, 1))
-    from_right = lax.ppermute(shard, "dp", _shift(ndp, -1))
-    far_a = lax.ppermute(from_left[:half], "dp", _shift(ndp, 1))
-    far_b = lax.ppermute(from_right[half:], "dp", _shift(ndp, -1))
+    left_a = lax.ppermute(shard[:half], "dp", _shift(ndp, 1))
+    right_b = lax.ppermute(shard[half:], "dp", _shift(ndp, -1))
+    left_b = lax.ppermute(shard[half:], "dp", _shift(ndp, 1))
+    right_a = lax.ppermute(shard[:half], "dp", _shift(ndp, -1))
+    far_a = lax.ppermute(left_a, "dp", _shift(ndp, 1))
+    far_b = lax.ppermute(right_b, "dp", _shift(ndp, -1))
     pieces = [
         (j * rows, shard),
-        (((j - 1) % ndp) * rows, from_left),
-        (((j + 1) % ndp) * rows, from_right),
+        (((j - 1) % ndp) * rows, left_a),
+        (((j - 1) % ndp) * rows + half, left_b),
+        (((j + 1) % ndp) * rows, right_a),
+        (((j + 1) % ndp) * rows + half, right_b),
         (((j + 2) % ndp) * rows, far_a),
         (((j + 2) % ndp) * rows + half, far_b),
     ]

time: 122 us -> 132 us (1.082)
  matrix products: 16 us -> 38.2 us
  waiting for transfers between devices: 49.4 us -> 33.7 us
  starting transfers between devices: 38.6 us -> 43.8 us
  local copies, waits for them, and re-layouts: 8.98 us -> 7.08 us
    dot_general x5 -> x7, matrix products: 4.44 us -> 19.4 us  [shards(): p2 = jnp.dot(gs, piece[:, 2 * ff:], preferred_element_type=jnp.float32)]
    ppermute x4 -> x6, waiting for transfers between devices: 24.9 us -> 12.2 us  [the longest x1 9.39 us: shards(): far_a = lax.ppermute(left_a, 'dp', _shift(ndp, 1))]
    dot_general x5 -> x7, matrix products: 5.88 us -> 13.1 us  [shards(): p1 = jnp.dot(xs, piece[:, :2 * ff], preferred_element_type=jnp.float32)]
    ppermute x3, waiting for transfers between devices: 8.68 us -> 2.61 us  [shards(): got = lax.ppermute(blk.astype(jnp.bfloat16), 'dp', _shift(ndp, s))]
    ppermute x4 -> x6, starting transfers between devices: 6.81 us -> 10.9 us  [the longest x1 3.59 us: shards(): far_b = lax.ppermute(right_b, 'dp', _shift(ndp, -1))]
    ppermute x8, starting transfers between devices: 19.5 us -> 22.8 us  [_z_reduce_scatter(): lax.ppermute(send_b.astype(jnp.bfloat16), 'mp', down).astype(jnp.float32)]
    ppermute x8, waiting for transfers between devices: 4.66 us -> 7.65 us  [_z_reduce_scatter(): lax.ppermute(send_a.astype(jnp.bfloat16), 'mp', up).astype(jnp.float32)]
    unnamed x16 -> x22, local copies, waits for them, and re-layouts: 5.29 us -> 2.58 us
  transfers between devices with their start and end apart: 26 -> 28, of which waited for: 12 -> 13; matrix products, arithmetic and copies ran while one was open for 15% -> 27% of each run, Pallas kernels for 0% -> 0%
where the time goes in v15:
time: 132 us
  starting transfers between devices  43.8 us (33%)
  matrix products  38.2 us (29%)
  waiting for transfers between devices  33.7 us (26%)
  other arithmetic  7.79 us (6%)
  local copies, waits for them, and re-layouts  7.08 us (5%)
    ppermute x8, starting transfers between devices, _z_reduce_scatter(): lax.ppermute(send_b.astype(jnp.bfloat16), 'mp', down).astype(jnp.float32)  22.8 us
    dot_general x7, matrix products, shards(): p2 = jnp.dot(gs, piece[:, 2 * ff:], preferred_element_type=jnp.float32)  19.4 us
    dot_general x7, matrix products, shards(): p1 = jnp.dot(xs, piece[:, :2 * ff], preferred_element_type=jnp.float32)  13.1 us
    ppermute x1, waiting for transfers between devices, shards(): far_a = lax.ppermute(left_a, 'dp', _shift(ndp, 1))  9.39 us
    ppermute x8, waiting for transfers between devices, _z_reduce_scatter(): lax.ppermute(send_a.astype(jnp.bfloat16), 'mp', up).astype(jnp.float32)  7.65 us
    ppermute x8, starting transfers between devices, _z_reduce_scatter(): lax.ppermute(send_a.astype(jnp.bfloat16), 'mp', up).astype(jnp.float32)  5.29 us
    ppermute x8, waiting for transfers between devices, _z_reduce_scatter(): lax.ppermute(send_b.astype(jnp.bfloat16), 'mp', down).astype(jnp.float32)  4.67 us
    ppermute x1, waiting for transfers between devices, _ring_reduce_scatter(): lax.ppermute(other.astype(jnp.bfloat16), 'mp', [(i, i ^ 1) for i in range...  4.5 us
  transfers between devices with their start and end apart: 28, of which 13 were waited for; matrix products, arithmetic and copies ran while one was open for 27% of the time, Pallas kernels for 0%

profile of v15, /device:TPU:8, one launch (start us, length us, event | category | flops | bytes accessed | tf_op | source)
XLA Modules:
  0.0 131.6 jit_solution(13309621760944258661)
XLA Ops:
  0.6 1.2 copy.14
  1.8 1.2 copy.15
  3.0 1.2 fusion.76
  4.3 1.1 fusion.113
  5.3 2.8 %collective-permute-start.3 = (bf16[256,1152]{0,1:T(8,128)(2,1)}, bf16[256,1152]{0,1:T(8,128)(2,1)S(1)}, u32[]{:S(2)}, u32[]{:S(2)}) collective-permute-start(bf16[256,1152]{0,1:T(8,128)(2,1)} %get-tuple-element.34), channel_id=1, source_target_pairs={{0,48},{16,0},{32,16},{48,32},{1,49},{17,1},{33,17},{49,33},{2,50}... | collective-permute-start | bytes 1769480 | tf_op jit(solution)/shard_map/ppermute | solution.py:86
  8.1 0.8 collective-permute-start
  8.9 2.5 %collective-permute-start.2 = (bf16[256,1152]{0,1:T(8,128)(2,1)}, bf16[256,1152]{0,1:T(8,128)(2,1)}, u32[]{:S(2)}, u32[]{:S(2)}) collective-permute-start(bf16[256,1152]{0,1:T(8,128)(2,1)} %get-tuple-element.35), channel_id=1, source_target_pairs={{0,48},{16,0},{32,16},{48,32},{1,49},{17,1},{33,17},{49,33},{2,50}... | collective-permute-start | bytes 1769480 | tf_op jit(solution)/shard_map/ppermute | solution.py:88
  11.4 0.4 broadcast_in_dim.12
  11.9 4.8 %fusion.6 = f32[1024,768]{0,1:T(8,128)} fusion(bf16[1,1024,2048]{2,1,0:T(8,128)(2,1)} %param.9, s32[]{:T(128)S(6)} %select_n.165, bf16[512,384]{0,1:T(8,128)(2,1)S(1)} %bitcast.156, bf16[512,384]{0,1:T(8,128)(2,1)S(1)} %bitcast.153), kind=kOutput, calls=%fused_computation.19 | convolution fusion | flops 806879232 | bytes 4980740 | tf_op jit(solution)/shard_map/dot_general | solution.py:108
  16.7 3.1 %fusion.8 = f32[1024,384]{0,1:T(8,128)} fusion(bf16[1,1024,2048]{2,1,0:T(8,128)(2,1)} %param.10, s32[]{:T(128)S(6)} %select_n.165, f32[1,384,512]{2,1,0:T(8,128)S(1)} %copy-done), kind=kOutput, calls=%fused_computation.21 | convolution fusion | flops 402849792 | bytes 3407876 | tf_op jit(solution)/shard_map/dot_general | solution.py:109
  19.8 2.4 %collective-permute-done.3 = bf16[256,1152]{0,1:T(8,128)(2,1)S(1)} collective-permute-done((bf16[256,1152]{0,1:T(8,128)(2,1)}, bf16[256,1152]{0,1:T(8,128)(2,1)S(1)}, u32[]{:S(2)}, u32[]{:S(2)}) %collective-permute-start.3) | collective-permute-done | bytes 589856 | tf_op jit(solution)/shard_map/ppermute | solution.py:86
  22.1 3.6 %collective-permute-start.5 = (bf16[256,1152]{0,1:T(8,128)(2,1)S(1)}, bf16[256,1152]{0,1:T(8,128)(2,1)S(1)}, u32[]{:S(2)}, u32[]{:S(2)}) collective-permute-start(bf16[256,1152]{0,1:T(8,128)(2,1)S(1)} %collective-permute-done.3), channel_id=1, source_target_pairs={{0,48},{16,0},{32,16},{48,32},{1,49},{17,1},{33,17},{49,33},{2,50}... | collective-permute-start | bytes 1769480 | tf_op jit(solution)/shard_map/ppermute | solution.py:90
  25.7 1.6 %fusion.41 = f32[1024,768]{0,1:T(8,128)S(1)} fusion(bf16[1,1024,2048]{2,1,0:T(8,128)(2,1)} %param.9, s32[]{:T(128)S(6)} %select_n.171, bf16[256,1152]{0,1:T(8,128)(2,1)S(1)} %collective-permute-done.3), kind=kOutput, calls=%fused_computation.79 | convolution fusion | flops 402653184 | bytes 4063236 | tf_op jit(solution)/shard_map/dot_general | solution.py:108
  27.4 2.8 %fusion.55 = f32[1024,384]{0,1:T(8,128)} fusion(bf16[1,1024,2048]{2,1,0:T(8,128)(2,1)} %param.10, s32[]{:T(128)S(6)} %select_n.171, bf16[256,1152]{0,1:T(8,128)(2,1)S(1)} %collective-permute-done.3), kind=kOutput, calls=%fused_computation.91 | convolution fusion | flops 201326592 | bytes 2293764 | tf_op jit(solution)/shard_map/dot_general | solution.py:109
  30.2 1.6 %fusion.45 = f32[1024,768]{0,1:T(8,128)S(1)} fusion(bf16[1,1024,2048]{2,1,0:T(8,128)(2,1)S(1)} %copy-done.7, s32[]{:T(128)S(6)} %select_n.168, bf16[256,1152]{0,1:T(8,128)(2,1)} %collective-permute-done.1), kind=kOutput, calls=%fused_computation.83 | convolution fusion | flops 402653184 | bytes 4063236 | tf_op jit(solution)/shard_map/dot_general | solution.py:108
  31.8 2.5 %fusion.59 = f32[1024,384]{0,1:T(8,128)} fusion(bf16[1,1024,2048]{2,1,0:T(8,128)(2,1)S(1)} %copy-done.1, s32[]{:T(128)S(6)} %select_n.168, bf16[256,1152]{0,1:T(8,128)(2,1)} %collective-permute-done.1), kind=kOutput, calls=%fused_computation.95 | convolution fusion | flops 201326592 | bytes 2293764 | tf_op jit(solution)/shard_map/dot_general | solution.py:109
  34.3 0.5 collective-permute-done.2
  34.8 2.8 %fusion.57 = f32[1024,384]{0,1:T(8,128)} fusion(bf16[1,1024,2048]{2,1,0:T(8,128)(2,1)S(1)} %copy-done.1, s32[]{:T(128)S(6)} %select_n.170, bf16[256,1152]{0,1:T(8,128)(2,1)} %collective-permute-done.2), kind=kOutput, calls=%fused_computation.93 | convolution fusion | flops 201326592 | bytes 2293764 | tf_op jit(solution)/shard_map/dot_general | solution.py:109
  37.6 1.6 %fusion.43 = f32[1024,768]{0,1:T(8,128)S(1)} fusion(bf16[1,1024,2048]{2,1,0:T(8,128)(2,1)S(1)} %copy-done.7, s32[]{:T(128)S(6)} %select_n.170, bf16[256,1152]{0,1:T(8,128)(2,1)} %collective-permute-done.2), kind=kOutput, calls=%fused_computation.81 | convolution fusion | flops 402653184 | bytes 4063236 | tf_op jit(solution)/shard_map/dot_general | solution.py:108
  39.2 1.2 collective-permute-start.4
  40.5 1.0 slice_dynamic-update-slice_fusion.4
  41.5 1.0 slice_dynamic-update-slice_fusion.3
  42.6 1.6 %fusion.61 = f32[1024,384]{0,1:T(8,128)} fusion(bf16[1,1024,2048]{2,1,0:T(8,128)(2,1)S(1)} %copy-done.1, s32[]{:T(128)S(6)} %select_n.167, bf16[256,1152]{0,1:T(8,128)(2,1)S(1)} %collective-permute-done), kind=kOutput, calls=%fused_computation.97 | convolution fusion | flops 201326592 | bytes 2293764 | tf_op jit(solution)/shard_map/dot_general | solution.py:109
  44.2 0.6 fusion.47
  44.8 9.4 %collective-permute-done.4 = bf16[256,1152]{0,1:T(8,128)(2,1)S(1)} collective-permute-done((bf16[256,1152]{0,1:T(8,128)(2,1)S(1)}, bf16[256,1152]{0,1:T(8,128)(2,1)S(1)}, u32[]{:S(2)}, u32[]{:S(2)}) %collective-permute-start.4) | collective-permute-done | bytes 589856 | tf_op jit(solution)/shard_map/ppermute | solution.py:89
  54.3 1.6 %fusion.53 = f32[1024,384]{0,1:T(8,128)} fusion(bf16[1,1024,2048]{2,1,0:T(8,128)(2,1)S(1)} %copy-done.1, s32[]{:T(128)S(6)} %select_n.173, bf16[256,1152]{0,1:T(8,128)(2,1)S(1)} %collective-permute-done.4), kind=kOutput, calls=%fused_computation.89 | convolution fusion | flops 201326592 | bytes 2293764 | tf_op jit(solution)/shard_map/dot_general | solution.py:109
  55.9 0.6 fusion.39
  56.7 2.2 %add_add_fusion = f32[1024,768]{0,1:T(8,128)S(1)} fusion(f32[1024,768]{0,1:T(8,128)S(1)} %fusion.39, f32[1024,768]{0,1:T(8,128)S(1)} %fusion.41, f32[1024,768]{0,1:T(8,128)S(1)} %fusion.43, f32[1024,768]{0,1:T(8,128)S(1)} %fusion.45, f32[1024,768]{0,1:T(8,128)S(1)} %copy-done.2, f32[1024,768]{0,1:T(8,128)S(1)} %fusion.47, bf16[1,1024,2048]{2,1,0:T(8,128)(2,1)} %param.9, ...), kind=kOutput, calls=%fused_computation.3 | convolution fusion | flops 407371776 | bytes 22937604 | tf_op jit(solution)/shard_map/dot_general | solution.py:108
  59.0 5.1 %multiply_convert_fusion.2 = (bf16[1024,384]{0,1:T(8,128)(2,1)S(1)}, bf16[1024,384]{0,1:T(8,128)(2,1)S(1)}) fusion(f32[1024,768]{0,1:T(8,128)S(1)} %add_add_fusion, bf16[256,1152]{0,1:T(8,128)(2,1)S(1)} %collective-permute-done.5, bf16[1,1024,2048]{2,1,0:T(8,128)(2,1)S(1)} %copy-done.1, s32[]{:T(128)S(6)} %select_n.174, f32[1024,384]{0,1:T(8,128)} %fusion.53, ...), kind=kOutput, calls=%fused_computation.9 | convolution fusion | flops 208797696 | bytes 14876676 | tf_op jit(solution)/shard_map/dot_general | solution.py:109
  64.0 3.8 %convolution_convert_fusion = bf16[1024,2048]{1,0:T(8,128)(2,1)S(1)} fusion(bf16[2048,768]{0,1:T(8,128)(2,1)S(1)} %slice_dynamic-update-slice_fusion, bf16[1024,384]{0,1:T(8,128)(2,1)S(1)} %get-tuple-element.14, bf16[1024,384]{0,1:T(8,128)(2,1)S(1)} %get-tuple-element.13), kind=kOutput, calls=%fused_computation.2 | convolution fusion | flops 3226468352 | bytes 8912896 | tf_op jit(solution)/shard_map/dot_general | solution.py:135
  67.9 0.5 fusion.112
  68.5 2.0 %collective-permute-start.14 = (bf16[128,512]{1,0:T(8,128)(2,1)S(1)}, bf16[128,512]{1,0:T(8,128)(2,1)S(1)}, u32[]{:S(2)}, u32[]{:S(2)}) collective-permute-start(bf16[128,512]{1,0:T(8,128)(2,1)S(1)} %get-tuple-element.36), channel_id=1, source_target_pairs={{0,2},{1,3},{2,4},{3,5},{4,6},{5,7},{6,8},{7,9},{8,10},{9,11},{10,... | collective-permute-start | bytes 393224 | tf_op jit(solution)/shard_map/ppermute | solution.py:25
  70.5 4.0 %collective-permute-start.18 = (bf16[128,512]{1,0:T(8,128)(2,1)S(1)}, bf16[128,512]{1,0:T(8,128)(2,1)S(1)}, u32[]{:S(2)}, u32[]{:S(2)}) collective-permute-start(bf16[128,512]{1,0:T(8,128)(2,1)S(1)} %get-tuple-element.37), channel_id=1, source_target_pairs={{0,14},{1,15},{2,0},{3,1},{4,2},{5,3},{6,4},{7,5},{8,6},{9,7},{10,... | collective-permute-start | bytes 393224 | tf_op jit(solution)/shard_map/ppermute | solution.py:26
  74.5 2.0 %collective-permute-start.10 = (bf16[128,512]{1,0:T(8,128)(2,1)S(1)}, bf16[128,512]{1,0:T(8,128)(2,1)S(1)}, u32[]{:S(2)}, u32[]{:S(2)}) collective-permute-start(bf16[128,512]{1,0:T(8,128)(2,1)S(1)} %get-tuple-element.39), channel_id=1, source_target_pairs={{0,14},{1,15},{2,0},{3,1},{4,2},{5,3},{6,4},{7,5},{8,6},{9,7},{10,... | collective-permute-start | bytes 393224 | tf_op jit(solution)/shard_map/ppermute | solution.py:26
  76.6 1.9 %fusion = f32[384,2048]{1,0:T(8,128)S(1)} fusion(bf16[1,1024,2048]{2,1,0:T(8,128)(2,1)S(1)} %copy-done.1, f32[1024,768]{0,1:T(8,128)S(1)} %add_add_fusion), kind=kOutput, calls=%fused_computation | convolution fusion | flops 1612972032 | bytes 10485760 | tf_op jit(solution)/shard_map/dot_general | solution.py:124
  78.8 3.4 %collective-permute-start.19 = (bf16[128,1024]{1,0:T(8,128)(2,1)S(1)}, bf16[128,1024]{1,0:T(8,128)(2,1)S(1)}, u32[]{:S(2)}, u32[]{:S(2)}) collective-permute-start(bf16[128,1024]{1,0:T(8,128)(2,1)S(1)} %get-tuple-element.25), channel_id=1, source_target_pairs={{0,14},{1,15},{2,0},{3,1},{4,2},{5,3},{6,4},{7,5},{8,6},{9,7},{10,... | collective-permute-start | bytes 786440 | tf_op jit(solution)/shard_map/ppermute | solution.py:26
  82.2 0.9 collective-permute-done.6
  83.2 0.9 collective-permute-start.11
  84.1 1.2 collective-permute-start.7
  85.5 3.2 %collective-permute-done.15 = bf16[128,1024]{1,0:T(8,128)(2,1)S(1)} collective-permute-done((bf16[128,1024]{1,0:T(8,128)(2,1)S(1)}, bf16[128,1024]{1,0:T(8,128)(2,1)S(1)}, u32[]{:S(2)}, u32[]{:S(2)}) %collective-permute-start.15) | collective-permute-done | bytes 262176 | tf_op jit(solution)/shard_map/ppermute | solution.py:25
  88.7 0.7 collective-permute-start.23
  89.4 1.1 collective-permute-start.24
  90.5 0.2 fusion.25
  90.8 0.6 collective-permute-start.16
  91.4 0.6 collective-permute-done.7
  92.0 2.1 %collective-permute-start.20 = (bf16[128,1024]{1,0:T(8,128)(2,1)S(1)}, bf16[128,1024]{1,0:T(8,128)(2,1)S(1)}, u32[]{:S(2)}, u32[]{:S(2)}) collective-permute-start(bf16[128,1024]{1,0:T(8,128)(2,1)S(1)} %get-tuple-element.23), channel_id=1, source_target_pairs={{0,14},{1,15},{2,0},{3,1},{4,2},{5,3},{6,4},{7,5},{8,6},{9,7},{10,... | collective-permute-start | bytes 786440 | tf_op jit(solution)/shard_map/ppermute | solution.py:26
  94.3 2.6 %collective-permute-done.22 = bf16[384,512]{1,0:T(8,128)(2,1)S(1)} collective-permute-done((bf16[384,512]{1,0:T(8,128)(2,1)S(1)}, bf16[384,512]{1,0:T(8,128)(2,1)S(1)}, u32[]{:S(2)}, u32[]{:S(2)}) %collective-permute-start.22) | collective-permute-done | bytes 393248 | tf_op jit(solution)/shard_map/ppermute | solution.py:131
  96.9 6.2 %collective-permute-start.12 = (bf16[128,1024]{1,0:T(8,128)(2,1)S(1)}, bf16[128,1024]{1,0:T(8,128)(2,1)S(1)}, u32[]{:S(2)}, u32[]{:S(2)}) collective-permute-start(bf16[128,1024]{1,0:T(8,128)(2,1)S(1)} %get-tuple-element.29), channel_id=1, source_target_pairs={{0,14},{1,15},{2,0},{3,1},{4,2},{5,3},{6,4},{7,5},{8,6},{9,7},{10,... | collective-permute-start | bytes 786440 | tf_op jit(solution)/shard_map/ppermute | solution.py:26
  103.2 1.3 fusion.87
  104.4 1.5 %fusion.86 = (f32[1,384,512]{2,1,0:T(8,128)}, bf16[384,512]{1,0:T(8,128)(2,1)S(1)}) fusion(f32[384,512]{1,0:T(8,128)S(1)} %get-tuple-element.10, f32[1,384,512]{2,1,0:T(8,128)S(1)} %copy-done.8, f32[384,512]{1,0:T(8,128)S(1)} %copy-done.6, f32[1,384,512]{2,1,0:T(8,128)S(1)} %copy-done.3, f32[1,384,512]{2,1,0:T(8,128)S(1)} %copy-done), kind=kLoop, calls=%fused_computation.130 | loop fusion | flops 3342336 | bytes 5111808 | tf_op jit(solution)/shard_map/broadcast_in_dim | solution.py:157
  106.3 3.3 %collective-permute-start.21 = (bf16[128,1024]{1,0:T(8,128)(2,1)S(1)}, bf16[128,1024]{1,0:T(8,128)(2,1)S(1)}, u32[]{:S(2)}, u32[]{:S(2)}) collective-permute-start(bf16[128,1024]{1,0:T(8,128)(2,1)S(1)} %get-tuple-element.21), channel_id=1, source_target_pairs={{0,14},{1,15},{2,0},{3,1},{4,2},{5,3},{6,4},{7,5},{8,6},{9,7},{10,... | collective-permute-start | bytes 786440 | tf_op jit(solution)/shard_map/ppermute | solution.py:26
  109.6 1.2 collective-permute-done.8
  110.7 0.2 fusion.31
  110.9 0.9 collective-permute-start.13
  111.8 1.2 collective-permute-start.9
  113.1 2.4 %collective-permute-start.26 = (bf16[384,512]{1,0:T(8,128)(2,1)S(1)}, bf16[384,512]{1,0:T(8,128)(2,1)S(1)}, u32[]{:S(2)}, u32[]{:S(2)}) collective-permute-start(bf16[384,512]{1,0:T(8,128)(2,1)S(1)} %add_convert_fusion), channel_id=1, source_target_pairs={{0,128},{64,192},{128,0},{192,64},{1,129},{65,193},{129,1},{193,65... | collective-permute-start | bytes 1179656 | tf_op jit(solution)/shard_map/ppermute | solution.py:151
  115.5 1.1 collective-permute-done.17
  116.8 4.6 %collective-permute-done.13 = bf16[128,1024]{1,0:T(8,128)(2,1)S(1)} collective-permute-done((bf16[128,1024]{1,0:T(8,128)(2,1)S(1)}, bf16[128,1024]{1,0:T(8,128)(2,1)S(1)}, u32[]{:S(2)}, u32[]{:S(2)}) %collective-permute-start.13) | collective-permute-done | bytes 262176 | tf_op jit(solution)/shard_map/ppermute | solution.py:26
  121.4 0.7 collective-permute-done.9
  122.2 2.0 %collective-permute-done.26 = bf16[384,512]{1,0:T(8,128)(2,1)S(1)} collective-permute-done((bf16[384,512]{1,0:T(8,128)(2,1)S(1)}, bf16[384,512]{1,0:T(8,128)(2,1)S(1)}, u32[]{:S(2)}, u32[]{:S(2)}) %collective-permute-start.26) | collective-permute-done | bytes 393248 | tf_op jit(solution)/shard_map/ppermute | solution.py:151
  124.4 0.5 collective-permute-start.27
  124.9 1.4 %multiply_subtract_fusion = (f32[384,512]{1,0:T(8,128)}, f32[384,512]{1,0:T(8,128)}) fusion(f32[384,512]{1,0:T(8,128)S(1)} %copy-done.6, f32[384,512]{1,0:T(8,128)S(1)} %convert_add_fusion, f32[384,512]{1,0:T(8,128)S(1)} %copy-done.9), kind=kLoop, calls=%fused_computation.35 | loop fusion | flops 1376256 | bytes 3932160 | tf_op jit(solution)/shard_map/sub | solution.py:156
  126.3 4.5 %collective-permute-done.27 = bf16[64,2048]{1,0:T(8,128)(2,1)S(1)} collective-permute-done((bf16[64,2048]{1,0:T(8,128)(2,1)S(1)}, bf16[64,2048]{1,0:T(8,128)(2,1)S(1)}, u32[]{:S(2)}, u32[]{:S(2)}) %collective-permute-start.27) | collective-permute-done | bytes 262176 | tf_op jit(solution)/shard_map/ppermute | solution.py:58
  130.8 0.8 fusion.85
  (61 shorter events, 2.3 us)
Async XLA Ops:
  5.3 16.8 %collective-permute-start.3 = (bf16[256,1152]{0,1:T(8,128)(2,1)}, bf16[256,1152]{0,1:T(8,128)(2,1)S(1)}, u32[]{:S(2)}, u32[]{:S(2)}) collective-permute-start(bf16[256,1152]{0,1:T(8,128)(2,1)} %get-tuple-element.34), channel_id=1, source_target_pairs={{0,48},{16,0},{32,16},{48,32},{1,49},{17,1},{33,17},{49,33},{2,50}... | collective-permute-start | bytes 1769480 | tf_op jit(solution)/shard_map/ppermute | solution.py:86
  8.1 22.1 %collective-permute-start.1 = (bf16[256,1152]{0,1:T(8,128)(2,1)}, bf16[256,1152]{0,1:T(8,128)(2,1)}, u32[]{:S(2)}, u32[]{:S(2)}) collective-permute-start(bf16[256,1152]{0,1:T(8,128)(2,1)} %get-tuple-element.34), channel_id=1, source_target_pairs={{0,16},{16,32},{32,48},{48,0},{1,17},{17,33},{33,49},{49,1},{2,18}... | collective-permute-start | bytes 1769480 | tf_op jit(solution)/shard_map/ppermute | solution.py:87
  8.1 31.1 %collective-permute-start = (bf16[256,1152]{0,1:T(8,128)(2,1)}, bf16[256,1152]{0,1:T(8,128)(2,1)S(1)}, u32[]{:S(2)}, u32[]{:S(2)}) collective-permute-start(bf16[256,1152]{0,1:T(8,128)(2,1)} %get-tuple-element.35), channel_id=1, source_target_pairs={{0,16},{16,32},{32,48},{48,0},{1,17},{17,33},{33,49},{49,1},{2,18}... | collective-permute-start | bytes 1769480 | tf_op jit(solution)/shard_map/ppermute | solution.py:85
  8.9 25.9 %collective-permute-start.2 = (bf16[256,1152]{0,1:T(8,128)(2,1)}, bf16[256,1152]{0,1:T(8,128)(2,1)}, u32[]{:S(2)}, u32[]{:S(2)}) collective-permute-start(bf16[256,1152]{0,1:T(8,128)(2,1)} %get-tuple-element.35), channel_id=1, source_target_pairs={{0,48},{16,0},{32,16},{48,32},{1,49},{17,1},{33,17},{49,33},{2,50}... | collective-permute-start | bytes 1769480 | tf_op jit(solution)/shard_map/ppermute | solution.py:88
  11.9 4.8 %copy-start.4 = (bf16[2048,768]{0,1:T(8,128)(2,1)}, bf16[2048,768]{0,1:T(8,128)(2,1)S(1)}, u32[]{:S(2)}) copy-start(bf16[2048,768]{0,1:T(8,128)(2,1)S(1)} %fusion.75) | copy-start | bytes 9437188
  11.9 4.8 %copy-start = (f32[1,384,512]{2,1,0:T(8,128)S(1)}, f32[1,384,512]{2,1,0:T(8,128)}, u32[]{:S(2)}) copy-start(f32[1,384,512]{2,1,0:T(8,128)} %param.13) | copy-start | bytes 2359300
  19.8 10.4 %copy-start.7 = (bf16[1,1024,2048]{2,1,0:T(8,128)(2,1)S(1)}, bf16[1,1024,2048]{2,1,0:T(8,128)(2,1)}, u32[]{:S(2)}) copy-start(bf16[1,1024,2048]{2,1,0:T(8,128)(2,1)} %param.9) | copy-start | bytes 12582916
  22.1 34.3 %collective-permute-start.5 = (bf16[256,1152]{0,1:T(8,128)(2,1)S(1)}, bf16[256,1152]{0,1:T(8,128)(2,1)S(1)}, u32[]{:S(2)}, u32[]{:S(2)}) collective-permute-start(bf16[256,1152]{0,1:T(8,128)(2,1)S(1)} %collective-permute-done.3), channel_id=1, source_target_pairs={{0,48},{16,0},{32,16},{48,32},{1,49},{17,1},{33,17},{49,33},{2,50}... | collective-permute-start | bytes 1769480 | tf_op jit(solution)/shard_map/ppermute | solution.py:90
  27.4 4.4 %copy-start.1 = (bf16[1,1024,2048]{2,1,0:T(8,128)(2,1)S(1)}, bf16[1,1024,2048]{2,1,0:T(8,128)(2,1)}, u32[]{:S(2)}) copy-start(bf16[1,1024,2048]{2,1,0:T(8,128)(2,1)} %param.10) | copy-start | bytes 12582916
  34.3 6.1 %copy-start.5 = (bf16[2048,768]{0,1:T(8,128)(2,1)S(1)}, bf16[2048,768]{0,1:T(8,128)(2,1)}, u32[]{:S(2)}) copy-start(bf16[2048,768]{0,1:T(8,128)(2,1)} %copy-done.4) | copy-start | bytes 9437188
  39.2 15.0 %collective-permute-start.4 = (bf16[256,1152]{0,1:T(8,128)(2,1)S(1)}, bf16[256,1152]{0,1:T(8,128)(2,1)S(1)}, u32[]{:S(2)}, u32[]{:S(2)}) collective-permute-start(bf16[256,1152]{0,1:T(8,128)(2,1)S(1)} %collective-permute-done), channel_id=1, source_target_pairs={{0,16},{16,32},{32,48},{48,0},{1,17},{17,33},{33,49},{49,1},{2,18}... | collective-permute-start | bytes 1769480 | tf_op jit(solution)/shard_map/ppermute | solution.py:89
  54.3 2.5 %copy-start.2 = (f32[1024,768]{0,1:T(8,128)S(1)}, f32[1024,768]{0,1:T(8,128)}, u32[]{:S(2)}) copy-start(f32[1024,768]{0,1:T(8,128)} %fusion.6) | copy-start | bytes 9437188
  68.5 10.1 %collective-permute-start.14 = (bf16[128,512]{1,0:T(8,128)(2,1)S(1)}, bf16[128,512]{1,0:T(8,128)(2,1)S(1)}, u32[]{:S(2)}, u32[]{:S(2)}) collective-permute-start(bf16[128,512]{1,0:T(8,128)(2,1)S(1)} %get-tuple-element.36), channel_id=1, source_target_pairs={{0,2},{1,3},{2,4},{3,5},{4,6},{5,7},{6,8},{7,9},{8,10},{9,11},{10,... | collective-permute-start | bytes 393224 | tf_op jit(solution)/shard_map/ppermute | solution.py:25
  70.5 8.1 %collective-permute-start.18 = (bf16[128,512]{1,0:T(8,128)(2,1)S(1)}, bf16[128,512]{1,0:T(8,128)(2,1)S(1)}, u32[]{:S(2)}, u32[]{:S(2)}) collective-permute-start(bf16[128,512]{1,0:T(8,128)(2,1)S(1)} %get-tuple-element.37), channel_id=1, source_target_pairs={{0,14},{1,15},{2,0},{3,1},{4,2},{5,3},{6,4},{7,5},{8,6},{9,7},{10,... | collective-permute-start | bytes 393224 | tf_op jit(solution)/shard_map/ppermute | solution.py:26
  74.5 7.6 %collective-permute-start.10 = (bf16[128,512]{1,0:T(8,128)(2,1)S(1)}, bf16[128,512]{1,0:T(8,128)(2,1)S(1)}, u32[]{:S(2)}, u32[]{:S(2)}) collective-permute-start(bf16[128,512]{1,0:T(8,128)(2,1)S(1)} %get-tuple-element.39), channel_id=1, source_target_pairs={{0,14},{1,15},{2,0},{3,1},{4,2},{5,3},{6,4},{7,5},{8,6},{9,7},{10,... | collective-permute-start | bytes 393224 | tf_op jit(solution)/shard_map/ppermute | solution.py:26
  76.5 6.5 %collective-permute-start.6 = (bf16[128,512]{1,0:T(8,128)(2,1)S(1)}, bf16[128,512]{1,0:T(8,128)(2,1)S(1)}, u32[]{:S(2)}, u32[]{:S(2)}) collective-permute-start(bf16[128,512]{1,0:T(8,128)(2,1)S(1)} %get-tuple-element.38), channel_id=1, source_target_pairs={{0,2},{1,3},{2,4},{3,5},{4,6},{5,7},{6,8},{7,9},{8,10},{9,11},{10,... | collective-permute-start | bytes 393224 | tf_op jit(solution)/shard_map/ppermute | solution.py:25
  78.6 10.1 %collective-permute-start.15 = (bf16[128,1024]{1,0:T(8,128)(2,1)S(1)}, bf16[128,1024]{1,0:T(8,128)(2,1)S(1)}, u32[]{:S(2)}, u32[]{:S(2)}) collective-permute-start(bf16[128,1024]{1,0:T(8,128)(2,1)S(1)} %get-tuple-element.24), channel_id=1, source_target_pairs={{0,2},{1,3},{2,4},{3,5},{4,6},{5,7},{6,8},{7,9},{8,10},{9,11},{10,... | collective-permute-start | bytes 786440 | tf_op jit(solution)/shard_map/ppermute | solution.py:25
  78.7 24.4 %copy-start.3 = (f32[1,384,512]{2,1,0:T(8,128)S(1)}, f32[1,384,512]{2,1,0:T(8,128)}, u32[]{:S(2)}) copy-start(f32[1,384,512]{2,1,0:T(8,128)} %param.15) | copy-start | bytes 2359300
  78.8 10.6 %collective-permute-start.19 = (bf16[128,1024]{1,0:T(8,128)(2,1)S(1)}, bf16[128,1024]{1,0:T(8,128)(2,1)S(1)}, u32[]{:S(2)}, u32[]{:S(2)}) collective-permute-start(bf16[128,1024]{1,0:T(8,128)(2,1)S(1)} %get-tuple-element.25), channel_id=1, source_target_pairs={{0,14},{1,15},{2,0},{3,1},{4,2},{5,3},{6,4},{7,5},{8,6},{9,7},{10,... | collective-permute-start | bytes 786440 | tf_op jit(solution)/shard_map/ppermute | solution.py:26
  83.2 7.6 %collective-permute-start.11 = (bf16[128,1024]{1,0:T(8,128)(2,1)S(1)}, bf16[128,1024]{1,0:T(8,128)(2,1)S(1)}, u32[]{:S(2)}, u32[]{:S(2)}) collective-permute-start(bf16[128,1024]{1,0:T(8,128)(2,1)S(1)} %get-tuple-element.31), channel_id=1, source_target_pairs={{0,14},{1,15},{2,0},{3,1},{4,2},{5,3},{6,4},{7,5},{8,6},{9,7},{10,... | collective-permute-start | bytes 786440 | tf_op jit(solution)/shard_map/ppermute | solution.py:26
  84.1 7.9 %collective-permute-start.7 = (bf16[128,1024]{1,0:T(8,128)(2,1)S(1)}, bf16[128,1024]{1,0:T(8,128)(2,1)S(1)}, u32[]{:S(2)}, u32[]{:S(2)}) collective-permute-start(bf16[128,1024]{1,0:T(8,128)(2,1)S(1)} %get-tuple-element.30), channel_id=1, source_target_pairs={{0,2},{1,3},{2,4},{3,5},{4,6},{5,7},{6,8},{7,9},{8,10},{9,11},{10,... | collective-permute-start | bytes 786440 | tf_op jit(solution)/shard_map/ppermute | solution.py:25
  85.4 11.5 %collective-permute-start.22 = (bf16[384,512]{1,0:T(8,128)(2,1)S(1)}, bf16[384,512]{1,0:T(8,128)(2,1)S(1)}, u32[]{:S(2)}, u32[]{:S(2)}) collective-permute-start(bf16[384,512]{1,0:T(8,128)(2,1)S(1)} %get-tuple-element.17), channel_id=1, source_target_pairs={{0,16},{16,32},{32,48},{48,0},{1,17},{17,33},{33,49},{49,1},{2,18}... | collective-permute-start | bytes 1179656 | tf_op jit(solution)/shard_map/ppermute | solution.py:131
  88.7 14.4 %collective-permute-start.23 = (bf16[384,512]{1,0:T(8,128)(2,1)S(1)}, bf16[384,512]{1,0:T(8,128)(2,1)S(1)}, u32[]{:S(2)}, u32[]{:S(2)}) collective-permute-start(bf16[384,512]{1,0:T(8,128)(2,1)S(1)} %get-tuple-element.19), channel_id=1, source_target_pairs={{0,32},{16,48},{32,0},{48,16},{1,33},{17,49},{33,1},{49,17},{2,34}... | collective-permute-start | bytes 1179656 | tf_op jit(solution)/shard_map/ppermute | solution.py:131
  89.4 13.7 %collective-permute-start.24 = (bf16[384,512]{1,0:T(8,128)(2,1)S(1)}, bf16[384,512]{1,0:T(8,128)(2,1)S(1)}, u32[]{:S(2)}, u32[]{:S(2)}) collective-permute-start(bf16[384,512]{1,0:T(8,128)(2,1)S(1)} %get-tuple-element.18), channel_id=1, source_target_pairs={{0,48},{16,0},{32,16},{48,32},{1,49},{17,1},{33,17},{49,33},{2,50}... | collective-permute-start | bytes 1179656 | tf_op jit(solution)/shard_map/ppermute | solution.py:131
  90.7 13.7 %copy-start.6 = (f32[384,512]{1,0:T(8,128)S(1)}, f32[384,512]{1,0:T(8,128)}, u32[]{:S(2)}) copy-start(f32[384,512]{1,0:T(8,128)} %param.16) | copy-start | bytes 2359300
  90.8 13.7 %copy-start.8 = (f32[1,384,512]{2,1,0:T(8,128)S(1)}, f32[1,384,512]{2,1,0:T(8,128)}, u32[]{:S(2)}) copy-start(f32[1,384,512]{2,1,0:T(8,128)} %param.14) | copy-start | bytes 2359300
  90.8 15.2 %collective-permute-start.16 = (bf16[128,1024]{1,0:T(8,128)(2,1)S(1)}, bf16[128,1024]{1,0:T(8,128)(2,1)S(1)}, u32[]{:S(2)}, u32[]{:S(2)}) collective-permute-start(bf16[128,1024]{1,0:T(8,128)(2,1)S(1)} %get-tuple-element.22), channel_id=1, source_target_pairs={{0,2},{1,3},{2,4},{3,5},{4,6},{5,7},{6,8},{7,9},{8,10},{9,11},{10,... | collective-permute-start | bytes 786440 | tf_op jit(solution)/shard_map/ppermute | solution.py:25
  92.0 14.0 %collective-permute-start.20 = (bf16[128,1024]{1,0:T(8,128)(2,1)S(1)}, bf16[128,1024]{1,0:T(8,128)(2,1)S(1)}, u32[]{:S(2)}, u32[]{:S(2)}) collective-permute-start(bf16[128,1024]{1,0:T(8,128)(2,1)S(1)} %get-tuple-element.23), channel_id=1, source_target_pairs={{0,14},{1,15},{2,0},{3,1},{4,2},{5,3},{6,4},{7,5},{8,6},{9,7},{10,... | collective-permute-start | bytes 786440 | tf_op jit(solution)/shard_map/ppermute | solution.py:26
  96.9 12.7 %collective-permute-start.12 = (bf16[128,1024]{1,0:T(8,128)(2,1)S(1)}, bf16[128,1024]{1,0:T(8,128)(2,1)S(1)}, u32[]{:S(2)}, u32[]{:S(2)}) collective-permute-start(bf16[128,1024]{1,0:T(8,128)(2,1)S(1)} %get-tuple-element.29), channel_id=1, source_target_pairs={{0,14},{1,15},{2,0},{3,1},{4,2},{5,3},{6,4},{7,5},{8,6},{9,7},{10,... | collective-permute-start | bytes 786440 | tf_op jit(solution)/shard_map/ppermute | solution.py:26
  103.1 7.6 %collective-permute-start.8 = (bf16[128,1024]{1,0:T(8,128)(2,1)S(1)}, bf16[128,1024]{1,0:T(8,128)(2,1)S(1)}, u32[]{:S(2)}, u32[]{:S(2)}) collective-permute-start(bf16[128,1024]{1,0:T(8,128)(2,1)S(1)} %get-tuple-element.28), channel_id=1, source_target_pairs={{0,2},{1,3},{2,4},{3,5},{4,6},{5,7},{6,8},{7,9},{8,10},{9,11},{10,... | collective-permute-start | bytes 786440 | tf_op jit(solution)/shard_map/ppermute | solution.py:25
  106.0 7.1 %collective-permute-start.25 = (bf16[384,512]{1,0:T(8,128)(2,1)S(1)}, bf16[384,512]{1,0:T(8,128)(2,1)S(1)}, u32[]{:S(2)}, u32[]{:S(2)}) collective-permute-start(bf16[384,512]{1,0:T(8,128)(2,1)S(1)} %get-tuple-element.33), channel_id=1, source_target_pairs={{0,64},{64,0},{128,192},{192,128},{1,65},{65,1},{129,193},{193,129... | collective-permute-start | bytes 1179656 | tf_op jit(solution)/shard_map/ppermute | solution.py:151
  106.2 10.5 %collective-permute-start.17 = (bf16[128,1024]{1,0:T(8,128)(2,1)S(1)}, bf16[128,1024]{1,0:T(8,128)(2,1)S(1)}, u32[]{:S(2)}, u32[]{:S(2)}) collective-permute-start(bf16[128,1024]{1,0:T(8,128)(2,1)S(1)} %get-tuple-element.20), channel_id=1, source_target_pairs={{0,2},{1,3},{2,4},{3,5},{4,6},{5,7},{6,8},{7,9},{8,10},{9,11},{10,... | collective-permute-start | bytes 786440 | tf_op jit(solution)/shard_map/ppermute | solution.py:25
  106.3 10.4 %collective-permute-start.21 = (bf16[128,1024]{1,0:T(8,128)(2,1)S(1)}, bf16[128,1024]{1,0:T(8,128)(2,1)S(1)}, u32[]{:S(2)}, u32[]{:S(2)}) collective-permute-start(bf16[128,1024]{1,0:T(8,128)(2,1)S(1)} %get-tuple-element.21), channel_id=1, source_target_pairs={{0,14},{1,15},{2,0},{3,1},{4,2},{5,3},{6,4},{7,5},{8,6},{9,7},{10,... | collective-permute-start | bytes 786440 | tf_op jit(solution)/shard_map/ppermute | solution.py:26
  110.9 10.5 %collective-permute-start.13 = (bf16[128,1024]{1,0:T(8,128)(2,1)S(1)}, bf16[128,1024]{1,0:T(8,128)(2,1)S(1)}, u32[]{:S(2)}, u32[]{:S(2)}) collective-permute-start(bf16[128,1024]{1,0:T(8,128)(2,1)S(1)} %get-tuple-element.27), channel_id=1, source_target_pairs={{0,14},{1,15},{2,0},{3,1},{4,2},{5,3},{6,4},{7,5},{8,6},{9,7},{10,... | collective-permute-start | bytes 786440 | tf_op jit(solution)/shard_map/ppermute | solution.py:26
  111.8 13.1 %copy-start.9 = (f32[384,512]{1,0:T(8,128)S(1)}, f32[384,512]{1,0:T(8,128)}, u32[]{:S(2)}) copy-start(f32[384,512]{1,0:T(8,128)} %param.17) | copy-start | bytes 2359300
  111.8 10.3 %collective-permute-start.9 = (bf16[128,1024]{1,0:T(8,128)(2,1)S(1)}, bf16[128,1024]{1,0:T(8,128)(2,1)S(1)}, u32[]{:S(2)}, u32[]{:S(2)}) collective-permute-start(bf16[128,1024]{1,0:T(8,128)(2,1)S(1)} %get-tuple-element.26), channel_id=1, source_target_pairs={{0,2},{1,3},{2,4},{3,5},{4,6},{5,7},{6,8},{7,9},{8,10},{9,11},{10,... | collective-permute-start | bytes 786440 | tf_op jit(solution)/shard_map/ppermute | solution.py:25
  113.1 11.1 %collective-permute-start.26 = (bf16[384,512]{1,0:T(8,128)(2,1)S(1)}, bf16[384,512]{1,0:T(8,128)(2,1)S(1)}, u32[]{:S(2)}, u32[]{:S(2)}) collective-permute-start(bf16[384,512]{1,0:T(8,128)(2,1)S(1)} %add_convert_fusion), channel_id=1, source_target_pairs={{0,128},{64,192},{128,0},{192,64},{1,129},{65,193},{129,1},{193,65... | collective-permute-start | bytes 1179656 | tf_op jit(solution)/shard_map/ppermute | solution.py:151
  124.4 6.5 %collective-permute-start.27 = (bf16[64,2048]{1,0:T(8,128)(2,1)S(1)}, bf16[64,2048]{1,0:T(8,128)(2,1)S(1)}, u32[]{:S(2)}, u32[]{:S(2)}) collective-permute-start(bf16[64,2048]{1,0:T(8,128)(2,1)S(1)} %fusion.20), channel_id=1, source_target_pairs={{0,1},{1,0},{2,3},{3,2},{4,5},{5,4},{6,7},{7,6},{8,9},{9,8},{10,11... | collective-permute-start | bytes 786440 | tf_op jit(solution)/shard_map/ppermute | solution.py:58
